TPU v7x, 32 devices: a whole 2x2x4 slice. The times are simulated.
32 devices in a mesh: pb: 8 (over z, x), ka: 4 (over y, core).
Axes of the slice: x: 2, y: 2, z: 4, core: 2. Of those that a mesh axis runs over, the one named last changes fastest.
Arguments:
- queries: bfloat16 [8192, 512], P('pb'), may hold values from -80 to 80
- key_cache: bfloat16 [8192, 128], P(('ka', 'pb')), may hold values from -4.1 to 4.1
- value_cache: bfloat16 [8192, 128], P(('ka', 'pb')), may hold values from -4 to 4
- block_list: int32 [64, 32], P('pb'), may hold values from 0 to 63, as said below
- block_count: int32 [64], P('pb'), may hold values from 1 to 32, as said below
Outputs:
- attended: bfloat16 [8192, 512], P(('pb', 'ka'))
Inputs may be any that keep to these rules, and one draw needn't show every extreme that they name: `block_list`: entries of row qb before block_count[qb] are distinct blocks at most qb, and qb itself is among them. They are the blocks v at most qb of one set of 16 vertical blocks, then the blocks qb - o at least 0 (and not already listed) of one set of 16 slash offsets; both sets contain 0 and lie below 16. Later entries equal qb. `block_count`: the number of distinct listed blocks of each query block.
All inputs are finite; a program needn't handle non-finite values.
Results may differ from a plain program's by a relative error of at most 0.0046.
Values may be sent and summed in bfloat16 or wider, within the bound.
No kernel may reach another device: no remote copies, remote signals or barrier semaphores. Data moves between devices by JAX's collectives and lax.ppermute only.
A program may use at most 128 MiB of HBM per device.

v0:
```python
import math

import jax
import jax.numpy as jnp
from jax import lax
from jax.sharding import PartitionSpec as P

HD = 128
QH = 4
BLK = 128
LIST = 32


masked_score = -1e30


def merged(shard, axis, combine):
    everything = jax.tree.map(lambda part: lax.all_gather(part, axis), shard)
    initial = jax.tree.map(lambda part: part[0], everything)

    def lap(k, so_far):
        return combine(so_far, jax.tree.map(lambda part: part[k], everything))

    return lax.fori_loop(1, lax.axis_size(axis), lap, initial)


def combine(first, second):
    peak_first, sum_first, out_first = first
    peak_second, sum_second, out_second = second
    peak_both = jnp.maximum(peak_first, peak_second)
    factor_first = jnp.exp(peak_first - peak_both)
    factor_second = jnp.exp(peak_second - peak_both)
    sum_both = factor_first * sum_first + factor_second * sum_second
    out_both = (
        jnp.repeat(factor_first, HD, axis=1) * out_first
        + jnp.repeat(factor_second, HD, axis=1) * out_second
    )
    return (peak_both, sum_both, out_both)


def shards(queries, key_cache, value_cache, block_list, block_count):
    shard_keys, shard_values = (
        lax.all_gather(key_cache, "pb", axis=0, tiled=True),
        lax.all_gather(value_cache, "pb", axis=0, tiled=True),
    )
    group_index = lax.axis_index("pb")
    shard_index = lax.axis_index("ka")
    ka_width = lax.axis_size("ka")
    score_scale = 1.0 / math.sqrt(HD)
    shard_width = shard_keys.shape[0] // BLK
    local_blocks = queries.shape[0] // BLK
    first_block = shard_index * shard_width
    all_key_tiles = shard_keys.reshape(shard_width, BLK, HD)
    all_value_tiles = shard_values.reshape(shard_width, BLK, HD)
    slot_ids = jnp.arange(LIST, dtype=jnp.int32)
    position = jnp.arange(BLK, dtype=jnp.int32)

    def one_block(block_pos):
        query_rows = lax.dynamic_slice_in_dim(queries, block_pos * BLK, BLK, 0).reshape(BLK, QH, HD)
        listed = lax.dynamic_index_in_dim(block_list, block_pos, 0, keepdims=False)
        live_count = lax.dynamic_index_in_dim(block_count, block_pos, 0, keepdims=False)
        global_pos = group_index * local_blocks + block_pos
        live_slot = slot_ids < live_count
        local_ids = listed - first_block
        tile_live = live_slot & (local_ids >= 0) & (local_ids < shard_width)
        picked = jnp.clip(local_ids, 0, shard_width - 1)
        key_tiles = all_key_tiles[picked]
        value_tiles = all_value_tiles[picked]
        scores = (
            jnp.einsum("qhd,skd->hqsk", query_rows, key_tiles, preferred_element_type=jnp.float32)
            * score_scale
        )
        earlier = (listed < global_pos)[None, :, None]
        diagonal = (listed == global_pos)[None, :, None] & (
            position[None, None, :] <= position[:, None, None]
        )
        valid = tile_live[None, :, None] & (earlier | diagonal)
        masked = jnp.where(valid[None], scores, masked_score)
        peak_row = jnp.max(masked, axis=(2, 3))
        weights = jnp.where(valid[None], jnp.exp(scores - peak_row[..., None, None]), 0.0)
        weight_sum = jnp.sum(weights, axis=(2, 3))
        partial_out = jnp.einsum(
            "hqsk,skd->qhd",
            weights.astype(jnp.bfloat16),
            value_tiles,
            preferred_element_type=jnp.float32,
        )
        return (peak_row.T, weight_sum.T, partial_out.reshape(BLK, QH * HD))

    peaks, sums, outputs = lax.map(one_block, jnp.arange(local_blocks, dtype=jnp.int32))
    peaks = peaks.reshape(local_blocks * BLK, QH)
    sums = sums.reshape(local_blocks * BLK, QH)
    outputs = outputs.reshape(local_blocks * BLK, QH * HD)
    merged_peak, merged_sum, merged_out = merged((peaks, sums, outputs), "ka", combine)
    owned = merged_out.shape[0] // ka_width
    out_share = lax.dynamic_slice_in_dim(merged_out, shard_index * owned, owned, 0)
    sum_share = lax.dynamic_slice_in_dim(merged_sum, shard_index * owned, owned, 0)
    return (out_share / jnp.repeat(sum_share, HD, axis=1)).astype(jnp.bfloat16)


def solution(mesh):
    placed = (P("pb", None), P(("ka", "pb"), None), P(("ka", "pb"), None), P("pb", None), P("pb"))
    return jax.shard_map(
        shards, mesh=mesh, in_specs=placed, out_specs=P(("pb", "ka"), None), check_vma=False
    )
```

profile of v0, /device:TPU:24, one launch (start us, length us, event | category | flops | bytes accessed | tf_op | source)
XLA Modules:
  0.0 291.7 jit_solution(3987702162450489174)
XLA Ops:
  6.5 28.7 %all_gather.15 = bf16[2048,128]{1,0:T(8,128)(2,1)S(1)} all-gather(bf16[256,128]{1,0:T(8,128)(2,1)} %param.10), channel_id=1, replica_groups=mesh['pb'=8,'ka'=4] {'pb'}, dimensions={0}, use_global_device_ids=true | all-gather | bytes 589824 | tf_op jit(solution)/shard_map/all_gather | solution.py:43
  35.3 31.4 %all_gather.16 = bf16[2048,128]{1,0:T(8,128)(2,1)S(1)} all-gather(bf16[256,128]{1,0:T(8,128)(2,1)} %param.11), channel_id=1, replica_groups=mesh['pb'=8,'ka'=4] {'pb'}, dimensions={0}, use_global_device_ids=true | all-gather | bytes 589824 | tf_op jit(solution)/shard_map/all_gather | solution.py:44
  66.7 134.8 %while.37 = (s32[]{:T(128)}, f32[8,128,4]{1,2,0:T(4,128)S(1)}, f32[8,128,4]{1,2,0:T(4,128)S(1)}, f32[8,128,512]{2,1,0:T(8,128)}, s32[8]{0:T(128)S(1)}, /*index=5...) while((s32[]{:T(128)}, f32[8,128,4]{1,2,0:T(4,128)S(1)}, ...), condition=%wide.region_3.4_spmd.clone, body=%wide.region_0.3_spmd.clone.sunk | while | flops 1098400256 | bytes 39769752 | solution.py:90
  70.4 1.3 dynamic_slice.85
  74.0 1.3 or_and_fusion.2
  75.3 1.6 gather_fusion.1
  79.0 1.8 fusion.41
  80.8 1.8 fusion.40
  87.2 1.3 dynamic_slice.85
  90.9 1.3 or_and_fusion.2
  92.2 1.6 gather_fusion.1
  95.8 1.8 fusion.41
  97.7 1.8 fusion.40
  107.8 1.3 or_and_fusion.2
  109.0 1.6 gather_fusion.1
  112.7 1.8 fusion.41
  114.5 1.8 fusion.40
  120.9 1.3 dynamic_slice.85
  124.6 1.3 or_and_fusion.2
  125.9 1.6 gather_fusion.1
  129.6 1.8 fusion.41
  131.4 1.8 fusion.40
  141.5 1.3 or_and_fusion.2
  142.7 1.6 gather_fusion.1
  146.4 1.8 fusion.41
  148.2 1.8 fusion.40
  158.3 1.3 or_and_fusion.2
  159.6 1.6 gather_fusion.1
  163.2 1.8 fusion.41
  165.1 1.8 fusion.40
  171.5 1.3 dynamic_slice.85
  175.1 1.3 or_and_fusion.2
  176.4 1.6 gather_fusion.1
  180.1 1.8 fusion.41
  181.9 1.8 fusion.40
  188.3 1.3 dynamic_slice.85
  192.0 1.3 or_and_fusion.2
  193.3 1.6 gather_fusion.1
  196.9 1.8 fusion.41
  198.7 1.8 fusion.40
  201.5 5.2 %all_gather.17 = f32[4,1024,4]{1,2,0:T(4,128)S(1)} all-gather(f32[1,1024,4]{1,2,0:T(4,128)S(1)} %bitcast.156), channel_id=1, replica_groups=mesh['pb'=8,'ka'=4] {'ka'}, dimensions={0}, use_global_device_ids=true | all-gather | bytes 81920 | tf_op jit(solution)/shard_map/all_gather | solution.py:18
  206.7 5.2 %all_gather.18 = f32[4,1024,4]{1,2,0:T(4,128)S(1)} all-gather(f32[1,1024,4]{1,2,0:T(4,128)S(1)} %bitcast.155), channel_id=1, replica_groups=mesh['pb'=8,'ka'=4] {'ka'}, dimensions={0}, use_global_device_ids=true | all-gather | bytes 81920 | tf_op jit(solution)/shard_map/all_gather | solution.py:18
  211.9 52.0 %all-gather.2.cloned.1.call-done = f32[4,1024,512]{2,1,0:T(8,128)} async-done(((f32[1,1024,512]{2,1,0:T(8,128)}), f32[4,1024,512]{2,1,0:T(8,128)}) %all-gather.2.cloned.1.call-update) | async-done | bytes 8388624 | tf_op jit(solution)/shard_map/all_gather | solution.py:18
  264.0 1.8 slice_bitcast_fusion
  265.7 17.8 %while.36 = (s32[]{:T(128)}, f32[1024,4]{0,1:T(4,128)S(1)}, f32[1024,4]{0,1:T(4,128)S(1)}, f32[1024,512]{1,0:T(8,128)S(1)}, f32[4,1024,4]{1,2,0:T(4,128)S(1)}, /...) while((s32[]{:T(128)}, f32[1024,4]{0,1:T(4,128)S(1)}, ...), condition=%wide.region_5.6_spmd, body=%wide.region_4.5_spmd.sunk | while | flops 1597445 | bytes 14909583 | solution.py:24
  268.7 2.9 %fusion.34 = f32[1024,512]{1,0:T(8,128)S(1)} fusion(f32[128,8,4,128]{3,2,1,0:T(4,128)S(1)} %bitcast.148, f32[1024,512]{1,0:T(8,128)S(1)} %get-tuple-element.648, f32[128,8,4,128]{3,2,1,0:T(4,128)S(1)} %bitcast.147, f32[4,1024,512]{2,1,0:T(8,128)} %get-tuple-element.661, s32[]{:T(128)S(6)} %select_n.78), kind=kLoop, calls=%fused_computation.5.clone.1 | loop fusion | flops 1572864 | bytes 10485764 | tf_op jit(solution)/shard_map/while/body/eval_jaxpr/add | solution.py:35
  274.7 2.9 %fusion.34 = f32[1024,512]{1,0:T(8,128)S(1)} fusion(f32[128,8,4,128]{3,2,1,0:T(4,128)S(1)} %bitcast.148, f32[1024,512]{1,0:T(8,128)S(1)} %get-tuple-element.648, f32[128,8,4,128]{3,2,1,0:T(4,128)S(1)} %bitcast.147, f32[4,1024,512]{2,1,0:T(8,128)} %get-tuple-element.661, s32[]{:T(128)S(6)} %select_n.78), kind=kLoop, calls=%fused_computation.5.clone.1 | loop fusion | flops 1572864 | bytes 10485764 | tf_op jit(solution)/shard_map/while/body/eval_jaxpr/add | solution.py:35
  280.6 2.9 %fusion.34 = f32[1024,512]{1,0:T(8,128)S(1)} fusion(f32[128,8,4,128]{3,2,1,0:T(4,128)S(1)} %bitcast.148, f32[1024,512]{1,0:T(8,128)S(1)} %get-tuple-element.648, f32[128,8,4,128]{3,2,1,0:T(4,128)S(1)} %bitcast.147, f32[4,1024,512]{2,1,0:T(8,128)} %get-tuple-element.661, s32[]{:T(128)S(6)} %select_n.78), kind=kLoop, calls=%fused_computation.5.clone.1 | loop fusion | flops 1572864 | bytes 10485764 | tf_op jit(solution)/shard_map/while/body/eval_jaxpr/add | solution.py:35
  (158 shorter events, 60.7 us)
Async XLA Ops:
  6.5 257.4 %all-gather.2.cloned.1.call-start = ((), (), s32[]{:S(2)}) async-start(), calls=%async_computation | async-start | bytes 10485760 | tf_op jit(solution)/shard_map/all_gather | solution.py:18
  77.7 1.3 copy-start
  94.6 1.3 copy-start
  111.4 1.3 copy-start
  128.3 1.3 copy-start
  145.1 1.3 copy-start
  162.0 1.3 copy-start
  178.8 1.2 copy-start
  195.7 1.3 copy-start
Sparse Core Ops, SparseCore 0:
  201.6 62.3 all-gather.1
where the time goes:
time: 295 us; the launch traced here: 292 us
  blocking collectives  70.6 us (24%)
  local copies, waits for them, and re-layouts  60.2 us (20%)
  waiting for transfers between devices  52 us (18%)
  other arithmetic  45.3 us (15%)
  loops' own time  25.8 us (9%)
  matrix products  24.4 us (8%)
  between operations  13.4 us (5%)
    all_gather x1, waiting for transfers between devices, merged(): everything = jax.tree.map(lambda part: lax.all_gather(part, axis), shard)  52 us
    all_gather x1, blocking collectives, shards(): lax.all_gather(value_cache, 'pb', axis=0, tiled=True)  31.4 us
    all_gather x1, blocking collectives, shards(): lax.all_gather(key_cache, 'pb', axis=0, tiled=True)  28.7 us
    another operation x1, loops' own time, shards(): lax.map(one_block, jnp.arange(local_blocks, dtype=jnp.int32))  25.6 us
    reduce_sum x8, other arithmetic, one_block(): weight_sum = jnp.sum(weights, axis=(2, 3))  14.7 us
    dot_general x8, matrix products, one_block(): jnp.einsum('hqsk,skd->qhd', weights.astype(jnp.bfloat16), value_tiles, pr...  14.5 us
    gather x8, local copies, waits for them, and re-layouts, one_block(): value_tiles = all_value_tiles[picked]  13.2 us
    all_gather x2, blocking collectives, merged(): everything = jax.tree.map(lambda part: lax.all_gather(part, axis), shard)  10.5 us
  transfers between devices with their start and end apart: 1, of which 1 were waited for; matrix products, arithmetic and copies ran while one was open for 0% of the time, Pallas kernels for 0%

commit v1 on v0

v1 whole, which is shorter than its diff:
```python
import functools
import math

import jax
import jax.numpy as jnp
from jax import lax
from jax.experimental import pallas as pl
from jax.experimental.pallas import tpu as pltpu
from jax.sharding import PartitionSpec as P

HD = 128
QH = 4
BLK = 128

masked_score = -1e30


def gather_pb(local, n_pb):
    p = lax.axis_index("pb")
    held = local[None]
    step = 1
    while step < n_pb:
        other = lax.ppermute(held, "pb", [(i, i ^ step) for i in range(n_pb)])
        upper = (p // step) % 2 == 1
        held = jnp.where(
            upper,
            jnp.concatenate([other, held], axis=0),
            jnp.concatenate([held, other], axis=0),
        )
        step *= 2
    return held.reshape(-1, local.shape[1])


def attend_kernel(bl_ref, cnt_ref, qb_ref, q_ref, kv_hbm, out_ref, kvbuf, sems, *, n_local, scale):
    qb0 = qb_ref[0]

    def copy(j, s):
        blk = bl_ref[j, s]
        start = pl.multiple_of(blk * BLK, BLK)
        return pltpu.make_async_copy(kv_hbm.at[pl.ds(start, BLK), :], kvbuf.at[j, s], sems.at[j, s])

    for j in range(n_local):
        def issue(s, c, j=j):
            copy(j, s).start()
            return c

        lax.fori_loop(0, cnt_ref[j], issue, 0)

    rows = QH * BLK
    rowpos = lax.broadcasted_iota(jnp.int32, (rows, BLK), 0) % BLK
    col = lax.broadcasted_iota(jnp.int32, (rows, BLK), 1)
    causal = col <= rowpos

    for j in range(n_local):
        qb = qb0 + j
        qrows = q_ref[j * BLK:(j + 1) * BLK, :]
        qs = jnp.concatenate([qrows[:, h * HD:(h + 1) * HD] for h in range(QH)], axis=0)

        def body(s, carry, j=j, qb=qb, qs=qs):
            m, l, acc = carry
            copy(j, s).wait()
            kvb = kvbuf[j, s]
            k = kvb[:, :HD]
            v = kvb[:, HD:]
            blk = bl_ref[j, s]
            sc = lax.dot_general(qs, k, (((1,), (1,)), ((), ())), preferred_element_type=jnp.float32) * scale
            valid = jnp.logical_or(blk < qb, jnp.logical_and(blk == qb, causal))
            masked = jnp.where(valid, sc, masked_score)
            m_new = jnp.maximum(m, jnp.max(masked, axis=1, keepdims=True))
            alpha = jnp.exp(m - m_new)
            w = jnp.where(valid, jnp.exp(sc - m_new), 0.0)
            l = alpha * l + jnp.sum(w, axis=1, keepdims=True)
            acc = alpha * acc + jnp.dot(w.astype(jnp.bfloat16), v, preferred_element_type=jnp.float32)
            return m_new, l, acc

        init = (
            jnp.full((rows, 1), masked_score, jnp.float32),
            jnp.zeros((rows, 1), jnp.float32),
            jnp.zeros((rows, HD), jnp.float32),
        )
        m, l, acc = lax.fori_loop(0, cnt_ref[j], body, init)
        res = (acc / l).astype(out_ref.dtype)
        for h in range(QH):
            out_ref[j * BLK:(j + 1) * BLK, h * HD:(h + 1) * HD] = res[h * BLK:(h + 1) * BLK, :]


def shards(queries, key_cache, value_cache, block_list, block_count, *, n_pb, n_ka):
    kv_local = jnp.concatenate([key_cache, value_cache], axis=1)
    shard = gather_pb(kv_local, n_pb)
    kv_all = lax.all_gather(shard, "ka", axis=0, tiled=True)

    p = lax.axis_index("pb")
    k = lax.axis_index("ka")
    rows_mine = queries.shape[0] // n_ka
    n_local = rows_mine // BLK
    listed = block_list.shape[1]
    q_mine = lax.dynamic_slice_in_dim(queries, k * rows_mine, rows_mine, 0)
    bl_mine = lax.dynamic_slice_in_dim(block_list, k * n_local, n_local, 0)
    cnt_mine = lax.dynamic_slice_in_dim(block_count, k * n_local, n_local, 0)
    qb0 = ((p * n_ka + k) * n_local).astype(jnp.int32).reshape(1)

    kernel = functools.partial(attend_kernel, n_local=n_local, scale=1.0 / math.sqrt(HD))
    return pl.pallas_call(
        kernel,
        out_shape=jax.ShapeDtypeStruct((rows_mine, queries.shape[1]), jnp.bfloat16),
        grid_spec=pltpu.PrefetchScalarGridSpec(
            num_scalar_prefetch=3,
            grid=(1,),
            in_specs=[
                pl.BlockSpec((rows_mine, queries.shape[1]), lambda i, *_: (0, 0)),
                pl.BlockSpec(memory_space=pl.ANY),
            ],
            out_specs=pl.BlockSpec((rows_mine, queries.shape[1]), lambda i, *_: (0, 0)),
            scratch_shapes=[
                pltpu.VMEM((n_local, listed, BLK, kv_local.shape[1]), jnp.bfloat16),
                pltpu.SemaphoreType.DMA((n_local, listed)),
            ],
        ),
        compiler_params=pltpu.CompilerParams(vmem_limit_bytes=48 * 1024 * 1024),
    )(bl_mine, cnt_mine, qb0, q_mine, kv_all)


def solution(mesh):
    placed = (P("pb", None), P(("ka", "pb"), None), P(("ka", "pb"), None), P("pb", None), P("pb"))
    body = functools.partial(shards, n_pb=mesh.shape["pb"], n_ka=mesh.shape["ka"])
    return jax.shard_map(
        body, mesh=mesh, in_specs=placed, out_specs=P(("pb", "ka"), None), check_vma=False
    )
```

time: 295 us -> 131 us (0.44); the launches traced: 292 us -> 131 us
  blocking collectives: 70.6 us -> 0 us
  local copies, waits for them, and re-layouts: 60.2 us -> 2.98 us
  other arithmetic: 45.3 us -> 2.22 us
  Pallas kernels: 0 us -> 40.7 us
  loops' own time: 25.8 us -> 0 us
  matrix products: 24.4 us -> 0 us
  waiting for transfers between devices: 52 us -> 68.9 us
    all_gather x4 -> x0, blocking collectives: 70.6 us -> none  [the longest x1 31.4 us: shards(): lax.all_gather(value_cache, 'pb', axis=0, tiled=True)]
    pallas_call x0 -> x1, Pallas kernels: none -> 40.7 us  [shards(): pl.pallas_call(kernel, out_shape=jax.ShapeDtypeStruct((rows_mine, queries...]
    ppermute x0 -> x3, waiting for transfers between devices: none -> 34.1 us  [gather_pb(): other = lax.ppermute(held, 'pb', [(i, i ^ step) for i in range(n_pb)])]
    another operation x2 -> x0, loops' own time: 25.8 us -> none  [the longest x1 25.6 us: shards(): lax.map(one_block, jnp.arange(local_blocks, dtype=jnp.int32))]
    dot_general x16 -> x0, matrix products: 24.4 us -> none  [the longest x8 14.5 us: one_block(): jnp.einsum('hqsk,skd->qhd', weights.astype(jnp.bfloat16), value_tiles, pr...]
    dynamic_slice x34 -> x3, local copies, waits for them, and re-layouts: 23.2 us -> 0.79 us  [the longest x1 0.69 us: shards(): bl_mine = lax.dynamic_slice_in_dim(block_list, k * n_local, n_local, 0)]
    gather x16 -> x0, local copies, waits for them, and re-layouts: 19.1 us -> none  [the longest x8 13.2 us: one_block(): value_tiles = all_value_tiles[picked]]
    all_gather x1, waiting for transfers between devices: 52 us -> 34.8 us  [shards(): kv_all = lax.all_gather(shard, 'ka', axis=0, tiled=True)]
  transfers between devices with their start and end apart: 1 -> 4, of which waited for: 1 -> 4; matrix products, arithmetic and copies ran while one was open for 0% -> 1% of each run, Pallas kernels for 0% -> 0%
where the time goes in v1:
time: 131 us
  waiting for transfers between devices  68.9 us (53%)
  Pallas kernels  40.7 us (31%)
  between operations  13.4 us (10%)
  local copies, waits for them, and re-layouts  2.98 us (2%)
  starting transfers between devices  2.47 us (2%)
  other arithmetic  2.22 us (2%)
    pallas_call x1, Pallas kernels, shards(): pl.pallas_call(kernel, out_shape=jax.ShapeDtypeStruct((rows_mine, queries...  40.7 us
    all_gather x1, waiting for transfers between devices, shards(): kv_all = lax.all_gather(shard, 'ka', axis=0, tiled=True)  34.8 us
    ppermute x3, waiting for transfers between devices, gather_pb(): other = lax.ppermute(held, 'pb', [(i, i ^ step) for i in range(n_pb)])  34.1 us
  transfers between devices with their start and end apart: 4, of which 4 were waited for; matrix products, arithmetic and copies ran while one was open for 1% of the time, Pallas kernels for 0%

profile of v1, /device:TPU:24, one launch (start us, length us, event | category | flops | bytes accessed | tf_op | source)
XLA Modules:
  0.0 130.8 jit_solution(2737374451719448186)
XLA Ops:
  6.5 0.0 copy-start
  6.5 0.0 copy-start.2
  6.5 0.0 all-gather.2.cloned.1.call-start
  6.5 1.0 maximum_bitcast_fusion
  7.5 1.6 %collective-permute-start = (bf16[1,256,256]{2,1,0:T(8,128)(2,1)S(1)}, bf16[1,256,256]{2,1,0:T(8,128)(2,1)S(1)}, u32[]{:S(2)}, u32[]{:S(2)}) collective-permute-start(bf16[1,256,256]{2,1,0:T(8,128)(2,1)S(1)} %maximum_bitcast_fusion), channel_id=1, source_target_pairs={{0,4},{4,0},{8,12},{12,8},{16,20},{20,16},{24,28},{28,24},{1,5},{5... | collective-permute-start | bytes 393224 | tf_op jit(solution)/shard_map/ppermute | solution.py:23
  9.1 3.7 %collective-permute-done = bf16[1,256,256]{2,1,0:T(8,128)(2,1)S(1)} collective-permute-done((bf16[1,256,256]{2,1,0:T(8,128)(2,1)S(1)}, bf16[1,256,256]{2,1,0:T(8,128)(2,1)S(1)}, u32[]{:S(2)}, u32[]{:S(2)}) %collective-permute-start) | collective-permute-done | bytes 131104 | tf_op jit(solution)/shard_map/ppermute | solution.py:23
  12.9 0.5 collective-permute-start.1
  13.4 6.7 %collective-permute-done.1 = bf16[2,256,256]{2,1,0:T(8,128)(2,1)S(1)} collective-permute-done((bf16[2,256,256]{2,1,0:T(8,128)(2,1)S(1)}, bf16[2,256,256]{2,1,0:T(8,128)(2,1)S(1)}, u32[]{:S(2)}, u32[]{:S(2)}) %collective-permute-start.1) | collective-permute-done | bytes 262176 | tf_op jit(solution)/shard_map/ppermute | solution.py:23
  20.1 0.1 maximum_select_fusion.1
  20.2 0.4 collective-permute-start.2
  20.6 23.6 %collective-permute-done.2 = bf16[4,256,256]{2,1,0:T(8,128)(2,1)S(1)} collective-permute-done((bf16[4,256,256]{2,1,0:T(8,128)(2,1)S(1)}, bf16[4,256,256]{2,1,0:T(8,128)(2,1)S(1)}, u32[]{:S(2)}, u32[]{:S(2)}) %collective-permute-start.2) | collective-permute-done | bytes 524320 | tf_op jit(solution)/shard_map/ppermute | solution.py:23
  44.2 1.1 maximum_select_fusion
  45.4 0.0 all-gather.2.cloned.1.call-update
  45.4 0.0 copy-done.2
  45.4 0.1 dynamic_slice.10.cnt_ref
  45.5 0.7 constant_dynamic-slice_fusion.1.bl_ref
  46.2 0.0 copy-done
  46.2 34.8 %all-gather.2.cloned.1.call-done.kv_hbm = bf16[8192,256]{1,0:T(8,128)(2,1)} async-done(((bf16[2048,256]{1,0:T(8,128)(2,1)}), bf16[8192,256]{1,0:T(8,128)(2,1)}) %all-gather.2.cloned.1.call-update) | async-done | bytes 4194320 | tf_op jit(solution)/shard_map/all_gather | solution.py:90
  81.0 0.0 copy-start.1
  81.0 2.2 %copy-done.1 = bf16[8192,256]{1,0:T(8,128)(2,1)S(1)} copy-done((bf16[8192,256]{1,0:T(8,128)(2,1)S(1)}, bf16[8192,256]{1,0:T(8,128)(2,1)}, u32[]{:S(2)}) %copy-start.1) | copy-done | bytes 4194328
  83.2 40.7 %shard_map.55 = bf16[256,512]{1,0:T(8,128)(2,1)} custom-call(s32[2,32]{1,0:T(2,128)S(1)} %constant_dynamic-slice_fusion.1.bl_ref, s32[2]{0:T(128)S(1)} %dynamic_slice.10.cnt_ref, s32[1]{0:T(128)} %bitcast.qb_ref, bf16[256,512]{1,0:T(8,128)(2,1)S(1)} %constant_dynamic-slice_fusion.q_ref, bf16[8192,256]{1,0:T(8,128)(2,1)S(1)} %copy-done.1), custom_call_target="tpu_custom_call" | custom-call | tf_op jit(solution)/shard_map/pallas_call | solution.py:103
  (2 shorter events, 0.0 us)
Async XLA Ops:
  6.5 39.7 %copy-start = (bf16[1024,512]{1,0:T(8,128)(2,1)S(1)}, bf16[1024,512]{1,0:T(8,128)(2,1)}, u32[]{:S(2)}) copy-start(bf16[1024,512]{1,0:T(8,128)(2,1)} %param.5) | copy-start | bytes 3145732
  6.5 38.9 %copy-start.2 = (s32[8]{0:T(128)S(1)}, s32[8]{0:T(128)}, u32[]{:S(2)}) copy-start(s32[8]{0:T(128)} %param.9) | copy-start | bytes 100
  6.5 74.4 %all-gather.2.cloned.1.call-start = ((), (), s32[]{:S(2)}) async-start(), calls=%async_computation | async-start | bytes 5242880 | tf_op jit(solution)/shard_map/all_gather | solution.py:90
  7.5 5.3 %collective-permute-start = (bf16[1,256,256]{2,1,0:T(8,128)(2,1)S(1)}, bf16[1,256,256]{2,1,0:T(8,128)(2,1)S(1)}, u32[]{:S(2)}, u32[]{:S(2)}) collective-permute-start(bf16[1,256,256]{2,1,0:T(8,128)(2,1)S(1)} %maximum_bitcast_fusion), channel_id=1, source_target_pairs={{0,4},{4,0},{8,12},{12,8},{16,20},{20,16},{24,28},{28,24},{1,5},{5... | collective-permute-start | bytes 393224 | tf_op jit(solution)/shard_map/ppermute | solution.py:23
  12.9 7.3 %collective-permute-start.1 = (bf16[2,256,256]{2,1,0:T(8,128)(2,1)S(1)}, bf16[2,256,256]{2,1,0:T(8,128)(2,1)S(1)}, u32[]{:S(2)}, u32[]{:S(2)}) collective-permute-start(bf16[2,256,256]{2,1,0:T(8,128)(2,1)S(1)} %maximum_select_fusion.2), channel_id=1, source_target_pairs={{0,8},{4,12},{8,0},{12,4},{16,24},{20,28},{24,16},{28,20},{1,9},{5... | collective-permute-start | bytes 786440 | tf_op jit(solution)/shard_map/ppermute | solution.py:23
  20.2 24.0 %collective-permute-start.2 = (bf16[4,256,256]{2,1,0:T(8,128)(2,1)S(1)}, bf16[4,256,256]{2,1,0:T(8,128)(2,1)S(1)}, u32[]{:S(2)}, u32[]{:S(2)}) collective-permute-start(bf16[4,256,256]{2,1,0:T(8,128)(2,1)S(1)} %maximum_select_fusion.1), channel_id=1, source_target_pairs={{0,16},{4,20},{8,24},{12,28},{16,0},{20,4},{24,8},{28,12},{1,17},{... | collective-permute-start | bytes 1572872 | tf_op jit(solution)/shard_map/ppermute | solution.py:23
  81.0 2.2 %copy-start.1 = (bf16[8192,256]{1,0:T(8,128)(2,1)S(1)}, bf16[8192,256]{1,0:T(8,128)(2,1)}, u32[]{:S(2)}) copy-start(bf16[8192,256]{1,0:T(8,128)(2,1)} %all-gather.2.cloned.1.call-done.kv_hbm) | copy-start | bytes 12582916
Sparse Core Ops, SparseCore 0:
  45.5 35.4 all-gather.1

commit v2 on v1

--- a/solution.py
+++ b/solution.py
@@ -15,20 +15,20 @@
 masked_score = -1e30
 
 
-def gather_pb(local, n_pb):
-    p = lax.axis_index("pb")
-    held = local[None]
-    step = 1
-    while step < n_pb:
-        other = lax.ppermute(held, "pb", [(i, i ^ step) for i in range(n_pb)])
-        upper = (p // step) % 2 == 1
+def gather_axis(local, axis, n):
+    idx = lax.axis_index(axis)
+    bits = n.bit_length() - 1
+    held = local.reshape((1,) * bits + local.shape)
+    for t in range(bits):
+        b = n >> (t + 1)
+        other = lax.ppermute(held, axis, [(i, i ^ b) for i in range(n)])
+        upper = (idx // b) % 2 == 1
         held = jnp.where(
             upper,
-            jnp.concatenate([other, held], axis=0),
-            jnp.concatenate([held, other], axis=0),
+            jnp.concatenate([other, held], axis=t),
+            jnp.concatenate([held, other], axis=t),
         )
-        step *= 2
-    return held.reshape(-1, local.shape[1])
+    return held.reshape((n * local.shape[0],) + local.shape[1:])
 
 
 def attend_kernel(bl_ref, cnt_ref, qb_ref, q_ref, kv_hbm, out_ref, kvbuf, sems, *, n_local, scale):
@@ -86,8 +86,8 @@
 
 def shards(queries, key_cache, value_cache, block_list, block_count, *, n_pb, n_ka):
     kv_local = jnp.concatenate([key_cache, value_cache], axis=1)
-    shard = gather_pb(kv_local, n_pb)
-    kv_all = lax.all_gather(shard, "ka", axis=0, tiled=True)
+    shard = gather_axis(kv_local, "pb", n_pb)
+    kv_all = gather_axis(shard, "ka", n_ka)
 
     p = lax.axis_index("pb")
     k = lax.axis_index("ka")

time: 131 us -> 107 us (0.82)
  waiting for transfers between devices: 68.9 us -> 53.5 us
  between operations: 13.4 us -> 0.13 us
  other arithmetic: 2.22 us -> 5.63 us
    all_gather x1 -> x0, waiting for transfers between devices: 34.8 us -> none  [shards(): kv_all = lax.all_gather(shard, 'ka', axis=0, tiled=True)]
    ppermute x3 -> x5, waiting for transfers between devices: 34.1 us -> 53.5 us  [gather_axis(): other = lax.ppermute(held, axis, [(i, i ^ b) for i in range(n)])]
    select_n x3 -> x5, other arithmetic: 1.23 us -> 5.6 us  [gather_axis(): jnp.where(upper, jnp.concatenate([other, held], axis=t), jnp.concatenate(...]
    ppermute x3 -> x5, starting transfers between devices: 2.47 us -> 3.69 us  [gather_axis(): other = lax.ppermute(held, axis, [(i, i ^ b) for i in range(n)])]
  transfers between devices with their start and end apart: 4 -> 5, of which waited for: 4 -> 5; matrix products, arithmetic and copies ran while one was open for 1% -> 1% of each run, Pallas kernels for 0% -> 0%
where the time goes in v2:
time: 107 us; the launch traced here: 106 us
  waiting for transfers between devices  53.5 us (50%)
  Pallas kernels  40.8 us (38%)
  other arithmetic  5.63 us (5%)
  starting transfers between devices  3.69 us (3%)
  local copies, waits for them, and re-layouts  2.6 us (2%)
    ppermute x5, waiting for transfers between devices, gather_axis(): other = lax.ppermute(held, axis, [(i, i ^ b) for i in range(n)])  53.5 us
    pallas_call x1, Pallas kernels, shards(): pl.pallas_call(kernel, out_shape=jax.ShapeDtypeStruct((rows_mine, queries...  40.8 us
    select_n x5, other arithmetic, gather_axis(): jnp.where(upper, jnp.concatenate([other, held], axis=t), jnp.concatenate(...  5.6 us
    ppermute x5, starting transfers between devices, gather_axis(): other = lax.ppermute(held, axis, [(i, i ^ b) for i in range(n)])  3.69 us
  transfers between devices with their start and end apart: 5, of which 5 were waited for; matrix products, arithmetic and copies ran while one was open for 1% of the time, Pallas kernels for 0%

profile of v2, /device:TPU:24, one launch (start us, length us, event | category | flops | bytes accessed | tf_op | source)
XLA Modules:
  0.0 106.3 jit_solution(10843381249065643885)
XLA Ops:
  0.0 0.0 copy-start
  0.0 0.9 constant_dynamic-update-slice_fusion.1
  0.9 0.9 constant_dynamic-update-slice_fusion
  1.8 0.4 collective-permute-start
  2.2 8.5 %collective-permute-done = bf16[1,1,1,256,256]{4,3,2,1,0:T(8,128)(2,1)S(1)} collective-permute-done((bf16[1,1,1,256,256]{4,3,2,1,0:T(8,128)(2,1)S(1)}, bf16[1,1,1,256,256]{4,3,2,1,0:T(8,128)(2,1)S(1)}, u32[]{:S(2)}, u32[]{:S(2)}) %collective-permute-start) | collective-permute-done | bytes 131104 | tf_op jit(solution)/shard_map/ppermute | solution.py:24
  10.7 0.1 collective-permute-start.1
  10.9 8.1 %collective-permute-done.1 = bf16[2,1,1,256,256]{4,3,2,1,0:T(8,128)(2,1)S(1)} collective-permute-done((bf16[2,1,1,256,256]{4,3,2,1,0:T(8,128)(2,1)S(1)}, bf16[2,1,1,256,256]{4,3,2,1,0:T(8,128)(2,1)S(1)}, u32[]{:S(2)}, u32[]{:S(2)}) %collective-permute-start.1) | collective-permute-done | bytes 262176 | tf_op jit(solution)/shard_map/ppermute | solution.py:24
  19.1 1.6 %collective-permute-start.2 = (bf16[2,2,1,256,256]{4,3,2,1,0:T(8,128)(2,1)S(1)}, bf16[2,2,1,256,256]{4,3,2,1,0:T(8,128)(2,1)S(1)}, u32[]{:S(2)}, u32[]{:S(2)}) collective-permute-start(bf16[2,2,1,256,256]{4,3,2,1,0:T(8,128)(2,1)S(1)} %maximum_select_fusion.3), channel_id=1, source_target_pairs={{0,4},{4,0},{8,12},{12,8},{16,20},{20,16},{24,28},{28,24},{1,5},{5... | collective-permute-start | bytes 1572872 | tf_op jit(solution)/shard_map/ppermute | solution.py:24
  20.6 11.5 %collective-permute-done.2 = bf16[2,2,1,256,256]{4,3,2,1,0:T(8,128)(2,1)S(1)} collective-permute-done((bf16[2,2,1,256,256]{4,3,2,1,0:T(8,128)(2,1)S(1)}, bf16[2,2,1,256,256]{4,3,2,1,0:T(8,128)(2,1)S(1)}, u32[]{:S(2)}, u32[]{:S(2)}) %collective-permute-start.2) | collective-permute-done | bytes 524320 | tf_op jit(solution)/shard_map/ppermute | solution.py:24
  32.1 0.1 maximum_select_fusion.2
  32.2 0.0 copy-start.1
  32.2 1.6 %collective-permute-start.3 = (bf16[1,1,2048,256]{3,2,1,0:T(8,128)(2,1)S(1)}, bf16[1,1,2048,256]{3,2,1,0:T(8,128)(2,1)}, u32[]{:S(2)}, u32[]{:S(2)}) collective-permute-start(bf16[1,1,2048,256]{3,2,1,0:T(8,128)(2,1)S(1)} %bitcast.9), channel_id=1, source_target_pairs={{0,2},{1,3},{2,0},{3,1},{4,6},{5,7},{6,4},{7,5},{8,10},{9,11},{10,... | collective-permute-start | bytes 3145736 | tf_op jit(solution)/shard_map/ppermute | solution.py:24
  33.8 0.0 copy-done.1
  33.8 0.0 copy-start.2
  33.8 21.9 %collective-permute-done.3 = bf16[1,1,2048,256]{3,2,1,0:T(8,128)(2,1)} collective-permute-done((bf16[1,1,2048,256]{3,2,1,0:T(8,128)(2,1)S(1)}, bf16[1,1,2048,256]{3,2,1,0:T(8,128)(2,1)}, u32[]{:S(2)}, u32[]{:S(2)}) %collective-permute-start.3) | collective-permute-done | bytes 1048608 | tf_op jit(solution)/shard_map/ppermute | solution.py:24
  55.8 2.6 %maximum_select_fusion.1 = bf16[2,1,2048,256]{3,2,1,0:T(8,128)(2,1)S(1)} fusion(bf16[1,1,2048,256]{3,2,1,0:T(8,128)(2,1)} %bitcast.10, bf16[1,1,2048,256]{3,2,1,0:T(8,128)(2,1)} %collective-permute-done.3, pred[]{:T(512)S(6)} %eq.22), kind=kLoop, calls=%fused_computation.1 | loop fusion | flops 3145728 | bytes 4194305 | tf_op jit(solution)/shard_map/jit(_where)/select_n | solution.py:26
  58.4 0.1 collective-permute-start.4
  58.5 0.0 copy-done.2
  58.5 0.1 dynamic_slice.10.cnt_ref
  58.6 0.7 constant_dynamic-slice_fusion.1.bl_ref
  59.3 0.0 copy-done
  59.3 3.5 %collective-permute-done.4 = bf16[2,1,2048,256]{3,2,1,0:T(8,128)(2,1)} collective-permute-done((bf16[2,1,2048,256]{3,2,1,0:T(8,128)(2,1)S(1)}, bf16[2,1,2048,256]{3,2,1,0:T(8,128)(2,1)}, u32[]{:S(2)}, u32[]{:S(2)}) %collective-permute-start.4) | collective-permute-done | bytes 2097184 | tf_op jit(solution)/shard_map/ppermute | solution.py:24
  62.7 2.8 %maximum_select_fusion = bf16[2,2,2048,256]{3,2,1,0:T(8,128)(2,1)S(1)} fusion(bf16[2,1,2048,256]{3,2,1,0:T(8,128)(2,1)S(1)} %maximum_select_fusion.1, bf16[2,1,2048,256]{3,2,1,0:T(8,128)(2,1)} %collective-permute-done.4, pred[]{:T(512)S(6)} %eq.21), kind=kLoop, calls=%fused_computation | loop fusion | flops 6291456 | bytes 8388609 | tf_op jit(solution)/shard_map/jit(_where)/select_n | solution.py:26
  65.6 40.8 %shard_map.55 = bf16[256,512]{1,0:T(8,128)(2,1)} custom-call(s32[2,32]{1,0:T(2,128)S(1)} %constant_dynamic-slice_fusion.1.bl_ref, s32[2]{0:T(128)S(1)} %dynamic_slice.10.cnt_ref, s32[1]{0:T(128)} %bitcast.qb_ref, bf16[256,512]{1,0:T(8,128)(2,1)S(1)} %constant_dynamic-slice_fusion.q_ref, bf16[8192,256]{1,0:T(8,128)(2,1)S(1)} %bitcast.8), custom_call_target="tpu_custom_call" | custom-call | tf_op jit(solution)/shard_map/pallas_call | solution.py:103
  (4 shorter events, 0.1 us)
Async XLA Ops:
  0.0 59.3 %copy-start = (bf16[1024,512]{1,0:T(8,128)(2,1)S(1)}, bf16[1024,512]{1,0:T(8,128)(2,1)}, u32[]{:S(2)}) copy-start(bf16[1024,512]{1,0:T(8,128)(2,1)} %param.5) | copy-start | bytes 3145732
  1.8 8.9 %collective-permute-start = (bf16[1,1,1,256,256]{4,3,2,1,0:T(8,128)(2,1)S(1)}, bf16[1,1,1,256,256]{4,3,2,1,0:T(8,128)(2,1)S(1)}, u32[]{:S(2)}, u32[]{:S(2)}) collective-permute-start(bf16[1,1,1,256,256]{4,3,2,1,0:T(8,128)(2,1)S(1)} %bitcast.11), channel_id=1, source_target_pairs={{0,16},{4,20},{8,24},{12,28},{16,0},{20,4},{24,8},{28,12},{1,17},{... | collective-permute-start | bytes 393224 | tf_op jit(solution)/shard_map/ppermute | solution.py:24
  10.7 8.3 %collective-permute-start.1 = (bf16[2,1,1,256,256]{4,3,2,1,0:T(8,128)(2,1)S(1)}, bf16[2,1,1,256,256]{4,3,2,1,0:T(8,128)(2,1)S(1)}, u32[]{:S(2)}, u32[]{:S(2)}) collective-permute-start(bf16[2,1,1,256,256]{4,3,2,1,0:T(8,128)(2,1)S(1)} %maximum_select_fusion.4), channel_id=1, source_target_pairs={{0,8},{4,12},{8,0},{12,4},{16,24},{20,28},{24,16},{28,20},{1,9},{5... | collective-permute-start | bytes 786440 | tf_op jit(solution)/shard_map/ppermute | solution.py:24
  19.1 13.1 %collective-permute-start.2 = (bf16[2,2,1,256,256]{4,3,2,1,0:T(8,128)(2,1)S(1)}, bf16[2,2,1,256,256]{4,3,2,1,0:T(8,128)(2,1)S(1)}, u32[]{:S(2)}, u32[]{:S(2)}) collective-permute-start(bf16[2,2,1,256,256]{4,3,2,1,0:T(8,128)(2,1)S(1)} %maximum_select_fusion.3), channel_id=1, source_target_pairs={{0,4},{4,0},{8,12},{12,8},{16,20},{20,16},{24,28},{28,24},{1,5},{5... | collective-permute-start | bytes 1572872 | tf_op jit(solution)/shard_map/ppermute | solution.py:24
  32.2 1.6 %copy-start.1 = (bf16[2,2,2,256,256]{4,3,2,1,0:T(8,128)(2,1)}, bf16[2,2,2,256,256]{4,3,2,1,0:T(8,128)(2,1)S(1)}, u32[]{:S(2)}) copy-start(bf16[2,2,2,256,256]{4,3,2,1,0:T(8,128)(2,1)S(1)} %maximum_select_fusion.2) | copy-start | bytes 3145732
  32.2 23.5 %collective-permute-start.3 = (bf16[1,1,2048,256]{3,2,1,0:T(8,128)(2,1)S(1)}, bf16[1,1,2048,256]{3,2,1,0:T(8,128)(2,1)}, u32[]{:S(2)}, u32[]{:S(2)}) collective-permute-start(bf16[1,1,2048,256]{3,2,1,0:T(8,128)(2,1)S(1)} %bitcast.9), channel_id=1, source_target_pairs={{0,2},{1,3},{2,0},{3,1},{4,6},{5,7},{6,4},{7,5},{8,10},{9,11},{10,... | collective-permute-start | bytes 3145736 | tf_op jit(solution)/shard_map/ppermute | solution.py:24
  33.8 24.7 %copy-start.2 = (s32[8]{0:T(128)S(1)}, s32[8]{0:T(128)}, u32[]{:S(2)}) copy-start(s32[8]{0:T(128)} %param.9) | copy-start | bytes 100
  58.4 4.4 %collective-permute-start.4 = (bf16[2,1,2048,256]{3,2,1,0:T(8,128)(2,1)S(1)}, bf16[2,1,2048,256]{3,2,1,0:T(8,128)(2,1)}, u32[]{:S(2)}, u32[]{:S(2)}) collective-permute-start(bf16[2,1,2048,256]{3,2,1,0:T(8,128)(2,1)S(1)} %maximum_select_fusion.1), channel_id=1, source_target_pairs={{0,1},{1,0},{2,3},{3,2},{4,5},{5,4},{6,7},{7,6},{8,9},{9,8},{10,11... | collective-permute-start | bytes 6291464 | tf_op jit(solution)/shard_map/ppermute | solution.py:24

commit v3 on v2

--- a/solution.py
+++ b/solution.py
@@ -31,54 +31,81 @@
     return held.reshape((n * local.shape[0],) + local.shape[1:])
 
 
-def attend_kernel(bl_ref, cnt_ref, qb_ref, q_ref, kv_hbm, out_ref, kvbuf, sems, *, n_local, scale):
+def attend_kernel(bl_ref, cnt_ref, qb_ref, q_ref, kv_hbm, out_ref, off_ref, kvbuf, dbuf, sems, dsems, *, n_local, group, scale):
     qb0 = qb_ref[0]
+    width = kvbuf.shape[-1]
+
+    def block_copy(blk, dst, sem):
+        start = pl.multiple_of(blk * BLK, BLK)
+        return pltpu.make_async_copy(kv_hbm.at[pl.ds(start, BLK), :], dst, sem)
 
     def copy(j, s):
-        blk = bl_ref[j, s]
-        start = pl.multiple_of(blk * BLK, BLK)
-        return pltpu.make_async_copy(kv_hbm.at[pl.ds(start, BLK), :], kvbuf.at[j, s], sems.at[j, s])
+        return block_copy(off_ref[j, s], kvbuf.at[j, s], sems.at[j, s])
 
+    n_off = []
     for j in range(n_local):
+        qb = qb0 + j
+        block_copy(qb, dbuf.at[j], dsems.at[j]).start()
+
+        def compact(s, n, j=j, qb=qb):
+            b = bl_ref[j, s]
+            off_ref[j, n] = b
+            return n + (b != qb).astype(jnp.int32)
+
+        n_j = lax.fori_loop(0, cnt_ref[j], compact, 0)
+        n_off.append(n_j)
+
         def issue(s, c, j=j):
             copy(j, s).start()
             return c
 
-        lax.fori_loop(0, cnt_ref[j], issue, 0)
+        lax.fori_loop(0, n_j, issue, 0)
 
     rows = QH * BLK
     rowpos = lax.broadcasted_iota(jnp.int32, (rows, BLK), 0) % BLK
     col = lax.broadcasted_iota(jnp.int32, (rows, BLK), 1)
     causal = col <= rowpos
+    dims = (((1,), (1,)), ((), ()))
+
+    def update(qs, kvb, carry):
+        m, l, acc = carry
+        k = kvb[:, :HD]
+        v = kvb[:, HD:]
+        sc = lax.dot_general(qs, k, dims, preferred_element_type=jnp.float32) * scale
+        m_new = jnp.maximum(m, jnp.max(sc, axis=1, keepdims=True))
+        alpha = jnp.exp(m - m_new)
+        w = jnp.exp(sc - m_new)
+        l = alpha * l + jnp.sum(w, axis=1, keepdims=True)
+        acc = alpha * acc + jnp.dot(w.astype(jnp.bfloat16), v, preferred_element_type=jnp.float32)
+        return m_new, l, acc
 
     for j in range(n_local):
         qb = qb0 + j
         qrows = q_ref[j * BLK:(j + 1) * BLK, :]
         qs = jnp.concatenate([qrows[:, h * HD:(h + 1) * HD] for h in range(QH)], axis=0)
 
-        def body(s, carry, j=j, qb=qb, qs=qs):
-            m, l, acc = carry
+        block_copy(qb, dbuf.at[j], dsems.at[j]).wait()
+        kvd = dbuf[j]
+        sc = lax.dot_general(qs, kvd[:, :HD], dims, preferred_element_type=jnp.float32) * scale
+        m = jnp.max(jnp.where(causal, sc, masked_score), axis=1, keepdims=True)
+        w = jnp.where(causal, jnp.exp(sc - m), 0.0)
+        l = jnp.sum(w, axis=1, keepdims=True)
+        acc = jnp.dot(w.astype(jnp.bfloat16), kvd[:, HD:], preferred_element_type=jnp.float32)
+
+        def grouped(g, carry, j=j, qs=qs):
+            first = g * group
+            for i in range(group):
+                copy(j, first + i).wait()
+            kvb = kvbuf[j, pl.ds(first, group)].reshape(group * BLK, width)
+            return update(qs, kvb, carry)
+
+        def single(s, carry, j=j, qs=qs):
             copy(j, s).wait()
-            kvb = kvbuf[j, s]
-            k = kvb[:, :HD]
-            v = kvb[:, HD:]
-            blk = bl_ref[j, s]
-            sc = lax.dot_general(qs, k, (((1,), (1,)), ((), ())), preferred_element_type=jnp.float32) * scale
-            valid = jnp.logical_or(blk < qb, jnp.logical_and(blk == qb, causal))
-            masked = jnp.where(valid, sc, masked_score)
-            m_new = jnp.maximum(m, jnp.max(masked, axis=1, keepdims=True))
-            alpha = jnp.exp(m - m_new)
-            w = jnp.where(valid, jnp.exp(sc - m_new), 0.0)
-            l = alpha * l + jnp.sum(w, axis=1, keepdims=True)
-            acc = alpha * acc + jnp.dot(w.astype(jnp.bfloat16), v, preferred_element_type=jnp.float32)
-            return m_new, l, acc
+            return update(qs, kvbuf[j, s], carry)
 
-        init = (
-            jnp.full((rows, 1), masked_score, jnp.float32),
-            jnp.zeros((rows, 1), jnp.float32),
-            jnp.zeros((rows, HD), jnp.float32),
-        )
-        m, l, acc = lax.fori_loop(0, cnt_ref[j], body, init)
+        n_groups = n_off[j] // group
+        carry = lax.fori_loop(0, n_groups, grouped, (m, l, acc))
+        m, l, acc = lax.fori_loop(n_groups * group, n_off[j], single, carry)
         res = (acc / l).astype(out_ref.dtype)
         for h in range(QH):
             out_ref[j * BLK:(j + 1) * BLK, h * HD:(h + 1) * HD] = res[h * BLK:(h + 1) * BLK, :]
@@ -99,7 +126,7 @@
     cnt_mine = lax.dynamic_slice_in_dim(block_count, k * n_local, n_local, 0)
     qb0 = ((p * n_ka + k) * n_local).astype(jnp.int32).reshape(1)
 
-    kernel = functools.partial(attend_kernel, n_local=n_local, scale=1.0 / math.sqrt(HD))
+    kernel = functools.partial(attend_kernel, n_local=n_local, group=4, scale=1.0 / math.sqrt(HD))
     return pl.pallas_call(
         kernel,
         out_shape=jax.ShapeDtypeStruct((rows_mine, queries.shape[1]), jnp.bfloat16),
@@ -112,8 +139,11 @@
             ],
             out_specs=pl.BlockSpec((rows_mine, queries.shape[1]), lambda i, *_: (0, 0)),
             scratch_shapes=[
+                pltpu.SMEM((n_local, listed), jnp.int32),
                 pltpu.VMEM((n_local, listed, BLK, kv_local.shape[1]), jnp.bfloat16),
+                pltpu.VMEM((n_local, BLK, kv_local.shape[1]), jnp.bfloat16),
                 pltpu.SemaphoreType.DMA((n_local, listed)),
+                pltpu.SemaphoreType.DMA((n_local,)),
             ],
         ),
         compiler_params=pltpu.CompilerParams(vmem_limit_bytes=48 * 1024 * 1024),

time: 107 us -> 89.2 us (0.83)
  Pallas kernels: 40.8 us -> 22.7 us
    pallas_call x1, Pallas kernels: 40.8 us -> 22.7 us  [shards(): pl.pallas_call(kernel, out_shape=jax.ShapeDtypeStruct((rows_mine, queries...]
where the time goes in v3:
time: 89.2 us; the launch traced here: 88.3 us
  waiting for transfers between devices  53.5 us (60%)
  Pallas kernels  22.7 us (25%)
  other arithmetic  5.63 us (6%)
  starting transfers between devices  3.69 us (4%)
  local copies, waits for them, and re-layouts  2.6 us (3%)
    ppermute x5, waiting for transfers between devices, gather_axis(): other = lax.ppermute(held, axis, [(i, i ^ b) for i in range(n)])  53.5 us
    pallas_call x1, Pallas kernels, shards(): pl.pallas_call(kernel, out_shape=jax.ShapeDtypeStruct((rows_mine, queries...  22.7 us
    select_n x5, other arithmetic, gather_axis(): jnp.where(upper, jnp.concatenate([other, held], axis=t), jnp.concatenate(...  5.6 us
    ppermute x5, starting transfers between devices, gather_axis(): other = lax.ppermute(held, axis, [(i, i ^ b) for i in range(n)])  3.69 us
  transfers between devices with their start and end apart: 5, of which 5 were waited for; matrix products, arithmetic and copies ran while one was open for 1% of the time, Pallas kernels for 0%

profile of v3, /device:TPU:24, one launch (start us, length us, event | category | flops | bytes accessed | tf_op | source)
XLA Modules:
  0.0 88.3 jit_solution(5809594296696225429)
XLA Ops:
  0.0 0.0 copy-start
  0.0 0.9 %constant_dynamic-update-slice_fusion.1 = bf16[256,256]{1,0:T(8,128)(2,1)S(1)} fusion(bf16[256,128]{1,0:T(8,128)(2,1)} %param.6), kind=kLoop, calls=%fused_computation.8 | loop fusion | bytes 131072
  0.9 0.9 constant_dynamic-update-slice_fusion
  1.8 0.4 collective-permute-start
  2.2 8.5 %collective-permute-done = bf16[1,1,1,256,256]{4,3,2,1,0:T(8,128)(2,1)S(1)} collective-permute-done((bf16[1,1,1,256,256]{4,3,2,1,0:T(8,128)(2,1)S(1)}, bf16[1,1,1,256,256]{4,3,2,1,0:T(8,128)(2,1)S(1)}, u32[]{:S(2)}, u32[]{:S(2)}) %collective-permute-start) | collective-permute-done | bytes 131104 | tf_op jit(solution)/shard_map/ppermute | solution.py:24
  10.7 0.1 collective-permute-start.1
  10.9 8.1 %collective-permute-done.1 = bf16[2,1,1,256,256]{4,3,2,1,0:T(8,128)(2,1)S(1)} collective-permute-done((bf16[2,1,1,256,256]{4,3,2,1,0:T(8,128)(2,1)S(1)}, bf16[2,1,1,256,256]{4,3,2,1,0:T(8,128)(2,1)S(1)}, u32[]{:S(2)}, u32[]{:S(2)}) %collective-permute-start.1) | collective-permute-done | bytes 262176 | tf_op jit(solution)/shard_map/ppermute | solution.py:24
  19.1 1.6 %collective-permute-start.2 = (bf16[2,2,1,256,256]{4,3,2,1,0:T(8,128)(2,1)S(1)}, bf16[2,2,1,256,256]{4,3,2,1,0:T(8,128)(2,1)S(1)}, u32[]{:S(2)}, u32[]{:S(2)}) collective-permute-start(bf16[2,2,1,256,256]{4,3,2,1,0:T(8,128)(2,1)S(1)} %maximum_select_fusion.3), channel_id=1, source_target_pairs={{0,4},{4,0},{8,12},{12,8},{16,20},{20,16},{24,28},{28,24},{1,5},{5... | collective-permute-start | bytes 1572872 | tf_op jit(solution)/shard_map/ppermute | solution.py:24
  20.6 11.5 %collective-permute-done.2 = bf16[2,2,1,256,256]{4,3,2,1,0:T(8,128)(2,1)S(1)} collective-permute-done((bf16[2,2,1,256,256]{4,3,2,1,0:T(8,128)(2,1)S(1)}, bf16[2,2,1,256,256]{4,3,2,1,0:T(8,128)(2,1)S(1)}, u32[]{:S(2)}, u32[]{:S(2)}) %collective-permute-start.2) | collective-permute-done | bytes 524320 | tf_op jit(solution)/shard_map/ppermute | solution.py:24
  32.1 0.1 maximum_select_fusion.2
  32.2 0.0 copy-start.1
  32.2 1.6 %collective-permute-start.3 = (bf16[1,1,2048,256]{3,2,1,0:T(8,128)(2,1)S(1)}, bf16[1,1,2048,256]{3,2,1,0:T(8,128)(2,1)}, u32[]{:S(2)}, u32[]{:S(2)}) collective-permute-start(bf16[1,1,2048,256]{3,2,1,0:T(8,128)(2,1)S(1)} %bitcast.9), channel_id=1, source_target_pairs={{0,2},{1,3},{2,0},{3,1},{4,6},{5,7},{6,4},{7,5},{8,10},{9,11},{10,... | collective-permute-start | bytes 3145736 | tf_op jit(solution)/shard_map/ppermute | solution.py:24
  33.8 0.0 copy-done.1
  33.8 0.0 copy-start.2
  33.8 21.9 %collective-permute-done.3 = bf16[1,1,2048,256]{3,2,1,0:T(8,128)(2,1)} collective-permute-done((bf16[1,1,2048,256]{3,2,1,0:T(8,128)(2,1)S(1)}, bf16[1,1,2048,256]{3,2,1,0:T(8,128)(2,1)}, u32[]{:S(2)}, u32[]{:S(2)}) %collective-permute-start.3) | collective-permute-done | bytes 1048608 | tf_op jit(solution)/shard_map/ppermute | solution.py:24
  55.8 2.6 %maximum_select_fusion.1 = bf16[2,1,2048,256]{3,2,1,0:T(8,128)(2,1)S(1)} fusion(bf16[1,1,2048,256]{3,2,1,0:T(8,128)(2,1)} %bitcast.10, bf16[1,1,2048,256]{3,2,1,0:T(8,128)(2,1)} %collective-permute-done.3, pred[]{:T(512)S(6)} %eq.22), kind=kLoop, calls=%fused_computation.1 | loop fusion | flops 3145728 | bytes 4194305 | tf_op jit(solution)/shard_map/jit(_where)/select_n | solution.py:26
  58.4 0.1 collective-permute-start.4
  58.5 0.0 copy-done.2
  58.5 0.1 dynamic_slice.10.cnt_ref
  58.6 0.7 constant_dynamic-slice_fusion.1.bl_ref
  59.3 0.0 copy-done
  59.3 3.5 %collective-permute-done.4 = bf16[2,1,2048,256]{3,2,1,0:T(8,128)(2,1)} collective-permute-done((bf16[2,1,2048,256]{3,2,1,0:T(8,128)(2,1)S(1)}, bf16[2,1,2048,256]{3,2,1,0:T(8,128)(2,1)}, u32[]{:S(2)}, u32[]{:S(2)}) %collective-permute-start.4) | collective-permute-done | bytes 2097184 | tf_op jit(solution)/shard_map/ppermute | solution.py:24
  62.7 2.8 %maximum_select_fusion = bf16[2,2,2048,256]{3,2,1,0:T(8,128)(2,1)S(1)} fusion(bf16[2,1,2048,256]{3,2,1,0:T(8,128)(2,1)S(1)} %maximum_select_fusion.1, bf16[2,1,2048,256]{3,2,1,0:T(8,128)(2,1)} %collective-permute-done.4, pred[]{:T(512)S(6)} %eq.21), kind=kLoop, calls=%fused_computation | loop fusion | flops 6291456 | bytes 8388609 | tf_op jit(solution)/shard_map/jit(_where)/select_n | solution.py:26
  65.6 22.7 %shard_map.55 = bf16[256,512]{1,0:T(8,128)(2,1)} custom-call(s32[2,32]{1,0:T(2,128)S(1)} %constant_dynamic-slice_fusion.1.bl_ref, s32[2]{0:T(128)S(1)} %dynamic_slice.10.cnt_ref, s32[1]{0:T(128)} %bitcast.qb_ref, bf16[256,512]{1,0:T(8,128)(2,1)S(1)} %constant_dynamic-slice_fusion.q_ref, bf16[8192,256]{1,0:T(8,128)(2,1)S(1)} %bitcast.8), custom_call_target="tpu_custom_call" | custom-call | tf_op jit(solution)/shard_map/pallas_call | solution.py:130
  (4 shorter events, 0.1 us)
Async XLA Ops:
  0.0 59.3 %copy-start = (bf16[1024,512]{1,0:T(8,128)(2,1)S(1)}, bf16[1024,512]{1,0:T(8,128)(2,1)}, u32[]{:S(2)}) copy-start(bf16[1024,512]{1,0:T(8,128)(2,1)} %param.5) | copy-start | bytes 3145732
  1.8 8.9 %collective-permute-start = (bf16[1,1,1,256,256]{4,3,2,1,0:T(8,128)(2,1)S(1)}, bf16[1,1,1,256,256]{4,3,2,1,0:T(8,128)(2,1)S(1)}, u32[]{:S(2)}, u32[]{:S(2)}) collective-permute-start(bf16[1,1,1,256,256]{4,3,2,1,0:T(8,128)(2,1)S(1)} %bitcast.11), channel_id=1, source_target_pairs={{0,16},{4,20},{8,24},{12,28},{16,0},{20,4},{24,8},{28,12},{1,17},{... | collective-permute-start | bytes 393224 | tf_op jit(solution)/shard_map/ppermute | solution.py:24
  10.7 8.3 %collective-permute-start.1 = (bf16[2,1,1,256,256]{4,3,2,1,0:T(8,128)(2,1)S(1)}, bf16[2,1,1,256,256]{4,3,2,1,0:T(8,128)(2,1)S(1)}, u32[]{:S(2)}, u32[]{:S(2)}) collective-permute-start(bf16[2,1,1,256,256]{4,3,2,1,0:T(8,128)(2,1)S(1)} %maximum_select_fusion.4), channel_id=1, source_target_pairs={{0,8},{4,12},{8,0},{12,4},{16,24},{20,28},{24,16},{28,20},{1,9},{5... | collective-permute-start | bytes 786440 | tf_op jit(solution)/shard_map/ppermute | solution.py:24
  19.1 13.1 %collective-permute-start.2 = (bf16[2,2,1,256,256]{4,3,2,1,0:T(8,128)(2,1)S(1)}, bf16[2,2,1,256,256]{4,3,2,1,0:T(8,128)(2,1)S(1)}, u32[]{:S(2)}, u32[]{:S(2)}) collective-permute-start(bf16[2,2,1,256,256]{4,3,2,1,0:T(8,128)(2,1)S(1)} %maximum_select_fusion.3), channel_id=1, source_target_pairs={{0,4},{4,0},{8,12},{12,8},{16,20},{20,16},{24,28},{28,24},{1,5},{5... | collective-permute-start | bytes 1572872 | tf_op jit(solution)/shard_map/ppermute | solution.py:24
  32.2 1.6 %copy-start.1 = (bf16[2,2,2,256,256]{4,3,2,1,0:T(8,128)(2,1)}, bf16[2,2,2,256,256]{4,3,2,1,0:T(8,128)(2,1)S(1)}, u32[]{:S(2)}) copy-start(bf16[2,2,2,256,256]{4,3,2,1,0:T(8,128)(2,1)S(1)} %maximum_select_fusion.2) | copy-start | bytes 3145732
  32.2 23.5 %collective-permute-start.3 = (bf16[1,1,2048,256]{3,2,1,0:T(8,128)(2,1)S(1)}, bf16[1,1,2048,256]{3,2,1,0:T(8,128)(2,1)}, u32[]{:S(2)}, u32[]{:S(2)}) collective-permute-start(bf16[1,1,2048,256]{3,2,1,0:T(8,128)(2,1)S(1)} %bitcast.9), channel_id=1, source_target_pairs={{0,2},{1,3},{2,0},{3,1},{4,6},{5,7},{6,4},{7,5},{8,10},{9,11},{10,... | collective-permute-start | bytes 3145736 | tf_op jit(solution)/shard_map/ppermute | solution.py:24
  33.8 24.7 %copy-start.2 = (s32[8]{0:T(128)S(1)}, s32[8]{0:T(128)}, u32[]{:S(2)}) copy-start(s32[8]{0:T(128)} %param.9) | copy-start | bytes 100
  58.4 4.4 %collective-permute-start.4 = (bf16[2,1,2048,256]{3,2,1,0:T(8,128)(2,1)S(1)}, bf16[2,1,2048,256]{3,2,1,0:T(8,128)(2,1)}, u32[]{:S(2)}, u32[]{:S(2)}) collective-permute-start(bf16[2,1,2048,256]{3,2,1,0:T(8,128)(2,1)S(1)} %maximum_select_fusion.1), channel_id=1, source_target_pairs={{0,1},{1,0},{2,3},{3,2},{4,5},{5,4},{6,7},{7,6},{8,9},{9,8},{10,11... | collective-permute-start | bytes 6291464 | tf_op jit(solution)/shard_map/ppermute | solution.py:24

commit v4 on v3

--- a/solution.py
+++ b/solution.py
@@ -31,13 +31,38 @@
     return held.reshape((n * local.shape[0],) + local.shape[1:])
 
 
-def attend_kernel(bl_ref, cnt_ref, qb_ref, q_ref, kv_hbm, out_ref, off_ref, kvbuf, dbuf, sems, dsems, *, n_local, group, scale):
+def pieces_axis(local, axis, n):
+    idx_pieces = {0: local}
+    b = n // 2
+    while b >= 1:
+        for x in sorted(idx_pieces):
+            idx_pieces[x | b] = lax.ppermute(idx_pieces[x], axis, [(i, i ^ b) for i in range(n)])
+        b //= 2
+    return [idx_pieces[x] for x in range(n)]
+
+
+def attend_kernel(bl_ref, cnt_ref, qb_ref, q_ref, *rest, n_local, n_pieces, group, scale):
+    kv_pieces = rest[:n_pieces]
+    out_ref, off_ref, kvbuf, dbuf, sems, dsems = rest[n_pieces:]
     qb0 = qb_ref[0]
+    me = qb_ref[1]
     width = kvbuf.shape[-1]
+    per_piece = kv_pieces[0].shape[0] // BLK
 
-    def block_copy(blk, dst, sem):
-        start = pl.multiple_of(blk * BLK, BLK)
-        return pltpu.make_async_copy(kv_hbm.at[pl.ds(start, BLK), :], dst, sem)
+    class block_copy:
+        def __init__(self, blk, dst, sem):
+            self.blk, self.dst, self.sem = blk, dst, sem
+
+        def start(self):
+            which = jnp.bitwise_xor(self.blk // per_piece, me)
+            start = pl.multiple_of((self.blk % per_piece) * BLK, BLK)
+            for x in range(n_pieces):
+                @pl.when(which == x)
+                def _(x=x, start=start):
+                    pltpu.make_async_copy(kv_pieces[x].at[pl.ds(start, BLK), :], self.dst, self.sem).start()
+
+        def wait(self):
+            pltpu.make_async_copy(kv_pieces[0].at[pl.ds(0, BLK), :], self.dst, self.sem).wait()
 
     def copy(j, s):
         return block_copy(off_ref[j, s], kvbuf.at[j, s], sems.at[j, s])
@@ -114,7 +139,7 @@
 def shards(queries, key_cache, value_cache, block_list, block_count, *, n_pb, n_ka):
     kv_local = jnp.concatenate([key_cache, value_cache], axis=1)
     shard = gather_axis(kv_local, "pb", n_pb)
-    kv_all = gather_axis(shard, "ka", n_ka)
+    kv_pieces = pieces_axis(shard, "ka", n_ka)
 
     p = lax.axis_index("pb")
     k = lax.axis_index("ka")
@@ -124,9 +149,11 @@
     q_mine = lax.dynamic_slice_in_dim(queries, k * rows_mine, rows_mine, 0)
     bl_mine = lax.dynamic_slice_in_dim(block_list, k * n_local, n_local, 0)
     cnt_mine = lax.dynamic_slice_in_dim(block_count, k * n_local, n_local, 0)
-    qb0 = ((p * n_ka + k) * n_local).astype(jnp.int32).reshape(1)
+    qb0 = jnp.stack([(p * n_ka + k) * n_local, k]).astype(jnp.int32)
 
-    kernel = functools.partial(attend_kernel, n_local=n_local, group=4, scale=1.0 / math.sqrt(HD))
+    kernel = functools.partial(
+        attend_kernel, n_local=n_local, n_pieces=n_ka, group=4, scale=1.0 / math.sqrt(HD)
+    )
     return pl.pallas_call(
         kernel,
         out_shape=jax.ShapeDtypeStruct((rows_mine, queries.shape[1]), jnp.bfloat16),
@@ -135,8 +162,8 @@
             grid=(1,),
             in_specs=[
                 pl.BlockSpec((rows_mine, queries.shape[1]), lambda i, *_: (0, 0)),
-                pl.BlockSpec(memory_space=pl.ANY),
-            ],
+            ]
+            + [pl.BlockSpec(memory_space=pl.ANY)] * n_ka,
             out_specs=pl.BlockSpec((rows_mine, queries.shape[1]), lambda i, *_: (0, 0)),
             scratch_shapes=[
                 pltpu.SMEM((n_local, listed), jnp.int32),
@@ -147,7 +174,7 @@
             ],
         ),
         compiler_params=pltpu.CompilerParams(vmem_limit_bytes=48 * 1024 * 1024),
-    )(bl_mine, cnt_mine, qb0, q_mine, kv_all)
+    )(bl_mine, cnt_mine, qb0, q_mine, *kv_pieces)
 
 
 def solution(mesh):

time: 89.2 us -> 81.9 us (0.918)
  other arithmetic: 5.63 us -> 0.35 us
  waiting for transfers between devices: 53.5 us -> 51.2 us
  Pallas kernels: 22.7 us -> 23.7 us
    ppermute x5 -> x3, waiting for transfers between devices: 53.5 us -> 28.1 us  [gather_axis(): other = lax.ppermute(held, axis, [(i, i ^ b) for i in range(n)])]
    ppermute x0 -> x3, waiting for transfers between devices: none -> 23.1 us  [pieces_axis(): lax.ppermute(idx_pieces[x], axis, [(i, i ^ b) for i in range(n)])]
    select_n x5 -> x3, other arithmetic: 5.6 us -> 0.25 us  [gather_axis(): jnp.where(upper, jnp.concatenate([other, held], axis=t), jnp.concatenate(...]
    ppermute x5 -> x3, starting transfers between devices: 3.69 us -> 2.03 us  [gather_axis(): other = lax.ppermute(held, axis, [(i, i ^ b) for i in range(n)])]
    ppermute x0 -> x3, starting transfers between devices: none -> 1.59 us  [pieces_axis(): lax.ppermute(idx_pieces[x], axis, [(i, i ^ b) for i in range(n)])]
    pallas_call x1, Pallas kernels: 22.7 us -> 23.7 us  [shards(): pl.pallas_call(kernel, out_shape=jax.ShapeDtypeStruct((rows_mine, queries...]
  transfers between devices with their start and end apart: 5 -> 6, of which waited for: 5 -> 5; matrix products, arithmetic and copies ran while one was open for 1% -> 1% of each run, Pallas kernels for 0% -> 0%
where the time goes in v4:
time: 81.9 us; the launch traced here: 81.5 us
  waiting for transfers between devices  51.2 us (63%)
  Pallas kernels  23.7 us (29%)
  starting transfers between devices  3.62 us (4%)
  local copies, waits for them, and re-layouts  2.49 us (3%)
    ppermute x3, waiting for transfers between devices, gather_axis(): other = lax.ppermute(held, axis, [(i, i ^ b) for i in range(n)])  28.1 us
    pallas_call x1, Pallas kernels, shards(): pl.pallas_call(kernel, out_shape=jax.ShapeDtypeStruct((rows_mine, queries...  23.7 us
    ppermute x3, waiting for transfers between devices, pieces_axis(): lax.ppermute(idx_pieces[x], axis, [(i, i ^ b) for i in range(n)])  23.1 us
    ppermute x3, starting transfers between devices, gather_axis(): other = lax.ppermute(held, axis, [(i, i ^ b) for i in range(n)])  2.03 us
  transfers between devices with their start and end apart: 6, of which 5 were waited for; matrix products, arithmetic and copies ran while one was open for 1% of the time, Pallas kernels for 0%

profile of v4, /device:TPU:24, one launch (start us, length us, event | category | flops | bytes accessed | tf_op | source)
XLA Modules:
  0.0 81.5 jit_solution(14933200294693147089)
XLA Ops:
  0.0 0.0 copy-start
  0.0 0.0 copy-start.1
  0.0 0.9 %constant_dynamic-update-slice_fusion.1 = bf16[256,256]{1,0:T(8,128)(2,1)S(1)} fusion(bf16[256,128]{1,0:T(8,128)(2,1)} %param.6), kind=kLoop, calls=%fused_computation.6 | loop fusion | bytes 131072
  1.0 0.0 copy-done.1
  1.0 0.4 collective-permute-start
  1.4 8.5 %collective-permute-done = bf16[1,1,1,256,256]{4,3,0,2,1:T(8,128)(2,1)S(1)} collective-permute-done((bf16[1,1,1,256,256]{4,3,0,2,1:T(8,128)(2,1)S(1)}, bf16[1,1,1,256,256]{4,3,0,2,1:T(8,128)(2,1)S(1)}, u32[]{:S(2)}, u32[]{:S(2)}) %collective-permute-start) | collective-permute-done | bytes 131104 | tf_op jit(solution)/shard_map/ppermute | solution.py:24
  9.9 0.1 collective-permute-start.1
  10.1 8.1 %collective-permute-done.1 = bf16[2,1,1,256,256]{4,3,0,2,1:T(8,128)(2,1)S(1)} collective-permute-done((bf16[2,1,1,256,256]{4,3,0,2,1:T(8,128)(2,1)S(1)}, bf16[2,1,1,256,256]{4,3,0,2,1:T(8,128)(2,1)S(1)}, u32[]{:S(2)}, u32[]{:S(2)}) %collective-permute-start.1) | collective-permute-done | bytes 262176 | tf_op jit(solution)/shard_map/ppermute | solution.py:24
  18.2 0.1 maximum_select_fusion.1
  18.3 1.6 %collective-permute-start.2 = (bf16[2,2,1,256,256]{4,3,0,2,1:T(8,128)(2,1)S(1)}, bf16[2,2,1,256,256]{4,3,0,2,1:T(8,128)(2,1)S(1)}, u32[]{:S(2)}, u32[]{:S(2)}) collective-permute-start(bf16[2,2,1,256,256]{4,3,0,2,1:T(8,128)(2,1)S(1)} %maximum_select_fusion.1), channel_id=1, source_target_pairs={{0,4},{4,0},{8,12},{12,8},{16,20},{20,16},{24,28},{28,24},{1,5},{5... | collective-permute-start | bytes 1572872 | tf_op jit(solution)/shard_map/ppermute | solution.py:24
  19.8 11.5 %collective-permute-done.2 = bf16[2,2,1,256,256]{4,3,0,2,1:T(8,128)(2,1)S(1)} collective-permute-done((bf16[2,2,1,256,256]{4,3,0,2,1:T(8,128)(2,1)S(1)}, bf16[2,2,1,256,256]{4,3,0,2,1:T(8,128)(2,1)S(1)}, u32[]{:S(2)}, u32[]{:S(2)}) %collective-permute-start.2) | collective-permute-done | bytes 524320 | tf_op jit(solution)/shard_map/ppermute | solution.py:24
  31.3 0.1 maximum_select_fusion
  31.5 0.1 copy.6
  31.6 1.6 %collective-permute-start.4 = (bf16[2048,256]{1,0:T(8,128)(2,1)S(1)}, bf16[2048,256]{1,0:T(8,128)(2,1)S(1)}, u32[]{:S(2)}, u32[]{:S(2)}) collective-permute-start(bf16[2048,256]{1,0:T(8,128)(2,1)S(1)} %bitcast.8), channel_id=1, source_target_pairs={{0,2},{1,3},{2,0},{3,1},{4,6},{5,7},{6,4},{7,5},{8,10},{9,11},{10,... | collective-permute-start | bytes 3145736 | tf_op jit(solution)/shard_map/ppermute | solution.py:39
  33.2 0.0 collective-permute-start.3
  33.2 21.8 %collective-permute-done.4.rest_2_ = bf16[2048,256]{1,0:T(8,128)(2,1)S(1)} collective-permute-done((bf16[2048,256]{1,0:T(8,128)(2,1)S(1)}, bf16[2048,256]{1,0:T(8,128)(2,1)S(1)}, u32[]{:S(2)}, u32[]{:S(2)}) %collective-permute-start.4) | collective-permute-done | bytes 1048608 | tf_op jit(solution)/shard_map/ppermute | solution.py:39
  55.0 0.0 collective-permute-start.5
  55.0 0.0 copy-start.2
  55.0 0.7 copy-done.2
  55.7 0.1 dynamic_slice.10.cnt_ref
  55.7 0.1 pad_add_fusion.qb_ref
  55.8 0.7 constant_dynamic-slice_fusion.1.bl_ref
  56.5 0.0 copy-done
  56.5 0.0 collective-permute-done.3.rest_1_
  56.5 1.3 %collective-permute-done.5.rest_3_ = bf16[2048,256]{1,0:T(8,128)(2,1)} collective-permute-done((bf16[2048,256]{1,0:T(8,128)(2,1)S(1)}, bf16[2048,256]{1,0:T(8,128)(2,1)}, u32[]{:S(2)}, u32[]{:S(2)}) %collective-permute-start.5) | collective-permute-done | bytes 1048608 | tf_op jit(solution)/shard_map/ppermute | solution.py:39
  57.8 23.7 %shard_map.55 = bf16[256,512]{1,0:T(8,128)(2,1)} custom-call(s32[2,32]{1,0:T(2,128)S(1)} %constant_dynamic-slice_fusion.1.bl_ref, s32[2]{0:T(128)S(1)} %dynamic_slice.10.cnt_ref, s32[2]{0:T(128)S(1)} %pad_add_fusion.qb_ref, bf16[256,512]{1,0:T(8,128)(2,1)S(1)} %constant_dynamic-slice_fusion.q_ref, bf16[2048,256]{1,0:T(8,128)(2,1)S(1)} %bitcast.10, ...), custom_call_target="tpu_custom_call" | custom-call | tf_op jit(solution)/shard_map/pallas_call | solution.py:157
  (4 shorter events, 0.1 us)
Async XLA Ops:
  0.0 56.5 %copy-start = (bf16[1024,512]{1,0:T(8,128)(2,1)S(1)}, bf16[1024,512]{1,0:T(8,128)(2,1)}, u32[]{:S(2)}) copy-start(bf16[1024,512]{1,0:T(8,128)(2,1)} %param.5) | copy-start | bytes 3145732
  0.0 1.0 %copy-start.1 = (bf16[256,128]{1,0:T(8,128)(2,1)S(1)}, bf16[256,128]{1,0:T(8,128)(2,1)}, u32[]{:S(2)}) copy-start(bf16[256,128]{1,0:T(8,128)(2,1)} %param.7) | copy-start | bytes 196612
  1.0 8.9 %collective-permute-start = (bf16[1,1,1,256,256]{4,3,0,2,1:T(8,128)(2,1)S(1)}, bf16[1,1,1,256,256]{4,3,0,2,1:T(8,128)(2,1)S(1)}, u32[]{:S(2)}, u32[]{:S(2)}) collective-permute-start(bf16[1,1,1,256,256]{4,3,0,2,1:T(8,128)(2,1)S(1)} %bitcast.11), channel_id=1, source_target_pairs={{0,16},{4,20},{8,24},{12,28},{16,0},{20,4},{24,8},{28,12},{1,17},{... | collective-permute-start | bytes 393224 | tf_op jit(solution)/shard_map/ppermute | solution.py:24
  9.9 8.3 %collective-permute-start.1 = (bf16[2,1,1,256,256]{4,3,0,2,1:T(8,128)(2,1)S(1)}, bf16[2,1,1,256,256]{4,3,0,2,1:T(8,128)(2,1)S(1)}, u32[]{:S(2)}, u32[]{:S(2)}) collective-permute-start(bf16[2,1,1,256,256]{4,3,0,2,1:T(8,128)(2,1)S(1)} %maximum_select_fusion.2), channel_id=1, source_target_pairs={{0,8},{4,12},{8,0},{12,4},{16,24},{20,28},{24,16},{28,20},{1,9},{5... | collective-permute-start | bytes 786440 | tf_op jit(solution)/shard_map/ppermute | solution.py:24
  18.3 13.1 %collective-permute-start.2 = (bf16[2,2,1,256,256]{4,3,0,2,1:T(8,128)(2,1)S(1)}, bf16[2,2,1,256,256]{4,3,0,2,1:T(8,128)(2,1)S(1)}, u32[]{:S(2)}, u32[]{:S(2)}) collective-permute-start(bf16[2,2,1,256,256]{4,3,0,2,1:T(8,128)(2,1)S(1)} %maximum_select_fusion.1), channel_id=1, source_target_pairs={{0,4},{4,0},{8,12},{12,8},{16,20},{20,16},{24,28},{28,24},{1,5},{5... | collective-permute-start | bytes 1572872 | tf_op jit(solution)/shard_map/ppermute | solution.py:24
  31.6 23.4 %collective-permute-start.4 = (bf16[2048,256]{1,0:T(8,128)(2,1)S(1)}, bf16[2048,256]{1,0:T(8,128)(2,1)S(1)}, u32[]{:S(2)}, u32[]{:S(2)}) collective-permute-start(bf16[2048,256]{1,0:T(8,128)(2,1)S(1)} %bitcast.8), channel_id=1, source_target_pairs={{0,2},{1,3},{2,0},{3,1},{4,6},{5,7},{6,4},{7,5},{8,10},{9,11},{10,... | collective-permute-start | bytes 3145736 | tf_op jit(solution)/shard_map/ppermute | solution.py:39
  33.2 23.4 %collective-permute-start.3 = (bf16[2048,256]{1,0:T(8,128)(2,1)S(1)}, bf16[2048,256]{1,0:T(8,128)(2,1)}, u32[]{:S(2)}, u32[]{:S(2)}) collective-permute-start(bf16[2048,256]{1,0:T(8,128)(2,1)S(1)} %bitcast.9), channel_id=1, source_target_pairs={{0,1},{1,0},{2,3},{3,2},{4,5},{5,4},{6,7},{7,6},{8,9},{9,8},{10,11... | collective-permute-start | bytes 3145736 | tf_op jit(solution)/shard_map/ppermute | solution.py:39
  55.0 2.8 %collective-permute-start.5 = (bf16[2048,256]{1,0:T(8,128)(2,1)S(1)}, bf16[2048,256]{1,0:T(8,128)(2,1)}, u32[]{:S(2)}, u32[]{:S(2)}) collective-permute-start(bf16[2048,256]{1,0:T(8,128)(2,1)S(1)} %collective-permute-done.4.rest_2_), channel_id=1, source_target_pairs={{0,1},{1,0},{2,3},{3,2},{4,5},{5,4},{6,7},{7,6},{8,9},{9,8},{10,11... | collective-permute-start | bytes 3145736 | tf_op jit(solution)/shard_map/ppermute | solution.py:39
  55.0 0.7 copy-start.2

commit v5 on v4

--- a/solution.py
+++ b/solution.py
@@ -41,21 +41,24 @@
     return [idx_pieces[x] for x in range(n)]
 
 
-def attend_kernel(bl_ref, cnt_ref, qb_ref, q_ref, *rest, n_local, n_pieces, group, scale):
+def attend_kernel(bl_ref, cnt_ref, qb_ref, q_ref, *rest, n_local, n_pieces, n_ka, group, scale):
     kv_pieces = rest[:n_pieces]
     out_ref, off_ref, kvbuf, dbuf, sems, dsems = rest[n_pieces:]
     qb0 = qb_ref[0]
     me = qb_ref[1]
     width = kvbuf.shape[-1]
     per_piece = kv_pieces[0].shape[0] // BLK
+    n_half = n_pieces // n_ka
 
     class block_copy:
         def __init__(self, blk, dst, sem):
             self.blk, self.dst, self.sem = blk, dst, sem
 
         def start(self):
-            which = jnp.bitwise_xor(self.blk // per_piece, me)
-            start = pl.multiple_of((self.blk % per_piece) * BLK, BLK)
+            per_shard = per_piece * n_half
+            within = self.blk % per_shard
+            which = (within % n_half) * n_ka + jnp.bitwise_xor(self.blk // per_shard, me)
+            start = pl.multiple_of((within // n_half) * BLK, BLK)
             for x in range(n_pieces):
                 @pl.when(which == x)
                 def _(x=x, start=start):
@@ -138,8 +141,16 @@
 
 def shards(queries, key_cache, value_cache, block_list, block_count, *, n_pb, n_ka):
     kv_local = jnp.concatenate([key_cache, value_cache], axis=1)
-    shard = gather_axis(kv_local, "pb", n_pb)
-    kv_pieces = pieces_axis(shard, "ka", n_ka)
+    n_half = kv_local.shape[0] // BLK
+    kv_pieces = []
+    shard = None
+    for h in range(n_half):
+        part = kv_local[h * BLK:(h + 1) * BLK]
+        if shard is not None:
+            part, shard = lax.optimization_barrier((part, shard))
+            kv_pieces += pieces_axis(shard, "ka", n_ka)
+        shard = gather_axis(part, "pb", n_pb)
+    kv_pieces += pieces_axis(shard, "ka", n_ka)
 
     p = lax.axis_index("pb")
     k = lax.axis_index("ka")
@@ -152,7 +163,7 @@
     qb0 = jnp.stack([(p * n_ka + k) * n_local, k]).astype(jnp.int32)
 
     kernel = functools.partial(
-        attend_kernel, n_local=n_local, n_pieces=n_ka, group=4, scale=1.0 / math.sqrt(HD)
+        attend_kernel, n_local=n_local, n_pieces=len(kv_pieces), n_ka=n_ka, group=4, scale=1.0 / math.sqrt(HD)
     )
     return pl.pallas_call(
         kernel,
@@ -163,7 +174,7 @@
             in_specs=[
                 pl.BlockSpec((rows_mine, queries.shape[1]), lambda i, *_: (0, 0)),
             ]
-            + [pl.BlockSpec(memory_space=pl.ANY)] * n_ka,
+            + [pl.BlockSpec(memory_space=pl.ANY)] * len(kv_pieces),
             out_specs=pl.BlockSpec((rows_mine, queries.shape[1]), lambda i, *_: (0, 0)),
             scratch_shapes=[
                 pltpu.SMEM((n_local, listed), jnp.int32),

time: 81.9 us -> 79.7 us (0.973)
  waiting for transfers between devices: 51.2 us -> 44.3 us
  starting transfers between devices: 3.62 us -> 7.63 us
  Pallas kernels: 23.7 us -> 24.6 us
    ppermute x3 -> x6, waiting for transfers between devices: 23.1 us -> 14.1 us  [pieces_axis(): lax.ppermute(idx_pieces[x], axis, [(i, i ^ b) for i in range(n)])]
    ppermute x3 -> x6, waiting for transfers between devices: 28.1 us -> 30.2 us  [gather_axis(): other = lax.ppermute(held, axis, [(i, i ^ b) for i in range(n)])]
    ppermute x3 -> x6, starting transfers between devices: 1.59 us -> 3.62 us  [pieces_axis(): lax.ppermute(idx_pieces[x], axis, [(i, i ^ b) for i in range(n)])]
    ppermute x3 -> x6, starting transfers between devices: 2.03 us -> 4.01 us  [gather_axis(): other = lax.ppermute(held, axis, [(i, i ^ b) for i in range(n)])]
    pallas_call x1, Pallas kernels: 23.7 us -> 24.6 us  [shards(): pl.pallas_call(kernel, out_shape=jax.ShapeDtypeStruct((rows_mine, queries...]
  transfers between devices with their start and end apart: 6 -> 12, of which waited for: 5 -> 9; matrix products, arithmetic and copies ran while one was open for 1% -> 1% of each run, Pallas kernels for 0% -> 0%
where the time goes in v5:
time: 79.7 us; the launch traced here: 79.5 us
  waiting for transfers between devices  44.3 us (56%)
  Pallas kernels  24.6 us (31%)
  starting transfers between devices  7.63 us (10%)
  local copies, waits for them, and re-layouts  2.5 us (3%)
    ppermute x6, waiting for transfers between devices, gather_axis(): other = lax.ppermute(held, axis, [(i, i ^ b) for i in range(n)])  30.2 us
    pallas_call x1, Pallas kernels, shards(): pl.pallas_call(kernel, out_shape=jax.ShapeDtypeStruct((rows_mine, queries...  24.6 us
    ppermute x6, waiting for transfers between devices, pieces_axis(): lax.ppermute(idx_pieces[x], axis, [(i, i ^ b) for i in range(n)])  14.1 us
    ppermute x6, starting transfers between devices, gather_axis(): other = lax.ppermute(held, axis, [(i, i ^ b) for i in range(n)])  4.01 us
    ppermute x6, starting transfers between devices, pieces_axis(): lax.ppermute(idx_pieces[x], axis, [(i, i ^ b) for i in range(n)])  3.62 us
    unnamed x7, local copies, waits for them, and re-layouts  1.62 us
  transfers between devices with their start and end apart: 12, of which 9 were waited for; matrix products, arithmetic and copies ran while one was open for 1% of the time, Pallas kernels for 0%

profile of v5, /device:TPU:24, one launch (start us, length us, event | category | flops | bytes accessed | tf_op | source)
XLA Modules:
  0.0 79.5 jit_solution(7863741268747831720)
XLA Ops:
  0.0 0.0 copy-start
  0.0 0.0 copy-start.1
  0.0 0.9 %constant_dynamic-update-slice_fusion.1 = bf16[256,256]{1,0:T(8,128)(2,1)S(1)} fusion(bf16[256,128]{1,0:T(8,128)(2,1)} %param.6), kind=kLoop, calls=%fused_computation.16 | loop fusion | bytes 131072
  1.0 0.0 copy-done.1
  1.0 0.4 collective-permute-start
  1.4 5.7 %collective-permute-done = bf16[1,1,1,128,256]{4,3,2,1,0:T(8,128)(2,1)S(1)} collective-permute-done((bf16[1,1,1,128,256]{4,3,2,1,0:T(8,128)(2,1)S(1)}, bf16[1,1,1,128,256]{4,3,2,1,0:T(8,128)(2,1)S(1)}, u32[]{:S(2)}, u32[]{:S(2)}) %collective-permute-start) | collective-permute-done | bytes 65568 | tf_op jit(solution)/shard_map/ppermute | solution.py:24
  7.1 0.1 collective-permute-start.1
  7.3 5.0 %collective-permute-done.1 = bf16[2,1,1,128,256]{4,3,2,1,0:T(8,128)(2,1)S(1)} collective-permute-done((bf16[2,1,1,128,256]{4,3,2,1,0:T(8,128)(2,1)S(1)}, bf16[2,1,1,128,256]{4,3,2,1,0:T(8,128)(2,1)S(1)}, u32[]{:S(2)}, u32[]{:S(2)}) %collective-permute-start.1) | collective-permute-done | bytes 131104 | tf_op jit(solution)/shard_map/ppermute | solution.py:24
  12.3 0.1 maximum_select_fusion.2
  12.3 1.6 %collective-permute-start.2 = (bf16[2,2,1,128,256]{4,3,0,2,1:T(8,128)(2,1)S(1)}, bf16[2,2,1,128,256]{4,3,0,2,1:T(8,128)(2,1)S(1)}, u32[]{:S(2)}, u32[]{:S(2)}) collective-permute-start(bf16[2,2,1,128,256]{4,3,0,2,1:T(8,128)(2,1)S(1)} %maximum_select_fusion.2), channel_id=1, source_target_pairs={{0,4},{4,0},{8,12},{12,8},{16,20},{20,16},{24,28},{28,24},{1,5},{5... | collective-permute-start | bytes 786440 | tf_op jit(solution)/shard_map/ppermute | solution.py:24
  13.9 5.5 %collective-permute-done.2 = bf16[2,2,1,128,256]{4,3,0,2,1:T(8,128)(2,1)S(1)} collective-permute-done((bf16[2,2,1,128,256]{4,3,0,2,1:T(8,128)(2,1)S(1)}, bf16[2,2,1,128,256]{4,3,0,2,1:T(8,128)(2,1)S(1)}, u32[]{:S(2)}, u32[]{:S(2)}) %collective-permute-start.2) | collective-permute-done | bytes 262176 | tf_op jit(solution)/shard_map/ppermute | solution.py:24
  19.5 0.1 collective-permute-start.6
  19.6 6.0 %collective-permute-done.6 = bf16[1,1,1,128,256]{4,3,2,1,0:T(8,128)(2,1)S(1)} collective-permute-done((bf16[1,1,1,128,256]{4,3,2,1,0:T(8,128)(2,1)S(1)}, bf16[1,1,1,128,256]{4,3,2,1,0:T(8,128)(2,1)S(1)}, u32[]{:S(2)}, u32[]{:S(2)}) %collective-permute-start.6) | collective-permute-done | bytes 65568 | tf_op jit(solution)/shard_map/ppermute | solution.py:24
  25.6 0.4 collective-permute-start.7
  26.0 4.7 %collective-permute-done.7 = bf16[2,1,1,128,256]{4,3,0,2,1:T(8,128)(2,1)S(1)} collective-permute-done((bf16[2,1,1,128,256]{4,3,0,2,1:T(8,128)(2,1)S(1)}, bf16[2,1,1,128,256]{4,3,0,2,1:T(8,128)(2,1)S(1)}, u32[]{:S(2)}, u32[]{:S(2)}) %collective-permute-start.7) | collective-permute-done | bytes 131104 | tf_op jit(solution)/shard_map/ppermute | solution.py:24
  30.6 1.6 %collective-permute-start.8 = (bf16[2,2,1,128,256]{4,3,0,2,1:T(8,128)(2,1)S(1)}, bf16[2,2,1,128,256]{4,3,0,2,1:T(8,128)(2,1)S(1)}, u32[]{:S(2)}, u32[]{:S(2)}) collective-permute-start(bf16[2,2,1,128,256]{4,3,0,2,1:T(8,128)(2,1)S(1)} %maximum_select_fusion.3), channel_id=1, source_target_pairs={{0,4},{4,0},{8,12},{12,8},{16,20},{20,16},{24,28},{28,24},{1,5},{5... | collective-permute-start | bytes 786440 | tf_op jit(solution)/shard_map/ppermute | solution.py:24
  32.2 1.5 %collective-permute-start.4 = (bf16[1024,256]{1,0:T(8,128)(2,1)S(1)}, bf16[1024,256]{1,0:T(8,128)(2,1)S(1)}, u32[]{:S(2)}, u32[]{:S(2)}) collective-permute-start(bf16[1024,256]{1,0:T(8,128)(2,1)S(1)} %bitcast.28), channel_id=1, source_target_pairs={{0,2},{1,3},{2,0},{3,1},{4,6},{5,7},{6,4},{7,5},{8,10},{9,11},{10,... | collective-permute-start | bytes 1572872 | tf_op jit(solution)/shard_map/ppermute | solution.py:39
  33.7 3.4 %collective-permute-done.8 = bf16[2,2,1,128,256]{4,3,0,2,1:T(8,128)(2,1)S(1)} collective-permute-done((bf16[2,2,1,128,256]{4,3,0,2,1:T(8,128)(2,1)S(1)}, bf16[2,2,1,128,256]{4,3,0,2,1:T(8,128)(2,1)S(1)}, u32[]{:S(2)}, u32[]{:S(2)}) %collective-permute-start.8) | collective-permute-done | bytes 262176 | tf_op jit(solution)/shard_map/ppermute | solution.py:24
  37.2 1.6 %collective-permute-start.10 = (bf16[1024,256]{1,0:T(8,128)(2,1)S(1)}, bf16[1024,256]{1,0:T(8,128)(2,1)S(1)}, u32[]{:S(2)}, u32[]{:S(2)}) collective-permute-start(bf16[1024,256]{1,0:T(8,128)(2,1)S(1)} %bitcast.31), channel_id=1, source_target_pairs={{0,2},{1,3},{2,0},{3,1},{4,6},{5,7},{6,4},{7,5},{8,10},{9,11},{10,... | collective-permute-start | bytes 1572872 | tf_op jit(solution)/shard_map/ppermute | solution.py:39
  38.8 0.0 collective-permute-start.3
  38.8 0.5 collective-permute-start.9
  39.3 7.7 %collective-permute-done.4.rest_2_ = bf16[1024,256]{1,0:T(8,128)(2,1)S(1)} collective-permute-done((bf16[1024,256]{1,0:T(8,128)(2,1)S(1)}, bf16[1024,256]{1,0:T(8,128)(2,1)S(1)}, u32[]{:S(2)}, u32[]{:S(2)}) %collective-permute-start.4) | collective-permute-done | bytes 524320 | tf_op jit(solution)/shard_map/ppermute | solution.py:39
  47.0 0.0 collective-permute-start.5
  47.0 5.9 %collective-permute-done.10.rest_6_ = bf16[1024,256]{1,0:T(8,128)(2,1)S(1)} collective-permute-done((bf16[1024,256]{1,0:T(8,128)(2,1)S(1)}, bf16[1024,256]{1,0:T(8,128)(2,1)S(1)}, u32[]{:S(2)}, u32[]{:S(2)}) %collective-permute-start.10) | collective-permute-done | bytes 524320 | tf_op jit(solution)/shard_map/ppermute | solution.py:39
  52.9 0.0 collective-permute-start.11
  52.9 0.0 copy-start.2
  52.9 0.7 copy-done.2
  53.6 0.1 dynamic_slice.10.cnt_ref
  53.6 0.1 pad_add_fusion.qb_ref
  53.7 0.7 constant_dynamic-slice_fusion.1.bl_ref
  54.4 0.0 copy-done
  54.4 0.0 collective-permute-done.3.rest_1_
  54.4 0.0 collective-permute-done.9.rest_5_
  54.4 0.0 collective-permute-done.5.rest_3_
  54.5 0.5 collective-permute-done.11.rest_7_
  54.9 24.6 %shard_map.55 = bf16[256,512]{1,0:T(8,128)(2,1)} custom-call(s32[2,32]{1,0:T(2,128)S(1)} %constant_dynamic-slice_fusion.1.bl_ref, s32[2]{0:T(128)S(1)} %dynamic_slice.10.cnt_ref, s32[2]{0:T(128)S(1)} %pad_add_fusion.qb_ref, bf16[256,512]{1,0:T(8,128)(2,1)S(1)} %constant_dynamic-slice_fusion.q_ref, bf16[1024,256]{1,0:T(8,128)(2,1)S(1)} %bitcast.30, ...), custom_call_target="tpu_custom_call" | custom-call | tf_op jit(solution)/shard_map/pallas_call | solution.py:168
  (12 shorter events, 0.3 us)
Async XLA Ops:
  0.0 54.4 %copy-start = (bf16[1024,512]{1,0:T(8,128)(2,1)S(1)}, bf16[1024,512]{1,0:T(8,128)(2,1)}, u32[]{:S(2)}) copy-start(bf16[1024,512]{1,0:T(8,128)(2,1)} %param.5) | copy-start | bytes 3145732
  0.0 1.0 %copy-start.1 = (bf16[256,128]{1,0:T(8,128)(2,1)S(1)}, bf16[256,128]{1,0:T(8,128)(2,1)}, u32[]{:S(2)}) copy-start(bf16[256,128]{1,0:T(8,128)(2,1)} %param.7) | copy-start | bytes 196612
  1.0 6.1 %collective-permute-start = (bf16[1,1,1,128,256]{4,3,2,1,0:T(8,128)(2,1)S(1)}, bf16[1,1,1,128,256]{4,3,2,1,0:T(8,128)(2,1)S(1)}, u32[]{:S(2)}, u32[]{:S(2)}) collective-permute-start(bf16[1,1,1,128,256]{4,3,2,1,0:T(8,128)(2,1)S(1)} %get-tuple-element.12), channel_id=1, source_target_pairs={{0,16},{4,20},{8,24},{12,28},{16,0},{20,4},{24,8},{28,12},{1,17},{... | collective-permute-start | bytes 196616 | tf_op jit(solution)/shard_map/ppermute | solution.py:24
  7.1 5.1 %collective-permute-start.1 = (bf16[2,1,1,128,256]{4,3,2,1,0:T(8,128)(2,1)S(1)}, bf16[2,1,1,128,256]{4,3,2,1,0:T(8,128)(2,1)S(1)}, u32[]{:S(2)}, u32[]{:S(2)}) collective-permute-start(bf16[2,1,1,128,256]{4,3,2,1,0:T(8,128)(2,1)S(1)} %maximum_select_fusion.4), channel_id=1, source_target_pairs={{0,8},{4,12},{8,0},{12,4},{16,24},{20,28},{24,16},{28,20},{1,9},{5... | collective-permute-start | bytes 393224 | tf_op jit(solution)/shard_map/ppermute | solution.py:24
  12.3 7.1 %collective-permute-start.2 = (bf16[2,2,1,128,256]{4,3,0,2,1:T(8,128)(2,1)S(1)}, bf16[2,2,1,128,256]{4,3,0,2,1:T(8,128)(2,1)S(1)}, u32[]{:S(2)}, u32[]{:S(2)}) collective-permute-start(bf16[2,2,1,128,256]{4,3,0,2,1:T(8,128)(2,1)S(1)} %maximum_select_fusion.2), channel_id=1, source_target_pairs={{0,4},{4,0},{8,12},{12,8},{16,20},{20,16},{24,28},{28,24},{1,5},{5... | collective-permute-start | bytes 786440 | tf_op jit(solution)/shard_map/ppermute | solution.py:24
  19.5 6.0 %collective-permute-start.6 = (bf16[1,1,1,128,256]{4,3,2,1,0:T(8,128)(2,1)S(1)}, bf16[1,1,1,128,256]{4,3,2,1,0:T(8,128)(2,1)S(1)}, u32[]{:S(2)}, u32[]{:S(2)}) collective-permute-start(bf16[1,1,1,128,256]{4,3,2,1,0:T(8,128)(2,1)S(1)} %bitcast.34), channel_id=1, source_target_pairs={{0,16},{4,20},{8,24},{12,28},{16,0},{20,4},{24,8},{28,12},{1,17},{... | collective-permute-start | bytes 196616 | tf_op jit(solution)/shard_map/ppermute | solution.py:24
  25.6 5.0 %collective-permute-start.7 = (bf16[2,1,1,128,256]{4,3,0,2,1:T(8,128)(2,1)S(1)}, bf16[2,1,1,128,256]{4,3,0,2,1:T(8,128)(2,1)S(1)}, u32[]{:S(2)}, u32[]{:S(2)}) collective-permute-start(bf16[2,1,1,128,256]{4,3,0,2,1:T(8,128)(2,1)S(1)} %fusion), channel_id=1, source_target_pairs={{0,8},{4,12},{8,0},{12,4},{16,24},{20,28},{24,16},{28,20},{1,9},{5... | collective-permute-start | bytes 393224 | tf_op jit(solution)/shard_map/ppermute | solution.py:24
  30.6 6.4 %collective-permute-start.8 = (bf16[2,2,1,128,256]{4,3,0,2,1:T(8,128)(2,1)S(1)}, bf16[2,2,1,128,256]{4,3,0,2,1:T(8,128)(2,1)S(1)}, u32[]{:S(2)}, u32[]{:S(2)}) collective-permute-start(bf16[2,2,1,128,256]{4,3,0,2,1:T(8,128)(2,1)S(1)} %maximum_select_fusion.3), channel_id=1, source_target_pairs={{0,4},{4,0},{8,12},{12,8},{16,20},{20,16},{24,28},{28,24},{1,5},{5... | collective-permute-start | bytes 786440 | tf_op jit(solution)/shard_map/ppermute | solution.py:24
  32.2 14.8 %collective-permute-start.4 = (bf16[1024,256]{1,0:T(8,128)(2,1)S(1)}, bf16[1024,256]{1,0:T(8,128)(2,1)S(1)}, u32[]{:S(2)}, u32[]{:S(2)}) collective-permute-start(bf16[1024,256]{1,0:T(8,128)(2,1)S(1)} %bitcast.28), channel_id=1, source_target_pairs={{0,2},{1,3},{2,0},{3,1},{4,6},{5,7},{6,4},{7,5},{8,10},{9,11},{10,... | collective-permute-start | bytes 1572872 | tf_op jit(solution)/shard_map/ppermute | solution.py:39
  37.2 15.7 %collective-permute-start.10 = (bf16[1024,256]{1,0:T(8,128)(2,1)S(1)}, bf16[1024,256]{1,0:T(8,128)(2,1)S(1)}, u32[]{:S(2)}, u32[]{:S(2)}) collective-permute-start(bf16[1024,256]{1,0:T(8,128)(2,1)S(1)} %bitcast.31), channel_id=1, source_target_pairs={{0,2},{1,3},{2,0},{3,1},{4,6},{5,7},{6,4},{7,5},{8,10},{9,11},{10,... | collective-permute-start | bytes 1572872 | tf_op jit(solution)/shard_map/ppermute | solution.py:39
  38.8 15.7 %collective-permute-start.3 = (bf16[1024,256]{1,0:T(8,128)(2,1)S(1)}, bf16[1024,256]{1,0:T(8,128)(2,1)}, u32[]{:S(2)}, u32[]{:S(2)}) collective-permute-start(bf16[1024,256]{1,0:T(8,128)(2,1)S(1)} %bitcast.29), channel_id=1, source_target_pairs={{0,1},{1,0},{2,3},{3,2},{4,5},{5,4},{6,7},{7,6},{8,9},{9,8},{10,11... | collective-permute-start | bytes 1572872 | tf_op jit(solution)/shard_map/ppermute | solution.py:39
  38.8 15.7 %collective-permute-start.9 = (bf16[1024,256]{1,0:T(8,128)(2,1)S(1)}, bf16[1024,256]{1,0:T(8,128)(2,1)}, u32[]{:S(2)}, u32[]{:S(2)}) collective-permute-start(bf16[1024,256]{1,0:T(8,128)(2,1)S(1)} %bitcast.32), channel_id=1, source_target_pairs={{0,1},{1,0},{2,3},{3,2},{4,5},{5,4},{6,7},{7,6},{8,9},{9,8},{10,11... | collective-permute-start | bytes 1572872 | tf_op jit(solution)/shard_map/ppermute | solution.py:39
  47.0 7.4 %collective-permute-start.5 = (bf16[1024,256]{1,0:T(8,128)(2,1)S(1)}, bf16[1024,256]{1,0:T(8,128)(2,1)}, u32[]{:S(2)}, u32[]{:S(2)}) collective-permute-start(bf16[1024,256]{1,0:T(8,128)(2,1)S(1)} %collective-permute-done.4.rest_2_), channel_id=1, source_target_pairs={{0,1},{1,0},{2,3},{3,2},{4,5},{5,4},{6,7},{7,6},{8,9},{9,8},{10,11... | collective-permute-start | bytes 1572872 | tf_op jit(solution)/shard_map/ppermute | solution.py:39
  52.9 2.0 %collective-permute-start.11 = (bf16[1024,256]{1,0:T(8,128)(2,1)S(1)}, bf16[1024,256]{1,0:T(8,128)(2,1)}, u32[]{:S(2)}, u32[]{:S(2)}) collective-permute-start(bf16[1024,256]{1,0:T(8,128)(2,1)S(1)} %collective-permute-done.10.rest_6_), channel_id=1, source_target_pairs={{0,1},{1,0},{2,3},{3,2},{4,5},{5,4},{6,7},{7,6},{8,9},{9,8},{10,11... | collective-permute-start | bytes 1572872 | tf_op jit(solution)/shard_map/ppermute | solution.py:39
  52.9 0.7 copy-start.2

commit v6 on v5

--- a/solution.py
+++ b/solution.py
@@ -101,8 +101,8 @@
         v = kvb[:, HD:]
         sc = lax.dot_general(qs, k, dims, preferred_element_type=jnp.float32) * scale
         m_new = jnp.maximum(m, jnp.max(sc, axis=1, keepdims=True))
-        alpha = jnp.exp(m - m_new)
-        w = jnp.exp(sc - m_new)
+        alpha = jnp.exp2(m - m_new)
+        w = jnp.exp2(sc - m_new)
         l = alpha * l + jnp.sum(w, axis=1, keepdims=True)
         acc = alpha * acc + jnp.dot(w.astype(jnp.bfloat16), v, preferred_element_type=jnp.float32)
         return m_new, l, acc
@@ -116,7 +116,7 @@
         kvd = dbuf[j]
         sc = lax.dot_general(qs, kvd[:, :HD], dims, preferred_element_type=jnp.float32) * scale
         m = jnp.max(jnp.where(causal, sc, masked_score), axis=1, keepdims=True)
-        w = jnp.where(causal, jnp.exp(sc - m), 0.0)
+        w = jnp.where(causal, jnp.exp2(sc - m), 0.0)
         l = jnp.sum(w, axis=1, keepdims=True)
         acc = jnp.dot(w.astype(jnp.bfloat16), kvd[:, HD:], preferred_element_type=jnp.float32)
 
@@ -163,7 +163,7 @@
     qb0 = jnp.stack([(p * n_ka + k) * n_local, k]).astype(jnp.int32)
 
     kernel = functools.partial(
-        attend_kernel, n_local=n_local, n_pieces=len(kv_pieces), n_ka=n_ka, group=4, scale=1.0 / math.sqrt(HD)
+        attend_kernel, n_local=n_local, n_pieces=len(kv_pieces), n_ka=n_ka, group=4, scale=math.log2(math.e) / math.sqrt(HD)
     )
     return pl.pallas_call(
         kernel,

time: 79.7 us -> 79 us (level)
  no operation moved by 1% of the time
where the time goes in v6:
time: 79 us; the launch traced here: 78.8 us
  waiting for transfers between devices  44.3 us (56%)
  Pallas kernels  23.9 us (30%)
  starting transfers between devices  7.63 us (10%)
  local copies, waits for them, and re-layouts  2.5 us (3%)
    ppermute x6, waiting for transfers between devices, gather_axis(): other = lax.ppermute(held, axis, [(i, i ^ b) for i in range(n)])  30.2 us
    pallas_call x1, Pallas kernels, shards(): pl.pallas_call(kernel, out_shape=jax.ShapeDtypeStruct((rows_mine, queries...  23.9 us
    ppermute x6, waiting for transfers between devices, pieces_axis(): lax.ppermute(idx_pieces[x], axis, [(i, i ^ b) for i in range(n)])  14.1 us
    ppermute x6, starting transfers between devices, gather_axis(): other = lax.ppermute(held, axis, [(i, i ^ b) for i in range(n)])  4.01 us
    ppermute x6, starting transfers between devices, pieces_axis(): lax.ppermute(idx_pieces[x], axis, [(i, i ^ b) for i in range(n)])  3.62 us
    unnamed x7, local copies, waits for them, and re-layouts  1.62 us
  transfers between devices with their start and end apart: 12, of which 9 were waited for; matrix products, arithmetic and copies ran while one was open for 1% of the time, Pallas kernels for 0%

profile of v6, /device:TPU:24, one launch (start us, length us, event | category | flops | bytes accessed | tf_op | source)
XLA Modules:
  0.0 78.8 jit_solution(17804870627413208575)
XLA Ops:
  0.0 0.0 copy-start
  0.0 0.0 copy-start.1
  0.0 0.9 %constant_dynamic-update-slice_fusion.1 = bf16[256,256]{1,0:T(8,128)(2,1)S(1)} fusion(bf16[256,128]{1,0:T(8,128)(2,1)} %param.6), kind=kLoop, calls=%fused_computation.16 | loop fusion | bytes 131072
  1.0 0.0 copy-done.1
  1.0 0.4 collective-permute-start
  1.4 5.7 %collective-permute-done = bf16[1,1,1,128,256]{4,3,2,1,0:T(8,128)(2,1)S(1)} collective-permute-done((bf16[1,1,1,128,256]{4,3,2,1,0:T(8,128)(2,1)S(1)}, bf16[1,1,1,128,256]{4,3,2,1,0:T(8,128)(2,1)S(1)}, u32[]{:S(2)}, u32[]{:S(2)}) %collective-permute-start) | collective-permute-done | bytes 65568 | tf_op jit(solution)/shard_map/ppermute | solution.py:24
  7.1 0.1 collective-permute-start.1
  7.3 5.0 %collective-permute-done.1 = bf16[2,1,1,128,256]{4,3,2,1,0:T(8,128)(2,1)S(1)} collective-permute-done((bf16[2,1,1,128,256]{4,3,2,1,0:T(8,128)(2,1)S(1)}, bf16[2,1,1,128,256]{4,3,2,1,0:T(8,128)(2,1)S(1)}, u32[]{:S(2)}, u32[]{:S(2)}) %collective-permute-start.1) | collective-permute-done | bytes 131104 | tf_op jit(solution)/shard_map/ppermute | solution.py:24
  12.3 0.1 maximum_select_fusion.2
  12.3 1.6 %collective-permute-start.2 = (bf16[2,2,1,128,256]{4,3,0,2,1:T(8,128)(2,1)S(1)}, bf16[2,2,1,128,256]{4,3,0,2,1:T(8,128)(2,1)S(1)}, u32[]{:S(2)}, u32[]{:S(2)}) collective-permute-start(bf16[2,2,1,128,256]{4,3,0,2,1:T(8,128)(2,1)S(1)} %maximum_select_fusion.2), channel_id=1, source_target_pairs={{0,4},{4,0},{8,12},{12,8},{16,20},{20,16},{24,28},{28,24},{1,5},{5... | collective-permute-start | bytes 786440 | tf_op jit(solution)/shard_map/ppermute | solution.py:24
  13.9 5.5 %collective-permute-done.2 = bf16[2,2,1,128,256]{4,3,0,2,1:T(8,128)(2,1)S(1)} collective-permute-done((bf16[2,2,1,128,256]{4,3,0,2,1:T(8,128)(2,1)S(1)}, bf16[2,2,1,128,256]{4,3,0,2,1:T(8,128)(2,1)S(1)}, u32[]{:S(2)}, u32[]{:S(2)}) %collective-permute-start.2) | collective-permute-done | bytes 262176 | tf_op jit(solution)/shard_map/ppermute | solution.py:24
  19.5 0.1 collective-permute-start.6
  19.6 6.0 %collective-permute-done.6 = bf16[1,1,1,128,256]{4,3,2,1,0:T(8,128)(2,1)S(1)} collective-permute-done((bf16[1,1,1,128,256]{4,3,2,1,0:T(8,128)(2,1)S(1)}, bf16[1,1,1,128,256]{4,3,2,1,0:T(8,128)(2,1)S(1)}, u32[]{:S(2)}, u32[]{:S(2)}) %collective-permute-start.6) | collective-permute-done | bytes 65568 | tf_op jit(solution)/shard_map/ppermute | solution.py:24
  25.6 0.4 collective-permute-start.7
  26.0 4.7 %collective-permute-done.7 = bf16[2,1,1,128,256]{4,3,0,2,1:T(8,128)(2,1)S(1)} collective-permute-done((bf16[2,1,1,128,256]{4,3,0,2,1:T(8,128)(2,1)S(1)}, bf16[2,1,1,128,256]{4,3,0,2,1:T(8,128)(2,1)S(1)}, u32[]{:S(2)}, u32[]{:S(2)}) %collective-permute-start.7) | collective-permute-done | bytes 131104 | tf_op jit(solution)/shard_map/ppermute | solution.py:24
  30.6 1.6 %collective-permute-start.8 = (bf16[2,2,1,128,256]{4,3,0,2,1:T(8,128)(2,1)S(1)}, bf16[2,2,1,128,256]{4,3,0,2,1:T(8,128)(2,1)S(1)}, u32[]{:S(2)}, u32[]{:S(2)}) collective-permute-start(bf16[2,2,1,128,256]{4,3,0,2,1:T(8,128)(2,1)S(1)} %maximum_select_fusion.3), channel_id=1, source_target_pairs={{0,4},{4,0},{8,12},{12,8},{16,20},{20,16},{24,28},{28,24},{1,5},{5... | collective-permute-start | bytes 786440 | tf_op jit(solution)/shard_map/ppermute | solution.py:24
  32.2 1.5 %collective-permute-start.4 = (bf16[1024,256]{1,0:T(8,128)(2,1)S(1)}, bf16[1024,256]{1,0:T(8,128)(2,1)S(1)}, u32[]{:S(2)}, u32[]{:S(2)}) collective-permute-start(bf16[1024,256]{1,0:T(8,128)(2,1)S(1)} %bitcast.28), channel_id=1, source_target_pairs={{0,2},{1,3},{2,0},{3,1},{4,6},{5,7},{6,4},{7,5},{8,10},{9,11},{10,... | collective-permute-start | bytes 1572872 | tf_op jit(solution)/shard_map/ppermute | solution.py:39
  33.7 3.4 %collective-permute-done.8 = bf16[2,2,1,128,256]{4,3,0,2,1:T(8,128)(2,1)S(1)} collective-permute-done((bf16[2,2,1,128,256]{4,3,0,2,1:T(8,128)(2,1)S(1)}, bf16[2,2,1,128,256]{4,3,0,2,1:T(8,128)(2,1)S(1)}, u32[]{:S(2)}, u32[]{:S(2)}) %collective-permute-start.8) | collective-permute-done | bytes 262176 | tf_op jit(solution)/shard_map/ppermute | solution.py:24
  37.2 1.6 %collective-permute-start.10 = (bf16[1024,256]{1,0:T(8,128)(2,1)S(1)}, bf16[1024,256]{1,0:T(8,128)(2,1)S(1)}, u32[]{:S(2)}, u32[]{:S(2)}) collective-permute-start(bf16[1024,256]{1,0:T(8,128)(2,1)S(1)} %bitcast.31), channel_id=1, source_target_pairs={{0,2},{1,3},{2,0},{3,1},{4,6},{5,7},{6,4},{7,5},{8,10},{9,11},{10,... | collective-permute-start | bytes 1572872 | tf_op jit(solution)/shard_map/ppermute | solution.py:39
  38.8 0.0 collective-permute-start.3
  38.8 0.5 collective-permute-start.9
  39.3 7.7 %collective-permute-done.4.rest_2_ = bf16[1024,256]{1,0:T(8,128)(2,1)S(1)} collective-permute-done((bf16[1024,256]{1,0:T(8,128)(2,1)S(1)}, bf16[1024,256]{1,0:T(8,128)(2,1)S(1)}, u32[]{:S(2)}, u32[]{:S(2)}) %collective-permute-start.4) | collective-permute-done | bytes 524320 | tf_op jit(solution)/shard_map/ppermute | solution.py:39
  47.0 0.0 collective-permute-start.5
  47.0 5.9 %collective-permute-done.10.rest_6_ = bf16[1024,256]{1,0:T(8,128)(2,1)S(1)} collective-permute-done((bf16[1024,256]{1,0:T(8,128)(2,1)S(1)}, bf16[1024,256]{1,0:T(8,128)(2,1)S(1)}, u32[]{:S(2)}, u32[]{:S(2)}) %collective-permute-start.10) | collective-permute-done | bytes 524320 | tf_op jit(solution)/shard_map/ppermute | solution.py:39
  52.9 0.0 collective-permute-start.11
  52.9 0.0 copy-start.2
  52.9 0.7 copy-done.2
  53.6 0.1 dynamic_slice.10.cnt_ref
  53.6 0.1 pad_add_fusion.qb_ref
  53.7 0.7 constant_dynamic-slice_fusion.1.bl_ref
  54.4 0.0 copy-done
  54.4 0.0 collective-permute-done.3.rest_1_
  54.4 0.0 collective-permute-done.9.rest_5_
  54.4 0.0 collective-permute-done.5.rest_3_
  54.5 0.5 collective-permute-done.11.rest_7_
  54.9 23.9 %shard_map.55 = bf16[256,512]{1,0:T(8,128)(2,1)} custom-call(s32[2,32]{1,0:T(2,128)S(1)} %constant_dynamic-slice_fusion.1.bl_ref, s32[2]{0:T(128)S(1)} %dynamic_slice.10.cnt_ref, s32[2]{0:T(128)S(1)} %pad_add_fusion.qb_ref, bf16[256,512]{1,0:T(8,128)(2,1)S(1)} %constant_dynamic-slice_fusion.q_ref, bf16[1024,256]{1,0:T(8,128)(2,1)S(1)} %bitcast.30, ...), custom_call_target="tpu_custom_call" | custom-call | tf_op jit(solution)/shard_map/pallas_call | solution.py:168
  (12 shorter events, 0.3 us)
Async XLA Ops:
  0.0 54.4 %copy-start = (bf16[1024,512]{1,0:T(8,128)(2,1)S(1)}, bf16[1024,512]{1,0:T(8,128)(2,1)}, u32[]{:S(2)}) copy-start(bf16[1024,512]{1,0:T(8,128)(2,1)} %param.5) | copy-start | bytes 3145732
  0.0 1.0 %copy-start.1 = (bf16[256,128]{1,0:T(8,128)(2,1)S(1)}, bf16[256,128]{1,0:T(8,128)(2,1)}, u32[]{:S(2)}) copy-start(bf16[256,128]{1,0:T(8,128)(2,1)} %param.7) | copy-start | bytes 196612
  1.0 6.1 %collective-permute-start = (bf16[1,1,1,128,256]{4,3,2,1,0:T(8,128)(2,1)S(1)}, bf16[1,1,1,128,256]{4,3,2,1,0:T(8,128)(2,1)S(1)}, u32[]{:S(2)}, u32[]{:S(2)}) collective-permute-start(bf16[1,1,1,128,256]{4,3,2,1,0:T(8,128)(2,1)S(1)} %get-tuple-element.12), channel_id=1, source_target_pairs={{0,16},{4,20},{8,24},{12,28},{16,0},{20,4},{24,8},{28,12},{1,17},{... | collective-permute-start | bytes 196616 | tf_op jit(solution)/shard_map/ppermute | solution.py:24
  7.1 5.1 %collective-permute-start.1 = (bf16[2,1,1,128,256]{4,3,2,1,0:T(8,128)(2,1)S(1)}, bf16[2,1,1,128,256]{4,3,2,1,0:T(8,128)(2,1)S(1)}, u32[]{:S(2)}, u32[]{:S(2)}) collective-permute-start(bf16[2,1,1,128,256]{4,3,2,1,0:T(8,128)(2,1)S(1)} %maximum_select_fusion.4), channel_id=1, source_target_pairs={{0,8},{4,12},{8,0},{12,4},{16,24},{20,28},{24,16},{28,20},{1,9},{5... | collective-permute-start | bytes 393224 | tf_op jit(solution)/shard_map/ppermute | solution.py:24
  12.3 7.1 %collective-permute-start.2 = (bf16[2,2,1,128,256]{4,3,0,2,1:T(8,128)(2,1)S(1)}, bf16[2,2,1,128,256]{4,3,0,2,1:T(8,128)(2,1)S(1)}, u32[]{:S(2)}, u32[]{:S(2)}) collective-permute-start(bf16[2,2,1,128,256]{4,3,0,2,1:T(8,128)(2,1)S(1)} %maximum_select_fusion.2), channel_id=1, source_target_pairs={{0,4},{4,0},{8,12},{12,8},{16,20},{20,16},{24,28},{28,24},{1,5},{5... | collective-permute-start | bytes 786440 | tf_op jit(solution)/shard_map/ppermute | solution.py:24
  19.5 6.0 %collective-permute-start.6 = (bf16[1,1,1,128,256]{4,3,2,1,0:T(8,128)(2,1)S(1)}, bf16[1,1,1,128,256]{4,3,2,1,0:T(8,128)(2,1)S(1)}, u32[]{:S(2)}, u32[]{:S(2)}) collective-permute-start(bf16[1,1,1,128,256]{4,3,2,1,0:T(8,128)(2,1)S(1)} %bitcast.34), channel_id=1, source_target_pairs={{0,16},{4,20},{8,24},{12,28},{16,0},{20,4},{24,8},{28,12},{1,17},{... | collective-permute-start | bytes 196616 | tf_op jit(solution)/shard_map/ppermute | solution.py:24
  25.6 5.0 %collective-permute-start.7 = (bf16[2,1,1,128,256]{4,3,0,2,1:T(8,128)(2,1)S(1)}, bf16[2,1,1,128,256]{4,3,0,2,1:T(8,128)(2,1)S(1)}, u32[]{:S(2)}, u32[]{:S(2)}) collective-permute-start(bf16[2,1,1,128,256]{4,3,0,2,1:T(8,128)(2,1)S(1)} %fusion), channel_id=1, source_target_pairs={{0,8},{4,12},{8,0},{12,4},{16,24},{20,28},{24,16},{28,20},{1,9},{5... | collective-permute-start | bytes 393224 | tf_op jit(solution)/shard_map/ppermute | solution.py:24
  30.6 6.4 %collective-permute-start.8 = (bf16[2,2,1,128,256]{4,3,0,2,1:T(8,128)(2,1)S(1)}, bf16[2,2,1,128,256]{4,3,0,2,1:T(8,128)(2,1)S(1)}, u32[]{:S(2)}, u32[]{:S(2)}) collective-permute-start(bf16[2,2,1,128,256]{4,3,0,2,1:T(8,128)(2,1)S(1)} %maximum_select_fusion.3), channel_id=1, source_target_pairs={{0,4},{4,0},{8,12},{12,8},{16,20},{20,16},{24,28},{28,24},{1,5},{5... | collective-permute-start | bytes 786440 | tf_op jit(solution)/shard_map/ppermute | solution.py:24
  32.2 14.8 %collective-permute-start.4 = (bf16[1024,256]{1,0:T(8,128)(2,1)S(1)}, bf16[1024,256]{1,0:T(8,128)(2,1)S(1)}, u32[]{:S(2)}, u32[]{:S(2)}) collective-permute-start(bf16[1024,256]{1,0:T(8,128)(2,1)S(1)} %bitcast.28), channel_id=1, source_target_pairs={{0,2},{1,3},{2,0},{3,1},{4,6},{5,7},{6,4},{7,5},{8,10},{9,11},{10,... | collective-permute-start | bytes 1572872 | tf_op jit(solution)/shard_map/ppermute | solution.py:39
  37.2 15.7 %collective-permute-start.10 = (bf16[1024,256]{1,0:T(8,128)(2,1)S(1)}, bf16[1024,256]{1,0:T(8,128)(2,1)S(1)}, u32[]{:S(2)}, u32[]{:S(2)}) collective-permute-start(bf16[1024,256]{1,0:T(8,128)(2,1)S(1)} %bitcast.31), channel_id=1, source_target_pairs={{0,2},{1,3},{2,0},{3,1},{4,6},{5,7},{6,4},{7,5},{8,10},{9,11},{10,... | collective-permute-start | bytes 1572872 | tf_op jit(solution)/shard_map/ppermute | solution.py:39
  38.8 15.7 %collective-permute-start.3 = (bf16[1024,256]{1,0:T(8,128)(2,1)S(1)}, bf16[1024,256]{1,0:T(8,128)(2,1)}, u32[]{:S(2)}, u32[]{:S(2)}) collective-permute-start(bf16[1024,256]{1,0:T(8,128)(2,1)S(1)} %bitcast.29), channel_id=1, source_target_pairs={{0,1},{1,0},{2,3},{3,2},{4,5},{5,4},{6,7},{7,6},{8,9},{9,8},{10,11... | collective-permute-start | bytes 1572872 | tf_op jit(solution)/shard_map/ppermute | solution.py:39
  38.8 15.7 %collective-permute-start.9 = (bf16[1024,256]{1,0:T(8,128)(2,1)S(1)}, bf16[1024,256]{1,0:T(8,128)(2,1)}, u32[]{:S(2)}, u32[]{:S(2)}) collective-permute-start(bf16[1024,256]{1,0:T(8,128)(2,1)S(1)} %bitcast.32), channel_id=1, source_target_pairs={{0,1},{1,0},{2,3},{3,2},{4,5},{5,4},{6,7},{7,6},{8,9},{9,8},{10,11... | collective-permute-start | bytes 1572872 | tf_op jit(solution)/shard_map/ppermute | solution.py:39
  47.0 7.4 %collective-permute-start.5 = (bf16[1024,256]{1,0:T(8,128)(2,1)S(1)}, bf16[1024,256]{1,0:T(8,128)(2,1)}, u32[]{:S(2)}, u32[]{:S(2)}) collective-permute-start(bf16[1024,256]{1,0:T(8,128)(2,1)S(1)} %collective-permute-done.4.rest_2_), channel_id=1, source_target_pairs={{0,1},{1,0},{2,3},{3,2},{4,5},{5,4},{6,7},{7,6},{8,9},{9,8},{10,11... | collective-permute-start | bytes 1572872 | tf_op jit(solution)/shard_map/ppermute | solution.py:39
  52.9 2.0 %collective-permute-start.11 = (bf16[1024,256]{1,0:T(8,128)(2,1)S(1)}, bf16[1024,256]{1,0:T(8,128)(2,1)}, u32[]{:S(2)}, u32[]{:S(2)}) collective-permute-start(bf16[1024,256]{1,0:T(8,128)(2,1)S(1)} %collective-permute-done.10.rest_6_), channel_id=1, source_target_pairs={{0,1},{1,0},{2,3},{3,2},{4,5},{5,4},{6,7},{7,6},{8,9},{9,8},{10,11... | collective-permute-start | bytes 1572872 | tf_op jit(solution)/shard_map/ppermute | solution.py:39
  52.9 0.7 copy-start.2

commit v7 on v6

--- a/solution.py
+++ b/solution.py
@@ -89,54 +89,59 @@
 
         lax.fori_loop(0, n_j, issue, 0)
 
-    rows = QH * BLK
-    rowpos = lax.broadcasted_iota(jnp.int32, (rows, BLK), 0) % BLK
-    col = lax.broadcasted_iota(jnp.int32, (rows, BLK), 1)
+    rowpos = lax.broadcasted_iota(jnp.int32, (BLK, BLK), 0)
+    col = lax.broadcasted_iota(jnp.int32, (BLK, BLK), 1)
     causal = col <= rowpos
     dims = (((1,), (1,)), ((), ()))
 
-    def update(qs, kvb, carry):
-        m, l, acc = carry
+    def update(qh, kvb, carry):
         k = kvb[:, :HD]
         v = kvb[:, HD:]
-        sc = lax.dot_general(qs, k, dims, preferred_element_type=jnp.float32) * scale
-        m_new = jnp.maximum(m, jnp.max(sc, axis=1, keepdims=True))
-        alpha = jnp.exp2(m - m_new)
-        w = jnp.exp2(sc - m_new)
-        l = alpha * l + jnp.sum(w, axis=1, keepdims=True)
-        acc = alpha * acc + jnp.dot(w.astype(jnp.bfloat16), v, preferred_element_type=jnp.float32)
-        return m_new, l, acc
+        out = []
+        for h in range(QH):
+            m, l, acc = carry[h]
+            sc = lax.dot_general(qh[h], k, dims, preferred_element_type=jnp.float32) * scale
+            m_new = jnp.maximum(m, jnp.max(sc, axis=1, keepdims=True))
+            alpha = jnp.exp2(m - m_new)
+            w = jnp.exp2(sc - m_new)
+            l = alpha * l + jnp.sum(w, axis=1, keepdims=True)
+            acc = alpha * acc + jnp.dot(w.astype(jnp.bfloat16), v, preferred_element_type=jnp.float32)
+            out.append((m_new, l, acc))
+        return tuple(out)
 
     for j in range(n_local):
         qb = qb0 + j
-        qrows = q_ref[j * BLK:(j + 1) * BLK, :]
-        qs = jnp.concatenate([qrows[:, h * HD:(h + 1) * HD] for h in range(QH)], axis=0)
+        qh = [q_ref[j * BLK:(j + 1) * BLK, h * HD:(h + 1) * HD] for h in range(QH)]
 
         block_copy(qb, dbuf.at[j], dsems.at[j]).wait()
         kvd = dbuf[j]
-        sc = lax.dot_general(qs, kvd[:, :HD], dims, preferred_element_type=jnp.float32) * scale
-        m = jnp.max(jnp.where(causal, sc, masked_score), axis=1, keepdims=True)
-        w = jnp.where(causal, jnp.exp2(sc - m), 0.0)
-        l = jnp.sum(w, axis=1, keepdims=True)
-        acc = jnp.dot(w.astype(jnp.bfloat16), kvd[:, HD:], preferred_element_type=jnp.float32)
-
-        def grouped(g, carry, j=j, qs=qs):
+        carry = []
+        for h in range(QH):
+            sc = lax.dot_general(qh[h], kvd[:, :HD], dims, preferred_element_type=jnp.float32) * scale
+            m = jnp.max(jnp.where(causal, sc, masked_score), axis=1, keepdims=True)
+            w = jnp.where(causal, jnp.exp2(sc - m), 0.0)
+            l = jnp.sum(w, axis=1, keepdims=True)
+            acc = jnp.dot(w.astype(jnp.bfloat16), kvd[:, HD:], preferred_element_type=jnp.float32)
+            carry.append((m, l, acc))
+        carry = tuple(carry)
+
+        def grouped(g, carry, j=j, qh=qh):
             first = g * group
             for i in range(group):
                 copy(j, first + i).wait()
             kvb = kvbuf[j, pl.ds(first, group)].reshape(group * BLK, width)
-            return update(qs, kvb, carry)
-
-        def single(s, carry, j=j, qs=qs):
+            return update(qh, kvb, carry)
+
+        def single(s, carry, j=j, qh=qh):
             copy(j, s).wait()
-            return update(qs, kvbuf[j, s], carry)
+            return update(qh, kvbuf[j, s], carry)
 
         n_groups = n_off[j] // group
-        carry = lax.fori_loop(0, n_groups, grouped, (m, l, acc))
-        m, l, acc = lax.fori_loop(n_groups * group, n_off[j], single, carry)
-        res = (acc / l).astype(out_ref.dtype)
+        carry = lax.fori_loop(0, n_groups, grouped, carry)
+        carry = lax.fori_loop(n_groups * group, n_off[j], single, carry)
         for h in range(QH):
-            out_ref[j * BLK:(j + 1) * BLK, h * HD:(h + 1) * HD] = res[h * BLK:(h + 1) * BLK, :]
+            m, l, acc = carry[h]
+            out_ref[j * BLK:(j + 1) * BLK, h * HD:(h + 1) * HD] = (acc / l).astype(out_ref.dtype)
 
 
 def shards(queries, key_cache, value_cache, block_list, block_count, *, n_pb, n_ka):

time: 79 us -> 93.2 us (1.18)
  Pallas kernels: 23.9 us -> 38.1 us
    pallas_call x1, Pallas kernels: 23.9 us -> 38.1 us  [shards(): pl.pallas_call(kernel, out_shape=jax.ShapeDtypeStruct((rows_mine, queries...]
where the time goes in v7:
time: 93.2 us; the launch traced here: 93 us
  waiting for transfers between devices  44.3 us (48%)
  Pallas kernels  38.1 us (41%)
  starting transfers between devices  7.63 us (8%)
  local copies, waits for them, and re-layouts  2.5 us (3%)
    pallas_call x1, Pallas kernels, shards(): pl.pallas_call(kernel, out_shape=jax.ShapeDtypeStruct((rows_mine, queries...  38.1 us
    ppermute x6, waiting for transfers between devices, gather_axis(): other = lax.ppermute(held, axis, [(i, i ^ b) for i in range(n)])  30.2 us
    ppermute x6, waiting for transfers between devices, pieces_axis(): lax.ppermute(idx_pieces[x], axis, [(i, i ^ b) for i in range(n)])  14.1 us
    ppermute x6, starting transfers between devices, gather_axis(): other = lax.ppermute(held, axis, [(i, i ^ b) for i in range(n)])  4.01 us
    ppermute x6, starting transfers between devices, pieces_axis(): lax.ppermute(idx_pieces[x], axis, [(i, i ^ b) for i in range(n)])  3.62 us
  transfers between devices with their start and end apart: 12, of which 9 were waited for; matrix products, arithmetic and copies ran while one was open for 1% of the time, Pallas kernels for 0%

profile of v7, /device:TPU:24, one launch (start us, length us, event | category | flops | bytes accessed | tf_op | source)
XLA Modules:
  0.0 93.0 jit_solution(2250338952276726908)
XLA Ops:
  0.0 0.0 copy-start
  0.0 0.0 copy-start.1
  0.0 0.9 %constant_dynamic-update-slice_fusion.1 = bf16[256,256]{1,0:T(8,128)(2,1)S(1)} fusion(bf16[256,128]{1,0:T(8,128)(2,1)} %param.6), kind=kLoop, calls=%fused_computation.16 | loop fusion | bytes 131072
  1.0 0.0 copy-done.1
  1.0 0.4 collective-permute-start
  1.4 5.7 %collective-permute-done = bf16[1,1,1,128,256]{4,3,2,1,0:T(8,128)(2,1)S(1)} collective-permute-done((bf16[1,1,1,128,256]{4,3,2,1,0:T(8,128)(2,1)S(1)}, bf16[1,1,1,128,256]{4,3,2,1,0:T(8,128)(2,1)S(1)}, u32[]{:S(2)}, u32[]{:S(2)}) %collective-permute-start) | collective-permute-done | bytes 65568 | tf_op jit(solution)/shard_map/ppermute | solution.py:24
  7.1 0.1 collective-permute-start.1
  7.3 5.0 %collective-permute-done.1 = bf16[2,1,1,128,256]{4,3,2,1,0:T(8,128)(2,1)S(1)} collective-permute-done((bf16[2,1,1,128,256]{4,3,2,1,0:T(8,128)(2,1)S(1)}, bf16[2,1,1,128,256]{4,3,2,1,0:T(8,128)(2,1)S(1)}, u32[]{:S(2)}, u32[]{:S(2)}) %collective-permute-start.1) | collective-permute-done | bytes 131104 | tf_op jit(solution)/shard_map/ppermute | solution.py:24
  12.3 0.1 maximum_select_fusion.2
  12.3 1.6 %collective-permute-start.2 = (bf16[2,2,1,128,256]{4,3,0,2,1:T(8,128)(2,1)S(1)}, bf16[2,2,1,128,256]{4,3,0,2,1:T(8,128)(2,1)S(1)}, u32[]{:S(2)}, u32[]{:S(2)}) collective-permute-start(bf16[2,2,1,128,256]{4,3,0,2,1:T(8,128)(2,1)S(1)} %maximum_select_fusion.2), channel_id=1, source_target_pairs={{0,4},{4,0},{8,12},{12,8},{16,20},{20,16},{24,28},{28,24},{1,5},{5... | collective-permute-start | bytes 786440 | tf_op jit(solution)/shard_map/ppermute | solution.py:24
  13.9 5.5 %collective-permute-done.2 = bf16[2,2,1,128,256]{4,3,0,2,1:T(8,128)(2,1)S(1)} collective-permute-done((bf16[2,2,1,128,256]{4,3,0,2,1:T(8,128)(2,1)S(1)}, bf16[2,2,1,128,256]{4,3,0,2,1:T(8,128)(2,1)S(1)}, u32[]{:S(2)}, u32[]{:S(2)}) %collective-permute-start.2) | collective-permute-done | bytes 262176 | tf_op jit(solution)/shard_map/ppermute | solution.py:24
  19.5 0.1 collective-permute-start.6
  19.6 6.0 %collective-permute-done.6 = bf16[1,1,1,128,256]{4,3,2,1,0:T(8,128)(2,1)S(1)} collective-permute-done((bf16[1,1,1,128,256]{4,3,2,1,0:T(8,128)(2,1)S(1)}, bf16[1,1,1,128,256]{4,3,2,1,0:T(8,128)(2,1)S(1)}, u32[]{:S(2)}, u32[]{:S(2)}) %collective-permute-start.6) | collective-permute-done | bytes 65568 | tf_op jit(solution)/shard_map/ppermute | solution.py:24
  25.6 0.4 collective-permute-start.7
  26.0 4.7 %collective-permute-done.7 = bf16[2,1,1,128,256]{4,3,0,2,1:T(8,128)(2,1)S(1)} collective-permute-done((bf16[2,1,1,128,256]{4,3,0,2,1:T(8,128)(2,1)S(1)}, bf16[2,1,1,128,256]{4,3,0,2,1:T(8,128)(2,1)S(1)}, u32[]{:S(2)}, u32[]{:S(2)}) %collective-permute-start.7) | collective-permute-done | bytes 131104 | tf_op jit(solution)/shard_map/ppermute | solution.py:24
  30.6 1.6 %collective-permute-start.8 = (bf16[2,2,1,128,256]{4,3,0,2,1:T(8,128)(2,1)S(1)}, bf16[2,2,1,128,256]{4,3,0,2,1:T(8,128)(2,1)S(1)}, u32[]{:S(2)}, u32[]{:S(2)}) collective-permute-start(bf16[2,2,1,128,256]{4,3,0,2,1:T(8,128)(2,1)S(1)} %maximum_select_fusion.3), channel_id=1, source_target_pairs={{0,4},{4,0},{8,12},{12,8},{16,20},{20,16},{24,28},{28,24},{1,5},{5... | collective-permute-start | bytes 786440 | tf_op jit(solution)/shard_map/ppermute | solution.py:24
  32.2 1.5 %collective-permute-start.4 = (bf16[1024,256]{1,0:T(8,128)(2,1)S(1)}, bf16[1024,256]{1,0:T(8,128)(2,1)S(1)}, u32[]{:S(2)}, u32[]{:S(2)}) collective-permute-start(bf16[1024,256]{1,0:T(8,128)(2,1)S(1)} %bitcast.28), channel_id=1, source_target_pairs={{0,2},{1,3},{2,0},{3,1},{4,6},{5,7},{6,4},{7,5},{8,10},{9,11},{10,... | collective-permute-start | bytes 1572872 | tf_op jit(solution)/shard_map/ppermute | solution.py:39
  33.7 3.4 %collective-permute-done.8 = bf16[2,2,1,128,256]{4,3,0,2,1:T(8,128)(2,1)S(1)} collective-permute-done((bf16[2,2,1,128,256]{4,3,0,2,1:T(8,128)(2,1)S(1)}, bf16[2,2,1,128,256]{4,3,0,2,1:T(8,128)(2,1)S(1)}, u32[]{:S(2)}, u32[]{:S(2)}) %collective-permute-start.8) | collective-permute-done | bytes 262176 | tf_op jit(solution)/shard_map/ppermute | solution.py:24
  37.2 1.6 %collective-permute-start.10 = (bf16[1024,256]{1,0:T(8,128)(2,1)S(1)}, bf16[1024,256]{1,0:T(8,128)(2,1)S(1)}, u32[]{:S(2)}, u32[]{:S(2)}) collective-permute-start(bf16[1024,256]{1,0:T(8,128)(2,1)S(1)} %bitcast.31), channel_id=1, source_target_pairs={{0,2},{1,3},{2,0},{3,1},{4,6},{5,7},{6,4},{7,5},{8,10},{9,11},{10,... | collective-permute-start | bytes 1572872 | tf_op jit(solution)/shard_map/ppermute | solution.py:39
  38.8 0.0 collective-permute-start.3
  38.8 0.5 collective-permute-start.9
  39.3 7.7 %collective-permute-done.4.rest_2_ = bf16[1024,256]{1,0:T(8,128)(2,1)S(1)} collective-permute-done((bf16[1024,256]{1,0:T(8,128)(2,1)S(1)}, bf16[1024,256]{1,0:T(8,128)(2,1)S(1)}, u32[]{:S(2)}, u32[]{:S(2)}) %collective-permute-start.4) | collective-permute-done | bytes 524320 | tf_op jit(solution)/shard_map/ppermute | solution.py:39
  47.0 0.0 collective-permute-start.5
  47.0 5.9 %collective-permute-done.10.rest_6_ = bf16[1024,256]{1,0:T(8,128)(2,1)S(1)} collective-permute-done((bf16[1024,256]{1,0:T(8,128)(2,1)S(1)}, bf16[1024,256]{1,0:T(8,128)(2,1)S(1)}, u32[]{:S(2)}, u32[]{:S(2)}) %collective-permute-start.10) | collective-permute-done | bytes 524320 | tf_op jit(solution)/shard_map/ppermute | solution.py:39
  52.9 0.0 collective-permute-start.11
  52.9 0.0 copy-start.2
  52.9 0.7 copy-done.2
  53.6 0.1 dynamic_slice.10.cnt_ref
  53.6 0.1 pad_add_fusion.qb_ref
  53.7 0.7 constant_dynamic-slice_fusion.1.bl_ref
  54.4 0.0 copy-done
  54.4 0.0 collective-permute-done.3.rest_1_
  54.4 0.0 collective-permute-done.9.rest_5_
  54.4 0.0 collective-permute-done.5.rest_3_
  54.5 0.5 collective-permute-done.11.rest_7_
  54.9 38.1 %shard_map.55 = bf16[256,512]{1,0:T(8,128)(2,1)} custom-call(s32[2,32]{1,0:T(2,128)S(1)} %constant_dynamic-slice_fusion.1.bl_ref, s32[2]{0:T(128)S(1)} %dynamic_slice.10.cnt_ref, s32[2]{0:T(128)S(1)} %pad_add_fusion.qb_ref, bf16[256,512]{1,0:T(8,128)(2,1)S(1)} %constant_dynamic-slice_fusion.q_ref, bf16[1024,256]{1,0:T(8,128)(2,1)S(1)} %bitcast.30, ...), custom_call_target="tpu_custom_call" | custom-call | tf_op jit(solution)/shard_map/pallas_call | solution.py:173
  (12 shorter events, 0.3 us)
Async XLA Ops:
  0.0 54.4 %copy-start = (bf16[1024,512]{1,0:T(8,128)(2,1)S(1)}, bf16[1024,512]{1,0:T(8,128)(2,1)}, u32[]{:S(2)}) copy-start(bf16[1024,512]{1,0:T(8,128)(2,1)} %param.5) | copy-start | bytes 3145732
  0.0 1.0 %copy-start.1 = (bf16[256,128]{1,0:T(8,128)(2,1)S(1)}, bf16[256,128]{1,0:T(8,128)(2,1)}, u32[]{:S(2)}) copy-start(bf16[256,128]{1,0:T(8,128)(2,1)} %param.7) | copy-start | bytes 196612
  1.0 6.1 %collective-permute-start = (bf16[1,1,1,128,256]{4,3,2,1,0:T(8,128)(2,1)S(1)}, bf16[1,1,1,128,256]{4,3,2,1,0:T(8,128)(2,1)S(1)}, u32[]{:S(2)}, u32[]{:S(2)}) collective-permute-start(bf16[1,1,1,128,256]{4,3,2,1,0:T(8,128)(2,1)S(1)} %get-tuple-element.12), channel_id=1, source_target_pairs={{0,16},{4,20},{8,24},{12,28},{16,0},{20,4},{24,8},{28,12},{1,17},{... | collective-permute-start | bytes 196616 | tf_op jit(solution)/shard_map/ppermute | solution.py:24
  7.1 5.1 %collective-permute-start.1 = (bf16[2,1,1,128,256]{4,3,2,1,0:T(8,128)(2,1)S(1)}, bf16[2,1,1,128,256]{4,3,2,1,0:T(8,128)(2,1)S(1)}, u32[]{:S(2)}, u32[]{:S(2)}) collective-permute-start(bf16[2,1,1,128,256]{4,3,2,1,0:T(8,128)(2,1)S(1)} %maximum_select_fusion.4), channel_id=1, source_target_pairs={{0,8},{4,12},{8,0},{12,4},{16,24},{20,28},{24,16},{28,20},{1,9},{5... | collective-permute-start | bytes 393224 | tf_op jit(solution)/shard_map/ppermute | solution.py:24
  12.3 7.1 %collective-permute-start.2 = (bf16[2,2,1,128,256]{4,3,0,2,1:T(8,128)(2,1)S(1)}, bf16[2,2,1,128,256]{4,3,0,2,1:T(8,128)(2,1)S(1)}, u32[]{:S(2)}, u32[]{:S(2)}) collective-permute-start(bf16[2,2,1,128,256]{4,3,0,2,1:T(8,128)(2,1)S(1)} %maximum_select_fusion.2), channel_id=1, source_target_pairs={{0,4},{4,0},{8,12},{12,8},{16,20},{20,16},{24,28},{28,24},{1,5},{5... | collective-permute-start | bytes 786440 | tf_op jit(solution)/shard_map/ppermute | solution.py:24
  19.5 6.0 %collective-permute-start.6 = (bf16[1,1,1,128,256]{4,3,2,1,0:T(8,128)(2,1)S(1)}, bf16[1,1,1,128,256]{4,3,2,1,0:T(8,128)(2,1)S(1)}, u32[]{:S(2)}, u32[]{:S(2)}) collective-permute-start(bf16[1,1,1,128,256]{4,3,2,1,0:T(8,128)(2,1)S(1)} %bitcast.34), channel_id=1, source_target_pairs={{0,16},{4,20},{8,24},{12,28},{16,0},{20,4},{24,8},{28,12},{1,17},{... | collective-permute-start | bytes 196616 | tf_op jit(solution)/shard_map/ppermute | solution.py:24
  25.6 5.0 %collective-permute-start.7 = (bf16[2,1,1,128,256]{4,3,0,2,1:T(8,128)(2,1)S(1)}, bf16[2,1,1,128,256]{4,3,0,2,1:T(8,128)(2,1)S(1)}, u32[]{:S(2)}, u32[]{:S(2)}) collective-permute-start(bf16[2,1,1,128,256]{4,3,0,2,1:T(8,128)(2,1)S(1)} %fusion), channel_id=1, source_target_pairs={{0,8},{4,12},{8,0},{12,4},{16,24},{20,28},{24,16},{28,20},{1,9},{5... | collective-permute-start | bytes 393224 | tf_op jit(solution)/shard_map/ppermute | solution.py:24
  30.6 6.4 %collective-permute-start.8 = (bf16[2,2,1,128,256]{4,3,0,2,1:T(8,128)(2,1)S(1)}, bf16[2,2,1,128,256]{4,3,0,2,1:T(8,128)(2,1)S(1)}, u32[]{:S(2)}, u32[]{:S(2)}) collective-permute-start(bf16[2,2,1,128,256]{4,3,0,2,1:T(8,128)(2,1)S(1)} %maximum_select_fusion.3), channel_id=1, source_target_pairs={{0,4},{4,0},{8,12},{12,8},{16,20},{20,16},{24,28},{28,24},{1,5},{5... | collective-permute-start | bytes 786440 | tf_op jit(solution)/shard_map/ppermute | solution.py:24
  32.2 14.8 %collective-permute-start.4 = (bf16[1024,256]{1,0:T(8,128)(2,1)S(1)}, bf16[1024,256]{1,0:T(8,128)(2,1)S(1)}, u32[]{:S(2)}, u32[]{:S(2)}) collective-permute-start(bf16[1024,256]{1,0:T(8,128)(2,1)S(1)} %bitcast.28), channel_id=1, source_target_pairs={{0,2},{1,3},{2,0},{3,1},{4,6},{5,7},{6,4},{7,5},{8,10},{9,11},{10,... | collective-permute-start | bytes 1572872 | tf_op jit(solution)/shard_map/ppermute | solution.py:39
  37.2 15.7 %collective-permute-start.10 = (bf16[1024,256]{1,0:T(8,128)(2,1)S(1)}, bf16[1024,256]{1,0:T(8,128)(2,1)S(1)}, u32[]{:S(2)}, u32[]{:S(2)}) collective-permute-start(bf16[1024,256]{1,0:T(8,128)(2,1)S(1)} %bitcast.31), channel_id=1, source_target_pairs={{0,2},{1,3},{2,0},{3,1},{4,6},{5,7},{6,4},{7,5},{8,10},{9,11},{10,... | collective-permute-start | bytes 1572872 | tf_op jit(solution)/shard_map/ppermute | solution.py:39
  38.8 15.7 %collective-permute-start.3 = (bf16[1024,256]{1,0:T(8,128)(2,1)S(1)}, bf16[1024,256]{1,0:T(8,128)(2,1)}, u32[]{:S(2)}, u32[]{:S(2)}) collective-permute-start(bf16[1024,256]{1,0:T(8,128)(2,1)S(1)} %bitcast.29), channel_id=1, source_target_pairs={{0,1},{1,0},{2,3},{3,2},{4,5},{5,4},{6,7},{7,6},{8,9},{9,8},{10,11... | collective-permute-start | bytes 1572872 | tf_op jit(solution)/shard_map/ppermute | solution.py:39
  38.8 15.7 %collective-permute-start.9 = (bf16[1024,256]{1,0:T(8,128)(2,1)S(1)}, bf16[1024,256]{1,0:T(8,128)(2,1)}, u32[]{:S(2)}, u32[]{:S(2)}) collective-permute-start(bf16[1024,256]{1,0:T(8,128)(2,1)S(1)} %bitcast.32), channel_id=1, source_target_pairs={{0,1},{1,0},{2,3},{3,2},{4,5},{5,4},{6,7},{7,6},{8,9},{9,8},{10,11... | collective-permute-start | bytes 1572872 | tf_op jit(solution)/shard_map/ppermute | solution.py:39
  47.0 7.4 %collective-permute-start.5 = (bf16[1024,256]{1,0:T(8,128)(2,1)S(1)}, bf16[1024,256]{1,0:T(8,128)(2,1)}, u32[]{:S(2)}, u32[]{:S(2)}) collective-permute-start(bf16[1024,256]{1,0:T(8,128)(2,1)S(1)} %collective-permute-done.4.rest_2_), channel_id=1, source_target_pairs={{0,1},{1,0},{2,3},{3,2},{4,5},{5,4},{6,7},{7,6},{8,9},{9,8},{10,11... | collective-permute-start | bytes 1572872 | tf_op jit(solution)/shard_map/ppermute | solution.py:39
  52.9 2.0 %collective-permute-start.11 = (bf16[1024,256]{1,0:T(8,128)(2,1)S(1)}, bf16[1024,256]{1,0:T(8,128)(2,1)}, u32[]{:S(2)}, u32[]{:S(2)}) collective-permute-start(bf16[1024,256]{1,0:T(8,128)(2,1)S(1)} %collective-permute-done.10.rest_6_), channel_id=1, source_target_pairs={{0,1},{1,0},{2,3},{3,2},{4,5},{5,4},{6,7},{7,6},{8,9},{9,8},{10,11... | collective-permute-start | bytes 1572872 | tf_op jit(solution)/shard_map/ppermute | solution.py:39
  52.9 0.7 copy-start.2

commit v8 on v6

--- a/solution.py
+++ b/solution.py
@@ -82,12 +82,19 @@
 
         n_j = lax.fori_loop(0, cnt_ref[j], compact, 0)
         n_off.append(n_j)
+        n_pad = (n_j + group - 1) // group * group
+
+        def pad(s, c, j=j, qb=qb):
+            off_ref[j, s] = qb
+            return c
+
+        lax.fori_loop(n_j, n_pad, pad, 0)
 
         def issue(s, c, j=j):
             copy(j, s).start()
             return c
 
-        lax.fori_loop(0, n_j, issue, 0)
+        lax.fori_loop(0, n_pad, issue, 0)
 
     rows = QH * BLK
     rowpos = lax.broadcasted_iota(jnp.int32, (rows, BLK), 0) % BLK
@@ -95,11 +102,15 @@
     causal = col <= rowpos
     dims = (((1,), (1,)), ((), ()))
 
-    def update(qs, kvb, carry):
+    slot_of = lax.broadcasted_iota(jnp.int32, (rows, group * BLK), 1) // BLK
+
+    def update(qs, kvb, carry, live=None):
         m, l, acc = carry
         k = kvb[:, :HD]
         v = kvb[:, HD:]
         sc = lax.dot_general(qs, k, dims, preferred_element_type=jnp.float32) * scale
+        if live is not None:
+            sc = jnp.where(slot_of < live, sc, masked_score)
         m_new = jnp.maximum(m, jnp.max(sc, axis=1, keepdims=True))
         alpha = jnp.exp2(m - m_new)
         w = jnp.exp2(sc - m_new)
@@ -127,13 +138,16 @@
             kvb = kvbuf[j, pl.ds(first, group)].reshape(group * BLK, width)
             return update(qs, kvb, carry)
 
-        def single(s, carry, j=j, qs=qs):
-            copy(j, s).wait()
-            return update(qs, kvbuf[j, s], carry)
+        def last(g, carry, j=j, qs=qs):
+            first = g * group
+            for i in range(group):
+                copy(j, first + i).wait()
+            kvb = kvbuf[j, pl.ds(first, group)].reshape(group * BLK, width)
+            return update(qs, kvb, carry, live=n_off[j] - first)
 
         n_groups = n_off[j] // group
         carry = lax.fori_loop(0, n_groups, grouped, (m, l, acc))
-        m, l, acc = lax.fori_loop(n_groups * group, n_off[j], single, carry)
+        m, l, acc = lax.fori_loop(n_groups, (n_off[j] + group - 1) // group, last, carry)
         res = (acc / l).astype(out_ref.dtype)
         for h in range(QH):
             out_ref[j * BLK:(j + 1) * BLK, h * HD:(h + 1) * HD] = res[h * BLK:(h + 1) * BLK, :]
@@ -163,7 +177,7 @@
     qb0 = jnp.stack([(p * n_ka + k) * n_local, k]).astype(jnp.int32)
 
     kernel = functools.partial(
-        attend_kernel, n_local=n_local, n_pieces=len(kv_pieces), n_ka=n_ka, group=4, scale=math.log2(math.e) / math.sqrt(HD)
+        attend_kernel, n_local=n_local, n_pieces=len(kv_pieces), n_ka=n_ka, group=8, scale=math.log2(math.e) / math.sqrt(HD)
     )
     return pl.pallas_call(
         kernel,

time: 79 us -> 76 us (0.962)
  Pallas kernels: 23.9 us -> 20.9 us
    pallas_call x1, Pallas kernels: 23.9 us -> 20.9 us  [shards(): pl.pallas_call(kernel, out_shape=jax.ShapeDtypeStruct((rows_mine, queries...]
where the time goes in v8:
time: 76 us; the launch traced here: 75.9 us
  waiting for transfers between devices  44.3 us (58%)
  Pallas kernels  20.9 us (28%)
  starting transfers between devices  7.63 us (10%)
  local copies, waits for them, and re-layouts  2.5 us (3%)
    ppermute x6, waiting for transfers between devices, gather_axis(): other = lax.ppermute(held, axis, [(i, i ^ b) for i in range(n)])  30.2 us
    pallas_call x1, Pallas kernels, shards(): pl.pallas_call(kernel, out_shape=jax.ShapeDtypeStruct((rows_mine, queries...  20.9 us
    ppermute x6, waiting for transfers between devices, pieces_axis(): lax.ppermute(idx_pieces[x], axis, [(i, i ^ b) for i in range(n)])  14.1 us
    ppermute x6, starting transfers between devices, gather_axis(): other = lax.ppermute(held, axis, [(i, i ^ b) for i in range(n)])  4.01 us
    ppermute x6, starting transfers between devices, pieces_axis(): lax.ppermute(idx_pieces[x], axis, [(i, i ^ b) for i in range(n)])  3.62 us
    unnamed x7, local copies, waits for them, and re-layouts  1.62 us
  transfers between devices with their start and end apart: 12, of which 9 were waited for; matrix products, arithmetic and copies ran while one was open for 1% of the time, Pallas kernels for 0%

profile of v8, /device:TPU:24, one launch (start us, length us, event | category | flops | bytes accessed | tf_op | source)
XLA Modules:
  0.0 75.9 jit_solution(17295833066150413355)
XLA Ops:
  0.0 0.0 copy-start
  0.0 0.0 copy-start.1
  0.0 0.9 %constant_dynamic-update-slice_fusion.1 = bf16[256,256]{1,0:T(8,128)(2,1)S(1)} fusion(bf16[256,128]{1,0:T(8,128)(2,1)} %param.6), kind=kLoop, calls=%fused_computation.16 | loop fusion | bytes 131072
  1.0 0.0 copy-done.1
  1.0 0.4 collective-permute-start
  1.4 5.7 %collective-permute-done = bf16[1,1,1,128,256]{4,3,2,1,0:T(8,128)(2,1)S(1)} collective-permute-done((bf16[1,1,1,128,256]{4,3,2,1,0:T(8,128)(2,1)S(1)}, bf16[1,1,1,128,256]{4,3,2,1,0:T(8,128)(2,1)S(1)}, u32[]{:S(2)}, u32[]{:S(2)}) %collective-permute-start) | collective-permute-done | bytes 65568 | tf_op jit(solution)/shard_map/ppermute | solution.py:24
  7.1 0.1 collective-permute-start.1
  7.3 5.0 %collective-permute-done.1 = bf16[2,1,1,128,256]{4,3,2,1,0:T(8,128)(2,1)S(1)} collective-permute-done((bf16[2,1,1,128,256]{4,3,2,1,0:T(8,128)(2,1)S(1)}, bf16[2,1,1,128,256]{4,3,2,1,0:T(8,128)(2,1)S(1)}, u32[]{:S(2)}, u32[]{:S(2)}) %collective-permute-start.1) | collective-permute-done | bytes 131104 | tf_op jit(solution)/shard_map/ppermute | solution.py:24
  12.3 0.1 maximum_select_fusion.2
  12.3 1.6 %collective-permute-start.2 = (bf16[2,2,1,128,256]{4,3,0,2,1:T(8,128)(2,1)S(1)}, bf16[2,2,1,128,256]{4,3,0,2,1:T(8,128)(2,1)S(1)}, u32[]{:S(2)}, u32[]{:S(2)}) collective-permute-start(bf16[2,2,1,128,256]{4,3,0,2,1:T(8,128)(2,1)S(1)} %maximum_select_fusion.2), channel_id=1, source_target_pairs={{0,4},{4,0},{8,12},{12,8},{16,20},{20,16},{24,28},{28,24},{1,5},{5... | collective-permute-start | bytes 786440 | tf_op jit(solution)/shard_map/ppermute | solution.py:24
  13.9 5.5 %collective-permute-done.2 = bf16[2,2,1,128,256]{4,3,0,2,1:T(8,128)(2,1)S(1)} collective-permute-done((bf16[2,2,1,128,256]{4,3,0,2,1:T(8,128)(2,1)S(1)}, bf16[2,2,1,128,256]{4,3,0,2,1:T(8,128)(2,1)S(1)}, u32[]{:S(2)}, u32[]{:S(2)}) %collective-permute-start.2) | collective-permute-done | bytes 262176 | tf_op jit(solution)/shard_map/ppermute | solution.py:24
  19.5 0.1 collective-permute-start.6
  19.6 6.0 %collective-permute-done.6 = bf16[1,1,1,128,256]{4,3,2,1,0:T(8,128)(2,1)S(1)} collective-permute-done((bf16[1,1,1,128,256]{4,3,2,1,0:T(8,128)(2,1)S(1)}, bf16[1,1,1,128,256]{4,3,2,1,0:T(8,128)(2,1)S(1)}, u32[]{:S(2)}, u32[]{:S(2)}) %collective-permute-start.6) | collective-permute-done | bytes 65568 | tf_op jit(solution)/shard_map/ppermute | solution.py:24
  25.6 0.4 collective-permute-start.7
  26.0 4.7 %collective-permute-done.7 = bf16[2,1,1,128,256]{4,3,0,2,1:T(8,128)(2,1)S(1)} collective-permute-done((bf16[2,1,1,128,256]{4,3,0,2,1:T(8,128)(2,1)S(1)}, bf16[2,1,1,128,256]{4,3,0,2,1:T(8,128)(2,1)S(1)}, u32[]{:S(2)}, u32[]{:S(2)}) %collective-permute-start.7) | collective-permute-done | bytes 131104 | tf_op jit(solution)/shard_map/ppermute | solution.py:24
  30.6 1.6 %collective-permute-start.8 = (bf16[2,2,1,128,256]{4,3,0,2,1:T(8,128)(2,1)S(1)}, bf16[2,2,1,128,256]{4,3,0,2,1:T(8,128)(2,1)S(1)}, u32[]{:S(2)}, u32[]{:S(2)}) collective-permute-start(bf16[2,2,1,128,256]{4,3,0,2,1:T(8,128)(2,1)S(1)} %maximum_select_fusion.3), channel_id=1, source_target_pairs={{0,4},{4,0},{8,12},{12,8},{16,20},{20,16},{24,28},{28,24},{1,5},{5... | collective-permute-start | bytes 786440 | tf_op jit(solution)/shard_map/ppermute | solution.py:24
  32.2 1.5 %collective-permute-start.4 = (bf16[1024,256]{1,0:T(8,128)(2,1)S(1)}, bf16[1024,256]{1,0:T(8,128)(2,1)S(1)}, u32[]{:S(2)}, u32[]{:S(2)}) collective-permute-start(bf16[1024,256]{1,0:T(8,128)(2,1)S(1)} %bitcast.28), channel_id=1, source_target_pairs={{0,2},{1,3},{2,0},{3,1},{4,6},{5,7},{6,4},{7,5},{8,10},{9,11},{10,... | collective-permute-start | bytes 1572872 | tf_op jit(solution)/shard_map/ppermute | solution.py:39
  33.7 3.4 %collective-permute-done.8 = bf16[2,2,1,128,256]{4,3,0,2,1:T(8,128)(2,1)S(1)} collective-permute-done((bf16[2,2,1,128,256]{4,3,0,2,1:T(8,128)(2,1)S(1)}, bf16[2,2,1,128,256]{4,3,0,2,1:T(8,128)(2,1)S(1)}, u32[]{:S(2)}, u32[]{:S(2)}) %collective-permute-start.8) | collective-permute-done | bytes 262176 | tf_op jit(solution)/shard_map/ppermute | solution.py:24
  37.2 1.6 %collective-permute-start.10 = (bf16[1024,256]{1,0:T(8,128)(2,1)S(1)}, bf16[1024,256]{1,0:T(8,128)(2,1)S(1)}, u32[]{:S(2)}, u32[]{:S(2)}) collective-permute-start(bf16[1024,256]{1,0:T(8,128)(2,1)S(1)} %bitcast.31), channel_id=1, source_target_pairs={{0,2},{1,3},{2,0},{3,1},{4,6},{5,7},{6,4},{7,5},{8,10},{9,11},{10,... | collective-permute-start | bytes 1572872 | tf_op jit(solution)/shard_map/ppermute | solution.py:39
  38.8 0.0 collective-permute-start.3
  38.8 0.5 collective-permute-start.9
  39.3 7.7 %collective-permute-done.4.rest_2_ = bf16[1024,256]{1,0:T(8,128)(2,1)S(1)} collective-permute-done((bf16[1024,256]{1,0:T(8,128)(2,1)S(1)}, bf16[1024,256]{1,0:T(8,128)(2,1)S(1)}, u32[]{:S(2)}, u32[]{:S(2)}) %collective-permute-start.4) | collective-permute-done | bytes 524320 | tf_op jit(solution)/shard_map/ppermute | solution.py:39
  47.0 0.0 collective-permute-start.5
  47.0 5.9 %collective-permute-done.10.rest_6_ = bf16[1024,256]{1,0:T(8,128)(2,1)S(1)} collective-permute-done((bf16[1024,256]{1,0:T(8,128)(2,1)S(1)}, bf16[1024,256]{1,0:T(8,128)(2,1)S(1)}, u32[]{:S(2)}, u32[]{:S(2)}) %collective-permute-start.10) | collective-permute-done | bytes 524320 | tf_op jit(solution)/shard_map/ppermute | solution.py:39
  52.9 0.0 collective-permute-start.11
  52.9 0.0 copy-start.2
  52.9 0.7 copy-done.2
  53.6 0.1 dynamic_slice.10.cnt_ref
  53.6 0.1 pad_add_fusion.qb_ref
  53.7 0.7 constant_dynamic-slice_fusion.1.bl_ref
  54.4 0.0 copy-done
  54.4 0.0 collective-permute-done.3.rest_1_
  54.4 0.0 collective-permute-done.9.rest_5_
  54.4 0.0 collective-permute-done.5.rest_3_
  54.5 0.5 collective-permute-done.11.rest_7_
  54.9 20.9 %shard_map.55 = bf16[256,512]{1,0:T(8,128)(2,1)} custom-call(s32[2,32]{1,0:T(2,128)S(1)} %constant_dynamic-slice_fusion.1.bl_ref, s32[2]{0:T(128)S(1)} %dynamic_slice.10.cnt_ref, s32[2]{0:T(128)S(1)} %pad_add_fusion.qb_ref, bf16[256,512]{1,0:T(8,128)(2,1)S(1)} %constant_dynamic-slice_fusion.q_ref, bf16[1024,256]{1,0:T(8,128)(2,1)S(1)} %bitcast.30, ...), custom_call_target="tpu_custom_call" | custom-call | tf_op jit(solution)/shard_map/pallas_call | solution.py:182
  (12 shorter events, 0.3 us)
Async XLA Ops:
  0.0 54.4 %copy-start = (bf16[1024,512]{1,0:T(8,128)(2,1)S(1)}, bf16[1024,512]{1,0:T(8,128)(2,1)}, u32[]{:S(2)}) copy-start(bf16[1024,512]{1,0:T(8,128)(2,1)} %param.5) | copy-start | bytes 3145732
  0.0 1.0 %copy-start.1 = (bf16[256,128]{1,0:T(8,128)(2,1)S(1)}, bf16[256,128]{1,0:T(8,128)(2,1)}, u32[]{:S(2)}) copy-start(bf16[256,128]{1,0:T(8,128)(2,1)} %param.7) | copy-start | bytes 196612
  1.0 6.1 %collective-permute-start = (bf16[1,1,1,128,256]{4,3,2,1,0:T(8,128)(2,1)S(1)}, bf16[1,1,1,128,256]{4,3,2,1,0:T(8,128)(2,1)S(1)}, u32[]{:S(2)}, u32[]{:S(2)}) collective-permute-start(bf16[1,1,1,128,256]{4,3,2,1,0:T(8,128)(2,1)S(1)} %get-tuple-element.12), channel_id=1, source_target_pairs={{0,16},{4,20},{8,24},{12,28},{16,0},{20,4},{24,8},{28,12},{1,17},{... | collective-permute-start | bytes 196616 | tf_op jit(solution)/shard_map/ppermute | solution.py:24
  7.1 5.1 %collective-permute-start.1 = (bf16[2,1,1,128,256]{4,3,2,1,0:T(8,128)(2,1)S(1)}, bf16[2,1,1,128,256]{4,3,2,1,0:T(8,128)(2,1)S(1)}, u32[]{:S(2)}, u32[]{:S(2)}) collective-permute-start(bf16[2,1,1,128,256]{4,3,2,1,0:T(8,128)(2,1)S(1)} %maximum_select_fusion.4), channel_id=1, source_target_pairs={{0,8},{4,12},{8,0},{12,4},{16,24},{20,28},{24,16},{28,20},{1,9},{5... | collective-permute-start | bytes 393224 | tf_op jit(solution)/shard_map/ppermute | solution.py:24
  12.3 7.1 %collective-permute-start.2 = (bf16[2,2,1,128,256]{4,3,0,2,1:T(8,128)(2,1)S(1)}, bf16[2,2,1,128,256]{4,3,0,2,1:T(8,128)(2,1)S(1)}, u32[]{:S(2)}, u32[]{:S(2)}) collective-permute-start(bf16[2,2,1,128,256]{4,3,0,2,1:T(8,128)(2,1)S(1)} %maximum_select_fusion.2), channel_id=1, source_target_pairs={{0,4},{4,0},{8,12},{12,8},{16,20},{20,16},{24,28},{28,24},{1,5},{5... | collective-permute-start | bytes 786440 | tf_op jit(solution)/shard_map/ppermute | solution.py:24
  19.5 6.0 %collective-permute-start.6 = (bf16[1,1,1,128,256]{4,3,2,1,0:T(8,128)(2,1)S(1)}, bf16[1,1,1,128,256]{4,3,2,1,0:T(8,128)(2,1)S(1)}, u32[]{:S(2)}, u32[]{:S(2)}) collective-permute-start(bf16[1,1,1,128,256]{4,3,2,1,0:T(8,128)(2,1)S(1)} %bitcast.34), channel_id=1, source_target_pairs={{0,16},{4,20},{8,24},{12,28},{16,0},{20,4},{24,8},{28,12},{1,17},{... | collective-permute-start | bytes 196616 | tf_op jit(solution)/shard_map/ppermute | solution.py:24
  25.6 5.0 %collective-permute-start.7 = (bf16[2,1,1,128,256]{4,3,0,2,1:T(8,128)(2,1)S(1)}, bf16[2,1,1,128,256]{4,3,0,2,1:T(8,128)(2,1)S(1)}, u32[]{:S(2)}, u32[]{:S(2)}) collective-permute-start(bf16[2,1,1,128,256]{4,3,0,2,1:T(8,128)(2,1)S(1)} %fusion), channel_id=1, source_target_pairs={{0,8},{4,12},{8,0},{12,4},{16,24},{20,28},{24,16},{28,20},{1,9},{5... | collective-permute-start | bytes 393224 | tf_op jit(solution)/shard_map/ppermute | solution.py:24
  30.6 6.4 %collective-permute-start.8 = (bf16[2,2,1,128,256]{4,3,0,2,1:T(8,128)(2,1)S(1)}, bf16[2,2,1,128,256]{4,3,0,2,1:T(8,128)(2,1)S(1)}, u32[]{:S(2)}, u32[]{:S(2)}) collective-permute-start(bf16[2,2,1,128,256]{4,3,0,2,1:T(8,128)(2,1)S(1)} %maximum_select_fusion.3), channel_id=1, source_target_pairs={{0,4},{4,0},{8,12},{12,8},{16,20},{20,16},{24,28},{28,24},{1,5},{5... | collective-permute-start | bytes 786440 | tf_op jit(solution)/shard_map/ppermute | solution.py:24
  32.2 14.8 %collective-permute-start.4 = (bf16[1024,256]{1,0:T(8,128)(2,1)S(1)}, bf16[1024,256]{1,0:T(8,128)(2,1)S(1)}, u32[]{:S(2)}, u32[]{:S(2)}) collective-permute-start(bf16[1024,256]{1,0:T(8,128)(2,1)S(1)} %bitcast.28), channel_id=1, source_target_pairs={{0,2},{1,3},{2,0},{3,1},{4,6},{5,7},{6,4},{7,5},{8,10},{9,11},{10,... | collective-permute-start | bytes 1572872 | tf_op jit(solution)/shard_map/ppermute | solution.py:39
  37.2 15.7 %collective-permute-start.10 = (bf16[1024,256]{1,0:T(8,128)(2,1)S(1)}, bf16[1024,256]{1,0:T(8,128)(2,1)S(1)}, u32[]{:S(2)}, u32[]{:S(2)}) collective-permute-start(bf16[1024,256]{1,0:T(8,128)(2,1)S(1)} %bitcast.31), channel_id=1, source_target_pairs={{0,2},{1,3},{2,0},{3,1},{4,6},{5,7},{6,4},{7,5},{8,10},{9,11},{10,... | collective-permute-start | bytes 1572872 | tf_op jit(solution)/shard_map/ppermute | solution.py:39
  38.8 15.7 %collective-permute-start.3 = (bf16[1024,256]{1,0:T(8,128)(2,1)S(1)}, bf16[1024,256]{1,0:T(8,128)(2,1)}, u32[]{:S(2)}, u32[]{:S(2)}) collective-permute-start(bf16[1024,256]{1,0:T(8,128)(2,1)S(1)} %bitcast.29), channel_id=1, source_target_pairs={{0,1},{1,0},{2,3},{3,2},{4,5},{5,4},{6,7},{7,6},{8,9},{9,8},{10,11... | collective-permute-start | bytes 1572872 | tf_op jit(solution)/shard_map/ppermute | solution.py:39
  38.8 15.7 %collective-permute-start.9 = (bf16[1024,256]{1,0:T(8,128)(2,1)S(1)}, bf16[1024,256]{1,0:T(8,128)(2,1)}, u32[]{:S(2)}, u32[]{:S(2)}) collective-permute-start(bf16[1024,256]{1,0:T(8,128)(2,1)S(1)} %bitcast.32), channel_id=1, source_target_pairs={{0,1},{1,0},{2,3},{3,2},{4,5},{5,4},{6,7},{7,6},{8,9},{9,8},{10,11... | collective-permute-start | bytes 1572872 | tf_op jit(solution)/shard_map/ppermute | solution.py:39
  47.0 7.4 %collective-permute-start.5 = (bf16[1024,256]{1,0:T(8,128)(2,1)S(1)}, bf16[1024,256]{1,0:T(8,128)(2,1)}, u32[]{:S(2)}, u32[]{:S(2)}) collective-permute-start(bf16[1024,256]{1,0:T(8,128)(2,1)S(1)} %collective-permute-done.4.rest_2_), channel_id=1, source_target_pairs={{0,1},{1,0},{2,3},{3,2},{4,5},{5,4},{6,7},{7,6},{8,9},{9,8},{10,11... | collective-permute-start | bytes 1572872 | tf_op jit(solution)/shard_map/ppermute | solution.py:39
  52.9 2.0 %collective-permute-start.11 = (bf16[1024,256]{1,0:T(8,128)(2,1)S(1)}, bf16[1024,256]{1,0:T(8,128)(2,1)}, u32[]{:S(2)}, u32[]{:S(2)}) collective-permute-start(bf16[1024,256]{1,0:T(8,128)(2,1)S(1)} %collective-permute-done.10.rest_6_), channel_id=1, source_target_pairs={{0,1},{1,0},{2,3},{3,2},{4,5},{5,4},{6,7},{7,6},{8,9},{9,8},{10,11... | collective-permute-start | bytes 1572872 | tf_op jit(solution)/shard_map/ppermute | solution.py:39
  52.9 0.7 copy-start.2

commit v9 on v8

--- a/solution.py
+++ b/solution.py
@@ -177,7 +177,7 @@
     qb0 = jnp.stack([(p * n_ka + k) * n_local, k]).astype(jnp.int32)
 
     kernel = functools.partial(
-        attend_kernel, n_local=n_local, n_pieces=len(kv_pieces), n_ka=n_ka, group=8, scale=math.log2(math.e) / math.sqrt(HD)
+        attend_kernel, n_local=n_local, n_pieces=len(kv_pieces), n_ka=n_ka, group=16, scale=math.log2(math.e) / math.sqrt(HD)
     )
     return pl.pallas_call(
         kernel,

time: 76 us -> 75.1 us (0.988)
  Pallas kernels: 20.9 us -> 20 us
    pallas_call x1, Pallas kernels: 20.9 us -> 20 us  [shards(): pl.pallas_call(kernel, out_shape=jax.ShapeDtypeStruct((rows_mine, queries...]
where the time goes in v9:
time: 75.1 us; the launch traced here: 74.9 us
  waiting for transfers between devices  44.3 us (59%)
  Pallas kernels  20 us (27%)
  starting transfers between devices  7.63 us (10%)
  local copies, waits for them, and re-layouts  2.5 us (3%)
    ppermute x6, waiting for transfers between devices, gather_axis(): other = lax.ppermute(held, axis, [(i, i ^ b) for i in range(n)])  30.2 us
    pallas_call x1, Pallas kernels, shards(): pl.pallas_call(kernel, out_shape=jax.ShapeDtypeStruct((rows_mine, queries...  20 us
    ppermute x6, waiting for transfers between devices, pieces_axis(): lax.ppermute(idx_pieces[x], axis, [(i, i ^ b) for i in range(n)])  14.1 us
    ppermute x6, starting transfers between devices, gather_axis(): other = lax.ppermute(held, axis, [(i, i ^ b) for i in range(n)])  4.01 us
    ppermute x6, starting transfers between devices, pieces_axis(): lax.ppermute(idx_pieces[x], axis, [(i, i ^ b) for i in range(n)])  3.62 us
    unnamed x7, local copies, waits for them, and re-layouts  1.62 us
  transfers between devices with their start and end apart: 12, of which 9 were waited for; matrix products, arithmetic and copies ran while one was open for 1% of the time, Pallas kernels for 0%

profile of v9, /device:TPU:24, one launch (start us, length us, event | category | flops | bytes accessed | tf_op | source)
XLA Modules:
  0.0 74.9 jit_solution(404514721865240973)
XLA Ops:
  0.0 0.0 copy-start
  0.0 0.0 copy-start.1
  0.0 0.9 %constant_dynamic-update-slice_fusion.1 = bf16[256,256]{1,0:T(8,128)(2,1)S(1)} fusion(bf16[256,128]{1,0:T(8,128)(2,1)} %param.6), kind=kLoop, calls=%fused_computation.16 | loop fusion | bytes 131072
  1.0 0.0 copy-done.1
  1.0 0.4 collective-permute-start
  1.4 5.7 %collective-permute-done = bf16[1,1,1,128,256]{4,3,2,1,0:T(8,128)(2,1)S(1)} collective-permute-done((bf16[1,1,1,128,256]{4,3,2,1,0:T(8,128)(2,1)S(1)}, bf16[1,1,1,128,256]{4,3,2,1,0:T(8,128)(2,1)S(1)}, u32[]{:S(2)}, u32[]{:S(2)}) %collective-permute-start) | collective-permute-done | bytes 65568 | tf_op jit(solution)/shard_map/ppermute | solution.py:24
  7.1 0.1 collective-permute-start.1
  7.3 5.0 %collective-permute-done.1 = bf16[2,1,1,128,256]{4,3,2,1,0:T(8,128)(2,1)S(1)} collective-permute-done((bf16[2,1,1,128,256]{4,3,2,1,0:T(8,128)(2,1)S(1)}, bf16[2,1,1,128,256]{4,3,2,1,0:T(8,128)(2,1)S(1)}, u32[]{:S(2)}, u32[]{:S(2)}) %collective-permute-start.1) | collective-permute-done | bytes 131104 | tf_op jit(solution)/shard_map/ppermute | solution.py:24
  12.3 0.1 maximum_select_fusion.2
  12.3 1.6 %collective-permute-start.2 = (bf16[2,2,1,128,256]{4,3,0,2,1:T(8,128)(2,1)S(1)}, bf16[2,2,1,128,256]{4,3,0,2,1:T(8,128)(2,1)S(1)}, u32[]{:S(2)}, u32[]{:S(2)}) collective-permute-start(bf16[2,2,1,128,256]{4,3,0,2,1:T(8,128)(2,1)S(1)} %maximum_select_fusion.2), channel_id=1, source_target_pairs={{0,4},{4,0},{8,12},{12,8},{16,20},{20,16},{24,28},{28,24},{1,5},{5... | collective-permute-start | bytes 786440 | tf_op jit(solution)/shard_map/ppermute | solution.py:24
  13.9 5.5 %collective-permute-done.2 = bf16[2,2,1,128,256]{4,3,0,2,1:T(8,128)(2,1)S(1)} collective-permute-done((bf16[2,2,1,128,256]{4,3,0,2,1:T(8,128)(2,1)S(1)}, bf16[2,2,1,128,256]{4,3,0,2,1:T(8,128)(2,1)S(1)}, u32[]{:S(2)}, u32[]{:S(2)}) %collective-permute-start.2) | collective-permute-done | bytes 262176 | tf_op jit(solution)/shard_map/ppermute | solution.py:24
  19.5 0.1 collective-permute-start.6
  19.6 6.0 %collective-permute-done.6 = bf16[1,1,1,128,256]{4,3,2,1,0:T(8,128)(2,1)S(1)} collective-permute-done((bf16[1,1,1,128,256]{4,3,2,1,0:T(8,128)(2,1)S(1)}, bf16[1,1,1,128,256]{4,3,2,1,0:T(8,128)(2,1)S(1)}, u32[]{:S(2)}, u32[]{:S(2)}) %collective-permute-start.6) | collective-permute-done | bytes 65568 | tf_op jit(solution)/shard_map/ppermute | solution.py:24
  25.6 0.4 collective-permute-start.7
  26.0 4.7 %collective-permute-done.7 = bf16[2,1,1,128,256]{4,3,0,2,1:T(8,128)(2,1)S(1)} collective-permute-done((bf16[2,1,1,128,256]{4,3,0,2,1:T(8,128)(2,1)S(1)}, bf16[2,1,1,128,256]{4,3,0,2,1:T(8,128)(2,1)S(1)}, u32[]{:S(2)}, u32[]{:S(2)}) %collective-permute-start.7) | collective-permute-done | bytes 131104 | tf_op jit(solution)/shard_map/ppermute | solution.py:24
  30.6 1.6 %collective-permute-start.8 = (bf16[2,2,1,128,256]{4,3,0,2,1:T(8,128)(2,1)S(1)}, bf16[2,2,1,128,256]{4,3,0,2,1:T(8,128)(2,1)S(1)}, u32[]{:S(2)}, u32[]{:S(2)}) collective-permute-start(bf16[2,2,1,128,256]{4,3,0,2,1:T(8,128)(2,1)S(1)} %maximum_select_fusion.3), channel_id=1, source_target_pairs={{0,4},{4,0},{8,12},{12,8},{16,20},{20,16},{24,28},{28,24},{1,5},{5... | collective-permute-start | bytes 786440 | tf_op jit(solution)/shard_map/ppermute | solution.py:24
  32.2 1.5 %collective-permute-start.4 = (bf16[1024,256]{1,0:T(8,128)(2,1)S(1)}, bf16[1024,256]{1,0:T(8,128)(2,1)S(1)}, u32[]{:S(2)}, u32[]{:S(2)}) collective-permute-start(bf16[1024,256]{1,0:T(8,128)(2,1)S(1)} %bitcast.28), channel_id=1, source_target_pairs={{0,2},{1,3},{2,0},{3,1},{4,6},{5,7},{6,4},{7,5},{8,10},{9,11},{10,... | collective-permute-start | bytes 1572872 | tf_op jit(solution)/shard_map/ppermute | solution.py:39
  33.7 3.4 %collective-permute-done.8 = bf16[2,2,1,128,256]{4,3,0,2,1:T(8,128)(2,1)S(1)} collective-permute-done((bf16[2,2,1,128,256]{4,3,0,2,1:T(8,128)(2,1)S(1)}, bf16[2,2,1,128,256]{4,3,0,2,1:T(8,128)(2,1)S(1)}, u32[]{:S(2)}, u32[]{:S(2)}) %collective-permute-start.8) | collective-permute-done | bytes 262176 | tf_op jit(solution)/shard_map/ppermute | solution.py:24
  37.2 1.6 %collective-permute-start.10 = (bf16[1024,256]{1,0:T(8,128)(2,1)S(1)}, bf16[1024,256]{1,0:T(8,128)(2,1)S(1)}, u32[]{:S(2)}, u32[]{:S(2)}) collective-permute-start(bf16[1024,256]{1,0:T(8,128)(2,1)S(1)} %bitcast.31), channel_id=1, source_target_pairs={{0,2},{1,3},{2,0},{3,1},{4,6},{5,7},{6,4},{7,5},{8,10},{9,11},{10,... | collective-permute-start | bytes 1572872 | tf_op jit(solution)/shard_map/ppermute | solution.py:39
  38.8 0.0 collective-permute-start.3
  38.8 0.5 collective-permute-start.9
  39.3 7.7 %collective-permute-done.4.rest_2_ = bf16[1024,256]{1,0:T(8,128)(2,1)S(1)} collective-permute-done((bf16[1024,256]{1,0:T(8,128)(2,1)S(1)}, bf16[1024,256]{1,0:T(8,128)(2,1)S(1)}, u32[]{:S(2)}, u32[]{:S(2)}) %collective-permute-start.4) | collective-permute-done | bytes 524320 | tf_op jit(solution)/shard_map/ppermute | solution.py:39
  47.0 0.0 collective-permute-start.5
  47.0 5.9 %collective-permute-done.10.rest_6_ = bf16[1024,256]{1,0:T(8,128)(2,1)S(1)} collective-permute-done((bf16[1024,256]{1,0:T(8,128)(2,1)S(1)}, bf16[1024,256]{1,0:T(8,128)(2,1)S(1)}, u32[]{:S(2)}, u32[]{:S(2)}) %collective-permute-start.10) | collective-permute-done | bytes 524320 | tf_op jit(solution)/shard_map/ppermute | solution.py:39
  52.9 0.0 collective-permute-start.11
  52.9 0.0 copy-start.2
  52.9 0.7 copy-done.2
  53.6 0.1 dynamic_slice.10.cnt_ref
  53.6 0.1 pad_add_fusion.qb_ref
  53.7 0.7 constant_dynamic-slice_fusion.1.bl_ref
  54.4 0.0 copy-done
  54.4 0.0 collective-permute-done.3.rest_1_
  54.4 0.0 collective-permute-done.9.rest_5_
  54.4 0.0 collective-permute-done.5.rest_3_
  54.5 0.5 collective-permute-done.11.rest_7_
  54.9 20.0 %shard_map.55 = bf16[256,512]{1,0:T(8,128)(2,1)} custom-call(s32[2,32]{1,0:T(2,128)S(1)} %constant_dynamic-slice_fusion.1.bl_ref, s32[2]{0:T(128)S(1)} %dynamic_slice.10.cnt_ref, s32[2]{0:T(128)S(1)} %pad_add_fusion.qb_ref, bf16[256,512]{1,0:T(8,128)(2,1)S(1)} %constant_dynamic-slice_fusion.q_ref, bf16[1024,256]{1,0:T(8,128)(2,1)S(1)} %bitcast.30, ...), custom_call_target="tpu_custom_call" | custom-call | tf_op jit(solution)/shard_map/pallas_call | solution.py:182
  (12 shorter events, 0.3 us)
Async XLA Ops:
  0.0 54.4 %copy-start = (bf16[1024,512]{1,0:T(8,128)(2,1)S(1)}, bf16[1024,512]{1,0:T(8,128)(2,1)}, u32[]{:S(2)}) copy-start(bf16[1024,512]{1,0:T(8,128)(2,1)} %param.5) | copy-start | bytes 3145732
  0.0 1.0 %copy-start.1 = (bf16[256,128]{1,0:T(8,128)(2,1)S(1)}, bf16[256,128]{1,0:T(8,128)(2,1)}, u32[]{:S(2)}) copy-start(bf16[256,128]{1,0:T(8,128)(2,1)} %param.7) | copy-start | bytes 196612
  1.0 6.1 %collective-permute-start = (bf16[1,1,1,128,256]{4,3,2,1,0:T(8,128)(2,1)S(1)}, bf16[1,1,1,128,256]{4,3,2,1,0:T(8,128)(2,1)S(1)}, u32[]{:S(2)}, u32[]{:S(2)}) collective-permute-start(bf16[1,1,1,128,256]{4,3,2,1,0:T(8,128)(2,1)S(1)} %get-tuple-element.12), channel_id=1, source_target_pairs={{0,16},{4,20},{8,24},{12,28},{16,0},{20,4},{24,8},{28,12},{1,17},{... | collective-permute-start | bytes 196616 | tf_op jit(solution)/shard_map/ppermute | solution.py:24
  7.1 5.1 %collective-permute-start.1 = (bf16[2,1,1,128,256]{4,3,2,1,0:T(8,128)(2,1)S(1)}, bf16[2,1,1,128,256]{4,3,2,1,0:T(8,128)(2,1)S(1)}, u32[]{:S(2)}, u32[]{:S(2)}) collective-permute-start(bf16[2,1,1,128,256]{4,3,2,1,0:T(8,128)(2,1)S(1)} %maximum_select_fusion.4), channel_id=1, source_target_pairs={{0,8},{4,12},{8,0},{12,4},{16,24},{20,28},{24,16},{28,20},{1,9},{5... | collective-permute-start | bytes 393224 | tf_op jit(solution)/shard_map/ppermute | solution.py:24
  12.3 7.1 %collective-permute-start.2 = (bf16[2,2,1,128,256]{4,3,0,2,1:T(8,128)(2,1)S(1)}, bf16[2,2,1,128,256]{4,3,0,2,1:T(8,128)(2,1)S(1)}, u32[]{:S(2)}, u32[]{:S(2)}) collective-permute-start(bf16[2,2,1,128,256]{4,3,0,2,1:T(8,128)(2,1)S(1)} %maximum_select_fusion.2), channel_id=1, source_target_pairs={{0,4},{4,0},{8,12},{12,8},{16,20},{20,16},{24,28},{28,24},{1,5},{5... | collective-permute-start | bytes 786440 | tf_op jit(solution)/shard_map/ppermute | solution.py:24
  19.5 6.0 %collective-permute-start.6 = (bf16[1,1,1,128,256]{4,3,2,1,0:T(8,128)(2,1)S(1)}, bf16[1,1,1,128,256]{4,3,2,1,0:T(8,128)(2,1)S(1)}, u32[]{:S(2)}, u32[]{:S(2)}) collective-permute-start(bf16[1,1,1,128,256]{4,3,2,1,0:T(8,128)(2,1)S(1)} %bitcast.34), channel_id=1, source_target_pairs={{0,16},{4,20},{8,24},{12,28},{16,0},{20,4},{24,8},{28,12},{1,17},{... | collective-permute-start | bytes 196616 | tf_op jit(solution)/shard_map/ppermute | solution.py:24
  25.6 5.0 %collective-permute-start.7 = (bf16[2,1,1,128,256]{4,3,0,2,1:T(8,128)(2,1)S(1)}, bf16[2,1,1,128,256]{4,3,0,2,1:T(8,128)(2,1)S(1)}, u32[]{:S(2)}, u32[]{:S(2)}) collective-permute-start(bf16[2,1,1,128,256]{4,3,0,2,1:T(8,128)(2,1)S(1)} %fusion), channel_id=1, source_target_pairs={{0,8},{4,12},{8,0},{12,4},{16,24},{20,28},{24,16},{28,20},{1,9},{5... | collective-permute-start | bytes 393224 | tf_op jit(solution)/shard_map/ppermute | solution.py:24
  30.6 6.4 %collective-permute-start.8 = (bf16[2,2,1,128,256]{4,3,0,2,1:T(8,128)(2,1)S(1)}, bf16[2,2,1,128,256]{4,3,0,2,1:T(8,128)(2,1)S(1)}, u32[]{:S(2)}, u32[]{:S(2)}) collective-permute-start(bf16[2,2,1,128,256]{4,3,0,2,1:T(8,128)(2,1)S(1)} %maximum_select_fusion.3), channel_id=1, source_target_pairs={{0,4},{4,0},{8,12},{12,8},{16,20},{20,16},{24,28},{28,24},{1,5},{5... | collective-permute-start | bytes 786440 | tf_op jit(solution)/shard_map/ppermute | solution.py:24
  32.2 14.8 %collective-permute-start.4 = (bf16[1024,256]{1,0:T(8,128)(2,1)S(1)}, bf16[1024,256]{1,0:T(8,128)(2,1)S(1)}, u32[]{:S(2)}, u32[]{:S(2)}) collective-permute-start(bf16[1024,256]{1,0:T(8,128)(2,1)S(1)} %bitcast.28), channel_id=1, source_target_pairs={{0,2},{1,3},{2,0},{3,1},{4,6},{5,7},{6,4},{7,5},{8,10},{9,11},{10,... | collective-permute-start | bytes 1572872 | tf_op jit(solution)/shard_map/ppermute | solution.py:39
  37.2 15.7 %collective-permute-start.10 = (bf16[1024,256]{1,0:T(8,128)(2,1)S(1)}, bf16[1024,256]{1,0:T(8,128)(2,1)S(1)}, u32[]{:S(2)}, u32[]{:S(2)}) collective-permute-start(bf16[1024,256]{1,0:T(8,128)(2,1)S(1)} %bitcast.31), channel_id=1, source_target_pairs={{0,2},{1,3},{2,0},{3,1},{4,6},{5,7},{6,4},{7,5},{8,10},{9,11},{10,... | collective-permute-start | bytes 1572872 | tf_op jit(solution)/shard_map/ppermute | solution.py:39
  38.8 15.7 %collective-permute-start.3 = (bf16[1024,256]{1,0:T(8,128)(2,1)S(1)}, bf16[1024,256]{1,0:T(8,128)(2,1)}, u32[]{:S(2)}, u32[]{:S(2)}) collective-permute-start(bf16[1024,256]{1,0:T(8,128)(2,1)S(1)} %bitcast.29), channel_id=1, source_target_pairs={{0,1},{1,0},{2,3},{3,2},{4,5},{5,4},{6,7},{7,6},{8,9},{9,8},{10,11... | collective-permute-start | bytes 1572872 | tf_op jit(solution)/shard_map/ppermute | solution.py:39
  38.8 15.7 %collective-permute-start.9 = (bf16[1024,256]{1,0:T(8,128)(2,1)S(1)}, bf16[1024,256]{1,0:T(8,128)(2,1)}, u32[]{:S(2)}, u32[]{:S(2)}) collective-permute-start(bf16[1024,256]{1,0:T(8,128)(2,1)S(1)} %bitcast.32), channel_id=1, source_target_pairs={{0,1},{1,0},{2,3},{3,2},{4,5},{5,4},{6,7},{7,6},{8,9},{9,8},{10,11... | collective-permute-start | bytes 1572872 | tf_op jit(solution)/shard_map/ppermute | solution.py:39
  47.0 7.4 %collective-permute-start.5 = (bf16[1024,256]{1,0:T(8,128)(2,1)S(1)}, bf16[1024,256]{1,0:T(8,128)(2,1)}, u32[]{:S(2)}, u32[]{:S(2)}) collective-permute-start(bf16[1024,256]{1,0:T(8,128)(2,1)S(1)} %collective-permute-done.4.rest_2_), channel_id=1, source_target_pairs={{0,1},{1,0},{2,3},{3,2},{4,5},{5,4},{6,7},{7,6},{8,9},{9,8},{10,11... | collective-permute-start | bytes 1572872 | tf_op jit(solution)/shard_map/ppermute | solution.py:39
  52.9 2.0 %collective-permute-start.11 = (bf16[1024,256]{1,0:T(8,128)(2,1)S(1)}, bf16[1024,256]{1,0:T(8,128)(2,1)}, u32[]{:S(2)}, u32[]{:S(2)}) collective-permute-start(bf16[1024,256]{1,0:T(8,128)(2,1)S(1)} %collective-permute-done.10.rest_6_), channel_id=1, source_target_pairs={{0,1},{1,0},{2,3},{3,2},{4,5},{5,4},{6,7},{7,6},{8,9},{9,8},{10,11... | collective-permute-start | bytes 1572872 | tf_op jit(solution)/shard_map/ppermute | solution.py:39
  52.9 0.7 copy-start.2

commit v10 on v9

--- a/solution.py
+++ b/solution.py
@@ -68,7 +68,9 @@
             pltpu.make_async_copy(kv_pieces[0].at[pl.ds(0, BLK), :], self.dst, self.sem).wait()
 
     def copy(j, s):
-        return block_copy(off_ref[j, s], kvbuf.at[j, s], sems.at[j, s])
+        return block_copy(off_ref[j, s], kvbuf.at[j, s, :, pl.ds(0, 2 * HD)], sems.at[j, s])
+
+    kvbuf[:, :, :, 2 * HD:] = jnp.ones(kvbuf.shape[:3] + (HD,), kvbuf.dtype)
 
     n_off = []
     for j in range(n_local):
@@ -114,8 +116,9 @@
         m_new = jnp.maximum(m, jnp.max(sc, axis=1, keepdims=True))
         alpha = jnp.exp2(m - m_new)
         w = jnp.exp2(sc - m_new)
-        l = alpha * l + jnp.sum(w, axis=1, keepdims=True)
-        acc = alpha * acc + jnp.dot(w.astype(jnp.bfloat16), v, preferred_element_type=jnp.float32)
+        both = jnp.dot(w.astype(jnp.bfloat16), v, preferred_element_type=jnp.float32)
+        l = alpha * l + both[:, HD:HD + 1]
+        acc = alpha * acc + both[:, :HD]
         return m_new, l, acc
 
     for j in range(n_local):
@@ -129,7 +132,7 @@
         m = jnp.max(jnp.where(causal, sc, masked_score), axis=1, keepdims=True)
         w = jnp.where(causal, jnp.exp2(sc - m), 0.0)
         l = jnp.sum(w, axis=1, keepdims=True)
-        acc = jnp.dot(w.astype(jnp.bfloat16), kvd[:, HD:], preferred_element_type=jnp.float32)
+        acc = jnp.dot(w.astype(jnp.bfloat16), kvd[:, HD:2 * HD], preferred_element_type=jnp.float32)
 
         def grouped(g, carry, j=j, qs=qs):
             first = g * group
@@ -192,7 +195,7 @@
             out_specs=pl.BlockSpec((rows_mine, queries.shape[1]), lambda i, *_: (0, 0)),
             scratch_shapes=[
                 pltpu.SMEM((n_local, listed), jnp.int32),
-                pltpu.VMEM((n_local, listed, BLK, kv_local.shape[1]), jnp.bfloat16),
+                pltpu.VMEM((n_local, listed, BLK, kv_local.shape[1] + HD), jnp.bfloat16),
                 pltpu.VMEM((n_local, BLK, kv_local.shape[1]), jnp.bfloat16),
                 pltpu.SemaphoreType.DMA((n_local, listed)),
                 pltpu.SemaphoreType.DMA((n_local,)),

time: 75.1 us -> 74 us (0.985)
  Pallas kernels: 20 us -> 18.4 us
    pallas_call x1, Pallas kernels: 20 us -> 18.4 us  [shards(): pl.pallas_call(kernel, out_shape=jax.ShapeDtypeStruct((rows_mine, queries...]
where the time goes in v10:
time: 74 us; the launch traced here: 73.5 us
  waiting for transfers between devices  44.3 us (60%)
  Pallas kernels  18.4 us (25%)
  starting transfers between devices  7.63 us (10%)
  local copies, waits for them, and re-layouts  2.5 us (3%)
    ppermute x6, waiting for transfers between devices, gather_axis(): other = lax.ppermute(held, axis, [(i, i ^ b) for i in range(n)])  30.2 us
    pallas_call x1, Pallas kernels, shards(): pl.pallas_call(kernel, out_shape=jax.ShapeDtypeStruct((rows_mine, queries...  18.4 us
    ppermute x6, waiting for transfers between devices, pieces_axis(): lax.ppermute(idx_pieces[x], axis, [(i, i ^ b) for i in range(n)])  14.1 us
    ppermute x6, starting transfers between devices, gather_axis(): other = lax.ppermute(held, axis, [(i, i ^ b) for i in range(n)])  4.01 us
    ppermute x6, starting transfers between devices, pieces_axis(): lax.ppermute(idx_pieces[x], axis, [(i, i ^ b) for i in range(n)])  3.62 us
    unnamed x7, local copies, waits for them, and re-layouts  1.62 us
  transfers between devices with their start and end apart: 12, of which 9 were waited for; matrix products, arithmetic and copies ran while one was open for 1% of the time, Pallas kernels for 0%

profile of v10, /device:TPU:24, one launch (start us, length us, event | category | flops | bytes accessed | tf_op | source)
XLA Modules:
  0.0 73.5 jit_solution(10977165338250980514)
XLA Ops:
  0.0 0.0 copy-start
  0.0 0.0 copy-start.1
  0.0 0.9 %constant_dynamic-update-slice_fusion.1 = bf16[256,256]{1,0:T(8,128)(2,1)S(1)} fusion(bf16[256,128]{1,0:T(8,128)(2,1)} %param.6), kind=kLoop, calls=%fused_computation.16 | loop fusion | bytes 131072
  1.0 0.0 copy-done.1
  1.0 0.4 collective-permute-start
  1.4 5.7 %collective-permute-done = bf16[1,1,1,128,256]{4,3,2,1,0:T(8,128)(2,1)S(1)} collective-permute-done((bf16[1,1,1,128,256]{4,3,2,1,0:T(8,128)(2,1)S(1)}, bf16[1,1,1,128,256]{4,3,2,1,0:T(8,128)(2,1)S(1)}, u32[]{:S(2)}, u32[]{:S(2)}) %collective-permute-start) | collective-permute-done | bytes 65568 | tf_op jit(solution)/shard_map/ppermute | solution.py:24
  7.1 0.1 collective-permute-start.1
  7.3 5.0 %collective-permute-done.1 = bf16[2,1,1,128,256]{4,3,2,1,0:T(8,128)(2,1)S(1)} collective-permute-done((bf16[2,1,1,128,256]{4,3,2,1,0:T(8,128)(2,1)S(1)}, bf16[2,1,1,128,256]{4,3,2,1,0:T(8,128)(2,1)S(1)}, u32[]{:S(2)}, u32[]{:S(2)}) %collective-permute-start.1) | collective-permute-done | bytes 131104 | tf_op jit(solution)/shard_map/ppermute | solution.py:24
  12.3 0.1 maximum_select_fusion.2
  12.3 1.6 %collective-permute-start.2 = (bf16[2,2,1,128,256]{4,3,0,2,1:T(8,128)(2,1)S(1)}, bf16[2,2,1,128,256]{4,3,0,2,1:T(8,128)(2,1)S(1)}, u32[]{:S(2)}, u32[]{:S(2)}) collective-permute-start(bf16[2,2,1,128,256]{4,3,0,2,1:T(8,128)(2,1)S(1)} %maximum_select_fusion.2), channel_id=1, source_target_pairs={{0,4},{4,0},{8,12},{12,8},{16,20},{20,16},{24,28},{28,24},{1,5},{5... | collective-permute-start | bytes 786440 | tf_op jit(solution)/shard_map/ppermute | solution.py:24
  13.9 5.5 %collective-permute-done.2 = bf16[2,2,1,128,256]{4,3,0,2,1:T(8,128)(2,1)S(1)} collective-permute-done((bf16[2,2,1,128,256]{4,3,0,2,1:T(8,128)(2,1)S(1)}, bf16[2,2,1,128,256]{4,3,0,2,1:T(8,128)(2,1)S(1)}, u32[]{:S(2)}, u32[]{:S(2)}) %collective-permute-start.2) | collective-permute-done | bytes 262176 | tf_op jit(solution)/shard_map/ppermute | solution.py:24
  19.5 0.1 collective-permute-start.6
  19.6 6.0 %collective-permute-done.6 = bf16[1,1,1,128,256]{4,3,2,1,0:T(8,128)(2,1)S(1)} collective-permute-done((bf16[1,1,1,128,256]{4,3,2,1,0:T(8,128)(2,1)S(1)}, bf16[1,1,1,128,256]{4,3,2,1,0:T(8,128)(2,1)S(1)}, u32[]{:S(2)}, u32[]{:S(2)}) %collective-permute-start.6) | collective-permute-done | bytes 65568 | tf_op jit(solution)/shard_map/ppermute | solution.py:24
  25.6 0.4 collective-permute-start.7
  26.0 4.7 %collective-permute-done.7 = bf16[2,1,1,128,256]{4,3,0,2,1:T(8,128)(2,1)S(1)} collective-permute-done((bf16[2,1,1,128,256]{4,3,0,2,1:T(8,128)(2,1)S(1)}, bf16[2,1,1,128,256]{4,3,0,2,1:T(8,128)(2,1)S(1)}, u32[]{:S(2)}, u32[]{:S(2)}) %collective-permute-start.7) | collective-permute-done | bytes 131104 | tf_op jit(solution)/shard_map/ppermute | solution.py:24
  30.6 1.6 %collective-permute-start.8 = (bf16[2,2,1,128,256]{4,3,0,2,1:T(8,128)(2,1)S(1)}, bf16[2,2,1,128,256]{4,3,0,2,1:T(8,128)(2,1)S(1)}, u32[]{:S(2)}, u32[]{:S(2)}) collective-permute-start(bf16[2,2,1,128,256]{4,3,0,2,1:T(8,128)(2,1)S(1)} %maximum_select_fusion.3), channel_id=1, source_target_pairs={{0,4},{4,0},{8,12},{12,8},{16,20},{20,16},{24,28},{28,24},{1,5},{5... | collective-permute-start | bytes 786440 | tf_op jit(solution)/shard_map/ppermute | solution.py:24
  32.2 1.5 %collective-permute-start.4 = (bf16[1024,256]{1,0:T(8,128)(2,1)S(1)}, bf16[1024,256]{1,0:T(8,128)(2,1)S(1)}, u32[]{:S(2)}, u32[]{:S(2)}) collective-permute-start(bf16[1024,256]{1,0:T(8,128)(2,1)S(1)} %bitcast.28), channel_id=1, source_target_pairs={{0,2},{1,3},{2,0},{3,1},{4,6},{5,7},{6,4},{7,5},{8,10},{9,11},{10,... | collective-permute-start | bytes 1572872 | tf_op jit(solution)/shard_map/ppermute | solution.py:39
  33.7 3.4 %collective-permute-done.8 = bf16[2,2,1,128,256]{4,3,0,2,1:T(8,128)(2,1)S(1)} collective-permute-done((bf16[2,2,1,128,256]{4,3,0,2,1:T(8,128)(2,1)S(1)}, bf16[2,2,1,128,256]{4,3,0,2,1:T(8,128)(2,1)S(1)}, u32[]{:S(2)}, u32[]{:S(2)}) %collective-permute-start.8) | collective-permute-done | bytes 262176 | tf_op jit(solution)/shard_map/ppermute | solution.py:24
  37.2 1.6 %collective-permute-start.10 = (bf16[1024,256]{1,0:T(8,128)(2,1)S(1)}, bf16[1024,256]{1,0:T(8,128)(2,1)S(1)}, u32[]{:S(2)}, u32[]{:S(2)}) collective-permute-start(bf16[1024,256]{1,0:T(8,128)(2,1)S(1)} %bitcast.31), channel_id=1, source_target_pairs={{0,2},{1,3},{2,0},{3,1},{4,6},{5,7},{6,4},{7,5},{8,10},{9,11},{10,... | collective-permute-start | bytes 1572872 | tf_op jit(solution)/shard_map/ppermute | solution.py:39
  38.8 0.0 collective-permute-start.3
  38.8 0.5 collective-permute-start.9
  39.3 7.7 %collective-permute-done.4.rest_2_ = bf16[1024,256]{1,0:T(8,128)(2,1)S(1)} collective-permute-done((bf16[1024,256]{1,0:T(8,128)(2,1)S(1)}, bf16[1024,256]{1,0:T(8,128)(2,1)S(1)}, u32[]{:S(2)}, u32[]{:S(2)}) %collective-permute-start.4) | collective-permute-done | bytes 524320 | tf_op jit(solution)/shard_map/ppermute | solution.py:39
  47.0 0.0 collective-permute-start.5
  47.0 5.9 %collective-permute-done.10.rest_6_ = bf16[1024,256]{1,0:T(8,128)(2,1)S(1)} collective-permute-done((bf16[1024,256]{1,0:T(8,128)(2,1)S(1)}, bf16[1024,256]{1,0:T(8,128)(2,1)S(1)}, u32[]{:S(2)}, u32[]{:S(2)}) %collective-permute-start.10) | collective-permute-done | bytes 524320 | tf_op jit(solution)/shard_map/ppermute | solution.py:39
  52.9 0.0 collective-permute-start.11
  52.9 0.0 copy-start.2
  52.9 0.7 copy-done.2
  53.6 0.1 dynamic_slice.10.cnt_ref
  53.6 0.1 pad_add_fusion.qb_ref
  53.7 0.7 constant_dynamic-slice_fusion.1.bl_ref
  54.4 0.0 copy-done
  54.4 0.0 collective-permute-done.3.rest_1_
  54.4 0.0 collective-permute-done.9.rest_5_
  54.4 0.0 collective-permute-done.5.rest_3_
  54.5 0.5 collective-permute-done.11.rest_7_
  54.9 18.4 %shard_map.55 = bf16[256,512]{1,0:T(8,128)(2,1)} custom-call(s32[2,32]{1,0:T(2,128)S(1)} %constant_dynamic-slice_fusion.1.bl_ref, s32[2]{0:T(128)S(1)} %dynamic_slice.10.cnt_ref, s32[2]{0:T(128)S(1)} %pad_add_fusion.qb_ref, bf16[256,512]{1,0:T(8,128)(2,1)S(1)} %constant_dynamic-slice_fusion.q_ref, bf16[1024,256]{1,0:T(8,128)(2,1)S(1)} %bitcast.30, ...), custom_call_target="tpu_custom_call" | custom-call | tf_op jit(solution)/shard_map/pallas_call | solution.py:185
  (12 shorter events, 0.3 us)
Async XLA Ops:
  0.0 54.4 %copy-start = (bf16[1024,512]{1,0:T(8,128)(2,1)S(1)}, bf16[1024,512]{1,0:T(8,128)(2,1)}, u32[]{:S(2)}) copy-start(bf16[1024,512]{1,0:T(8,128)(2,1)} %param.5) | copy-start | bytes 3145732
  0.0 1.0 %copy-start.1 = (bf16[256,128]{1,0:T(8,128)(2,1)S(1)}, bf16[256,128]{1,0:T(8,128)(2,1)}, u32[]{:S(2)}) copy-start(bf16[256,128]{1,0:T(8,128)(2,1)} %param.7) | copy-start | bytes 196612
  1.0 6.1 %collective-permute-start = (bf16[1,1,1,128,256]{4,3,2,1,0:T(8,128)(2,1)S(1)}, bf16[1,1,1,128,256]{4,3,2,1,0:T(8,128)(2,1)S(1)}, u32[]{:S(2)}, u32[]{:S(2)}) collective-permute-start(bf16[1,1,1,128,256]{4,3,2,1,0:T(8,128)(2,1)S(1)} %get-tuple-element.12), channel_id=1, source_target_pairs={{0,16},{4,20},{8,24},{12,28},{16,0},{20,4},{24,8},{28,12},{1,17},{... | collective-permute-start | bytes 196616 | tf_op jit(solution)/shard_map/ppermute | solution.py:24
  7.1 5.1 %collective-permute-start.1 = (bf16[2,1,1,128,256]{4,3,2,1,0:T(8,128)(2,1)S(1)}, bf16[2,1,1,128,256]{4,3,2,1,0:T(8,128)(2,1)S(1)}, u32[]{:S(2)}, u32[]{:S(2)}) collective-permute-start(bf16[2,1,1,128,256]{4,3,2,1,0:T(8,128)(2,1)S(1)} %maximum_select_fusion.4), channel_id=1, source_target_pairs={{0,8},{4,12},{8,0},{12,4},{16,24},{20,28},{24,16},{28,20},{1,9},{5... | collective-permute-start | bytes 393224 | tf_op jit(solution)/shard_map/ppermute | solution.py:24
  12.3 7.1 %collective-permute-start.2 = (bf16[2,2,1,128,256]{4,3,0,2,1:T(8,128)(2,1)S(1)}, bf16[2,2,1,128,256]{4,3,0,2,1:T(8,128)(2,1)S(1)}, u32[]{:S(2)}, u32[]{:S(2)}) collective-permute-start(bf16[2,2,1,128,256]{4,3,0,2,1:T(8,128)(2,1)S(1)} %maximum_select_fusion.2), channel_id=1, source_target_pairs={{0,4},{4,0},{8,12},{12,8},{16,20},{20,16},{24,28},{28,24},{1,5},{5... | collective-permute-start | bytes 786440 | tf_op jit(solution)/shard_map/ppermute | solution.py:24
  19.5 6.0 %collective-permute-start.6 = (bf16[1,1,1,128,256]{4,3,2,1,0:T(8,128)(2,1)S(1)}, bf16[1,1,1,128,256]{4,3,2,1,0:T(8,128)(2,1)S(1)}, u32[]{:S(2)}, u32[]{:S(2)}) collective-permute-start(bf16[1,1,1,128,256]{4,3,2,1,0:T(8,128)(2,1)S(1)} %bitcast.34), channel_id=1, source_target_pairs={{0,16},{4,20},{8,24},{12,28},{16,0},{20,4},{24,8},{28,12},{1,17},{... | collective-permute-start | bytes 196616 | tf_op jit(solution)/shard_map/ppermute | solution.py:24
  25.6 5.0 %collective-permute-start.7 = (bf16[2,1,1,128,256]{4,3,0,2,1:T(8,128)(2,1)S(1)}, bf16[2,1,1,128,256]{4,3,0,2,1:T(8,128)(2,1)S(1)}, u32[]{:S(2)}, u32[]{:S(2)}) collective-permute-start(bf16[2,1,1,128,256]{4,3,0,2,1:T(8,128)(2,1)S(1)} %fusion), channel_id=1, source_target_pairs={{0,8},{4,12},{8,0},{12,4},{16,24},{20,28},{24,16},{28,20},{1,9},{5... | collective-permute-start | bytes 393224 | tf_op jit(solution)/shard_map/ppermute | solution.py:24
  30.6 6.4 %collective-permute-start.8 = (bf16[2,2,1,128,256]{4,3,0,2,1:T(8,128)(2,1)S(1)}, bf16[2,2,1,128,256]{4,3,0,2,1:T(8,128)(2,1)S(1)}, u32[]{:S(2)}, u32[]{:S(2)}) collective-permute-start(bf16[2,2,1,128,256]{4,3,0,2,1:T(8,128)(2,1)S(1)} %maximum_select_fusion.3), channel_id=1, source_target_pairs={{0,4},{4,0},{8,12},{12,8},{16,20},{20,16},{24,28},{28,24},{1,5},{5... | collective-permute-start | bytes 786440 | tf_op jit(solution)/shard_map/ppermute | solution.py:24
  32.2 14.8 %collective-permute-start.4 = (bf16[1024,256]{1,0:T(8,128)(2,1)S(1)}, bf16[1024,256]{1,0:T(8,128)(2,1)S(1)}, u32[]{:S(2)}, u32[]{:S(2)}) collective-permute-start(bf16[1024,256]{1,0:T(8,128)(2,1)S(1)} %bitcast.28), channel_id=1, source_target_pairs={{0,2},{1,3},{2,0},{3,1},{4,6},{5,7},{6,4},{7,5},{8,10},{9,11},{10,... | collective-permute-start | bytes 1572872 | tf_op jit(solution)/shard_map/ppermute | solution.py:39
  37.2 15.7 %collective-permute-start.10 = (bf16[1024,256]{1,0:T(8,128)(2,1)S(1)}, bf16[1024,256]{1,0:T(8,128)(2,1)S(1)}, u32[]{:S(2)}, u32[]{:S(2)}) collective-permute-start(bf16[1024,256]{1,0:T(8,128)(2,1)S(1)} %bitcast.31), channel_id=1, source_target_pairs={{0,2},{1,3},{2,0},{3,1},{4,6},{5,7},{6,4},{7,5},{8,10},{9,11},{10,... | collective-permute-start | bytes 1572872 | tf_op jit(solution)/shard_map/ppermute | solution.py:39
  38.8 15.7 %collective-permute-start.3 = (bf16[1024,256]{1,0:T(8,128)(2,1)S(1)}, bf16[1024,256]{1,0:T(8,128)(2,1)}, u32[]{:S(2)}, u32[]{:S(2)}) collective-permute-start(bf16[1024,256]{1,0:T(8,128)(2,1)S(1)} %bitcast.29), channel_id=1, source_target_pairs={{0,1},{1,0},{2,3},{3,2},{4,5},{5,4},{6,7},{7,6},{8,9},{9,8},{10,11... | collective-permute-start | bytes 1572872 | tf_op jit(solution)/shard_map/ppermute | solution.py:39
  38.8 15.7 %collective-permute-start.9 = (bf16[1024,256]{1,0:T(8,128)(2,1)S(1)}, bf16[1024,256]{1,0:T(8,128)(2,1)}, u32[]{:S(2)}, u32[]{:S(2)}) collective-permute-start(bf16[1024,256]{1,0:T(8,128)(2,1)S(1)} %bitcast.32), channel_id=1, source_target_pairs={{0,1},{1,0},{2,3},{3,2},{4,5},{5,4},{6,7},{7,6},{8,9},{9,8},{10,11... | collective-permute-start | bytes 1572872 | tf_op jit(solution)/shard_map/ppermute | solution.py:39
  47.0 7.4 %collective-permute-start.5 = (bf16[1024,256]{1,0:T(8,128)(2,1)S(1)}, bf16[1024,256]{1,0:T(8,128)(2,1)}, u32[]{:S(2)}, u32[]{:S(2)}) collective-permute-start(bf16[1024,256]{1,0:T(8,128)(2,1)S(1)} %collective-permute-done.4.rest_2_), channel_id=1, source_target_pairs={{0,1},{1,0},{2,3},{3,2},{4,5},{5,4},{6,7},{7,6},{8,9},{9,8},{10,11... | collective-permute-start | bytes 1572872 | tf_op jit(solution)/shard_map/ppermute | solution.py:39
  52.9 2.0 %collective-permute-start.11 = (bf16[1024,256]{1,0:T(8,128)(2,1)S(1)}, bf16[1024,256]{1,0:T(8,128)(2,1)}, u32[]{:S(2)}, u32[]{:S(2)}) collective-permute-start(bf16[1024,256]{1,0:T(8,128)(2,1)S(1)} %collective-permute-done.10.rest_6_), channel_id=1, source_target_pairs={{0,1},{1,0},{2,3},{3,2},{4,5},{5,4},{6,7},{7,6},{8,9},{9,8},{10,11... | collective-permute-start | bytes 1572872 | tf_op jit(solution)/shard_map/ppermute | solution.py:39
  52.9 0.7 copy-start.2

commit v11 on v10

--- a/solution.py
+++ b/solution.py
@@ -110,12 +110,12 @@
         m, l, acc = carry
         k = kvb[:, :HD]
         v = kvb[:, HD:]
-        sc = lax.dot_general(qs, k, dims, preferred_element_type=jnp.float32) * scale
+        sc = lax.dot_general(qs, k, dims, preferred_element_type=jnp.float32)
         if live is not None:
             sc = jnp.where(slot_of < live, sc, masked_score)
-        m_new = jnp.maximum(m, jnp.max(sc, axis=1, keepdims=True))
+        m_new = jnp.maximum(m, jnp.max(sc, axis=1, keepdims=True) * scale)
         alpha = jnp.exp2(m - m_new)
-        w = jnp.exp2(sc - m_new)
+        w = jnp.exp2(sc * scale - m_new)
         both = jnp.dot(w.astype(jnp.bfloat16), v, preferred_element_type=jnp.float32)
         l = alpha * l + both[:, HD:HD + 1]
         acc = alpha * acc + both[:, :HD]

time: 74 us -> 73.3 us (level)
  no operation moved by 1% of the time
where the time goes in v11:
time: 73.3 us; the launch traced here: 72.8 us
  waiting for transfers between devices  44.3 us (60%)
  Pallas kernels  17.7 us (24%)
  starting transfers between devices  7.63 us (10%)
  local copies, waits for them, and re-layouts  2.5 us (3%)
    ppermute x6, waiting for transfers between devices, gather_axis(): other = lax.ppermute(held, axis, [(i, i ^ b) for i in range(n)])  30.2 us
    pallas_call x1, Pallas kernels, shards(): pl.pallas_call(kernel, out_shape=jax.ShapeDtypeStruct((rows_mine, queries...  17.7 us
    ppermute x6, waiting for transfers between devices, pieces_axis(): lax.ppermute(idx_pieces[x], axis, [(i, i ^ b) for i in range(n)])  14.1 us
    ppermute x6, starting transfers between devices, gather_axis(): other = lax.ppermute(held, axis, [(i, i ^ b) for i in range(n)])  4.01 us
    ppermute x6, starting transfers between devices, pieces_axis(): lax.ppermute(idx_pieces[x], axis, [(i, i ^ b) for i in range(n)])  3.62 us
    unnamed x7, local copies, waits for them, and re-layouts  1.62 us
  transfers between devices with their start and end apart: 12, of which 9 were waited for; matrix products, arithmetic and copies ran while one was open for 1% of the time, Pallas kernels for 0%

profile of v11, /device:TPU:24, one launch (start us, length us, event | category | flops | bytes accessed | tf_op | source)
XLA Modules:
  0.0 72.8 jit_solution(1596808862515975749)
XLA Ops:
  0.0 0.0 copy-start
  0.0 0.0 copy-start.1
  0.0 0.9 %constant_dynamic-update-slice_fusion.1 = bf16[256,256]{1,0:T(8,128)(2,1)S(1)} fusion(bf16[256,128]{1,0:T(8,128)(2,1)} %param.6), kind=kLoop, calls=%fused_computation.16 | loop fusion | bytes 131072
  1.0 0.0 copy-done.1
  1.0 0.4 collective-permute-start
  1.4 5.7 %collective-permute-done = bf16[1,1,1,128,256]{4,3,2,1,0:T(8,128)(2,1)S(1)} collective-permute-done((bf16[1,1,1,128,256]{4,3,2,1,0:T(8,128)(2,1)S(1)}, bf16[1,1,1,128,256]{4,3,2,1,0:T(8,128)(2,1)S(1)}, u32[]{:S(2)}, u32[]{:S(2)}) %collective-permute-start) | collective-permute-done | bytes 65568 | tf_op jit(solution)/shard_map/ppermute | solution.py:24
  7.1 0.1 collective-permute-start.1
  7.3 5.0 %collective-permute-done.1 = bf16[2,1,1,128,256]{4,3,2,1,0:T(8,128)(2,1)S(1)} collective-permute-done((bf16[2,1,1,128,256]{4,3,2,1,0:T(8,128)(2,1)S(1)}, bf16[2,1,1,128,256]{4,3,2,1,0:T(8,128)(2,1)S(1)}, u32[]{:S(2)}, u32[]{:S(2)}) %collective-permute-start.1) | collective-permute-done | bytes 131104 | tf_op jit(solution)/shard_map/ppermute | solution.py:24
  12.3 0.1 maximum_select_fusion.2
  12.3 1.6 %collective-permute-start.2 = (bf16[2,2,1,128,256]{4,3,0,2,1:T(8,128)(2,1)S(1)}, bf16[2,2,1,128,256]{4,3,0,2,1:T(8,128)(2,1)S(1)}, u32[]{:S(2)}, u32[]{:S(2)}) collective-permute-start(bf16[2,2,1,128,256]{4,3,0,2,1:T(8,128)(2,1)S(1)} %maximum_select_fusion.2), channel_id=1, source_target_pairs={{0,4},{4,0},{8,12},{12,8},{16,20},{20,16},{24,28},{28,24},{1,5},{5... | collective-permute-start | bytes 786440 | tf_op jit(solution)/shard_map/ppermute | solution.py:24
  13.9 5.5 %collective-permute-done.2 = bf16[2,2,1,128,256]{4,3,0,2,1:T(8,128)(2,1)S(1)} collective-permute-done((bf16[2,2,1,128,256]{4,3,0,2,1:T(8,128)(2,1)S(1)}, bf16[2,2,1,128,256]{4,3,0,2,1:T(8,128)(2,1)S(1)}, u32[]{:S(2)}, u32[]{:S(2)}) %collective-permute-start.2) | collective-permute-done | bytes 262176 | tf_op jit(solution)/shard_map/ppermute | solution.py:24
  19.5 0.1 collective-permute-start.6
  19.6 6.0 %collective-permute-done.6 = bf16[1,1,1,128,256]{4,3,2,1,0:T(8,128)(2,1)S(1)} collective-permute-done((bf16[1,1,1,128,256]{4,3,2,1,0:T(8,128)(2,1)S(1)}, bf16[1,1,1,128,256]{4,3,2,1,0:T(8,128)(2,1)S(1)}, u32[]{:S(2)}, u32[]{:S(2)}) %collective-permute-start.6) | collective-permute-done | bytes 65568 | tf_op jit(solution)/shard_map/ppermute | solution.py:24
  25.6 0.4 collective-permute-start.7
  26.0 4.7 %collective-permute-done.7 = bf16[2,1,1,128,256]{4,3,0,2,1:T(8,128)(2,1)S(1)} collective-permute-done((bf16[2,1,1,128,256]{4,3,0,2,1:T(8,128)(2,1)S(1)}, bf16[2,1,1,128,256]{4,3,0,2,1:T(8,128)(2,1)S(1)}, u32[]{:S(2)}, u32[]{:S(2)}) %collective-permute-start.7) | collective-permute-done | bytes 131104 | tf_op jit(solution)/shard_map/ppermute | solution.py:24
  30.6 1.6 %collective-permute-start.8 = (bf16[2,2,1,128,256]{4,3,0,2,1:T(8,128)(2,1)S(1)}, bf16[2,2,1,128,256]{4,3,0,2,1:T(8,128)(2,1)S(1)}, u32[]{:S(2)}, u32[]{:S(2)}) collective-permute-start(bf16[2,2,1,128,256]{4,3,0,2,1:T(8,128)(2,1)S(1)} %maximum_select_fusion.3), channel_id=1, source_target_pairs={{0,4},{4,0},{8,12},{12,8},{16,20},{20,16},{24,28},{28,24},{1,5},{5... | collective-permute-start | bytes 786440 | tf_op jit(solution)/shard_map/ppermute | solution.py:24
  32.2 1.5 %collective-permute-start.4 = (bf16[1024,256]{1,0:T(8,128)(2,1)S(1)}, bf16[1024,256]{1,0:T(8,128)(2,1)S(1)}, u32[]{:S(2)}, u32[]{:S(2)}) collective-permute-start(bf16[1024,256]{1,0:T(8,128)(2,1)S(1)} %bitcast.28), channel_id=1, source_target_pairs={{0,2},{1,3},{2,0},{3,1},{4,6},{5,7},{6,4},{7,5},{8,10},{9,11},{10,... | collective-permute-start | bytes 1572872 | tf_op jit(solution)/shard_map/ppermute | solution.py:39
  33.7 3.4 %collective-permute-done.8 = bf16[2,2,1,128,256]{4,3,0,2,1:T(8,128)(2,1)S(1)} collective-permute-done((bf16[2,2,1,128,256]{4,3,0,2,1:T(8,128)(2,1)S(1)}, bf16[2,2,1,128,256]{4,3,0,2,1:T(8,128)(2,1)S(1)}, u32[]{:S(2)}, u32[]{:S(2)}) %collective-permute-start.8) | collective-permute-done | bytes 262176 | tf_op jit(solution)/shard_map/ppermute | solution.py:24
  37.2 1.6 %collective-permute-start.10 = (bf16[1024,256]{1,0:T(8,128)(2,1)S(1)}, bf16[1024,256]{1,0:T(8,128)(2,1)S(1)}, u32[]{:S(2)}, u32[]{:S(2)}) collective-permute-start(bf16[1024,256]{1,0:T(8,128)(2,1)S(1)} %bitcast.31), channel_id=1, source_target_pairs={{0,2},{1,3},{2,0},{3,1},{4,6},{5,7},{6,4},{7,5},{8,10},{9,11},{10,... | collective-permute-start | bytes 1572872 | tf_op jit(solution)/shard_map/ppermute | solution.py:39
  38.8 0.0 collective-permute-start.3
  38.8 0.5 collective-permute-start.9
  39.3 7.7 %collective-permute-done.4.rest_2_ = bf16[1024,256]{1,0:T(8,128)(2,1)S(1)} collective-permute-done((bf16[1024,256]{1,0:T(8,128)(2,1)S(1)}, bf16[1024,256]{1,0:T(8,128)(2,1)S(1)}, u32[]{:S(2)}, u32[]{:S(2)}) %collective-permute-start.4) | collective-permute-done | bytes 524320 | tf_op jit(solution)/shard_map/ppermute | solution.py:39
  47.0 0.0 collective-permute-start.5
  47.0 5.9 %collective-permute-done.10.rest_6_ = bf16[1024,256]{1,0:T(8,128)(2,1)S(1)} collective-permute-done((bf16[1024,256]{1,0:T(8,128)(2,1)S(1)}, bf16[1024,256]{1,0:T(8,128)(2,1)S(1)}, u32[]{:S(2)}, u32[]{:S(2)}) %collective-permute-start.10) | collective-permute-done | bytes 524320 | tf_op jit(solution)/shard_map/ppermute | solution.py:39
  52.9 0.0 collective-permute-start.11
  52.9 0.0 copy-start.2
  52.9 0.7 copy-done.2
  53.6 0.1 dynamic_slice.10.cnt_ref
  53.6 0.1 pad_add_fusion.qb_ref
  53.7 0.7 constant_dynamic-slice_fusion.1.bl_ref
  54.4 0.0 copy-done
  54.4 0.0 collective-permute-done.3.rest_1_
  54.4 0.0 collective-permute-done.9.rest_5_
  54.4 0.0 collective-permute-done.5.rest_3_
  54.5 0.5 collective-permute-done.11.rest_7_
  54.9 17.7 %shard_map.55 = bf16[256,512]{1,0:T(8,128)(2,1)} custom-call(s32[2,32]{1,0:T(2,128)S(1)} %constant_dynamic-slice_fusion.1.bl_ref, s32[2]{0:T(128)S(1)} %dynamic_slice.10.cnt_ref, s32[2]{0:T(128)S(1)} %pad_add_fusion.qb_ref, bf16[256,512]{1,0:T(8,128)(2,1)S(1)} %constant_dynamic-slice_fusion.q_ref, bf16[1024,256]{1,0:T(8,128)(2,1)S(1)} %bitcast.30, ...), custom_call_target="tpu_custom_call" | custom-call | tf_op jit(solution)/shard_map/pallas_call | solution.py:185
  (12 shorter events, 0.3 us)
Async XLA Ops:
  0.0 54.4 %copy-start = (bf16[1024,512]{1,0:T(8,128)(2,1)S(1)}, bf16[1024,512]{1,0:T(8,128)(2,1)}, u32[]{:S(2)}) copy-start(bf16[1024,512]{1,0:T(8,128)(2,1)} %param.5) | copy-start | bytes 3145732
  0.0 1.0 %copy-start.1 = (bf16[256,128]{1,0:T(8,128)(2,1)S(1)}, bf16[256,128]{1,0:T(8,128)(2,1)}, u32[]{:S(2)}) copy-start(bf16[256,128]{1,0:T(8,128)(2,1)} %param.7) | copy-start | bytes 196612
  1.0 6.1 %collective-permute-start = (bf16[1,1,1,128,256]{4,3,2,1,0:T(8,128)(2,1)S(1)}, bf16[1,1,1,128,256]{4,3,2,1,0:T(8,128)(2,1)S(1)}, u32[]{:S(2)}, u32[]{:S(2)}) collective-permute-start(bf16[1,1,1,128,256]{4,3,2,1,0:T(8,128)(2,1)S(1)} %get-tuple-element.12), channel_id=1, source_target_pairs={{0,16},{4,20},{8,24},{12,28},{16,0},{20,4},{24,8},{28,12},{1,17},{... | collective-permute-start | bytes 196616 | tf_op jit(solution)/shard_map/ppermute | solution.py:24
  7.1 5.1 %collective-permute-start.1 = (bf16[2,1,1,128,256]{4,3,2,1,0:T(8,128)(2,1)S(1)}, bf16[2,1,1,128,256]{4,3,2,1,0:T(8,128)(2,1)S(1)}, u32[]{:S(2)}, u32[]{:S(2)}) collective-permute-start(bf16[2,1,1,128,256]{4,3,2,1,0:T(8,128)(2,1)S(1)} %maximum_select_fusion.4), channel_id=1, source_target_pairs={{0,8},{4,12},{8,0},{12,4},{16,24},{20,28},{24,16},{28,20},{1,9},{5... | collective-permute-start | bytes 393224 | tf_op jit(solution)/shard_map/ppermute | solution.py:24
  12.3 7.1 %collective-permute-start.2 = (bf16[2,2,1,128,256]{4,3,0,2,1:T(8,128)(2,1)S(1)}, bf16[2,2,1,128,256]{4,3,0,2,1:T(8,128)(2,1)S(1)}, u32[]{:S(2)}, u32[]{:S(2)}) collective-permute-start(bf16[2,2,1,128,256]{4,3,0,2,1:T(8,128)(2,1)S(1)} %maximum_select_fusion.2), channel_id=1, source_target_pairs={{0,4},{4,0},{8,12},{12,8},{16,20},{20,16},{24,28},{28,24},{1,5},{5... | collective-permute-start | bytes 786440 | tf_op jit(solution)/shard_map/ppermute | solution.py:24
  19.5 6.0 %collective-permute-start.6 = (bf16[1,1,1,128,256]{4,3,2,1,0:T(8,128)(2,1)S(1)}, bf16[1,1,1,128,256]{4,3,2,1,0:T(8,128)(2,1)S(1)}, u32[]{:S(2)}, u32[]{:S(2)}) collective-permute-start(bf16[1,1,1,128,256]{4,3,2,1,0:T(8,128)(2,1)S(1)} %bitcast.34), channel_id=1, source_target_pairs={{0,16},{4,20},{8,24},{12,28},{16,0},{20,4},{24,8},{28,12},{1,17},{... | collective-permute-start | bytes 196616 | tf_op jit(solution)/shard_map/ppermute | solution.py:24
  25.6 5.0 %collective-permute-start.7 = (bf16[2,1,1,128,256]{4,3,0,2,1:T(8,128)(2,1)S(1)}, bf16[2,1,1,128,256]{4,3,0,2,1:T(8,128)(2,1)S(1)}, u32[]{:S(2)}, u32[]{:S(2)}) collective-permute-start(bf16[2,1,1,128,256]{4,3,0,2,1:T(8,128)(2,1)S(1)} %fusion), channel_id=1, source_target_pairs={{0,8},{4,12},{8,0},{12,4},{16,24},{20,28},{24,16},{28,20},{1,9},{5... | collective-permute-start | bytes 393224 | tf_op jit(solution)/shard_map/ppermute | solution.py:24
  30.6 6.4 %collective-permute-start.8 = (bf16[2,2,1,128,256]{4,3,0,2,1:T(8,128)(2,1)S(1)}, bf16[2,2,1,128,256]{4,3,0,2,1:T(8,128)(2,1)S(1)}, u32[]{:S(2)}, u32[]{:S(2)}) collective-permute-start(bf16[2,2,1,128,256]{4,3,0,2,1:T(8,128)(2,1)S(1)} %maximum_select_fusion.3), channel_id=1, source_target_pairs={{0,4},{4,0},{8,12},{12,8},{16,20},{20,16},{24,28},{28,24},{1,5},{5... | collective-permute-start | bytes 786440 | tf_op jit(solution)/shard_map/ppermute | solution.py:24
  32.2 14.8 %collective-permute-start.4 = (bf16[1024,256]{1,0:T(8,128)(2,1)S(1)}, bf16[1024,256]{1,0:T(8,128)(2,1)S(1)}, u32[]{:S(2)}, u32[]{:S(2)}) collective-permute-start(bf16[1024,256]{1,0:T(8,128)(2,1)S(1)} %bitcast.28), channel_id=1, source_target_pairs={{0,2},{1,3},{2,0},{3,1},{4,6},{5,7},{6,4},{7,5},{8,10},{9,11},{10,... | collective-permute-start | bytes 1572872 | tf_op jit(solution)/shard_map/ppermute | solution.py:39
  37.2 15.7 %collective-permute-start.10 = (bf16[1024,256]{1,0:T(8,128)(2,1)S(1)}, bf16[1024,256]{1,0:T(8,128)(2,1)S(1)}, u32[]{:S(2)}, u32[]{:S(2)}) collective-permute-start(bf16[1024,256]{1,0:T(8,128)(2,1)S(1)} %bitcast.31), channel_id=1, source_target_pairs={{0,2},{1,3},{2,0},{3,1},{4,6},{5,7},{6,4},{7,5},{8,10},{9,11},{10,... | collective-permute-start | bytes 1572872 | tf_op jit(solution)/shard_map/ppermute | solution.py:39
  38.8 15.7 %collective-permute-start.3 = (bf16[1024,256]{1,0:T(8,128)(2,1)S(1)}, bf16[1024,256]{1,0:T(8,128)(2,1)}, u32[]{:S(2)}, u32[]{:S(2)}) collective-permute-start(bf16[1024,256]{1,0:T(8,128)(2,1)S(1)} %bitcast.29), channel_id=1, source_target_pairs={{0,1},{1,0},{2,3},{3,2},{4,5},{5,4},{6,7},{7,6},{8,9},{9,8},{10,11... | collective-permute-start | bytes 1572872 | tf_op jit(solution)/shard_map/ppermute | solution.py:39
  38.8 15.7 %collective-permute-start.9 = (bf16[1024,256]{1,0:T(8,128)(2,1)S(1)}, bf16[1024,256]{1,0:T(8,128)(2,1)}, u32[]{:S(2)}, u32[]{:S(2)}) collective-permute-start(bf16[1024,256]{1,0:T(8,128)(2,1)S(1)} %bitcast.32), channel_id=1, source_target_pairs={{0,1},{1,0},{2,3},{3,2},{4,5},{5,4},{6,7},{7,6},{8,9},{9,8},{10,11... | collective-permute-start | bytes 1572872 | tf_op jit(solution)/shard_map/ppermute | solution.py:39
  47.0 7.4 %collective-permute-start.5 = (bf16[1024,256]{1,0:T(8,128)(2,1)S(1)}, bf16[1024,256]{1,0:T(8,128)(2,1)}, u32[]{:S(2)}, u32[]{:S(2)}) collective-permute-start(bf16[1024,256]{1,0:T(8,128)(2,1)S(1)} %collective-permute-done.4.rest_2_), channel_id=1, source_target_pairs={{0,1},{1,0},{2,3},{3,2},{4,5},{5,4},{6,7},{7,6},{8,9},{9,8},{10,11... | collective-permute-start | bytes 1572872 | tf_op jit(solution)/shard_map/ppermute | solution.py:39
  52.9 2.0 %collective-permute-start.11 = (bf16[1024,256]{1,0:T(8,128)(2,1)S(1)}, bf16[1024,256]{1,0:T(8,128)(2,1)}, u32[]{:S(2)}, u32[]{:S(2)}) collective-permute-start(bf16[1024,256]{1,0:T(8,128)(2,1)S(1)} %collective-permute-done.10.rest_6_), channel_id=1, source_target_pairs={{0,1},{1,0},{2,3},{3,2},{4,5},{5,4},{6,7},{7,6},{8,9},{9,8},{10,11... | collective-permute-start | bytes 1572872 | tf_op jit(solution)/shard_map/ppermute | solution.py:39
  52.9 0.7 copy-start.2

commit v12 on v11

--- a/solution.py
+++ b/solution.py
@@ -180,7 +180,7 @@
     qb0 = jnp.stack([(p * n_ka + k) * n_local, k]).astype(jnp.int32)
 
     kernel = functools.partial(
-        attend_kernel, n_local=n_local, n_pieces=len(kv_pieces), n_ka=n_ka, group=16, scale=math.log2(math.e) / math.sqrt(HD)
+        attend_kernel, n_local=n_local, n_pieces=len(kv_pieces), n_ka=n_ka, group=32, scale=math.log2(math.e) / math.sqrt(HD)
     )
     return pl.pallas_call(
         kernel,

time: 73.3 us -> 74.9 us (1.022)
  Pallas kernels: 17.7 us -> 18.8 us
    pallas_call x1, Pallas kernels: 17.7 us -> 18.8 us  [shards(): pl.pallas_call(kernel, out_shape=jax.ShapeDtypeStruct((rows_mine, queries...]
where the time goes in v12:
time: 74.9 us; the launch traced here: 73.9 us
  waiting for transfers between devices  44.3 us (59%)
  Pallas kernels  18.8 us (25%)
  starting transfers between devices  7.63 us (10%)
  local copies, waits for them, and re-layouts  2.5 us (3%)
    ppermute x6, waiting for transfers between devices, gather_axis(): other = lax.ppermute(held, axis, [(i, i ^ b) for i in range(n)])  30.2 us
    pallas_call x1, Pallas kernels, shards(): pl.pallas_call(kernel, out_shape=jax.ShapeDtypeStruct((rows_mine, queries...  18.8 us
    ppermute x6, waiting for transfers between devices, pieces_axis(): lax.ppermute(idx_pieces[x], axis, [(i, i ^ b) for i in range(n)])  14.1 us
    ppermute x6, starting transfers between devices, gather_axis(): other = lax.ppermute(held, axis, [(i, i ^ b) for i in range(n)])  4.01 us
    ppermute x6, starting transfers between devices, pieces_axis(): lax.ppermute(idx_pieces[x], axis, [(i, i ^ b) for i in range(n)])  3.62 us
    unnamed x7, local copies, waits for them, and re-layouts  1.62 us
  transfers between devices with their start and end apart: 12, of which 9 were waited for; matrix products, arithmetic and copies ran while one was open for 1% of the time, Pallas kernels for 0%

profile of v12, /device:TPU:24, one launch (start us, length us, event | category | flops | bytes accessed | tf_op | source)
XLA Modules:
  0.0 73.9 jit_solution(13739650862120661000)
XLA Ops:
  0.0 0.0 copy-start
  0.0 0.0 copy-start.1
  0.0 0.9 %constant_dynamic-update-slice_fusion.1 = bf16[256,256]{1,0:T(8,128)(2,1)S(1)} fusion(bf16[256,128]{1,0:T(8,128)(2,1)} %param.6), kind=kLoop, calls=%fused_computation.16 | loop fusion | bytes 131072
  1.0 0.0 copy-done.1
  1.0 0.4 collective-permute-start
  1.4 5.7 %collective-permute-done = bf16[1,1,1,128,256]{4,3,2,1,0:T(8,128)(2,1)S(1)} collective-permute-done((bf16[1,1,1,128,256]{4,3,2,1,0:T(8,128)(2,1)S(1)}, bf16[1,1,1,128,256]{4,3,2,1,0:T(8,128)(2,1)S(1)}, u32[]{:S(2)}, u32[]{:S(2)}) %collective-permute-start) | collective-permute-done | bytes 65568 | tf_op jit(solution)/shard_map/ppermute | solution.py:24
  7.1 0.1 collective-permute-start.1
  7.3 5.0 %collective-permute-done.1 = bf16[2,1,1,128,256]{4,3,2,1,0:T(8,128)(2,1)S(1)} collective-permute-done((bf16[2,1,1,128,256]{4,3,2,1,0:T(8,128)(2,1)S(1)}, bf16[2,1,1,128,256]{4,3,2,1,0:T(8,128)(2,1)S(1)}, u32[]{:S(2)}, u32[]{:S(2)}) %collective-permute-start.1) | collective-permute-done | bytes 131104 | tf_op jit(solution)/shard_map/ppermute | solution.py:24
  12.3 0.1 maximum_select_fusion.2
  12.3 1.6 %collective-permute-start.2 = (bf16[2,2,1,128,256]{4,3,0,2,1:T(8,128)(2,1)S(1)}, bf16[2,2,1,128,256]{4,3,0,2,1:T(8,128)(2,1)S(1)}, u32[]{:S(2)}, u32[]{:S(2)}) collective-permute-start(bf16[2,2,1,128,256]{4,3,0,2,1:T(8,128)(2,1)S(1)} %maximum_select_fusion.2), channel_id=1, source_target_pairs={{0,4},{4,0},{8,12},{12,8},{16,20},{20,16},{24,28},{28,24},{1,5},{5... | collective-permute-start | bytes 786440 | tf_op jit(solution)/shard_map/ppermute | solution.py:24
  13.9 5.5 %collective-permute-done.2 = bf16[2,2,1,128,256]{4,3,0,2,1:T(8,128)(2,1)S(1)} collective-permute-done((bf16[2,2,1,128,256]{4,3,0,2,1:T(8,128)(2,1)S(1)}, bf16[2,2,1,128,256]{4,3,0,2,1:T(8,128)(2,1)S(1)}, u32[]{:S(2)}, u32[]{:S(2)}) %collective-permute-start.2) | collective-permute-done | bytes 262176 | tf_op jit(solution)/shard_map/ppermute | solution.py:24
  19.5 0.1 collective-permute-start.6
  19.6 6.0 %collective-permute-done.6 = bf16[1,1,1,128,256]{4,3,2,1,0:T(8,128)(2,1)S(1)} collective-permute-done((bf16[1,1,1,128,256]{4,3,2,1,0:T(8,128)(2,1)S(1)}, bf16[1,1,1,128,256]{4,3,2,1,0:T(8,128)(2,1)S(1)}, u32[]{:S(2)}, u32[]{:S(2)}) %collective-permute-start.6) | collective-permute-done | bytes 65568 | tf_op jit(solution)/shard_map/ppermute | solution.py:24
  25.6 0.4 collective-permute-start.7
  26.0 4.7 %collective-permute-done.7 = bf16[2,1,1,128,256]{4,3,0,2,1:T(8,128)(2,1)S(1)} collective-permute-done((bf16[2,1,1,128,256]{4,3,0,2,1:T(8,128)(2,1)S(1)}, bf16[2,1,1,128,256]{4,3,0,2,1:T(8,128)(2,1)S(1)}, u32[]{:S(2)}, u32[]{:S(2)}) %collective-permute-start.7) | collective-permute-done | bytes 131104 | tf_op jit(solution)/shard_map/ppermute | solution.py:24
  30.6 1.6 %collective-permute-start.8 = (bf16[2,2,1,128,256]{4,3,0,2,1:T(8,128)(2,1)S(1)}, bf16[2,2,1,128,256]{4,3,0,2,1:T(8,128)(2,1)S(1)}, u32[]{:S(2)}, u32[]{:S(2)}) collective-permute-start(bf16[2,2,1,128,256]{4,3,0,2,1:T(8,128)(2,1)S(1)} %maximum_select_fusion.3), channel_id=1, source_target_pairs={{0,4},{4,0},{8,12},{12,8},{16,20},{20,16},{24,28},{28,24},{1,5},{5... | collective-permute-start | bytes 786440 | tf_op jit(solution)/shard_map/ppermute | solution.py:24
  32.2 1.5 %collective-permute-start.4 = (bf16[1024,256]{1,0:T(8,128)(2,1)S(1)}, bf16[1024,256]{1,0:T(8,128)(2,1)S(1)}, u32[]{:S(2)}, u32[]{:S(2)}) collective-permute-start(bf16[1024,256]{1,0:T(8,128)(2,1)S(1)} %bitcast.28), channel_id=1, source_target_pairs={{0,2},{1,3},{2,0},{3,1},{4,6},{5,7},{6,4},{7,5},{8,10},{9,11},{10,... | collective-permute-start | bytes 1572872 | tf_op jit(solution)/shard_map/ppermute | solution.py:39
  33.7 3.4 %collective-permute-done.8 = bf16[2,2,1,128,256]{4,3,0,2,1:T(8,128)(2,1)S(1)} collective-permute-done((bf16[2,2,1,128,256]{4,3,0,2,1:T(8,128)(2,1)S(1)}, bf16[2,2,1,128,256]{4,3,0,2,1:T(8,128)(2,1)S(1)}, u32[]{:S(2)}, u32[]{:S(2)}) %collective-permute-start.8) | collective-permute-done | bytes 262176 | tf_op jit(solution)/shard_map/ppermute | solution.py:24
  37.2 1.6 %collective-permute-start.10 = (bf16[1024,256]{1,0:T(8,128)(2,1)S(1)}, bf16[1024,256]{1,0:T(8,128)(2,1)S(1)}, u32[]{:S(2)}, u32[]{:S(2)}) collective-permute-start(bf16[1024,256]{1,0:T(8,128)(2,1)S(1)} %bitcast.31), channel_id=1, source_target_pairs={{0,2},{1,3},{2,0},{3,1},{4,6},{5,7},{6,4},{7,5},{8,10},{9,11},{10,... | collective-permute-start | bytes 1572872 | tf_op jit(solution)/shard_map/ppermute | solution.py:39
  38.8 0.0 collective-permute-start.3
  38.8 0.5 collective-permute-start.9
  39.3 7.7 %collective-permute-done.4.rest_2_ = bf16[1024,256]{1,0:T(8,128)(2,1)S(1)} collective-permute-done((bf16[1024,256]{1,0:T(8,128)(2,1)S(1)}, bf16[1024,256]{1,0:T(8,128)(2,1)S(1)}, u32[]{:S(2)}, u32[]{:S(2)}) %collective-permute-start.4) | collective-permute-done | bytes 524320 | tf_op jit(solution)/shard_map/ppermute | solution.py:39
  47.0 0.0 collective-permute-start.5
  47.0 5.9 %collective-permute-done.10.rest_6_ = bf16[1024,256]{1,0:T(8,128)(2,1)S(1)} collective-permute-done((bf16[1024,256]{1,0:T(8,128)(2,1)S(1)}, bf16[1024,256]{1,0:T(8,128)(2,1)S(1)}, u32[]{:S(2)}, u32[]{:S(2)}) %collective-permute-start.10) | collective-permute-done | bytes 524320 | tf_op jit(solution)/shard_map/ppermute | solution.py:39
  52.9 0.0 collective-permute-start.11
  52.9 0.0 copy-start.2
  52.9 0.7 copy-done.2
  53.6 0.1 dynamic_slice.10.cnt_ref
  53.6 0.1 pad_add_fusion.qb_ref
  53.7 0.7 constant_dynamic-slice_fusion.1.bl_ref
  54.4 0.0 copy-done
  54.4 0.0 collective-permute-done.3.rest_1_
  54.4 0.0 collective-permute-done.9.rest_5_
  54.4 0.0 collective-permute-done.5.rest_3_
  54.5 0.5 collective-permute-done.11.rest_7_
  54.9 18.8 %shard_map.55 = bf16[256,512]{1,0:T(8,128)(2,1)} custom-call(s32[2,32]{1,0:T(2,128)S(1)} %constant_dynamic-slice_fusion.1.bl_ref, s32[2]{0:T(128)S(1)} %dynamic_slice.10.cnt_ref, s32[2]{0:T(128)S(1)} %pad_add_fusion.qb_ref, bf16[256,512]{1,0:T(8,128)(2,1)S(1)} %constant_dynamic-slice_fusion.q_ref, bf16[1024,256]{1,0:T(8,128)(2,1)S(1)} %bitcast.30, ...), custom_call_target="tpu_custom_call" | custom-call | tf_op jit(solution)/shard_map/pallas_call | solution.py:185
  (12 shorter events, 0.3 us)
Async XLA Ops:
  0.0 54.4 %copy-start = (bf16[1024,512]{1,0:T(8,128)(2,1)S(1)}, bf16[1024,512]{1,0:T(8,128)(2,1)}, u32[]{:S(2)}) copy-start(bf16[1024,512]{1,0:T(8,128)(2,1)} %param.5) | copy-start | bytes 3145732
  0.0 1.0 %copy-start.1 = (bf16[256,128]{1,0:T(8,128)(2,1)S(1)}, bf16[256,128]{1,0:T(8,128)(2,1)}, u32[]{:S(2)}) copy-start(bf16[256,128]{1,0:T(8,128)(2,1)} %param.7) | copy-start | bytes 196612
  1.0 6.1 %collective-permute-start = (bf16[1,1,1,128,256]{4,3,2,1,0:T(8,128)(2,1)S(1)}, bf16[1,1,1,128,256]{4,3,2,1,0:T(8,128)(2,1)S(1)}, u32[]{:S(2)}, u32[]{:S(2)}) collective-permute-start(bf16[1,1,1,128,256]{4,3,2,1,0:T(8,128)(2,1)S(1)} %get-tuple-element.12), channel_id=1, source_target_pairs={{0,16},{4,20},{8,24},{12,28},{16,0},{20,4},{24,8},{28,12},{1,17},{... | collective-permute-start | bytes 196616 | tf_op jit(solution)/shard_map/ppermute | solution.py:24
  7.1 5.1 %collective-permute-start.1 = (bf16[2,1,1,128,256]{4,3,2,1,0:T(8,128)(2,1)S(1)}, bf16[2,1,1,128,256]{4,3,2,1,0:T(8,128)(2,1)S(1)}, u32[]{:S(2)}, u32[]{:S(2)}) collective-permute-start(bf16[2,1,1,128,256]{4,3,2,1,0:T(8,128)(2,1)S(1)} %maximum_select_fusion.4), channel_id=1, source_target_pairs={{0,8},{4,12},{8,0},{12,4},{16,24},{20,28},{24,16},{28,20},{1,9},{5... | collective-permute-start | bytes 393224 | tf_op jit(solution)/shard_map/ppermute | solution.py:24
  12.3 7.1 %collective-permute-start.2 = (bf16[2,2,1,128,256]{4,3,0,2,1:T(8,128)(2,1)S(1)}, bf16[2,2,1,128,256]{4,3,0,2,1:T(8,128)(2,1)S(1)}, u32[]{:S(2)}, u32[]{:S(2)}) collective-permute-start(bf16[2,2,1,128,256]{4,3,0,2,1:T(8,128)(2,1)S(1)} %maximum_select_fusion.2), channel_id=1, source_target_pairs={{0,4},{4,0},{8,12},{12,8},{16,20},{20,16},{24,28},{28,24},{1,5},{5... | collective-permute-start | bytes 786440 | tf_op jit(solution)/shard_map/ppermute | solution.py:24
  19.5 6.0 %collective-permute-start.6 = (bf16[1,1,1,128,256]{4,3,2,1,0:T(8,128)(2,1)S(1)}, bf16[1,1,1,128,256]{4,3,2,1,0:T(8,128)(2,1)S(1)}, u32[]{:S(2)}, u32[]{:S(2)}) collective-permute-start(bf16[1,1,1,128,256]{4,3,2,1,0:T(8,128)(2,1)S(1)} %bitcast.34), channel_id=1, source_target_pairs={{0,16},{4,20},{8,24},{12,28},{16,0},{20,4},{24,8},{28,12},{1,17},{... | collective-permute-start | bytes 196616 | tf_op jit(solution)/shard_map/ppermute | solution.py:24
  25.6 5.0 %collective-permute-start.7 = (bf16[2,1,1,128,256]{4,3,0,2,1:T(8,128)(2,1)S(1)}, bf16[2,1,1,128,256]{4,3,0,2,1:T(8,128)(2,1)S(1)}, u32[]{:S(2)}, u32[]{:S(2)}) collective-permute-start(bf16[2,1,1,128,256]{4,3,0,2,1:T(8,128)(2,1)S(1)} %fusion), channel_id=1, source_target_pairs={{0,8},{4,12},{8,0},{12,4},{16,24},{20,28},{24,16},{28,20},{1,9},{5... | collective-permute-start | bytes 393224 | tf_op jit(solution)/shard_map/ppermute | solution.py:24
  30.6 6.4 %collective-permute-start.8 = (bf16[2,2,1,128,256]{4,3,0,2,1:T(8,128)(2,1)S(1)}, bf16[2,2,1,128,256]{4,3,0,2,1:T(8,128)(2,1)S(1)}, u32[]{:S(2)}, u32[]{:S(2)}) collective-permute-start(bf16[2,2,1,128,256]{4,3,0,2,1:T(8,128)(2,1)S(1)} %maximum_select_fusion.3), channel_id=1, source_target_pairs={{0,4},{4,0},{8,12},{12,8},{16,20},{20,16},{24,28},{28,24},{1,5},{5... | collective-permute-start | bytes 786440 | tf_op jit(solution)/shard_map/ppermute | solution.py:24
  32.2 14.8 %collective-permute-start.4 = (bf16[1024,256]{1,0:T(8,128)(2,1)S(1)}, bf16[1024,256]{1,0:T(8,128)(2,1)S(1)}, u32[]{:S(2)}, u32[]{:S(2)}) collective-permute-start(bf16[1024,256]{1,0:T(8,128)(2,1)S(1)} %bitcast.28), channel_id=1, source_target_pairs={{0,2},{1,3},{2,0},{3,1},{4,6},{5,7},{6,4},{7,5},{8,10},{9,11},{10,... | collective-permute-start | bytes 1572872 | tf_op jit(solution)/shard_map/ppermute | solution.py:39
  37.2 15.7 %collective-permute-start.10 = (bf16[1024,256]{1,0:T(8,128)(2,1)S(1)}, bf16[1024,256]{1,0:T(8,128)(2,1)S(1)}, u32[]{:S(2)}, u32[]{:S(2)}) collective-permute-start(bf16[1024,256]{1,0:T(8,128)(2,1)S(1)} %bitcast.31), channel_id=1, source_target_pairs={{0,2},{1,3},{2,0},{3,1},{4,6},{5,7},{6,4},{7,5},{8,10},{9,11},{10,... | collective-permute-start | bytes 1572872 | tf_op jit(solution)/shard_map/ppermute | solution.py:39
  38.8 15.7 %collective-permute-start.3 = (bf16[1024,256]{1,0:T(8,128)(2,1)S(1)}, bf16[1024,256]{1,0:T(8,128)(2,1)}, u32[]{:S(2)}, u32[]{:S(2)}) collective-permute-start(bf16[1024,256]{1,0:T(8,128)(2,1)S(1)} %bitcast.29), channel_id=1, source_target_pairs={{0,1},{1,0},{2,3},{3,2},{4,5},{5,4},{6,7},{7,6},{8,9},{9,8},{10,11... | collective-permute-start | bytes 1572872 | tf_op jit(solution)/shard_map/ppermute | solution.py:39
  38.8 15.7 %collective-permute-start.9 = (bf16[1024,256]{1,0:T(8,128)(2,1)S(1)}, bf16[1024,256]{1,0:T(8,128)(2,1)}, u32[]{:S(2)}, u32[]{:S(2)}) collective-permute-start(bf16[1024,256]{1,0:T(8,128)(2,1)S(1)} %bitcast.32), channel_id=1, source_target_pairs={{0,1},{1,0},{2,3},{3,2},{4,5},{5,4},{6,7},{7,6},{8,9},{9,8},{10,11... | collective-permute-start | bytes 1572872 | tf_op jit(solution)/shard_map/ppermute | solution.py:39
  47.0 7.4 %collective-permute-start.5 = (bf16[1024,256]{1,0:T(8,128)(2,1)S(1)}, bf16[1024,256]{1,0:T(8,128)(2,1)}, u32[]{:S(2)}, u32[]{:S(2)}) collective-permute-start(bf16[1024,256]{1,0:T(8,128)(2,1)S(1)} %collective-permute-done.4.rest_2_), channel_id=1, source_target_pairs={{0,1},{1,0},{2,3},{3,2},{4,5},{5,4},{6,7},{7,6},{8,9},{9,8},{10,11... | collective-permute-start | bytes 1572872 | tf_op jit(solution)/shard_map/ppermute | solution.py:39
  52.9 2.0 %collective-permute-start.11 = (bf16[1024,256]{1,0:T(8,128)(2,1)S(1)}, bf16[1024,256]{1,0:T(8,128)(2,1)}, u32[]{:S(2)}, u32[]{:S(2)}) collective-permute-start(bf16[1024,256]{1,0:T(8,128)(2,1)S(1)} %collective-permute-done.10.rest_6_), channel_id=1, source_target_pairs={{0,1},{1,0},{2,3},{3,2},{4,5},{5,4},{6,7},{7,6},{8,9},{9,8},{10,11... | collective-permute-start | bytes 1572872 | tf_op jit(solution)/shard_map/ppermute | solution.py:39
  52.9 0.7 copy-start.2

commit v13 on v11

--- a/solution.py
+++ b/solution.py
@@ -46,6 +46,7 @@
     out_ref, off_ref, kvbuf, dbuf, sems, dsems = rest[n_pieces:]
     qb0 = qb_ref[0]
     me = qb_ref[1]
+    row0 = me * n_local
     width = kvbuf.shape[-1]
     per_piece = kv_pieces[0].shape[0] // BLK
     n_half = n_pieces // n_ka
@@ -78,11 +79,11 @@
         block_copy(qb, dbuf.at[j], dsems.at[j]).start()
 
         def compact(s, n, j=j, qb=qb):
-            b = bl_ref[j, s]
+            b = bl_ref[row0 + j, s]
             off_ref[j, n] = b
             return n + (b != qb).astype(jnp.int32)
 
-        n_j = lax.fori_loop(0, cnt_ref[j], compact, 0)
+        n_j = lax.fori_loop(0, cnt_ref[row0 + j], compact, 0)
         n_off.append(n_j)
         n_pad = (n_j + group - 1) // group * group
 
@@ -174,9 +175,6 @@
     rows_mine = queries.shape[0] // n_ka
     n_local = rows_mine // BLK
     listed = block_list.shape[1]
-    q_mine = lax.dynamic_slice_in_dim(queries, k * rows_mine, rows_mine, 0)
-    bl_mine = lax.dynamic_slice_in_dim(block_list, k * n_local, n_local, 0)
-    cnt_mine = lax.dynamic_slice_in_dim(block_count, k * n_local, n_local, 0)
     qb0 = jnp.stack([(p * n_ka + k) * n_local, k]).astype(jnp.int32)
 
     kernel = functools.partial(
@@ -189,7 +187,7 @@
             num_scalar_prefetch=3,
             grid=(1,),
             in_specs=[
-                pl.BlockSpec((rows_mine, queries.shape[1]), lambda i, *_: (0, 0)),
+                pl.BlockSpec((rows_mine, queries.shape[1]), lambda i, bl, cnt, qb: (qb[1], 0)),
             ]
             + [pl.BlockSpec(memory_space=pl.ANY)] * len(kv_pieces),
             out_specs=pl.BlockSpec((rows_mine, queries.shape[1]), lambda i, *_: (0, 0)),
@@ -202,7 +200,7 @@
             ],
         ),
         compiler_params=pltpu.CompilerParams(vmem_limit_bytes=48 * 1024 * 1024),
-    )(bl_mine, cnt_mine, qb0, q_mine, *kv_pieces)
+    )(block_list, block_count, qb0, queries, *kv_pieces)
 
 
 def solution(mesh):

time: 73.3 us -> 73 us (level)
  waiting for transfers between devices: 44.3 us -> 45.8 us
  local copies, waits for them, and re-layouts: 2.5 us -> 1.01 us
    ppermute x6, waiting for transfers between devices: 14.1 us -> 15.6 us  [pieces_axis(): lax.ppermute(idx_pieces[x], axis, [(i, i ^ b) for i in range(n)])]
    dynamic_slice x3 -> x0, local copies, waits for them, and re-layouts: 0.78 us -> none  [the longest x1 0.69 us: shards(): bl_mine = lax.dynamic_slice_in_dim(block_list, k * n_local, n_local, 0)]
    unnamed x7 -> x9, local copies, waits for them, and re-layouts: 1.62 us -> 0.9 us
  transfers between devices with their start and end apart: 12 -> 12, of which waited for: 9 -> 9; matrix products, arithmetic and copies ran while one was open for 1% -> 0% of each run, Pallas kernels for 0% -> 0%
where the time goes in v13:
time: 73 us; the launch traced here: 72.6 us
  waiting for transfers between devices  45.8 us (63%)
  Pallas kernels  17.7 us (24%)
  starting transfers between devices  7.63 us (10%)
  local copies, waits for them, and re-layouts  1.01 us (1%)
    ppermute x6, waiting for transfers between devices, gather_axis(): other = lax.ppermute(held, axis, [(i, i ^ b) for i in range(n)])  30.2 us
    pallas_call x1, Pallas kernels, shards(): pl.pallas_call(kernel, out_shape=jax.ShapeDtypeStruct((rows_mine, queries...  17.7 us
    ppermute x6, waiting for transfers between devices, pieces_axis(): lax.ppermute(idx_pieces[x], axis, [(i, i ^ b) for i in range(n)])  15.6 us
    ppermute x6, starting transfers between devices, gather_axis(): other = lax.ppermute(held, axis, [(i, i ^ b) for i in range(n)])  4.01 us
    ppermute x6, starting transfers between devices, pieces_axis(): lax.ppermute(idx_pieces[x], axis, [(i, i ^ b) for i in range(n)])  3.62 us
  transfers between devices with their start and end apart: 12, of which 9 were waited for; matrix products, arithmetic and copies ran while one was open for 0% of the time, Pallas kernels for 0%

profile of v13, /device:TPU:24, one launch (start us, length us, event | category | flops | bytes accessed | tf_op | source)
XLA Modules:
  0.0 72.6 jit_solution(4999642114600895159)
XLA Ops:
  0.0 0.0 copy-start.3
  0.0 0.9 %constant_dynamic-update-slice_fusion.1 = bf16[256,256]{1,0:T(8,128)(2,1)S(1)} fusion(bf16[256,128]{1,0:T(8,128)(2,1)} %param.6), kind=kLoop, calls=%fused_computation.16 | loop fusion | bytes 131072
  0.9 0.0 copy-done.3
  0.9 0.4 collective-permute-start
  1.3 5.7 %collective-permute-done = bf16[1,1,1,128,256]{4,3,2,1,0:T(8,128)(2,1)S(1)} collective-permute-done((bf16[1,1,1,128,256]{4,3,2,1,0:T(8,128)(2,1)S(1)}, bf16[1,1,1,128,256]{4,3,2,1,0:T(8,128)(2,1)S(1)}, u32[]{:S(2)}, u32[]{:S(2)}) %collective-permute-start) | collective-permute-done | bytes 65568 | tf_op jit(solution)/shard_map/ppermute | solution.py:24
  7.1 0.1 collective-permute-start.1
  7.2 5.0 %collective-permute-done.1 = bf16[2,1,1,128,256]{4,3,2,1,0:T(8,128)(2,1)S(1)} collective-permute-done((bf16[2,1,1,128,256]{4,3,2,1,0:T(8,128)(2,1)S(1)}, bf16[2,1,1,128,256]{4,3,2,1,0:T(8,128)(2,1)S(1)}, u32[]{:S(2)}, u32[]{:S(2)}) %collective-permute-start.1) | collective-permute-done | bytes 131104 | tf_op jit(solution)/shard_map/ppermute | solution.py:24
  12.2 0.1 maximum_select_fusion.2
  12.3 1.6 %collective-permute-start.2 = (bf16[2,2,1,128,256]{4,3,0,2,1:T(8,128)(2,1)S(1)}, bf16[2,2,1,128,256]{4,3,0,2,1:T(8,128)(2,1)S(1)}, u32[]{:S(2)}, u32[]{:S(2)}) collective-permute-start(bf16[2,2,1,128,256]{4,3,0,2,1:T(8,128)(2,1)S(1)} %maximum_select_fusion.2), channel_id=1, source_target_pairs={{0,4},{4,0},{8,12},{12,8},{16,20},{20,16},{24,28},{28,24},{1,5},{5... | collective-permute-start | bytes 786440 | tf_op jit(solution)/shard_map/ppermute | solution.py:24
  13.8 5.5 %collective-permute-done.2 = bf16[2,2,1,128,256]{4,3,0,2,1:T(8,128)(2,1)S(1)} collective-permute-done((bf16[2,2,1,128,256]{4,3,0,2,1:T(8,128)(2,1)S(1)}, bf16[2,2,1,128,256]{4,3,0,2,1:T(8,128)(2,1)S(1)}, u32[]{:S(2)}, u32[]{:S(2)}) %collective-permute-start.2) | collective-permute-done | bytes 262176 | tf_op jit(solution)/shard_map/ppermute | solution.py:24
  19.5 0.1 collective-permute-start.6
  19.5 6.0 %collective-permute-done.6 = bf16[1,1,1,128,256]{4,3,2,1,0:T(8,128)(2,1)S(1)} collective-permute-done((bf16[1,1,1,128,256]{4,3,2,1,0:T(8,128)(2,1)S(1)}, bf16[1,1,1,128,256]{4,3,2,1,0:T(8,128)(2,1)S(1)}, u32[]{:S(2)}, u32[]{:S(2)}) %collective-permute-start.6) | collective-permute-done | bytes 65568 | tf_op jit(solution)/shard_map/ppermute | solution.py:24
  25.5 0.4 collective-permute-start.7
  25.9 4.7 %collective-permute-done.7 = bf16[2,1,1,128,256]{4,3,0,2,1:T(8,128)(2,1)S(1)} collective-permute-done((bf16[2,1,1,128,256]{4,3,0,2,1:T(8,128)(2,1)S(1)}, bf16[2,1,1,128,256]{4,3,0,2,1:T(8,128)(2,1)S(1)}, u32[]{:S(2)}, u32[]{:S(2)}) %collective-permute-start.7) | collective-permute-done | bytes 131104 | tf_op jit(solution)/shard_map/ppermute | solution.py:24
  30.6 0.0 copy-start
  30.6 1.6 %collective-permute-start.8 = (bf16[2,2,1,128,256]{4,3,0,2,1:T(8,128)(2,1)S(1)}, bf16[2,2,1,128,256]{4,3,0,2,1:T(8,128)(2,1)S(1)}, u32[]{:S(2)}, u32[]{:S(2)}) collective-permute-start(bf16[2,2,1,128,256]{4,3,0,2,1:T(8,128)(2,1)S(1)} %maximum_select_fusion.3), channel_id=1, source_target_pairs={{0,4},{4,0},{8,12},{12,8},{16,20},{20,16},{24,28},{28,24},{1,5},{5... | collective-permute-start | bytes 786440 | tf_op jit(solution)/shard_map/ppermute | solution.py:24
  32.1 1.5 %collective-permute-start.4 = (bf16[1024,256]{1,0:T(8,128)(2,1)S(1)}, bf16[1024,256]{1,0:T(8,128)(2,1)S(1)}, u32[]{:S(2)}, u32[]{:S(2)}) collective-permute-start(bf16[1024,256]{1,0:T(8,128)(2,1)S(1)} %bitcast.28), channel_id=1, source_target_pairs={{0,2},{1,3},{2,0},{3,1},{4,6},{5,7},{6,4},{7,5},{8,10},{9,11},{10,... | collective-permute-start | bytes 1572872 | tf_op jit(solution)/shard_map/ppermute | solution.py:39
  33.7 3.4 %collective-permute-done.8 = bf16[2,2,1,128,256]{4,3,0,2,1:T(8,128)(2,1)S(1)} collective-permute-done((bf16[2,2,1,128,256]{4,3,0,2,1:T(8,128)(2,1)S(1)}, bf16[2,2,1,128,256]{4,3,0,2,1:T(8,128)(2,1)S(1)}, u32[]{:S(2)}, u32[]{:S(2)}) %collective-permute-start.8) | collective-permute-done | bytes 262176 | tf_op jit(solution)/shard_map/ppermute | solution.py:24
  37.1 1.6 %collective-permute-start.10 = (bf16[1024,256]{1,0:T(8,128)(2,1)S(1)}, bf16[1024,256]{1,0:T(8,128)(2,1)S(1)}, u32[]{:S(2)}, u32[]{:S(2)}) collective-permute-start(bf16[1024,256]{1,0:T(8,128)(2,1)S(1)} %bitcast.31), channel_id=1, source_target_pairs={{0,2},{1,3},{2,0},{3,1},{4,6},{5,7},{6,4},{7,5},{8,10},{9,11},{10,... | collective-permute-start | bytes 1572872 | tf_op jit(solution)/shard_map/ppermute | solution.py:39
  38.7 0.0 collective-permute-start.3
  38.7 0.5 collective-permute-start.9
  39.2 7.7 %collective-permute-done.4.rest_2_ = bf16[1024,256]{1,0:T(8,128)(2,1)S(1)} collective-permute-done((bf16[1024,256]{1,0:T(8,128)(2,1)S(1)}, bf16[1024,256]{1,0:T(8,128)(2,1)S(1)}, u32[]{:S(2)}, u32[]{:S(2)}) %collective-permute-start.4) | collective-permute-done | bytes 524320 | tf_op jit(solution)/shard_map/ppermute | solution.py:39
  46.9 0.0 collective-permute-start.5
  47.0 5.9 %collective-permute-done.10.rest_6_ = bf16[1024,256]{1,0:T(8,128)(2,1)S(1)} collective-permute-done((bf16[1024,256]{1,0:T(8,128)(2,1)S(1)}, bf16[1024,256]{1,0:T(8,128)(2,1)S(1)}, u32[]{:S(2)}, u32[]{:S(2)}) %collective-permute-start.10) | collective-permute-done | bytes 524320 | tf_op jit(solution)/shard_map/ppermute | solution.py:39
  52.8 0.0 collective-permute-start.11
  52.8 0.0 copy-start.1
  52.9 0.0 copy-start.2
  52.9 0.1 pad_add_fusion.qb_ref
  52.9 0.0 collective-permute-done.3.rest_1_
  52.9 0.0 collective-permute-done.9.rest_5_
  52.9 0.0 collective-permute-done.5.rest_3_
  52.9 1.9 %collective-permute-done.11.rest_7_ = bf16[1024,256]{1,0:T(8,128)(2,1)} collective-permute-done((bf16[1024,256]{1,0:T(8,128)(2,1)S(1)}, bf16[1024,256]{1,0:T(8,128)(2,1)}, u32[]{:S(2)}, u32[]{:S(2)}) %collective-permute-start.11) | collective-permute-done | bytes 524320 | tf_op jit(solution)/shard_map/ppermute | solution.py:39
  54.9 0.0 copy-done
  54.9 0.0 copy-done.1
  54.9 0.0 copy-done.2
  54.9 17.7 %shard_map.55 = bf16[256,512]{1,0:T(8,128)(2,1)} custom-call(s32[8,32]{1,0:T(8,128)S(1)} %copy-done.1, s32[8]{0:T(128)S(1)} %copy-done.2, s32[2]{0:T(128)S(1)} %pad_add_fusion.qb_ref, bf16[1024,512]{1,0:T(8,128)(2,1)S(1)} %copy-done, bf16[1024,256]{1,0:T(8,128)(2,1)S(1)} %bitcast.30, bf16[1024,256]{1,0:T(8,128)(2,1)} %collective-permute-done.3.rest_1_, ...), custom_call_target="tpu_custom_call" | custom-call | tf_op jit(solution)/shard_map/pallas_call | solution.py:183
  (11 shorter events, 0.3 us)
Async XLA Ops:
  0.0 0.9 %copy-start.3 = (bf16[256,128]{1,0:T(8,128)(2,1)S(1)}, bf16[256,128]{1,0:T(8,128)(2,1)}, u32[]{:S(2)}) copy-start(bf16[256,128]{1,0:T(8,128)(2,1)} %param.7) | copy-start | bytes 196612
  0.9 6.1 %collective-permute-start = (bf16[1,1,1,128,256]{4,3,2,1,0:T(8,128)(2,1)S(1)}, bf16[1,1,1,128,256]{4,3,2,1,0:T(8,128)(2,1)S(1)}, u32[]{:S(2)}, u32[]{:S(2)}) collective-permute-start(bf16[1,1,1,128,256]{4,3,2,1,0:T(8,128)(2,1)S(1)} %get-tuple-element.12), channel_id=1, source_target_pairs={{0,16},{4,20},{8,24},{12,28},{16,0},{20,4},{24,8},{28,12},{1,17},{... | collective-permute-start | bytes 196616 | tf_op jit(solution)/shard_map/ppermute | solution.py:24
  7.1 5.1 %collective-permute-start.1 = (bf16[2,1,1,128,256]{4,3,2,1,0:T(8,128)(2,1)S(1)}, bf16[2,1,1,128,256]{4,3,2,1,0:T(8,128)(2,1)S(1)}, u32[]{:S(2)}, u32[]{:S(2)}) collective-permute-start(bf16[2,1,1,128,256]{4,3,2,1,0:T(8,128)(2,1)S(1)} %maximum_select_fusion.4), channel_id=1, source_target_pairs={{0,8},{4,12},{8,0},{12,4},{16,24},{20,28},{24,16},{28,20},{1,9},{5... | collective-permute-start | bytes 393224 | tf_op jit(solution)/shard_map/ppermute | solution.py:24
  12.3 7.1 %collective-permute-start.2 = (bf16[2,2,1,128,256]{4,3,0,2,1:T(8,128)(2,1)S(1)}, bf16[2,2,1,128,256]{4,3,0,2,1:T(8,128)(2,1)S(1)}, u32[]{:S(2)}, u32[]{:S(2)}) collective-permute-start(bf16[2,2,1,128,256]{4,3,0,2,1:T(8,128)(2,1)S(1)} %maximum_select_fusion.2), channel_id=1, source_target_pairs={{0,4},{4,0},{8,12},{12,8},{16,20},{20,16},{24,28},{28,24},{1,5},{5... | collective-permute-start | bytes 786440 | tf_op jit(solution)/shard_map/ppermute | solution.py:24
  19.5 6.0 %collective-permute-start.6 = (bf16[1,1,1,128,256]{4,3,2,1,0:T(8,128)(2,1)S(1)}, bf16[1,1,1,128,256]{4,3,2,1,0:T(8,128)(2,1)S(1)}, u32[]{:S(2)}, u32[]{:S(2)}) collective-permute-start(bf16[1,1,1,128,256]{4,3,2,1,0:T(8,128)(2,1)S(1)} %bitcast.34), channel_id=1, source_target_pairs={{0,16},{4,20},{8,24},{12,28},{16,0},{20,4},{24,8},{28,12},{1,17},{... | collective-permute-start | bytes 196616 | tf_op jit(solution)/shard_map/ppermute | solution.py:24
  25.5 5.0 %collective-permute-start.7 = (bf16[2,1,1,128,256]{4,3,0,2,1:T(8,128)(2,1)S(1)}, bf16[2,1,1,128,256]{4,3,0,2,1:T(8,128)(2,1)S(1)}, u32[]{:S(2)}, u32[]{:S(2)}) collective-permute-start(bf16[2,1,1,128,256]{4,3,0,2,1:T(8,128)(2,1)S(1)} %fusion), channel_id=1, source_target_pairs={{0,8},{4,12},{8,0},{12,4},{16,24},{20,28},{24,16},{28,20},{1,9},{5... | collective-permute-start | bytes 393224 | tf_op jit(solution)/shard_map/ppermute | solution.py:24
  30.6 24.3 %copy-start = (bf16[1024,512]{1,0:T(8,128)(2,1)S(1)}, bf16[1024,512]{1,0:T(8,128)(2,1)}, u32[]{:S(2)}) copy-start(bf16[1024,512]{1,0:T(8,128)(2,1)} %q_ref.1) | copy-start | bytes 3145732
  30.6 6.4 %collective-permute-start.8 = (bf16[2,2,1,128,256]{4,3,0,2,1:T(8,128)(2,1)S(1)}, bf16[2,2,1,128,256]{4,3,0,2,1:T(8,128)(2,1)S(1)}, u32[]{:S(2)}, u32[]{:S(2)}) collective-permute-start(bf16[2,2,1,128,256]{4,3,0,2,1:T(8,128)(2,1)S(1)} %maximum_select_fusion.3), channel_id=1, source_target_pairs={{0,4},{4,0},{8,12},{12,8},{16,20},{20,16},{24,28},{28,24},{1,5},{5... | collective-permute-start | bytes 786440 | tf_op jit(solution)/shard_map/ppermute | solution.py:24
  32.1 14.8 %collective-permute-start.4 = (bf16[1024,256]{1,0:T(8,128)(2,1)S(1)}, bf16[1024,256]{1,0:T(8,128)(2,1)S(1)}, u32[]{:S(2)}, u32[]{:S(2)}) collective-permute-start(bf16[1024,256]{1,0:T(8,128)(2,1)S(1)} %bitcast.28), channel_id=1, source_target_pairs={{0,2},{1,3},{2,0},{3,1},{4,6},{5,7},{6,4},{7,5},{8,10},{9,11},{10,... | collective-permute-start | bytes 1572872 | tf_op jit(solution)/shard_map/ppermute | solution.py:39
  37.1 15.7 %collective-permute-start.10 = (bf16[1024,256]{1,0:T(8,128)(2,1)S(1)}, bf16[1024,256]{1,0:T(8,128)(2,1)S(1)}, u32[]{:S(2)}, u32[]{:S(2)}) collective-permute-start(bf16[1024,256]{1,0:T(8,128)(2,1)S(1)} %bitcast.31), channel_id=1, source_target_pairs={{0,2},{1,3},{2,0},{3,1},{4,6},{5,7},{6,4},{7,5},{8,10},{9,11},{10,... | collective-permute-start | bytes 1572872 | tf_op jit(solution)/shard_map/ppermute | solution.py:39
  38.7 14.2 %collective-permute-start.3 = (bf16[1024,256]{1,0:T(8,128)(2,1)S(1)}, bf16[1024,256]{1,0:T(8,128)(2,1)}, u32[]{:S(2)}, u32[]{:S(2)}) collective-permute-start(bf16[1024,256]{1,0:T(8,128)(2,1)S(1)} %bitcast.29), channel_id=1, source_target_pairs={{0,1},{1,0},{2,3},{3,2},{4,5},{5,4},{6,7},{7,6},{8,9},{9,8},{10,11... | collective-permute-start | bytes 1572872 | tf_op jit(solution)/shard_map/ppermute | solution.py:39
  38.7 14.2 %collective-permute-start.9 = (bf16[1024,256]{1,0:T(8,128)(2,1)S(1)}, bf16[1024,256]{1,0:T(8,128)(2,1)}, u32[]{:S(2)}, u32[]{:S(2)}) collective-permute-start(bf16[1024,256]{1,0:T(8,128)(2,1)S(1)} %bitcast.32), channel_id=1, source_target_pairs={{0,1},{1,0},{2,3},{3,2},{4,5},{5,4},{6,7},{7,6},{8,9},{9,8},{10,11... | collective-permute-start | bytes 1572872 | tf_op jit(solution)/shard_map/ppermute | solution.py:39
  46.9 6.0 %collective-permute-start.5 = (bf16[1024,256]{1,0:T(8,128)(2,1)S(1)}, bf16[1024,256]{1,0:T(8,128)(2,1)}, u32[]{:S(2)}, u32[]{:S(2)}) collective-permute-start(bf16[1024,256]{1,0:T(8,128)(2,1)S(1)} %collective-permute-done.4.rest_2_), channel_id=1, source_target_pairs={{0,1},{1,0},{2,3},{3,2},{4,5},{5,4},{6,7},{7,6},{8,9},{9,8},{10,11... | collective-permute-start | bytes 1572872 | tf_op jit(solution)/shard_map/ppermute | solution.py:39
  52.8 2.0 %collective-permute-start.11 = (bf16[1024,256]{1,0:T(8,128)(2,1)S(1)}, bf16[1024,256]{1,0:T(8,128)(2,1)}, u32[]{:S(2)}, u32[]{:S(2)}) collective-permute-start(bf16[1024,256]{1,0:T(8,128)(2,1)S(1)} %collective-permute-done.10.rest_6_), channel_id=1, source_target_pairs={{0,1},{1,0},{2,3},{3,2},{4,5},{5,4},{6,7},{7,6},{8,9},{9,8},{10,11... | collective-permute-start | bytes 1572872 | tf_op jit(solution)/shard_map/ppermute | solution.py:39
  52.8 2.0 %copy-start.1 = (s32[8,32]{1,0:T(8,128)S(1)}, s32[8,32]{1,0:T(8,128)}, u32[]{:S(2)}) copy-start(s32[8,32]{1,0:T(8,128)} %bl_ref.1) | copy-start | bytes 3076
  52.9 2.0 %copy-start.2 = (s32[8]{0:T(128)S(1)}, s32[8]{0:T(128)}, u32[]{:S(2)}) copy-start(s32[8]{0:T(128)} %cnt_ref.1) | copy-start | bytes 100

commit v14 on v13

--- a/solution.py
+++ b/solution.py
@@ -41,32 +41,46 @@
     return [idx_pieces[x] for x in range(n)]
 
 
-def attend_kernel(bl_ref, cnt_ref, qb_ref, q_ref, *rest, n_local, n_pieces, n_ka, group, scale):
-    kv_pieces = rest[:n_pieces]
-    out_ref, off_ref, kvbuf, dbuf, sems, dsems = rest[n_pieces:]
+def attend_kernel(bl_ref, cnt_ref, qb_ref, q_ref, *rest, n_local, n_pieces, n_ka, group, scale, phase):
+    n_refs = n_pieces - 1 if phase == 0 else 1
+    kv_refs = rest[:n_refs]
+    if phase == 0:
+        m_io, l_io, acc_io, off_ref, kvbuf, dbuf, sems, dsems = rest[n_refs:]
+    else:
+        m_io, l_io, acc_io, out_ref, off_ref, kvbuf, dbuf, sems, dsems = rest[n_refs:]
     qb0 = qb_ref[0]
     me = qb_ref[1]
     row0 = me * n_local
     width = kvbuf.shape[-1]
-    per_piece = kv_pieces[0].shape[0] // BLK
+    per_piece = kv_refs[0].shape[0] // BLK
     n_half = n_pieces // n_ka
+    per_shard = per_piece * n_half
+    final = n_pieces - 1
+
+    def piece_of(blk):
+        within = blk % per_shard
+        return (within % n_half) * n_ka + jnp.bitwise_xor(blk // per_shard, me)
+
+    def mine(blk):
+        return piece_of(blk) != final if phase == 0 else piece_of(blk) == final
 
     class block_copy:
         def __init__(self, blk, dst, sem):
             self.blk, self.dst, self.sem = blk, dst, sem
 
         def start(self):
-            per_shard = per_piece * n_half
-            within = self.blk % per_shard
-            which = (within % n_half) * n_ka + jnp.bitwise_xor(self.blk // per_shard, me)
-            start = pl.multiple_of((within // n_half) * BLK, BLK)
-            for x in range(n_pieces):
+            start = pl.multiple_of(((self.blk % per_shard) // n_half) * BLK, BLK)
+            if phase == 1:
+                pltpu.make_async_copy(kv_refs[0].at[pl.ds(start, BLK), :], self.dst, self.sem).start()
+                return
+            which = piece_of(self.blk)
+            for x in range(n_refs):
                 @pl.when(which == x)
                 def _(x=x, start=start):
-                    pltpu.make_async_copy(kv_pieces[x].at[pl.ds(start, BLK), :], self.dst, self.sem).start()
+                    pltpu.make_async_copy(kv_refs[x].at[pl.ds(start, BLK), :], self.dst, self.sem).start()
 
         def wait(self):
-            pltpu.make_async_copy(kv_pieces[0].at[pl.ds(0, BLK), :], self.dst, self.sem).wait()
+            pltpu.make_async_copy(kv_refs[0].at[pl.ds(0, BLK), :], self.dst, self.sem).wait()
 
     def copy(j, s):
         return block_copy(off_ref[j, s], kvbuf.at[j, s, :, pl.ds(0, 2 * HD)], sems.at[j, s])
@@ -74,21 +88,27 @@
     kvbuf[:, :, :, 2 * HD:] = jnp.ones(kvbuf.shape[:3] + (HD,), kvbuf.dtype)
 
     n_off = []
+    diag_here = []
     for j in range(n_local):
         qb = qb0 + j
-        block_copy(qb, dbuf.at[j], dsems.at[j]).start()
+        here = mine(qb)
+        diag_here.append(here)
+
+        @pl.when(here)
+        def _(j=j, qb=qb):
+            block_copy(qb, dbuf.at[j], dsems.at[j]).start()
 
         def compact(s, n, j=j, qb=qb):
             b = bl_ref[row0 + j, s]
             off_ref[j, n] = b
-            return n + (b != qb).astype(jnp.int32)
+            return n + jnp.logical_and(b != qb, mine(b)).astype(jnp.int32)
 
         n_j = lax.fori_loop(0, cnt_ref[row0 + j], compact, 0)
         n_off.append(n_j)
         n_pad = (n_j + group - 1) // group * group
 
         def pad(s, c, j=j, qb=qb):
-            off_ref[j, s] = qb
+            off_ref[j, s] = off_ref[j, 0]
             return c
 
         lax.fori_loop(n_j, n_pad, pad, 0)
@@ -104,7 +124,6 @@
     col = lax.broadcasted_iota(jnp.int32, (rows, BLK), 1)
     causal = col <= rowpos
     dims = (((1,), (1,)), ((), ()))
-
     slot_of = lax.broadcasted_iota(jnp.int32, (rows, group * BLK), 1) // BLK
 
     def update(qs, kvb, carry, live=None):
@@ -126,14 +145,28 @@
         qb = qb0 + j
         qrows = q_ref[j * BLK:(j + 1) * BLK, :]
         qs = jnp.concatenate([qrows[:, h * HD:(h + 1) * HD] for h in range(QH)], axis=0)
-
-        block_copy(qb, dbuf.at[j], dsems.at[j]).wait()
-        kvd = dbuf[j]
-        sc = lax.dot_general(qs, kvd[:, :HD], dims, preferred_element_type=jnp.float32) * scale
-        m = jnp.max(jnp.where(causal, sc, masked_score), axis=1, keepdims=True)
-        w = jnp.where(causal, jnp.exp2(sc - m), 0.0)
-        l = jnp.sum(w, axis=1, keepdims=True)
-        acc = jnp.dot(w.astype(jnp.bfloat16), kvd[:, HD:2 * HD], preferred_element_type=jnp.float32)
+        if phase == 0:
+            carry = (
+                jnp.full((rows, 1), masked_score, jnp.float32),
+                jnp.zeros((rows, 1), jnp.float32),
+                jnp.zeros((rows, HD), jnp.float32),
+            )
+        else:
+            carry = (m_io[j], l_io[j], acc_io[j])
+
+        def diag(carry, j=j, qb=qb, qs=qs):
+            m, l, acc = carry
+            block_copy(qb, dbuf.at[j], dsems.at[j]).wait()
+            kvd = dbuf[j]
+            sc = lax.dot_general(qs, kvd[:, :HD], dims, preferred_element_type=jnp.float32)
+            m_new = jnp.maximum(m, jnp.max(jnp.where(causal, sc, masked_score), axis=1, keepdims=True) * scale)
+            alpha = jnp.exp2(m - m_new)
+            w = jnp.where(causal, jnp.exp2(sc * scale - m_new), 0.0)
+            l = alpha * l + jnp.sum(w, axis=1, keepdims=True)
+            acc = alpha * acc + jnp.dot(w.astype(jnp.bfloat16), kvd[:, HD:2 * HD], preferred_element_type=jnp.float32)
+            return m_new, l, acc
+
+        carry = lax.cond(diag_here[j], diag, lambda c: c, carry)
 
         def grouped(g, carry, j=j, qs=qs):
             first = g * group
@@ -150,11 +183,16 @@
             return update(qs, kvb, carry, live=n_off[j] - first)
 
         n_groups = n_off[j] // group
-        carry = lax.fori_loop(0, n_groups, grouped, (m, l, acc))
+        carry = lax.fori_loop(0, n_groups, grouped, carry)
         m, l, acc = lax.fori_loop(n_groups, (n_off[j] + group - 1) // group, last, carry)
-        res = (acc / l).astype(out_ref.dtype)
-        for h in range(QH):
-            out_ref[j * BLK:(j + 1) * BLK, h * HD:(h + 1) * HD] = res[h * BLK:(h + 1) * BLK, :]
+        if phase == 0:
+            m_io[j] = m
+            l_io[j] = l
+            acc_io[j] = acc
+        else:
+            res = (acc / l).astype(out_ref.dtype)
+            for h in range(QH):
+                out_ref[j * BLK:(j + 1) * BLK, h * HD:(h + 1) * HD] = res[h * BLK:(h + 1) * BLK, :]
 
 
 def shards(queries, key_cache, value_cache, block_list, block_count, *, n_pb, n_ka):
@@ -177,30 +215,54 @@
     listed = block_list.shape[1]
     qb0 = jnp.stack([(p * n_ka + k) * n_local, k]).astype(jnp.int32)
 
-    kernel = functools.partial(
-        attend_kernel, n_local=n_local, n_pieces=len(kv_pieces), n_ka=n_ka, group=16, scale=math.log2(math.e) / math.sqrt(HD)
-    )
-    return pl.pallas_call(
-        kernel,
-        out_shape=jax.ShapeDtypeStruct((rows_mine, queries.shape[1]), jnp.bfloat16),
+    rows = QH * BLK
+    width = queries.shape[1]
+    state_shapes = [
+        jax.ShapeDtypeStruct((n_local, rows, 1), jnp.float32),
+        jax.ShapeDtypeStruct((n_local, rows, 1), jnp.float32),
+        jax.ShapeDtypeStruct((n_local, rows, HD), jnp.float32),
+    ]
+    state_specs = [pl.BlockSpec(st.shape, lambda i, *_: (0, 0, 0)) for st in state_shapes]
+    q_spec = pl.BlockSpec((rows_mine, width), lambda i, bl, cnt, qb: (qb[1], 0))
+    scratch = [
+        pltpu.SMEM((n_local, listed), jnp.int32),
+        pltpu.VMEM((n_local, listed, BLK, kv_local.shape[1] + HD), jnp.bfloat16),
+        pltpu.VMEM((n_local, BLK, kv_local.shape[1]), jnp.bfloat16),
+        pltpu.SemaphoreType.DMA((n_local, listed)),
+        pltpu.SemaphoreType.DMA((n_local,)),
+    ]
+    params = pltpu.CompilerParams(vmem_limit_bytes=48 * 1024 * 1024)
+
+    def phase_call(phase):
+        return functools.partial(
+            attend_kernel, n_local=n_local, n_pieces=len(kv_pieces), n_ka=n_ka,
+            group=16, scale=math.log2(math.e) / math.sqrt(HD), phase=phase,
+        )
+
+    state = pl.pallas_call(
+        phase_call(0),
+        out_shape=state_shapes,
         grid_spec=pltpu.PrefetchScalarGridSpec(
             num_scalar_prefetch=3,
             grid=(1,),
-            in_specs=[
-                pl.BlockSpec((rows_mine, queries.shape[1]), lambda i, bl, cnt, qb: (qb[1], 0)),
-            ]
-            + [pl.BlockSpec(memory_space=pl.ANY)] * len(kv_pieces),
-            out_specs=pl.BlockSpec((rows_mine, queries.shape[1]), lambda i, *_: (0, 0)),
-            scratch_shapes=[
-                pltpu.SMEM((n_local, listed), jnp.int32),
-                pltpu.VMEM((n_local, listed, BLK, kv_local.shape[1] + HD), jnp.bfloat16),
-                pltpu.VMEM((n_local, BLK, kv_local.shape[1]), jnp.bfloat16),
-                pltpu.SemaphoreType.DMA((n_local, listed)),
-                pltpu.SemaphoreType.DMA((n_local,)),
-            ],
+            in_specs=[q_spec] + [pl.BlockSpec(memory_space=pl.ANY)] * (len(kv_pieces) - 1),
+            out_specs=state_specs,
+            scratch_shapes=scratch,
         ),
-        compiler_params=pltpu.CompilerParams(vmem_limit_bytes=48 * 1024 * 1024),
-    )(block_list, block_count, qb0, queries, *kv_pieces)
+        compiler_params=params,
+    )(block_list, block_count, qb0, queries, *kv_pieces[:-1])
+    return pl.pallas_call(
+        phase_call(1),
+        out_shape=jax.ShapeDtypeStruct((rows_mine, width), jnp.bfloat16),
+        grid_spec=pltpu.PrefetchScalarGridSpec(
+            num_scalar_prefetch=3,
+            grid=(1,),
+            in_specs=[q_spec, pl.BlockSpec(memory_space=pl.ANY)] + state_specs,
+            out_specs=pl.BlockSpec((rows_mine, width), lambda i, *_: (0, 0)),
+            scratch_shapes=scratch,
+        ),
+        compiler_params=params,
+    )(block_list, block_count, qb0, queries, kv_pieces[-1], *state)
 
 
 def solution(mesh):

time: 73 us -> 86.1 us (1.18)
  the two profiles are of different devices: /device:TPU:24 before, /device:TPU:25 now
where the time goes in v14:
time: 86.1 us; the launch traced here: 86 us
  Pallas kernels  31.6 us (37%)
  waiting for transfers between devices  26.7 us (31%)
  starting transfers between devices  25.4 us (30%)
  local copies, waits for them, and re-layouts  1.59 us (2%)
    ppermute x6, waiting for transfers between devices, gather_axis(): other = lax.ppermute(held, axis, [(i, i ^ b) for i in range(n)])  26.5 us
    ppermute x6, starting transfers between devices, pieces_axis(): lax.ppermute(idx_pieces[x], axis, [(i, i ^ b) for i in range(n)])  22.5 us
    pallas_call x1, Pallas kernels, shards(): pl.pallas_call(phase_call(0), out_shape=state_shapes, grid_spec=pltpu.Pre...  20.1 us
    pallas_call x1, Pallas kernels, shards(): pl.pallas_call(phase_call(1), out_shape=jax.ShapeDtypeStruct((rows_mine,...  11.5 us
    ppermute x6, starting transfers between devices, gather_axis(): other = lax.ppermute(held, axis, [(i, i ^ b) for i in range(n)])  2.89 us
  transfers between devices with their start and end apart: 12, of which 7 were waited for; matrix products, arithmetic and copies ran while one was open for 0% of the time, Pallas kernels for 23%

profile of v14, /device:TPU:25, one launch (start us, length us, event | category | flops | bytes accessed | tf_op | source)
XLA Modules:
  0.0 86.0 jit_solution(9854078011544607065)
XLA Ops:
  0.0 0.0 copy-start.3
  0.0 0.9 %constant_dynamic-update-slice_fusion.1 = bf16[256,256]{1,0:T(8,128)(2,1)S(1)} fusion(bf16[256,128]{1,0:T(8,128)(2,1)} %param.6), kind=kLoop, calls=%fused_computation.16 | loop fusion | bytes 131072
  0.9 0.0 copy-done.3
  0.9 0.1 collective-permute-start
  1.1 5.8 %collective-permute-done = bf16[1,1,1,128,256]{4,3,2,1,0:T(8,128)(2,1)S(1)} collective-permute-done((bf16[1,1,1,128,256]{4,3,2,1,0:T(8,128)(2,1)S(1)}, bf16[1,1,1,128,256]{4,3,2,1,0:T(8,128)(2,1)S(1)}, u32[]{:S(2)}, u32[]{:S(2)}) %collective-permute-start) | collective-permute-done | bytes 65568 | tf_op jit(solution)/shard_map/ppermute | solution.py:24
  6.9 0.1 collective-permute-start.1
  7.0 4.2 %collective-permute-done.1 = bf16[2,1,1,128,256]{4,3,2,1,0:T(8,128)(2,1)S(1)} collective-permute-done((bf16[2,1,1,128,256]{4,3,2,1,0:T(8,128)(2,1)S(1)}, bf16[2,1,1,128,256]{4,3,2,1,0:T(8,128)(2,1)S(1)}, u32[]{:S(2)}, u32[]{:S(2)}) %collective-permute-start.1) | collective-permute-done | bytes 131104 | tf_op jit(solution)/shard_map/ppermute | solution.py:24
  11.2 0.1 maximum_select_fusion.2
  11.3 1.3 %collective-permute-start.2 = (bf16[2,2,1,128,256]{4,3,0,2,1:T(8,128)(2,1)S(1)}, bf16[2,2,1,128,256]{4,3,0,2,1:T(8,128)(2,1)S(1)}, u32[]{:S(2)}, u32[]{:S(2)}) collective-permute-start(bf16[2,2,1,128,256]{4,3,0,2,1:T(8,128)(2,1)S(1)} %maximum_select_fusion.2), channel_id=1, source_target_pairs={{0,4},{4,0},{8,12},{12,8},{16,20},{20,16},{24,28},{28,24},{1,5},{5... | collective-permute-start | bytes 786440 | tf_op jit(solution)/shard_map/ppermute | solution.py:24
  12.5 5.0 %collective-permute-done.2 = bf16[2,2,1,128,256]{4,3,0,2,1:T(8,128)(2,1)S(1)} collective-permute-done((bf16[2,2,1,128,256]{4,3,0,2,1:T(8,128)(2,1)S(1)}, bf16[2,2,1,128,256]{4,3,0,2,1:T(8,128)(2,1)S(1)}, u32[]{:S(2)}, u32[]{:S(2)}) %collective-permute-start.2) | collective-permute-done | bytes 262176 | tf_op jit(solution)/shard_map/ppermute | solution.py:24
  17.6 0.1 collective-permute-start.3
  17.7 4.7 %collective-permute-done.3 = bf16[1,1,1,128,256]{4,3,2,1,0:T(8,128)(2,1)S(1)} collective-permute-done((bf16[1,1,1,128,256]{4,3,2,1,0:T(8,128)(2,1)S(1)}, bf16[1,1,1,128,256]{4,3,2,1,0:T(8,128)(2,1)S(1)}, u32[]{:S(2)}, u32[]{:S(2)}) %collective-permute-start.3) | collective-permute-done | bytes 65568 | tf_op jit(solution)/shard_map/ppermute | solution.py:24
  22.4 0.1 collective-permute-start.4
  22.5 4.1 %collective-permute-done.4 = bf16[2,1,1,128,256]{4,3,0,2,1:T(8,128)(2,1)S(1)} collective-permute-done((bf16[2,1,1,128,256]{4,3,0,2,1:T(8,128)(2,1)S(1)}, bf16[2,1,1,128,256]{4,3,0,2,1:T(8,128)(2,1)S(1)}, u32[]{:S(2)}, u32[]{:S(2)}) %collective-permute-start.4) | collective-permute-done | bytes 131104 | tf_op jit(solution)/shard_map/ppermute | solution.py:24
  26.7 1.3 %collective-permute-start.5 = (bf16[2,2,1,128,256]{4,3,0,2,1:T(8,128)(2,1)S(1)}, bf16[2,2,1,128,256]{4,3,0,2,1:T(8,128)(2,1)S(1)}, u32[]{:S(2)}, u32[]{:S(2)}) collective-permute-start(bf16[2,2,1,128,256]{4,3,0,2,1:T(8,128)(2,1)S(1)} %maximum_select_fusion.3), channel_id=1, source_target_pairs={{0,4},{4,0},{8,12},{12,8},{16,20},{20,16},{24,28},{28,24},{1,5},{5... | collective-permute-start | bytes 786440 | tf_op jit(solution)/shard_map/ppermute | solution.py:24
  27.9 1.2 %collective-permute-start.9 = (bf16[1024,256]{1,0:T(8,128)(2,1)S(1)}, bf16[1024,256]{1,0:T(8,128)(2,1)S(1)}, u32[]{:S(2)}, u32[]{:S(2)}) collective-permute-start(bf16[1024,256]{1,0:T(8,128)(2,1)S(1)} %bitcast.28), channel_id=1, source_target_pairs={{0,2},{1,3},{2,0},{3,1},{4,6},{5,7},{6,4},{7,5},{8,10},{9,11},{10,... | collective-permute-start | bytes 1572872 | tf_op jit(solution)/shard_map/ppermute | solution.py:39
  29.2 2.8 %collective-permute-done.5 = bf16[2,2,1,128,256]{4,3,0,2,1:T(8,128)(2,1)S(1)} collective-permute-done((bf16[2,2,1,128,256]{4,3,0,2,1:T(8,128)(2,1)S(1)}, bf16[2,2,1,128,256]{4,3,0,2,1:T(8,128)(2,1)S(1)}, u32[]{:S(2)}, u32[]{:S(2)}) %collective-permute-start.5) | collective-permute-done | bytes 262176 | tf_op jit(solution)/shard_map/ppermute | solution.py:24
  32.0 1.3 %collective-permute-start.6 = (bf16[1024,256]{1,0:T(8,128)(2,1)S(1)}, bf16[1024,256]{1,0:T(8,128)(2,1)S(1)}, u32[]{:S(2)}, u32[]{:S(2)}) collective-permute-start(bf16[1024,256]{1,0:T(8,128)(2,1)S(1)} %bitcast.31), channel_id=1, source_target_pairs={{0,2},{1,3},{2,0},{3,1},{4,6},{5,7},{6,4},{7,5},{8,10},{9,11},{10,... | collective-permute-start | bytes 1572872 | tf_op jit(solution)/shard_map/ppermute | solution.py:39
  33.3 6.0 %collective-permute-start.8 = (bf16[1024,256]{1,0:T(8,128)(2,1)S(1)}, bf16[1024,256]{1,0:T(8,128)(2,1)S(1)}, u32[]{:S(2)}, u32[]{:S(2)}) collective-permute-start(bf16[1024,256]{1,0:T(8,128)(2,1)S(1)} %bitcast.29), channel_id=1, source_target_pairs={{0,1},{1,0},{2,3},{3,2},{4,5},{5,4},{6,7},{7,6},{8,9},{9,8},{10,11... | collective-permute-start | bytes 1572872 | tf_op jit(solution)/shard_map/ppermute | solution.py:39
  39.4 0.0 collective-permute-start.11
  39.4 0.0 collective-permute-done.9.rest_2_
  39.4 8.2 %collective-permute-start.10 = (bf16[1024,256]{1,0:T(8,128)(2,1)S(1)}, bf16[1024,256]{1,0:T(8,128)(2,1)}, u32[]{:S(2)}, u32[]{:S(2)}) collective-permute-start(bf16[1024,256]{1,0:T(8,128)(2,1)S(1)} %collective-permute-done.9.rest_2_), channel_id=1, source_target_pairs={{0,1},{1,0},{2,3},{3,2},{4,5},{5,4},{6,7},{7,6},{8,9},{9,8},{10,11... | collective-permute-start | bytes 1572872 | tf_op jit(solution)/shard_map/ppermute | solution.py:39
  47.6 0.2 collective-permute-done.6.rest_6_
  47.8 5.7 %collective-permute-start.7 = (bf16[1024,256]{1,0:T(8,128)(2,1)S(1)}, bf16[1024,256]{1,0:T(8,128)(2,1)}, u32[]{:S(2)}, u32[]{:S(2)}) collective-permute-start(bf16[1024,256]{1,0:T(8,128)(2,1)S(1)} %collective-permute-done.6.rest_6_), channel_id=1, source_target_pairs={{0,1},{1,0},{2,3},{3,2},{4,5},{5,4},{6,7},{7,6},{8,9},{9,8},{10,11... | collective-permute-start | bytes 1572872 | tf_op jit(solution)/shard_map/ppermute | solution.py:39
  53.5 0.0 copy-start.1
  53.5 0.0 copy-start.2
  53.5 0.1 pad_add_fusion.qb_ref
  53.6 0.0 copy-start
  53.6 0.0 collective-permute-done.8.rest_1_
  53.6 0.0 collective-permute-done.11.rest_5_
  53.6 0.0 collective-permute-done.10.rest_3_
  53.6 0.6 copy-done.1
  54.2 0.0 copy-done.2
  54.2 20.1 %shard_map.55 = (f32[2,512,1]{2,1,0:T(8,128)S(1)}, f32[2,512,1]{2,1,0:T(8,128)S(1)}, f32[2,512,128]{2,1,0:T(8,128)S(1)}) custom-call(s32[8,32]{1,0:T(8,128)S(1)} %copy-done.1, s32[8]{0:T(128)S(1)} %copy-done.2, s32[2]{0:T(128)S(1)} %pad_add_fusion.qb_ref, bf16[1024,512]{1,0:T(8,128)(2,1)} %q_ref.3, bf16[1024,256]{1,0:T(8,128)(2,1)S(1)} %bitcast.30, ...), custom_call_target="tpu_custom_call" | custom-call | tf_op jit(solution)/shard_map/pallas_call | solution.py:242
  74.3 0.0 collective-permute-done.7.rest_0_
  74.3 0.0 copy-done
  74.3 11.5 %shard_map.56 = bf16[256,512]{1,0:T(8,128)(2,1)} custom-call(s32[8,32]{1,0:T(8,128)S(1)} %copy-done.1, s32[8]{0:T(128)S(1)} %copy-done.2, s32[2]{0:T(128)S(1)} %pad_add_fusion.qb_ref, bf16[1024,512]{1,0:T(8,128)(2,1)S(1)} %copy-done, bf16[1024,256]{1,0:T(8,128)(2,1)} %collective-permute-done.7.rest_0_, f32[2,512,1]{2,1,0:T(8,128)S(1)} %get-tuple-element.12.rest_1_, ...), custom_call_target="tpu_custom_call" | custom-call | tf_op jit(solution)/shard_map/pallas_call | solution.py:254
  (11 shorter events, 0.3 us)
Async XLA Ops:
  0.0 0.9 %copy-start.3 = (bf16[256,128]{1,0:T(8,128)(2,1)S(1)}, bf16[256,128]{1,0:T(8,128)(2,1)}, u32[]{:S(2)}) copy-start(bf16[256,128]{1,0:T(8,128)(2,1)} %param.7) | copy-start | bytes 196612
  0.9 5.9 %collective-permute-start = (bf16[1,1,1,128,256]{4,3,2,1,0:T(8,128)(2,1)S(1)}, bf16[1,1,1,128,256]{4,3,2,1,0:T(8,128)(2,1)S(1)}, u32[]{:S(2)}, u32[]{:S(2)}) collective-permute-start(bf16[1,1,1,128,256]{4,3,2,1,0:T(8,128)(2,1)S(1)} %get-tuple-element.18), channel_id=1, source_target_pairs={{0,16},{4,20},{8,24},{12,28},{16,0},{20,4},{24,8},{28,12},{1,17},{... | collective-permute-start | bytes 196616 | tf_op jit(solution)/shard_map/ppermute | solution.py:24
  6.9 4.3 %collective-permute-start.1 = (bf16[2,1,1,128,256]{4,3,2,1,0:T(8,128)(2,1)S(1)}, bf16[2,1,1,128,256]{4,3,2,1,0:T(8,128)(2,1)S(1)}, u32[]{:S(2)}, u32[]{:S(2)}) collective-permute-start(bf16[2,1,1,128,256]{4,3,2,1,0:T(8,128)(2,1)S(1)} %maximum_select_fusion.4), channel_id=1, source_target_pairs={{0,8},{4,12},{8,0},{12,4},{16,24},{20,28},{24,16},{28,20},{1,9},{5... | collective-permute-start | bytes 393224 | tf_op jit(solution)/shard_map/ppermute | solution.py:24
  11.3 6.2 %collective-permute-start.2 = (bf16[2,2,1,128,256]{4,3,0,2,1:T(8,128)(2,1)S(1)}, bf16[2,2,1,128,256]{4,3,0,2,1:T(8,128)(2,1)S(1)}, u32[]{:S(2)}, u32[]{:S(2)}) collective-permute-start(bf16[2,2,1,128,256]{4,3,0,2,1:T(8,128)(2,1)S(1)} %maximum_select_fusion.2), channel_id=1, source_target_pairs={{0,4},{4,0},{8,12},{12,8},{16,20},{20,16},{24,28},{28,24},{1,5},{5... | collective-permute-start | bytes 786440 | tf_op jit(solution)/shard_map/ppermute | solution.py:24
  17.6 4.8 %collective-permute-start.3 = (bf16[1,1,1,128,256]{4,3,2,1,0:T(8,128)(2,1)S(1)}, bf16[1,1,1,128,256]{4,3,2,1,0:T(8,128)(2,1)S(1)}, u32[]{:S(2)}, u32[]{:S(2)}) collective-permute-start(bf16[1,1,1,128,256]{4,3,2,1,0:T(8,128)(2,1)S(1)} %bitcast.34), channel_id=1, source_target_pairs={{0,16},{4,20},{8,24},{12,28},{16,0},{20,4},{24,8},{28,12},{1,17},{... | collective-permute-start | bytes 196616 | tf_op jit(solution)/shard_map/ppermute | solution.py:24
  22.4 4.2 %collective-permute-start.4 = (bf16[2,1,1,128,256]{4,3,0,2,1:T(8,128)(2,1)S(1)}, bf16[2,1,1,128,256]{4,3,0,2,1:T(8,128)(2,1)S(1)}, u32[]{:S(2)}, u32[]{:S(2)}) collective-permute-start(bf16[2,1,1,128,256]{4,3,0,2,1:T(8,128)(2,1)S(1)} %fusion), channel_id=1, source_target_pairs={{0,8},{4,12},{8,0},{12,4},{16,24},{20,28},{24,16},{28,20},{1,9},{5... | collective-permute-start | bytes 393224 | tf_op jit(solution)/shard_map/ppermute | solution.py:24
  26.7 5.3 %collective-permute-start.5 = (bf16[2,2,1,128,256]{4,3,0,2,1:T(8,128)(2,1)S(1)}, bf16[2,2,1,128,256]{4,3,0,2,1:T(8,128)(2,1)S(1)}, u32[]{:S(2)}, u32[]{:S(2)}) collective-permute-start(bf16[2,2,1,128,256]{4,3,0,2,1:T(8,128)(2,1)S(1)} %maximum_select_fusion.3), channel_id=1, source_target_pairs={{0,4},{4,0},{8,12},{12,8},{16,20},{20,16},{24,28},{28,24},{1,5},{5... | collective-permute-start | bytes 786440 | tf_op jit(solution)/shard_map/ppermute | solution.py:24
  27.9 11.4 %collective-permute-start.9 = (bf16[1024,256]{1,0:T(8,128)(2,1)S(1)}, bf16[1024,256]{1,0:T(8,128)(2,1)S(1)}, u32[]{:S(2)}, u32[]{:S(2)}) collective-permute-start(bf16[1024,256]{1,0:T(8,128)(2,1)S(1)} %bitcast.28), channel_id=1, source_target_pairs={{0,2},{1,3},{2,0},{3,1},{4,6},{5,7},{6,4},{7,5},{8,10},{9,11},{10,... | collective-permute-start | bytes 1572872 | tf_op jit(solution)/shard_map/ppermute | solution.py:39
  32.0 15.7 %collective-permute-start.6 = (bf16[1024,256]{1,0:T(8,128)(2,1)S(1)}, bf16[1024,256]{1,0:T(8,128)(2,1)S(1)}, u32[]{:S(2)}, u32[]{:S(2)}) collective-permute-start(bf16[1024,256]{1,0:T(8,128)(2,1)S(1)} %bitcast.31), channel_id=1, source_target_pairs={{0,2},{1,3},{2,0},{3,1},{4,6},{5,7},{6,4},{7,5},{8,10},{9,11},{10,... | collective-permute-start | bytes 1572872 | tf_op jit(solution)/shard_map/ppermute | solution.py:39
  33.3 20.2 %collective-permute-start.8 = (bf16[1024,256]{1,0:T(8,128)(2,1)S(1)}, bf16[1024,256]{1,0:T(8,128)(2,1)S(1)}, u32[]{:S(2)}, u32[]{:S(2)}) collective-permute-start(bf16[1024,256]{1,0:T(8,128)(2,1)S(1)} %bitcast.29), channel_id=1, source_target_pairs={{0,1},{1,0},{2,3},{3,2},{4,5},{5,4},{6,7},{7,6},{8,9},{9,8},{10,11... | collective-permute-start | bytes 1572872 | tf_op jit(solution)/shard_map/ppermute | solution.py:39
  39.4 14.2 %collective-permute-start.11 = (bf16[1024,256]{1,0:T(8,128)(2,1)S(1)}, bf16[1024,256]{1,0:T(8,128)(2,1)S(1)}, u32[]{:S(2)}, u32[]{:S(2)}) collective-permute-start(bf16[1024,256]{1,0:T(8,128)(2,1)S(1)} %bitcast.32), channel_id=1, source_target_pairs={{0,1},{1,0},{2,3},{3,2},{4,5},{5,4},{6,7},{7,6},{8,9},{9,8},{10,11... | collective-permute-start | bytes 1572872 | tf_op jit(solution)/shard_map/ppermute | solution.py:39
  39.4 14.2 %collective-permute-start.10 = (bf16[1024,256]{1,0:T(8,128)(2,1)S(1)}, bf16[1024,256]{1,0:T(8,128)(2,1)}, u32[]{:S(2)}, u32[]{:S(2)}) collective-permute-start(bf16[1024,256]{1,0:T(8,128)(2,1)S(1)} %collective-permute-done.9.rest_2_), channel_id=1, source_target_pairs={{0,1},{1,0},{2,3},{3,2},{4,5},{5,4},{6,7},{7,6},{8,9},{9,8},{10,11... | collective-permute-start | bytes 1572872 | tf_op jit(solution)/shard_map/ppermute | solution.py:39
  47.8 26.5 %collective-permute-start.7 = (bf16[1024,256]{1,0:T(8,128)(2,1)S(1)}, bf16[1024,256]{1,0:T(8,128)(2,1)}, u32[]{:S(2)}, u32[]{:S(2)}) collective-permute-start(bf16[1024,256]{1,0:T(8,128)(2,1)S(1)} %collective-permute-done.6.rest_6_), channel_id=1, source_target_pairs={{0,1},{1,0},{2,3},{3,2},{4,5},{5,4},{6,7},{7,6},{8,9},{9,8},{10,11... | collective-permute-start | bytes 1572872 | tf_op jit(solution)/shard_map/ppermute | solution.py:39
  53.5 0.7 copy-start.1
  53.5 0.7 copy-start.2
  53.6 20.7 %copy-start = (bf16[1024,512]{1,0:T(8,128)(2,1)S(1)}, bf16[1024,512]{1,0:T(8,128)(2,1)}, u32[]{:S(2)}) copy-start(bf16[1024,512]{1,0:T(8,128)(2,1)} %q_ref.3) | copy-start | bytes 3145732

commit v15 on v13

--- a/solution.py
+++ b/solution.py
@@ -161,14 +161,21 @@
     kv_local = jnp.concatenate([key_cache, value_cache], axis=1)
     n_half = kv_local.shape[0] // BLK
     kv_pieces = []
-    shard = None
     for h in range(n_half):
         part = kv_local[h * BLK:(h + 1) * BLK]
-        if shard is not None:
-            part, shard = lax.optimization_barrier((part, shard))
-            kv_pieces += pieces_axis(shard, "ka", n_ka)
-        shard = gather_axis(part, "pb", n_pb)
-    kv_pieces += pieces_axis(shard, "ka", n_ka)
+        if h % 2 == 0:
+            kv_pieces += pieces_axis(gather_axis(part, "pb", n_pb), "ka", n_ka)
+            continue
+        b = n_ka // 2
+        across = lax.ppermute(part, "ka", [(i, i ^ b) for i in range(n_ka)])
+        both = gather_axis(jnp.stack([part, across]), "pb", n_pb).reshape(n_pb, 2, BLK, part.shape[1])
+        held = {0: both[:, 0].reshape(-1, part.shape[1]), b: both[:, 1].reshape(-1, part.shape[1])}
+        step = b // 2
+        while step >= 1:
+            for x in sorted(held):
+                held[x | step] = lax.ppermute(held[x], "ka", [(i, i ^ step) for i in range(n_ka)])
+            step //= 2
+        kv_pieces += [held[x] for x in range(n_ka)]
 
     p = lax.axis_index("pb")
     k = lax.axis_index("ka")

time: 73 us -> 73 us (level)
  waiting for transfers between devices: 45.8 us -> 41.5 us
  starting transfers between devices: 7.63 us -> 10.9 us
    ppermute x6 -> x3, waiting for transfers between devices: 15.6 us -> 10.2 us  [pieces_axis(): lax.ppermute(idx_pieces[x], axis, [(i, i ^ b) for i in range(n)])]
    ppermute x6, starting transfers between devices: 4.01 us -> 7.12 us  [gather_axis(): other = lax.ppermute(held, axis, [(i, i ^ b) for i in range(n)])]
    ppermute x0 -> x3, waiting for transfers between devices: none -> 2.75 us  [the longest x1 2.75 us: shards(): across = lax.ppermute(part, 'ka', [(i, i ^ b) for i in range(n_ka)])]
    ppermute x0 -> x3, starting transfers between devices: none -> 2.24 us  [the longest x1 1.58 us: shards(): across = lax.ppermute(part, 'ka', [(i, i ^ b) for i in range(n_ka)])]
    ppermute x6 -> x3, starting transfers between devices: 3.62 us -> 1.59 us  [pieces_axis(): lax.ppermute(idx_pieces[x], axis, [(i, i ^ b) for i in range(n)])]
    ppermute x6, waiting for transfers between devices: 30.2 us -> 28.5 us  [gather_axis(): other = lax.ppermute(held, axis, [(i, i ^ b) for i in range(n)])]
  transfers between devices with their start and end apart: 12 -> 12, of which waited for: 9 -> 7; matrix products, arithmetic and copies ran while one was open for 0% -> 1% of each run, Pallas kernels for 0% -> 0%
where the time goes in v15:
time: 73 us; the launch traced here: 72.1 us
  waiting for transfers between devices  41.5 us (57%)
  Pallas kernels  17.8 us (24%)
  starting transfers between devices  10.9 us (15%)
  local copies, waits for them, and re-layouts  1.06 us (1%)
    ppermute x6, waiting for transfers between devices, gather_axis(): other = lax.ppermute(held, axis, [(i, i ^ b) for i in range(n)])  28.5 us
    pallas_call x1, Pallas kernels, shards(): pl.pallas_call(kernel, out_shape=jax.ShapeDtypeStruct((rows_mine, queries...  17.8 us
    ppermute x3, waiting for transfers between devices, pieces_axis(): lax.ppermute(idx_pieces[x], axis, [(i, i ^ b) for i in range(n)])  10.2 us
    ppermute x6, starting transfers between devices, gather_axis(): other = lax.ppermute(held, axis, [(i, i ^ b) for i in range(n)])  7.12 us
    ppermute x1, waiting for transfers between devices, shards(): across = lax.ppermute(part, 'ka', [(i, i ^ b) for i in range(n_ka)])  2.75 us
    ppermute x3, starting transfers between devices, pieces_axis(): lax.ppermute(idx_pieces[x], axis, [(i, i ^ b) for i in range(n)])  1.59 us
    ppermute x1, starting transfers between devices, shards(): across = lax.ppermute(part, 'ka', [(i, i ^ b) for i in range(n_ka)])  1.58 us
  transfers between devices with their start and end apart: 12, of which 7 were waited for; matrix products, arithmetic and copies ran while one was open for 1% of the time, Pallas kernels for 0%

profile of v15, /device:TPU:24, one launch (start us, length us, event | category | flops | bytes accessed | tf_op | source)
XLA Modules:
  0.0 72.1 jit_solution(1747530600151756072)
XLA Ops:
  0.0 0.0 copy-start.3
  0.0 0.9 %constant_dynamic-update-slice_fusion.1 = bf16[256,256]{1,0:T(8,128)(2,1)S(1)} fusion(bf16[256,128]{1,0:T(8,128)(2,1)} %param.6), kind=kLoop, calls=%fused_computation.16 | loop fusion | bytes 131072
  0.9 0.0 copy-done.3
  1.0 1.6 %collective-permute-start.6 = (bf16[128,256]{1,0:T(8,128)(2,1)S(1)}, bf16[128,256]{1,0:T(8,128)(2,1)S(1)}, u32[]{:S(2)}, u32[]{:S(2)}) collective-permute-start(bf16[128,256]{1,0:T(8,128)(2,1)S(1)} %get-tuple-element.11), channel_id=1, source_target_pairs={{0,2},{1,3},{2,0},{3,1},{4,6},{5,7},{6,4},{7,5},{8,10},{9,11},{10,... | collective-permute-start | bytes 196616 | tf_op jit(solution)/shard_map/ppermute | solution.py:170
  2.5 2.7 %collective-permute-done.6 = bf16[128,256]{1,0:T(8,128)(2,1)S(1)} collective-permute-done((bf16[128,256]{1,0:T(8,128)(2,1)S(1)}, bf16[128,256]{1,0:T(8,128)(2,1)S(1)}, u32[]{:S(2)}, u32[]{:S(2)}) %collective-permute-start.6) | collective-permute-done | bytes 65568 | tf_op jit(solution)/shard_map/ppermute | solution.py:170
  5.3 0.4 collective-permute-start.7
  5.7 2.6 %collective-permute-start = (bf16[1,1,1,128,256]{4,3,0,2,1:T(8,128)(2,1)S(1)}, bf16[1,1,1,128,256]{4,3,0,2,1:T(8,128)(2,1)S(1)}, u32[]{:S(2)}, u32[]{:S(2)}) collective-permute-start(bf16[1,1,1,128,256]{4,3,0,2,1:T(8,128)(2,1)S(1)} %get-tuple-element.12), channel_id=1, source_target_pairs={{0,16},{4,20},{8,24},{12,28},{16,0},{20,4},{24,8},{28,12},{1,17},{... | collective-permute-start | bytes 196616 | tf_op jit(solution)/shard_map/ppermute | solution.py:24
  8.3 6.3 %collective-permute-done.7 = bf16[1,1,1,2,128,256]{5,4,3,2,1,0:T(8,128)(2,1)S(1)} collective-permute-done((bf16[1,1,1,2,128,256]{5,4,3,2,1,0:T(8,128)(2,1)S(1)}, bf16[1,1,1,2,128,256]{5,4,3,2,1,0:T(8,128)(2,1)S(1)}, u32[]{:S(2)}, u32[]{:S(2)}) %collective-permute-start.7) | collective-permute-done | bytes 131104 | tf_op jit(solution)/shard_map/ppermute | solution.py:24
  14.7 0.1 collective-permute-start.8
  14.7 1.1 %collective-permute-done = bf16[1,1,1,128,256]{4,3,0,2,1:T(8,128)(2,1)S(1)} collective-permute-done((bf16[1,1,1,128,256]{4,3,0,2,1:T(8,128)(2,1)S(1)}, bf16[1,1,1,128,256]{4,3,0,2,1:T(8,128)(2,1)S(1)}, u32[]{:S(2)}, u32[]{:S(2)}) %collective-permute-start) | collective-permute-done | bytes 65568 | tf_op jit(solution)/shard_map/ppermute | solution.py:24
  15.9 1.0 %collective-permute-start.1 = (bf16[2,1,1,128,256]{4,3,0,2,1:T(8,128)(2,1)S(1)}, bf16[2,1,1,128,256]{4,3,0,2,1:T(8,128)(2,1)S(1)}, u32[]{:S(2)}, u32[]{:S(2)}) collective-permute-start(bf16[2,1,1,128,256]{4,3,0,2,1:T(8,128)(2,1)S(1)} %maximum_select_fusion.6), channel_id=1, source_target_pairs={{0,8},{4,12},{8,0},{12,4},{16,24},{20,28},{24,16},{28,20},{1,9},{5... | collective-permute-start | bytes 393224 | tf_op jit(solution)/shard_map/ppermute | solution.py:24
  16.9 7.0 %collective-permute-done.8 = bf16[2,1,1,2,128,256]{5,4,3,2,1,0:T(8,128)(2,1)S(1)} collective-permute-done((bf16[2,1,1,2,128,256]{5,4,3,2,1,0:T(8,128)(2,1)S(1)}, bf16[2,1,1,2,128,256]{5,4,3,2,1,0:T(8,128)(2,1)S(1)}, u32[]{:S(2)}, u32[]{:S(2)}) %collective-permute-start.8) | collective-permute-done | bytes 262176 | tf_op jit(solution)/shard_map/ppermute | solution.py:24
  24.0 1.6 %collective-permute-start.9 = (bf16[2,2,1,2,128,256]{5,4,3,2,1,0:T(8,128)(2,1)S(1)}, bf16[2,2,1,2,128,256]{5,4,3,2,1,0:T(8,128)(2,1)S(1)}, u32[]{:S(2)}, u32[]{:S(2)}) collective-permute-start(bf16[2,2,1,2,128,256]{5,4,3,2,1,0:T(8,128)(2,1)S(1)} %maximum_select_fusion.2), channel_id=1, source_target_pairs={{0,4},{4,0},{8,12},{12,8},{16,20},{20,16},{24,28},{28,24},{1,5},{5... | collective-permute-start | bytes 1572872 | tf_op jit(solution)/shard_map/ppermute | solution.py:24
  25.5 0.0 collective-permute-done.1
  25.5 1.5 %collective-permute-start.2 = (bf16[2,2,1,128,256]{4,3,0,2,1:T(8,128)(2,1)S(1)}, bf16[2,2,1,128,256]{4,3,0,2,1:T(8,128)(2,1)S(1)}, u32[]{:S(2)}, u32[]{:S(2)}) collective-permute-start(bf16[2,2,1,128,256]{4,3,0,2,1:T(8,128)(2,1)S(1)} %maximum_select_fusion.3), channel_id=1, source_target_pairs={{0,4},{4,0},{8,12},{12,8},{16,20},{20,16},{24,28},{28,24},{1,5},{5... | collective-permute-start | bytes 786440 | tf_op jit(solution)/shard_map/ppermute | solution.py:24
  27.1 14.1 %collective-permute-done.2 = bf16[2,2,1,128,256]{4,3,0,2,1:T(8,128)(2,1)S(1)} collective-permute-done((bf16[2,2,1,128,256]{4,3,0,2,1:T(8,128)(2,1)S(1)}, bf16[2,2,1,128,256]{4,3,0,2,1:T(8,128)(2,1)S(1)}, u32[]{:S(2)}, u32[]{:S(2)}) %collective-permute-start.2) | collective-permute-done | bytes 262176 | tf_op jit(solution)/shard_map/ppermute | solution.py:24
  41.3 1.6 %collective-permute-start.4 = (bf16[1024,256]{1,0:T(8,128)(2,1)S(1)}, bf16[1024,256]{1,0:T(8,128)(2,1)S(1)}, u32[]{:S(2)}, u32[]{:S(2)}) collective-permute-start(bf16[1024,256]{1,0:T(8,128)(2,1)S(1)} %bitcast.23), channel_id=1, source_target_pairs={{0,2},{1,3},{2,0},{3,1},{4,6},{5,7},{6,4},{7,5},{8,10},{9,11},{10,... | collective-permute-start | bytes 1572872 | tf_op jit(solution)/shard_map/ppermute | solution.py:39
  42.8 0.0 collective-permute-start.3
  42.9 0.0 collective-permute-done.9
  42.9 0.1 maximum_select_fusion
  43.0 0.0 copy-start
  43.0 0.1 fusion.4
  43.1 0.6 collective-permute-start.10
  43.6 0.1 collective-permute-start.11
  43.7 8.3 %collective-permute-done.4.rest_2_ = bf16[1024,256]{1,0:T(8,128)(2,1)S(1)} collective-permute-done((bf16[1024,256]{1,0:T(8,128)(2,1)S(1)}, bf16[1024,256]{1,0:T(8,128)(2,1)S(1)}, u32[]{:S(2)}, u32[]{:S(2)}) %collective-permute-start.4) | collective-permute-done | bytes 524320 | tf_op jit(solution)/shard_map/ppermute | solution.py:39
  52.0 0.0 collective-permute-start.5
  52.0 0.0 copy-start.1
  52.0 0.0 copy-start.2
  52.0 0.1 pad_add_fusion.qb_ref
  52.1 0.0 collective-permute-done.3.rest_1_
  52.1 0.0 collective-permute-done.10.rest_5_
  52.1 0.0 collective-permute-done.11.rest_7_
  52.1 1.9 %collective-permute-done.5.rest_3_ = bf16[1024,256]{1,0:T(8,128)(2,1)} collective-permute-done((bf16[1024,256]{1,0:T(8,128)(2,1)S(1)}, bf16[1024,256]{1,0:T(8,128)(2,1)}, u32[]{:S(2)}, u32[]{:S(2)}) %collective-permute-start.5) | collective-permute-done | bytes 524320 | tf_op jit(solution)/shard_map/ppermute | solution.py:39
  54.0 0.0 copy-done
  54.0 0.0 copy-done.1
  54.0 0.0 copy-done.2
  54.1 17.8 %shard_map.55 = bf16[256,512]{1,0:T(8,128)(2,1)} custom-call(s32[8,32]{1,0:T(8,128)S(1)} %copy-done.1, s32[8]{0:T(128)S(1)} %copy-done.2, s32[2]{0:T(128)S(1)} %pad_add_fusion.qb_ref, bf16[1024,512]{1,0:T(8,128)(2,1)S(1)} %copy-done, bf16[1024,256]{1,0:T(8,128)(2,1)S(1)} %bitcast.25, bf16[1024,256]{1,0:T(8,128)(2,1)} %collective-permute-done.3.rest_1_, ...), custom_call_target="tpu_custom_call" | custom-call | tf_op jit(solution)/shard_map/pallas_call | solution.py:190
  (11 shorter events, 0.3 us)
Async XLA Ops:
  0.0 0.9 %copy-start.3 = (bf16[256,128]{1,0:T(8,128)(2,1)S(1)}, bf16[256,128]{1,0:T(8,128)(2,1)}, u32[]{:S(2)}) copy-start(bf16[256,128]{1,0:T(8,128)(2,1)} %param.7) | copy-start | bytes 196612
  1.0 4.3 %collective-permute-start.6 = (bf16[128,256]{1,0:T(8,128)(2,1)S(1)}, bf16[128,256]{1,0:T(8,128)(2,1)S(1)}, u32[]{:S(2)}, u32[]{:S(2)}) collective-permute-start(bf16[128,256]{1,0:T(8,128)(2,1)S(1)} %get-tuple-element.11), channel_id=1, source_target_pairs={{0,2},{1,3},{2,0},{3,1},{4,6},{5,7},{6,4},{7,5},{8,10},{9,11},{10,... | collective-permute-start | bytes 196616 | tf_op jit(solution)/shard_map/ppermute | solution.py:170
  5.3 9.3 %collective-permute-start.7 = (bf16[1,1,1,2,128,256]{5,4,3,2,1,0:T(8,128)(2,1)S(1)}, bf16[1,1,1,2,128,256]{5,4,3,2,1,0:T(8,128)(2,1)S(1)}, u32[]{:S(2)}, u32[]{:S(2)}) collective-permute-start(bf16[1,1,1,2,128,256]{5,4,3,2,1,0:T(8,128)(2,1)S(1)} %get-tuple-element.7), channel_id=1, source_target_pairs={{0,16},{4,20},{8,24},{12,28},{16,0},{20,4},{24,8},{28,12},{1,17},{... | collective-permute-start | bytes 393224 | tf_op jit(solution)/shard_map/ppermute | solution.py:24
  5.7 10.2 %collective-permute-start = (bf16[1,1,1,128,256]{4,3,0,2,1:T(8,128)(2,1)S(1)}, bf16[1,1,1,128,256]{4,3,0,2,1:T(8,128)(2,1)S(1)}, u32[]{:S(2)}, u32[]{:S(2)}) collective-permute-start(bf16[1,1,1,128,256]{4,3,0,2,1:T(8,128)(2,1)S(1)} %get-tuple-element.12), channel_id=1, source_target_pairs={{0,16},{4,20},{8,24},{12,28},{16,0},{20,4},{24,8},{28,12},{1,17},{... | collective-permute-start | bytes 196616 | tf_op jit(solution)/shard_map/ppermute | solution.py:24
  14.7 9.2 %collective-permute-start.8 = (bf16[2,1,1,2,128,256]{5,4,3,2,1,0:T(8,128)(2,1)S(1)}, bf16[2,1,1,2,128,256]{5,4,3,2,1,0:T(8,128)(2,1)S(1)}, u32[]{:S(2)}, u32[]{:S(2)}) collective-permute-start(bf16[2,1,1,2,128,256]{5,4,3,2,1,0:T(8,128)(2,1)S(1)} %maximum_select_fusion.4), channel_id=1, source_target_pairs={{0,8},{4,12},{8,0},{12,4},{16,24},{20,28},{24,16},{28,20},{1,9},{5... | collective-permute-start | bytes 786440 | tf_op jit(solution)/shard_map/ppermute | solution.py:24
  15.9 9.6 %collective-permute-start.1 = (bf16[2,1,1,128,256]{4,3,0,2,1:T(8,128)(2,1)S(1)}, bf16[2,1,1,128,256]{4,3,0,2,1:T(8,128)(2,1)S(1)}, u32[]{:S(2)}, u32[]{:S(2)}) collective-permute-start(bf16[2,1,1,128,256]{4,3,0,2,1:T(8,128)(2,1)S(1)} %maximum_select_fusion.6), channel_id=1, source_target_pairs={{0,8},{4,12},{8,0},{12,4},{16,24},{20,28},{24,16},{28,20},{1,9},{5... | collective-permute-start | bytes 393224 | tf_op jit(solution)/shard_map/ppermute | solution.py:24
  24.0 18.9 %collective-permute-start.9 = (bf16[2,2,1,2,128,256]{5,4,3,2,1,0:T(8,128)(2,1)S(1)}, bf16[2,2,1,2,128,256]{5,4,3,2,1,0:T(8,128)(2,1)S(1)}, u32[]{:S(2)}, u32[]{:S(2)}) collective-permute-start(bf16[2,2,1,2,128,256]{5,4,3,2,1,0:T(8,128)(2,1)S(1)} %maximum_select_fusion.2), channel_id=1, source_target_pairs={{0,4},{4,0},{8,12},{12,8},{16,20},{20,16},{24,28},{28,24},{1,5},{5... | collective-permute-start | bytes 1572872 | tf_op jit(solution)/shard_map/ppermute | solution.py:24
  25.5 15.6 %collective-permute-start.2 = (bf16[2,2,1,128,256]{4,3,0,2,1:T(8,128)(2,1)S(1)}, bf16[2,2,1,128,256]{4,3,0,2,1:T(8,128)(2,1)S(1)}, u32[]{:S(2)}, u32[]{:S(2)}) collective-permute-start(bf16[2,2,1,128,256]{4,3,0,2,1:T(8,128)(2,1)S(1)} %maximum_select_fusion.3), channel_id=1, source_target_pairs={{0,4},{4,0},{8,12},{12,8},{16,20},{20,16},{24,28},{28,24},{1,5},{5... | collective-permute-start | bytes 786440 | tf_op jit(solution)/shard_map/ppermute | solution.py:24
  41.3 10.7 %collective-permute-start.4 = (bf16[1024,256]{1,0:T(8,128)(2,1)S(1)}, bf16[1024,256]{1,0:T(8,128)(2,1)S(1)}, u32[]{:S(2)}, u32[]{:S(2)}) collective-permute-start(bf16[1024,256]{1,0:T(8,128)(2,1)S(1)} %bitcast.23), channel_id=1, source_target_pairs={{0,2},{1,3},{2,0},{3,1},{4,6},{5,7},{6,4},{7,5},{8,10},{9,11},{10,... | collective-permute-start | bytes 1572872 | tf_op jit(solution)/shard_map/ppermute | solution.py:39
  42.8 9.2 %collective-permute-start.3 = (bf16[1024,256]{1,0:T(8,128)(2,1)S(1)}, bf16[1024,256]{1,0:T(8,128)(2,1)}, u32[]{:S(2)}, u32[]{:S(2)}) collective-permute-start(bf16[1024,256]{1,0:T(8,128)(2,1)S(1)} %bitcast.24), channel_id=1, source_target_pairs={{0,1},{1,0},{2,3},{3,2},{4,5},{5,4},{6,7},{7,6},{8,9},{9,8},{10,11... | collective-permute-start | bytes 1572872 | tf_op jit(solution)/shard_map/ppermute | solution.py:39
  43.0 11.1 %copy-start = (bf16[1024,512]{1,0:T(8,128)(2,1)S(1)}, bf16[1024,512]{1,0:T(8,128)(2,1)}, u32[]{:S(2)}) copy-start(bf16[1024,512]{1,0:T(8,128)(2,1)} %q_ref.1) | copy-start | bytes 3145732
  43.1 9.0 %collective-permute-start.10 = (bf16[1024,256]{1,0:T(8,128)(2,1)S(1)}, bf16[1024,256]{1,0:T(8,128)(2,1)}, u32[]{:S(2)}, u32[]{:S(2)}) collective-permute-start(bf16[1024,256]{1,0:T(8,128)(2,1)S(1)} %bitcast.28), channel_id=1, source_target_pairs={{0,1},{1,0},{2,3},{3,2},{4,5},{5,4},{6,7},{7,6},{8,9},{9,8},{10,11... | collective-permute-start | bytes 1572872 | tf_op jit(solution)/shard_map/ppermute | solution.py:176
  43.6 8.5 %collective-permute-start.11 = (bf16[1024,256]{1,0:T(8,128)(2,1)S(1)}, bf16[1024,256]{1,0:T(8,128)(2,1)}, u32[]{:S(2)}, u32[]{:S(2)}) collective-permute-start(bf16[1024,256]{1,0:T(8,128)(2,1)S(1)} %bitcast.26), channel_id=1, source_target_pairs={{0,1},{1,0},{2,3},{3,2},{4,5},{5,4},{6,7},{7,6},{8,9},{9,8},{10,11... | collective-permute-start | bytes 1572872 | tf_op jit(solution)/shard_map/ppermute | solution.py:176
  52.0 2.0 %collective-permute-start.5 = (bf16[1024,256]{1,0:T(8,128)(2,1)S(1)}, bf16[1024,256]{1,0:T(8,128)(2,1)}, u32[]{:S(2)}, u32[]{:S(2)}) collective-permute-start(bf16[1024,256]{1,0:T(8,128)(2,1)S(1)} %collective-permute-done.4.rest_2_), channel_id=1, source_target_pairs={{0,1},{1,0},{2,3},{3,2},{4,5},{5,4},{6,7},{7,6},{8,9},{9,8},{10,11... | collective-permute-start | bytes 1572872 | tf_op jit(solution)/shard_map/ppermute | solution.py:39
  52.0 2.0 %copy-start.1 = (s32[8,32]{1,0:T(8,128)S(1)}, s32[8,32]{1,0:T(8,128)}, u32[]{:S(2)}) copy-start(s32[8,32]{1,0:T(8,128)} %bl_ref.1) | copy-start | bytes 3076
  52.0 2.0 %copy-start.2 = (s32[8]{0:T(128)S(1)}, s32[8]{0:T(128)}, u32[]{:S(2)}) copy-start(s32[8]{0:T(128)} %cnt_ref.1) | copy-start | bytes 100

commit v16 on v15

--- a/solution.py
+++ b/solution.py
@@ -161,14 +161,18 @@
     kv_local = jnp.concatenate([key_cache, value_cache], axis=1)
     n_half = kv_local.shape[0] // BLK
     kv_pieces = []
+    shard = None
     for h in range(n_half):
         part = kv_local[h * BLK:(h + 1) * BLK]
         if h % 2 == 0:
-            kv_pieces += pieces_axis(gather_axis(part, "pb", n_pb), "ka", n_ka)
+            shard = gather_axis(part, "pb", n_pb)
             continue
         b = n_ka // 2
         across = lax.ppermute(part, "ka", [(i, i ^ b) for i in range(n_ka)])
-        both = gather_axis(jnp.stack([part, across]), "pb", n_pb).reshape(n_pb, 2, BLK, part.shape[1])
+        pair, shard = lax.optimization_barrier((jnp.stack([part, across]), shard))
+        kv_pieces += pieces_axis(shard, "ka", n_ka)
+        shard = None
+        both = gather_axis(pair, "pb", n_pb).reshape(n_pb, 2, BLK, part.shape[1])
         held = {0: both[:, 0].reshape(-1, part.shape[1]), b: both[:, 1].reshape(-1, part.shape[1])}
         step = b // 2
         while step >= 1:
@@ -176,6 +180,8 @@
                 held[x | step] = lax.ppermute(held[x], "ka", [(i, i ^ step) for i in range(n_ka)])
             step //= 2
         kv_pieces += [held[x] for x in range(n_ka)]
+    if shard is not None:
+        kv_pieces += pieces_axis(shard, "ka", n_ka)
 
     p = lax.axis_index("pb")
     k = lax.axis_index("ka")

time: 73 us -> 64.9 us (0.89)
  waiting for transfers between devices: 41.5 us -> 37.4 us
  starting transfers between devices: 10.9 us -> 7.4 us
    ppermute x3, waiting for transfers between devices: 10.2 us -> 2.7 us  [pieces_axis(): lax.ppermute(idx_pieces[x], axis, [(i, i ^ b) for i in range(n)])]
    ppermute x6, starting transfers between devices: 7.12 us -> 3.73 us  [gather_axis(): other = lax.ppermute(held, axis, [(i, i ^ b) for i in range(n)])]
    ppermute x2, waiting for transfers between devices: 0.01 us -> 2.19 us  [shards(): lax.ppermute(held[x], 'ka', [(i, i ^ step) for i in range(n_ka)])]
    ppermute x6, waiting for transfers between devices: 28.5 us -> 29.8 us  [gather_axis(): other = lax.ppermute(held, axis, [(i, i ^ b) for i in range(n)])]
  transfers between devices with their start and end apart: 12 -> 12, of which waited for: 7 -> 10; matrix products, arithmetic and copies ran while one was open for 1% -> 1% of each run, Pallas kernels for 0% -> 0%
where the time goes in v16:
time: 64.9 us; the launch traced here: 64.4 us
  waiting for transfers between devices  37.4 us (58%)
  Pallas kernels  17.8 us (27%)
  starting transfers between devices  7.4 us (11%)
  local copies, waits for them, and re-layouts  1.06 us (2%)
    ppermute x6, waiting for transfers between devices, gather_axis(): other = lax.ppermute(held, axis, [(i, i ^ b) for i in range(n)])  29.8 us
    pallas_call x1, Pallas kernels, shards(): pl.pallas_call(kernel, out_shape=jax.ShapeDtypeStruct((rows_mine, queries...  17.8 us
    ppermute x6, starting transfers between devices, gather_axis(): other = lax.ppermute(held, axis, [(i, i ^ b) for i in range(n)])  3.73 us
    ppermute x1, waiting for transfers between devices, shards(): across = lax.ppermute(part, 'ka', [(i, i ^ b) for i in range(n_ka)])  2.75 us
    ppermute x3, waiting for transfers between devices, pieces_axis(): lax.ppermute(idx_pieces[x], axis, [(i, i ^ b) for i in range(n)])  2.7 us
    ppermute x2, waiting for transfers between devices, shards(): lax.ppermute(held[x], 'ka', [(i, i ^ step) for i in range(n_ka)])  2.19 us
    ppermute x3, starting transfers between devices, pieces_axis(): lax.ppermute(idx_pieces[x], axis, [(i, i ^ b) for i in range(n)])  1.59 us
    ppermute x1, starting transfers between devices, shards(): across = lax.ppermute(part, 'ka', [(i, i ^ b) for i in range(n_ka)])  1.52 us
  transfers between devices with their start and end apart: 12, of which 10 were waited for; matrix products, arithmetic and copies ran while one was open for 1% of the time, Pallas kernels for 0%

profile of v16, /device:TPU:24, one launch (start us, length us, event | category | flops | bytes accessed | tf_op | source)
XLA Modules:
  0.0 64.4 jit_solution(1367801485695787119)
XLA Ops:
  0.0 0.0 copy-start.3
  0.0 0.9 %constant_dynamic-update-slice_fusion.1 = bf16[256,256]{1,0:T(8,128)(2,1)S(1)} fusion(bf16[256,128]{1,0:T(8,128)(2,1)} %param.6), kind=kLoop, calls=%fused_computation.14 | loop fusion | bytes 131072
  0.9 0.0 copy-done.3
  1.0 0.4 collective-permute-start.1
  1.4 5.7 %collective-permute-done.1 = bf16[1,1,1,128,256]{4,3,0,2,1:T(8,128)(2,1)S(1)} collective-permute-done((bf16[1,1,1,128,256]{4,3,0,2,1:T(8,128)(2,1)S(1)}, bf16[1,1,1,128,256]{4,3,0,2,1:T(8,128)(2,1)S(1)}, u32[]{:S(2)}, u32[]{:S(2)}) %collective-permute-start.1) | collective-permute-done | bytes 65568 | tf_op jit(solution)/shard_map/ppermute | solution.py:24
  7.1 0.1 collective-permute-start.2
  7.2 5.0 %collective-permute-done.2 = bf16[2,1,1,128,256]{4,3,0,2,1:T(8,128)(2,1)S(1)} collective-permute-done((bf16[2,1,1,128,256]{4,3,0,2,1:T(8,128)(2,1)S(1)}, bf16[2,1,1,128,256]{4,3,0,2,1:T(8,128)(2,1)S(1)}, u32[]{:S(2)}, u32[]{:S(2)}) %collective-permute-start.2) | collective-permute-done | bytes 131104 | tf_op jit(solution)/shard_map/ppermute | solution.py:24
  12.2 1.6 %collective-permute-start.3 = (bf16[2,2,1,128,256]{4,3,0,2,1:T(8,128)(2,1)S(1)}, bf16[2,2,1,128,256]{4,3,0,2,1:T(8,128)(2,1)S(1)}, u32[]{:S(2)}, u32[]{:S(2)}) collective-permute-start(bf16[2,2,1,128,256]{4,3,0,2,1:T(8,128)(2,1)S(1)} %maximum_select_fusion.3), channel_id=1, source_target_pairs={{0,4},{4,0},{8,12},{12,8},{16,20},{20,16},{24,28},{28,24},{1,5},{5... | collective-permute-start | bytes 786440 | tf_op jit(solution)/shard_map/ppermute | solution.py:24
  13.8 1.5 %collective-permute-start = (bf16[128,256]{1,0:T(8,128)(2,1)S(1)}, bf16[128,256]{1,0:T(8,128)(2,1)S(1)}, u32[]{:S(2)}, u32[]{:S(2)}) collective-permute-start(bf16[128,256]{1,0:T(8,128)(2,1)S(1)} %get-tuple-element.14), channel_id=1, source_target_pairs={{0,2},{1,3},{2,0},{3,1},{4,6},{5,7},{6,4},{7,5},{8,10},{9,11},{10,... | collective-permute-start | bytes 196616 | tf_op jit(solution)/shard_map/ppermute | solution.py:171
  15.3 2.7 %collective-permute-done = bf16[128,256]{1,0:T(8,128)(2,1)S(1)} collective-permute-done((bf16[128,256]{1,0:T(8,128)(2,1)S(1)}, bf16[128,256]{1,0:T(8,128)(2,1)S(1)}, u32[]{:S(2)}, u32[]{:S(2)}) %collective-permute-start) | collective-permute-done | bytes 65568 | tf_op jit(solution)/shard_map/ppermute | solution.py:171
  18.1 1.3 %collective-permute-done.3 = bf16[2,2,1,128,256]{4,3,0,2,1:T(8,128)(2,1)S(1)} collective-permute-done((bf16[2,2,1,128,256]{4,3,0,2,1:T(8,128)(2,1)S(1)}, bf16[2,2,1,128,256]{4,3,0,2,1:T(8,128)(2,1)S(1)}, u32[]{:S(2)}, u32[]{:S(2)}) %collective-permute-start.3) | collective-permute-done | bytes 262176 | tf_op jit(solution)/shard_map/ppermute | solution.py:24
  19.4 0.1 collective-permute-start.7
  19.5 7.3 %collective-permute-done.7 = bf16[1,1,1,2,128,256]{5,4,3,2,1,0:T(8,128)(2,1)S(1)} collective-permute-done((bf16[1,1,1,2,128,256]{5,4,3,2,1,0:T(8,128)(2,1)S(1)}, bf16[1,1,1,2,128,256]{5,4,3,2,1,0:T(8,128)(2,1)S(1)}, u32[]{:S(2)}, u32[]{:S(2)}) %collective-permute-start.7) | collective-permute-done | bytes 131104 | tf_op jit(solution)/shard_map/ppermute | solution.py:24
  26.9 0.1 collective-permute-start.8
  26.9 1.6 %collective-permute-start.5 = (bf16[1024,256]{1,0:T(8,128)(2,1)S(1)}, bf16[1024,256]{1,0:T(8,128)(2,1)S(1)}, u32[]{:S(2)}, u32[]{:S(2)}) collective-permute-start(bf16[1024,256]{1,0:T(8,128)(2,1)S(1)} %bitcast.21), channel_id=1, source_target_pairs={{0,2},{1,3},{2,0},{3,1},{4,6},{5,7},{6,4},{7,5},{8,10},{9,11},{10,... | collective-permute-start | bytes 1572872 | tf_op jit(solution)/shard_map/ppermute | solution.py:39
  28.5 4.7 %collective-permute-done.8 = bf16[2,1,1,2,128,256]{5,4,3,2,1,0:T(8,128)(2,1)S(1)} collective-permute-done((bf16[2,1,1,2,128,256]{5,4,3,2,1,0:T(8,128)(2,1)S(1)}, bf16[2,1,1,2,128,256]{5,4,3,2,1,0:T(8,128)(2,1)S(1)}, u32[]{:S(2)}, u32[]{:S(2)}) %collective-permute-start.8) | collective-permute-done | bytes 262176 | tf_op jit(solution)/shard_map/ppermute | solution.py:24
  33.3 1.6 %collective-permute-start.9 = (bf16[2,2,1,2,128,256]{5,4,3,2,1,0:T(8,128)(2,1)S(1)}, bf16[2,2,1,2,128,256]{5,4,3,2,1,0:T(8,128)(2,1)S(1)}, u32[]{:S(2)}, u32[]{:S(2)}) collective-permute-start(bf16[2,2,1,2,128,256]{5,4,3,2,1,0:T(8,128)(2,1)S(1)} %maximum_select_fusion.2), channel_id=1, source_target_pairs={{0,4},{4,0},{8,12},{12,8},{16,20},{20,16},{24,28},{28,24},{1,5},{5... | collective-permute-start | bytes 1572872 | tf_op jit(solution)/shard_map/ppermute | solution.py:24
  34.9 0.0 collective-permute-start.4
  34.9 2.7 %collective-permute-done.5.rest_2_ = bf16[1024,256]{1,0:T(8,128)(2,1)S(1)} collective-permute-done((bf16[1024,256]{1,0:T(8,128)(2,1)S(1)}, bf16[1024,256]{1,0:T(8,128)(2,1)S(1)}, u32[]{:S(2)}, u32[]{:S(2)}) %collective-permute-start.5) | collective-permute-done | bytes 524320 | tf_op jit(solution)/shard_map/ppermute | solution.py:39
  37.6 0.0 collective-permute-start.6
  37.6 5.7 %collective-permute-done.9 = bf16[2,2,1,2,128,256]{5,4,3,2,1,0:T(8,128)(2,1)S(1)} collective-permute-done((bf16[2,2,1,2,128,256]{5,4,3,2,1,0:T(8,128)(2,1)S(1)}, bf16[2,2,1,2,128,256]{5,4,3,2,1,0:T(8,128)(2,1)S(1)}, u32[]{:S(2)}, u32[]{:S(2)}) %collective-permute-start.9) | collective-permute-done | bytes 524320 | tf_op jit(solution)/shard_map/ppermute | solution.py:24
  43.4 0.1 maximum_select_fusion
  43.5 0.0 copy-start
  43.5 0.1 fusion.2
  43.6 0.1 collective-permute-start.10
  43.6 0.5 collective-permute-start.11
  44.1 0.0 copy-start.1
  44.1 0.0 copy-start.2
  44.1 0.1 pad_add_fusion.qb_ref
  44.2 0.0 collective-permute-done.4.rest_1_
  44.2 0.0 collective-permute-done.6.rest_3_
  44.2 1.4 %collective-permute-done.10.rest_5_ = bf16[1024,256]{1,0:T(8,128)(2,1)} collective-permute-done((bf16[1024,256]{1,0:T(8,128)(2,1)S(1)}, bf16[1024,256]{1,0:T(8,128)(2,1)}, u32[]{:S(2)}, u32[]{:S(2)}) %collective-permute-start.10) | collective-permute-done | bytes 524320 | tf_op jit(solution)/shard_map/ppermute | solution.py:180
  45.7 0.7 %collective-permute-done.11.rest_7_ = bf16[1024,256]{1,0:T(8,128)(2,1)} collective-permute-done((bf16[1024,256]{1,0:T(8,128)(2,1)S(1)}, bf16[1024,256]{1,0:T(8,128)(2,1)}, u32[]{:S(2)}, u32[]{:S(2)}) %collective-permute-start.11) | collective-permute-done | bytes 524320 | tf_op jit(solution)/shard_map/ppermute | solution.py:180
  46.4 0.0 copy-done
  46.4 0.0 copy-done.1
  46.4 0.0 copy-done.2
  46.4 17.8 %shard_map.55 = bf16[256,512]{1,0:T(8,128)(2,1)} custom-call(s32[8,32]{1,0:T(8,128)S(1)} %copy-done.1, s32[8]{0:T(128)S(1)} %copy-done.2, s32[2]{0:T(128)S(1)} %pad_add_fusion.qb_ref, bf16[1024,512]{1,0:T(8,128)(2,1)S(1)} %copy-done, bf16[1024,256]{1,0:T(8,128)(2,1)S(1)} %bitcast.23, bf16[1024,256]{1,0:T(8,128)(2,1)} %collective-permute-done.4.rest_1_, ...), custom_call_target="tpu_custom_call" | custom-call | tf_op jit(solution)/shard_map/pallas_call | solution.py:196
  (11 shorter events, 0.3 us)
Async XLA Ops:
  0.0 0.9 %copy-start.3 = (bf16[256,128]{1,0:T(8,128)(2,1)S(1)}, bf16[256,128]{1,0:T(8,128)(2,1)}, u32[]{:S(2)}) copy-start(bf16[256,128]{1,0:T(8,128)(2,1)} %param.7) | copy-start | bytes 196612
  1.0 6.1 %collective-permute-start.1 = (bf16[1,1,1,128,256]{4,3,0,2,1:T(8,128)(2,1)S(1)}, bf16[1,1,1,128,256]{4,3,0,2,1:T(8,128)(2,1)S(1)}, u32[]{:S(2)}, u32[]{:S(2)}) collective-permute-start(bf16[1,1,1,128,256]{4,3,0,2,1:T(8,128)(2,1)S(1)} %get-tuple-element.11), channel_id=1, source_target_pairs={{0,16},{4,20},{8,24},{12,28},{16,0},{20,4},{24,8},{28,12},{1,17},{... | collective-permute-start | bytes 196616 | tf_op jit(solution)/shard_map/ppermute | solution.py:24
  7.1 5.1 %collective-permute-start.2 = (bf16[2,1,1,128,256]{4,3,0,2,1:T(8,128)(2,1)S(1)}, bf16[2,1,1,128,256]{4,3,0,2,1:T(8,128)(2,1)S(1)}, u32[]{:S(2)}, u32[]{:S(2)}) collective-permute-start(bf16[2,1,1,128,256]{4,3,0,2,1:T(8,128)(2,1)S(1)} %maximum_select_fusion.6), channel_id=1, source_target_pairs={{0,8},{4,12},{8,0},{12,4},{16,24},{20,28},{24,16},{28,20},{1,9},{5... | collective-permute-start | bytes 393224 | tf_op jit(solution)/shard_map/ppermute | solution.py:24
  12.2 7.1 %collective-permute-start.3 = (bf16[2,2,1,128,256]{4,3,0,2,1:T(8,128)(2,1)S(1)}, bf16[2,2,1,128,256]{4,3,0,2,1:T(8,128)(2,1)S(1)}, u32[]{:S(2)}, u32[]{:S(2)}) collective-permute-start(bf16[2,2,1,128,256]{4,3,0,2,1:T(8,128)(2,1)S(1)} %maximum_select_fusion.3), channel_id=1, source_target_pairs={{0,4},{4,0},{8,12},{12,8},{16,20},{20,16},{24,28},{28,24},{1,5},{5... | collective-permute-start | bytes 786440 | tf_op jit(solution)/shard_map/ppermute | solution.py:24
  13.8 4.3 %collective-permute-start = (bf16[128,256]{1,0:T(8,128)(2,1)S(1)}, bf16[128,256]{1,0:T(8,128)(2,1)S(1)}, u32[]{:S(2)}, u32[]{:S(2)}) collective-permute-start(bf16[128,256]{1,0:T(8,128)(2,1)S(1)} %get-tuple-element.14), channel_id=1, source_target_pairs={{0,2},{1,3},{2,0},{3,1},{4,6},{5,7},{6,4},{7,5},{8,10},{9,11},{10,... | collective-permute-start | bytes 196616 | tf_op jit(solution)/shard_map/ppermute | solution.py:171
  19.4 7.4 %collective-permute-start.7 = (bf16[1,1,1,2,128,256]{5,4,3,2,1,0:T(8,128)(2,1)S(1)}, bf16[1,1,1,2,128,256]{5,4,3,2,1,0:T(8,128)(2,1)S(1)}, u32[]{:S(2)}, u32[]{:S(2)}) collective-permute-start(bf16[1,1,1,2,128,256]{5,4,3,2,1,0:T(8,128)(2,1)S(1)} %bitcast.29), channel_id=1, source_target_pairs={{0,16},{4,20},{8,24},{12,28},{16,0},{20,4},{24,8},{28,12},{1,17},{... | collective-permute-start | bytes 393224 | tf_op jit(solution)/shard_map/ppermute | solution.py:24
  26.9 6.4 %collective-permute-start.8 = (bf16[2,1,1,2,128,256]{5,4,3,2,1,0:T(8,128)(2,1)S(1)}, bf16[2,1,1,2,128,256]{5,4,3,2,1,0:T(8,128)(2,1)S(1)}, u32[]{:S(2)}, u32[]{:S(2)}) collective-permute-start(bf16[2,1,1,2,128,256]{5,4,3,2,1,0:T(8,128)(2,1)S(1)} %maximum_select_fusion.4), channel_id=1, source_target_pairs={{0,8},{4,12},{8,0},{12,4},{16,24},{20,28},{24,16},{28,20},{1,9},{5... | collective-permute-start | bytes 786440 | tf_op jit(solution)/shard_map/ppermute | solution.py:24
  26.9 10.7 %collective-permute-start.5 = (bf16[1024,256]{1,0:T(8,128)(2,1)S(1)}, bf16[1024,256]{1,0:T(8,128)(2,1)S(1)}, u32[]{:S(2)}, u32[]{:S(2)}) collective-permute-start(bf16[1024,256]{1,0:T(8,128)(2,1)S(1)} %bitcast.21), channel_id=1, source_target_pairs={{0,2},{1,3},{2,0},{3,1},{4,6},{5,7},{6,4},{7,5},{8,10},{9,11},{10,... | collective-permute-start | bytes 1572872 | tf_op jit(solution)/shard_map/ppermute | solution.py:39
  33.3 10.0 %collective-permute-start.9 = (bf16[2,2,1,2,128,256]{5,4,3,2,1,0:T(8,128)(2,1)S(1)}, bf16[2,2,1,2,128,256]{5,4,3,2,1,0:T(8,128)(2,1)S(1)}, u32[]{:S(2)}, u32[]{:S(2)}) collective-permute-start(bf16[2,2,1,2,128,256]{5,4,3,2,1,0:T(8,128)(2,1)S(1)} %maximum_select_fusion.2), channel_id=1, source_target_pairs={{0,4},{4,0},{8,12},{12,8},{16,20},{20,16},{24,28},{28,24},{1,5},{5... | collective-permute-start | bytes 1572872 | tf_op jit(solution)/shard_map/ppermute | solution.py:24
  34.9 9.3 %collective-permute-start.4 = (bf16[1024,256]{1,0:T(8,128)(2,1)S(1)}, bf16[1024,256]{1,0:T(8,128)(2,1)}, u32[]{:S(2)}, u32[]{:S(2)}) collective-permute-start(bf16[1024,256]{1,0:T(8,128)(2,1)S(1)} %bitcast.22), channel_id=1, source_target_pairs={{0,1},{1,0},{2,3},{3,2},{4,5},{5,4},{6,7},{7,6},{8,9},{9,8},{10,11... | collective-permute-start | bytes 1572872 | tf_op jit(solution)/shard_map/ppermute | solution.py:39
  37.6 6.6 %collective-permute-start.6 = (bf16[1024,256]{1,0:T(8,128)(2,1)S(1)}, bf16[1024,256]{1,0:T(8,128)(2,1)}, u32[]{:S(2)}, u32[]{:S(2)}) collective-permute-start(bf16[1024,256]{1,0:T(8,128)(2,1)S(1)} %collective-permute-done.5.rest_2_), channel_id=1, source_target_pairs={{0,1},{1,0},{2,3},{3,2},{4,5},{5,4},{6,7},{7,6},{8,9},{9,8},{10,11... | collective-permute-start | bytes 1572872 | tf_op jit(solution)/shard_map/ppermute | solution.py:39
  43.5 3.0 %copy-start = (bf16[1024,512]{1,0:T(8,128)(2,1)S(1)}, bf16[1024,512]{1,0:T(8,128)(2,1)}, u32[]{:S(2)}) copy-start(bf16[1024,512]{1,0:T(8,128)(2,1)} %q_ref.1) | copy-start | bytes 3145732
  43.6 2.1 %collective-permute-start.10 = (bf16[1024,256]{1,0:T(8,128)(2,1)S(1)}, bf16[1024,256]{1,0:T(8,128)(2,1)}, u32[]{:S(2)}, u32[]{:S(2)}) collective-permute-start(bf16[1024,256]{1,0:T(8,128)(2,1)S(1)} %bitcast.26), channel_id=1, source_target_pairs={{0,1},{1,0},{2,3},{3,2},{4,5},{5,4},{6,7},{7,6},{8,9},{9,8},{10,11... | collective-permute-start | bytes 1572872 | tf_op jit(solution)/shard_map/ppermute | solution.py:180
  43.6 2.8 %collective-permute-start.11 = (bf16[1024,256]{1,0:T(8,128)(2,1)S(1)}, bf16[1024,256]{1,0:T(8,128)(2,1)}, u32[]{:S(2)}, u32[]{:S(2)}) collective-permute-start(bf16[1024,256]{1,0:T(8,128)(2,1)S(1)} %bitcast.24), channel_id=1, source_target_pairs={{0,1},{1,0},{2,3},{3,2},{4,5},{5,4},{6,7},{7,6},{8,9},{9,8},{10,11... | collective-permute-start | bytes 1572872 | tf_op jit(solution)/shard_map/ppermute | solution.py:180
  44.1 2.3 %copy-start.1 = (s32[8,32]{1,0:T(8,128)S(1)}, s32[8,32]{1,0:T(8,128)}, u32[]{:S(2)}) copy-start(s32[8,32]{1,0:T(8,128)} %bl_ref.1) | copy-start | bytes 3076
  44.1 2.3 %copy-start.2 = (s32[8]{0:T(128)S(1)}, s32[8]{0:T(128)}, u32[]{:S(2)}) copy-start(s32[8]{0:T(128)} %cnt_ref.1) | copy-start | bytes 100

commit v17 on v16

--- a/solution.py
+++ b/solution.py
@@ -41,9 +41,13 @@
     return [idx_pieces[x] for x in range(n)]
 
 
-def attend_kernel(bl_ref, cnt_ref, qb_ref, q_ref, *rest, n_local, n_pieces, n_ka, group, scale):
-    kv_pieces = rest[:n_pieces]
-    out_ref, off_ref, kvbuf, dbuf, sems, dsems = rest[n_pieces:]
+def attend_kernel(bl_ref, cnt_ref, qb_ref, q_ref, *rest, n_local, sources, n_ka, group, scale):
+    n_pieces = len(sources)
+    n_direct = sum(1 for kind, _ in sources if kind == 0)
+    direct = rest[:n_direct]
+    fwd = rest[n_direct]
+    out_ref, off_ref, kvbuf, dbuf, sems, dsems = rest[n_direct + 1:]
+    kv_pieces = [direct[i] if kind == 0 else fwd.at[i] for kind, i in sources]
     qb0 = qb_ref[0]
     me = qb_ref[1]
     row0 = me * n_local
@@ -160,28 +164,40 @@
 def shards(queries, key_cache, value_cache, block_list, block_count, *, n_pb, n_ka):
     kv_local = jnp.concatenate([key_cache, value_cache], axis=1)
     n_half = kv_local.shape[0] // BLK
-    kv_pieces = []
+    halves = []
     shard = None
+    b = n_ka // 2
     for h in range(n_half):
         part = kv_local[h * BLK:(h + 1) * BLK]
         if h % 2 == 0:
             shard = gather_axis(part, "pb", n_pb)
             continue
-        b = n_ka // 2
         across = lax.ppermute(part, "ka", [(i, i ^ b) for i in range(n_ka)])
         pair, shard = lax.optimization_barrier((jnp.stack([part, across]), shard))
-        kv_pieces += pieces_axis(shard, "ka", n_ka)
+        halves.append({0: shard})
         shard = None
         both = gather_axis(pair, "pb", n_pb).reshape(n_pb, 2, BLK, part.shape[1])
-        held = {0: both[:, 0].reshape(-1, part.shape[1]), b: both[:, 1].reshape(-1, part.shape[1])}
-        step = b // 2
-        while step >= 1:
+        halves.append({0: both[:, 0].reshape(-1, part.shape[1]), b: both[:, 1].reshape(-1, part.shape[1])})
+    if shard is not None:
+        halves.append({0: shard})
+    for held in halves:
+        step = b
+        while step >= 2:
             for x in sorted(held):
-                held[x | step] = lax.ppermute(held[x], "ka", [(i, i ^ step) for i in range(n_ka)])
+                if x & step == 0 and (x | step) not in held:
+                    held[x | step] = lax.ppermute(held[x], "ka", [(i, i ^ step) for i in range(n_ka)])
             step //= 2
-        kv_pieces += [held[x] for x in range(n_ka)]
-    if shard is not None:
-        kv_pieces += pieces_axis(shard, "ka", n_ka)
+    order = [(h, x) for h in range(len(halves)) for x in sorted(halves[h])]
+    fwd = lax.ppermute(jnp.stack([halves[h][x] for h, x in order]), "ka", [(i, i ^ 1) for i in range(n_ka)])
+    direct = [halves[h][x] for h, x in order]
+    sources = []
+    for h in range(len(halves)):
+        for x in range(n_ka):
+            if x % 2 == 0:
+                sources.append((0, order.index((h, x))))
+            else:
+                sources.append((1, order.index((h, x - 1))))
+    kv_pieces = direct + [fwd]
 
     p = lax.axis_index("pb")
     k = lax.axis_index("ka")
@@ -191,7 +207,7 @@
     qb0 = jnp.stack([(p * n_ka + k) * n_local, k]).astype(jnp.int32)
 
     kernel = functools.partial(
-        attend_kernel, n_local=n_local, n_pieces=len(kv_pieces), n_ka=n_ka, group=16, scale=math.log2(math.e) / math.sqrt(HD)
+        attend_kernel, n_local=n_local, sources=tuple(sources), n_ka=n_ka, group=16, scale=math.log2(math.e) / math.sqrt(HD)
     )
     return pl.pallas_call(
         kernel,

time: 64.9 us -> 69.9 us (1.077)
  waiting for transfers between devices: 37.4 us -> 40.7 us
  other arithmetic: 0.39 us -> 1.98 us
  local copies, waits for them, and re-layouts: 1.06 us -> 1.86 us
    ppermute x6, waiting for transfers between devices: 29.8 us -> 32.5 us  [gather_axis(): other = lax.ppermute(held, axis, [(i, i ^ b) for i in range(n)])]
    ppermute x3 -> x1, waiting for transfers between devices: 2.7 us -> 4.42 us  [shards(): lax.ppermute(jnp.stack([halves[h][x] for h, x in order]), 'ka', [(i, i ^...]
    another operation x0 -> x1, other arithmetic: none -> 1.59 us  [shards(): jnp.stack([halves[h][x] for h, x in order])]
    ppermute x3 -> x1, starting transfers between devices: 1.59 us -> 0.01 us  [shards(): lax.ppermute(jnp.stack([halves[h][x] for h, x in order]), 'ka', [(i, i ^...]
    ppermute x2 -> x1, waiting for transfers between devices: 2.19 us -> 1.02 us  [shards(): lax.ppermute(held[x], 'ka', [(i, i ^ step) for i in range(n_ka)])]
    ppermute x2 -> x1, starting transfers between devices: 0.57 us -> 1.52 us  [shards(): lax.ppermute(held[x], 'ka', [(i, i ^ step) for i in range(n_ka)])]
    concatenate x1, local copies, waits for them, and re-layouts: 0.02 us -> 0.86 us  [shards(): kv_local = jnp.concatenate([key_cache, value_cache], axis=1)]
  transfers between devices with their start and end apart: 12 -> 9, of which waited for: 10 -> 9; matrix products, arithmetic and copies ran while one was open for 1% -> 0% of each run, Pallas kernels for 0% -> 0%
where the time goes in v17:
time: 69.9 us; the launch traced here: 69.5 us
  waiting for transfers between devices  40.7 us (58%)
  Pallas kernels  17.8 us (25%)
  starting transfers between devices  6.77 us (10%)
  other arithmetic  1.98 us (3%)
  local copies, waits for them, and re-layouts  1.86 us (3%)
    ppermute x6, waiting for transfers between devices, gather_axis(): other = lax.ppermute(held, axis, [(i, i ^ b) for i in range(n)])  32.5 us
    pallas_call x1, Pallas kernels, shards(): pl.pallas_call(kernel, out_shape=jax.ShapeDtypeStruct((rows_mine, queries...  17.8 us
    ppermute x1, waiting for transfers between devices, shards(): lax.ppermute(jnp.stack([halves[h][x] for h, x in order]), 'ka', [(i, i ^...  4.42 us
    ppermute x6, starting transfers between devices, gather_axis(): other = lax.ppermute(held, axis, [(i, i ^ b) for i in range(n)])  3.73 us
    ppermute x1, waiting for transfers between devices, shards(): across = lax.ppermute(part, 'ka', [(i, i ^ b) for i in range(n_ka)])  2.75 us
    another operation x1, other arithmetic, shards(): jnp.stack([halves[h][x] for h, x in order])  1.59 us
    ppermute x1, starting transfers between devices, shards(): across = lax.ppermute(part, 'ka', [(i, i ^ b) for i in range(n_ka)])  1.52 us
    ppermute x1, starting transfers between devices, shards(): lax.ppermute(held[x], 'ka', [(i, i ^ step) for i in range(n_ka)])  1.52 us
  transfers between devices with their start and end apart: 9, of which 9 were waited for; matrix products, arithmetic and copies ran while one was open for 0% of the time, Pallas kernels for 0%

profile of v17, /device:TPU:24, one launch (start us, length us, event | category | flops | bytes accessed | tf_op | source)
XLA Modules:
  0.0 69.5 jit_solution(3913029902056362803)
XLA Ops:
  0.0 0.9 %constant_dynamic-update-slice_fusion.1 = bf16[256,256]{1,0:T(8,128)(2,1)S(1)} fusion(bf16[256,128]{1,0:T(8,128)(2,1)} %param.6), kind=kLoop, calls=%fused_computation.15 | loop fusion | bytes 131072
  0.9 0.9 %constant_dynamic-update-slice_fusion = bf16[256,256]{1,0:T(8,128)(2,1)S(1)} fusion(bf16[256,256]{1,0:T(8,128)(2,1)S(1)} %constant_dynamic-update-slice_fusion.1, bf16[256,128]{1,0:T(8,128)(2,1)} %param.7), kind=kLoop, calls=%fused_computation.14 | loop fusion | bytes 131072 | tf_op jit(solution)/shard_map/concatenate | solution.py:165
  1.7 0.4 collective-permute-start.1
  2.1 5.7 %collective-permute-done.1 = bf16[1,1,1,128,256]{4,3,0,2,1:T(8,128)(2,1)S(1)} collective-permute-done((bf16[1,1,1,128,256]{4,3,0,2,1:T(8,128)(2,1)S(1)}, bf16[1,1,1,128,256]{4,3,0,2,1:T(8,128)(2,1)S(1)}, u32[]{:S(2)}, u32[]{:S(2)}) %collective-permute-start.1) | collective-permute-done | bytes 65568 | tf_op jit(solution)/shard_map/ppermute | solution.py:24
  7.8 0.1 collective-permute-start.2
  8.0 5.0 %collective-permute-done.2 = bf16[2,1,1,128,256]{4,3,0,2,1:T(8,128)(2,1)S(1)} collective-permute-done((bf16[2,1,1,128,256]{4,3,0,2,1:T(8,128)(2,1)S(1)}, bf16[2,1,1,128,256]{4,3,0,2,1:T(8,128)(2,1)S(1)}, u32[]{:S(2)}, u32[]{:S(2)}) %collective-permute-start.2) | collective-permute-done | bytes 131104 | tf_op jit(solution)/shard_map/ppermute | solution.py:24
  13.0 1.6 %collective-permute-start.3 = (bf16[2,2,1,128,256]{4,3,0,2,1:T(8,128)(2,1)S(1)}, bf16[2,2,1,128,256]{4,3,0,2,1:T(8,128)(2,1)S(1)}, u32[]{:S(2)}, u32[]{:S(2)}) collective-permute-start(bf16[2,2,1,128,256]{4,3,0,2,1:T(8,128)(2,1)S(1)} %maximum_select_fusion.3), channel_id=1, source_target_pairs={{0,4},{4,0},{8,12},{12,8},{16,20},{20,16},{24,28},{28,24},{1,5},{5... | collective-permute-start | bytes 786440 | tf_op jit(solution)/shard_map/ppermute | solution.py:24
  14.6 1.5 %collective-permute-start = (bf16[128,256]{1,0:T(8,128)(2,1)S(1)}, bf16[128,256]{1,0:T(8,128)(2,1)S(1)}, u32[]{:S(2)}, u32[]{:S(2)}) collective-permute-start(bf16[128,256]{1,0:T(8,128)(2,1)S(1)} %get-tuple-element.14), channel_id=1, source_target_pairs={{0,2},{1,3},{2,0},{3,1},{4,6},{5,7},{6,4},{7,5},{8,10},{9,11},{10,... | collective-permute-start | bytes 196616 | tf_op jit(solution)/shard_map/ppermute | solution.py:175
  16.1 2.7 %collective-permute-done = bf16[128,256]{1,0:T(8,128)(2,1)S(1)} collective-permute-done((bf16[128,256]{1,0:T(8,128)(2,1)S(1)}, bf16[128,256]{1,0:T(8,128)(2,1)S(1)}, u32[]{:S(2)}, u32[]{:S(2)}) %collective-permute-start) | collective-permute-done | bytes 65568 | tf_op jit(solution)/shard_map/ppermute | solution.py:175
  18.9 1.3 %collective-permute-done.3 = bf16[2,2,1,128,256]{4,3,0,2,1:T(8,128)(2,1)S(1)} collective-permute-done((bf16[2,2,1,128,256]{4,3,0,2,1:T(8,128)(2,1)S(1)}, bf16[2,2,1,128,256]{4,3,0,2,1:T(8,128)(2,1)S(1)}, u32[]{:S(2)}, u32[]{:S(2)}) %collective-permute-start.3) | collective-permute-done | bytes 262176 | tf_op jit(solution)/shard_map/ppermute | solution.py:24
  20.2 0.1 collective-permute-start.5
  20.3 7.3 %collective-permute-done.5 = bf16[1,1,1,2,128,256]{5,4,3,2,1,0:T(8,128)(2,1)S(1)} collective-permute-done((bf16[1,1,1,2,128,256]{5,4,3,2,1,0:T(8,128)(2,1)S(1)}, bf16[1,1,1,2,128,256]{5,4,3,2,1,0:T(8,128)(2,1)S(1)}, u32[]{:S(2)}, u32[]{:S(2)}) %collective-permute-start.5) | collective-permute-done | bytes 131104 | tf_op jit(solution)/shard_map/ppermute | solution.py:24
  27.6 0.1 collective-permute-start.6
  27.8 6.3 %collective-permute-done.6 = bf16[2,1,1,2,128,256]{5,4,3,2,1,0:T(8,128)(2,1)S(1)} collective-permute-done((bf16[2,1,1,2,128,256]{5,4,3,2,1,0:T(8,128)(2,1)S(1)}, bf16[2,1,1,2,128,256]{5,4,3,2,1,0:T(8,128)(2,1)S(1)}, u32[]{:S(2)}, u32[]{:S(2)}) %collective-permute-start.6) | collective-permute-done | bytes 262176 | tf_op jit(solution)/shard_map/ppermute | solution.py:24
  34.1 1.6 %collective-permute-start.7 = (bf16[2,2,1,2,128,256]{5,4,3,2,1,0:T(8,128)(2,1)S(1)}, bf16[2,2,1,2,128,256]{5,4,3,2,1,0:T(8,128)(2,1)S(1)}, u32[]{:S(2)}, u32[]{:S(2)}) collective-permute-start(bf16[2,2,1,2,128,256]{5,4,3,2,1,0:T(8,128)(2,1)S(1)} %maximum_select_fusion.2), channel_id=1, source_target_pairs={{0,4},{4,0},{8,12},{12,8},{16,20},{20,16},{24,28},{28,24},{1,5},{5... | collective-permute-start | bytes 1572872 | tf_op jit(solution)/shard_map/ppermute | solution.py:24
  35.7 1.5 %collective-permute-start.4 = (bf16[1024,256]{1,0:T(8,128)(2,1)S(1)}, bf16[1024,256]{1,0:T(8,128)(2,1)S(1)}, u32[]{:S(2)}, u32[]{:S(2)}) collective-permute-start(bf16[1024,256]{1,0:T(8,128)(2,1)S(1)} %bitcast.25), channel_id=1, source_target_pairs={{0,2},{1,3},{2,0},{3,1},{4,6},{5,7},{6,4},{7,5},{8,10},{9,11},{10,... | collective-permute-start | bytes 1572872 | tf_op jit(solution)/shard_map/ppermute | solution.py:188
  37.2 6.9 %collective-permute-done.7 = bf16[2,2,1,2,128,256]{5,4,3,2,1,0:T(8,128)(2,1)S(1)} collective-permute-done((bf16[2,2,1,2,128,256]{5,4,3,2,1,0:T(8,128)(2,1)S(1)}, bf16[2,2,1,2,128,256]{5,4,3,2,1,0:T(8,128)(2,1)S(1)}, u32[]{:S(2)}, u32[]{:S(2)}) %collective-permute-start.7) | collective-permute-done | bytes 524320 | tf_op jit(solution)/shard_map/ppermute | solution.py:24
  44.1 0.1 maximum_select_fusion
  44.2 0.1 fusion.2
  44.3 1.0 %collective-permute-done.4.rest_1_ = bf16[1024,256]{1,0:T(8,128)(2,1)S(1)} collective-permute-done((bf16[1024,256]{1,0:T(8,128)(2,1)S(1)}, bf16[1024,256]{1,0:T(8,128)(2,1)S(1)}, u32[]{:S(2)}, u32[]{:S(2)}) %collective-permute-start.4) | collective-permute-done | bytes 524320 | tf_op jit(solution)/shard_map/ppermute | solution.py:188
  45.4 0.0 copy-start
  45.4 0.0 copy-start.1
  45.4 0.0 copy-start.2
  45.4 1.6 %pad_maximum_fusion = bf16[4,1024,256]{2,1,0:T(8,128)(2,1)} fusion(bf16[1,1024,256]{2,1,0:T(8,128)(2,1)S(1)} %bitcast.28, bf16[1,1024,256]{2,1,0:T(8,128)(2,1)S(1)} %bitcast.30, bf16[1,1024,256]{2,1,0:T(8,128)(2,1)S(1)} %bitcast.32, bf16[1,1024,256]{2,1,0:T(8,128)(2,1)S(1)} %bitcast.26), kind=kLoop, calls=%fused_computation | loop fusion | flops 3145728 | bytes 4194304 | tf_op jit(solution)/shard_map/stack | solution.py:191
  47.0 0.0 collective-permute-start.8
  47.0 0.1 pad_add_fusion.qb_ref
  47.0 4.4 %collective-permute-done.8.rest_4_ = bf16[4,1024,256]{2,1,0:T(8,128)(2,1)} collective-permute-done((bf16[4,1024,256]{2,1,0:T(8,128)(2,1)}, bf16[4,1024,256]{2,1,0:T(8,128)(2,1)}, u32[]{:S(2)}, u32[]{:S(2)}) %collective-permute-start.8) | collective-permute-done | bytes 2097184 | tf_op jit(solution)/shard_map/ppermute | solution.py:191
  51.5 0.0 copy-done
  51.5 0.0 copy-done.1
  51.5 0.0 copy-done.2
  51.5 17.8 %shard_map.55 = bf16[256,512]{1,0:T(8,128)(2,1)} custom-call(s32[8,32]{1,0:T(8,128)S(1)} %copy-done.1, s32[8]{0:T(128)S(1)} %copy-done.2, s32[2]{0:T(128)S(1)} %pad_add_fusion.qb_ref, bf16[1024,512]{1,0:T(8,128)(2,1)S(1)} %copy-done, bf16[1024,256]{1,0:T(8,128)(2,1)S(1)} %bitcast.27, bf16[1024,256]{1,0:T(8,128)(2,1)S(1)} %collective-permute-done.4.rest_1_, ...), custom_call_target="tpu_custom_call" | custom-call | tf_op jit(solution)/shard_map/pallas_call | solution.py:212
  (10 shorter events, 0.3 us)
Async XLA Ops:
  1.7 6.1 %collective-permute-start.1 = (bf16[1,1,1,128,256]{4,3,0,2,1:T(8,128)(2,1)S(1)}, bf16[1,1,1,128,256]{4,3,0,2,1:T(8,128)(2,1)S(1)}, u32[]{:S(2)}, u32[]{:S(2)}) collective-permute-start(bf16[1,1,1,128,256]{4,3,0,2,1:T(8,128)(2,1)S(1)} %get-tuple-element.11), channel_id=1, source_target_pairs={{0,16},{4,20},{8,24},{12,28},{16,0},{20,4},{24,8},{28,12},{1,17},{... | collective-permute-start | bytes 196616 | tf_op jit(solution)/shard_map/ppermute | solution.py:24
  7.8 5.1 %collective-permute-start.2 = (bf16[2,1,1,128,256]{4,3,0,2,1:T(8,128)(2,1)S(1)}, bf16[2,1,1,128,256]{4,3,0,2,1:T(8,128)(2,1)S(1)}, u32[]{:S(2)}, u32[]{:S(2)}) collective-permute-start(bf16[2,1,1,128,256]{4,3,0,2,1:T(8,128)(2,1)S(1)} %maximum_select_fusion.6), channel_id=1, source_target_pairs={{0,8},{4,12},{8,0},{12,4},{16,24},{20,28},{24,16},{28,20},{1,9},{5... | collective-permute-start | bytes 393224 | tf_op jit(solution)/shard_map/ppermute | solution.py:24
  13.0 7.1 %collective-permute-start.3 = (bf16[2,2,1,128,256]{4,3,0,2,1:T(8,128)(2,1)S(1)}, bf16[2,2,1,128,256]{4,3,0,2,1:T(8,128)(2,1)S(1)}, u32[]{:S(2)}, u32[]{:S(2)}) collective-permute-start(bf16[2,2,1,128,256]{4,3,0,2,1:T(8,128)(2,1)S(1)} %maximum_select_fusion.3), channel_id=1, source_target_pairs={{0,4},{4,0},{8,12},{12,8},{16,20},{20,16},{24,28},{28,24},{1,5},{5... | collective-permute-start | bytes 786440 | tf_op jit(solution)/shard_map/ppermute | solution.py:24
  14.6 4.3 %collective-permute-start = (bf16[128,256]{1,0:T(8,128)(2,1)S(1)}, bf16[128,256]{1,0:T(8,128)(2,1)S(1)}, u32[]{:S(2)}, u32[]{:S(2)}) collective-permute-start(bf16[128,256]{1,0:T(8,128)(2,1)S(1)} %get-tuple-element.14), channel_id=1, source_target_pairs={{0,2},{1,3},{2,0},{3,1},{4,6},{5,7},{6,4},{7,5},{8,10},{9,11},{10,... | collective-permute-start | bytes 196616 | tf_op jit(solution)/shard_map/ppermute | solution.py:175
  20.2 7.4 %collective-permute-start.5 = (bf16[1,1,1,2,128,256]{5,4,3,2,1,0:T(8,128)(2,1)S(1)}, bf16[1,1,1,2,128,256]{5,4,3,2,1,0:T(8,128)(2,1)S(1)}, u32[]{:S(2)}, u32[]{:S(2)}) collective-permute-start(bf16[1,1,1,2,128,256]{5,4,3,2,1,0:T(8,128)(2,1)S(1)} %bitcast.34), channel_id=1, source_target_pairs={{0,16},{4,20},{8,24},{12,28},{16,0},{20,4},{24,8},{28,12},{1,17},{... | collective-permute-start | bytes 393224 | tf_op jit(solution)/shard_map/ppermute | solution.py:24
  27.6 6.4 %collective-permute-start.6 = (bf16[2,1,1,2,128,256]{5,4,3,2,1,0:T(8,128)(2,1)S(1)}, bf16[2,1,1,2,128,256]{5,4,3,2,1,0:T(8,128)(2,1)S(1)}, u32[]{:S(2)}, u32[]{:S(2)}) collective-permute-start(bf16[2,1,1,2,128,256]{5,4,3,2,1,0:T(8,128)(2,1)S(1)} %maximum_select_fusion.4), channel_id=1, source_target_pairs={{0,8},{4,12},{8,0},{12,4},{16,24},{20,28},{24,16},{28,20},{1,9},{5... | collective-permute-start | bytes 786440 | tf_op jit(solution)/shard_map/ppermute | solution.py:24
  34.1 10.0 %collective-permute-start.7 = (bf16[2,2,1,2,128,256]{5,4,3,2,1,0:T(8,128)(2,1)S(1)}, bf16[2,2,1,2,128,256]{5,4,3,2,1,0:T(8,128)(2,1)S(1)}, u32[]{:S(2)}, u32[]{:S(2)}) collective-permute-start(bf16[2,2,1,2,128,256]{5,4,3,2,1,0:T(8,128)(2,1)S(1)} %maximum_select_fusion.2), channel_id=1, source_target_pairs={{0,4},{4,0},{8,12},{12,8},{16,20},{20,16},{24,28},{28,24},{1,5},{5... | collective-permute-start | bytes 1572872 | tf_op jit(solution)/shard_map/ppermute | solution.py:24
  35.7 9.7 %collective-permute-start.4 = (bf16[1024,256]{1,0:T(8,128)(2,1)S(1)}, bf16[1024,256]{1,0:T(8,128)(2,1)S(1)}, u32[]{:S(2)}, u32[]{:S(2)}) collective-permute-start(bf16[1024,256]{1,0:T(8,128)(2,1)S(1)} %bitcast.25), channel_id=1, source_target_pairs={{0,2},{1,3},{2,0},{3,1},{4,6},{5,7},{6,4},{7,5},{8,10},{9,11},{10,... | collective-permute-start | bytes 1572872 | tf_op jit(solution)/shard_map/ppermute | solution.py:188
  45.4 6.1 %copy-start = (bf16[1024,512]{1,0:T(8,128)(2,1)S(1)}, bf16[1024,512]{1,0:T(8,128)(2,1)}, u32[]{:S(2)}) copy-start(bf16[1024,512]{1,0:T(8,128)(2,1)} %q_ref.1) | copy-start | bytes 3145732
  45.4 6.1 %copy-start.1 = (s32[8,32]{1,0:T(8,128)S(1)}, s32[8,32]{1,0:T(8,128)}, u32[]{:S(2)}) copy-start(s32[8,32]{1,0:T(8,128)} %bl_ref.1) | copy-start | bytes 3076
  45.4 6.1 %copy-start.2 = (s32[8]{0:T(128)S(1)}, s32[8]{0:T(128)}, u32[]{:S(2)}) copy-start(s32[8]{0:T(128)} %cnt_ref.1) | copy-start | bytes 100
  47.0 4.5 %collective-permute-start.8 = (bf16[4,1024,256]{2,1,0:T(8,128)(2,1)}, bf16[4,1024,256]{2,1,0:T(8,128)(2,1)}, u32[]{:S(2)}, u32[]{:S(2)}) collective-permute-start(bf16[4,1024,256]{2,1,0:T(8,128)(2,1)} %pad_maximum_fusion), channel_id=1, source_target_pairs={{0,1},{1,0},{2,3},{3,2},{4,5},{5,4},{6,7},{7,6},{8,9},{9,8},{10,11... | collective-permute-start | bytes 6291464 | tf_op jit(solution)/shard_map/ppermute | solution.py:191

commit v18 on v13

--- a/solution.py
+++ b/solution.py
@@ -41,14 +41,16 @@
     return [idx_pieces[x] for x in range(n)]
 
 
-def attend_kernel(bl_ref, cnt_ref, qb_ref, q_ref, *rest, n_local, n_pieces, n_ka, group, scale):
-    kv_pieces = rest[:n_pieces]
-    out_ref, off_ref, kvbuf, dbuf, sems, dsems = rest[n_pieces:]
+def attend_kernel(bl_ref, cnt_ref, qb_ref, q_ref, *rest, n_local, sources, n_refs, n_ka, group, scale):
+    n_pieces = len(sources)
+    kv_pieces = rest[:n_refs]
+    out_ref, off_ref, kvbuf, dbuf, sems, dsems = rest[n_refs:]
     qb0 = qb_ref[0]
     me = qb_ref[1]
     row0 = me * n_local
     width = kvbuf.shape[-1]
     per_piece = kv_pieces[0].shape[0] // BLK
+    assert sources[0] == (0, -1)
     n_half = n_pieces // n_ka
 
     class block_copy:
@@ -60,10 +62,16 @@
             within = self.blk % per_shard
             which = (within % n_half) * n_ka + jnp.bitwise_xor(self.blk // per_shard, me)
             start = pl.multiple_of((within // n_half) * BLK, BLK)
+            chunk = within // n_half
             for x in range(n_pieces):
                 @pl.when(which == x)
-                def _(x=x, start=start):
-                    pltpu.make_async_copy(kv_pieces[x].at[pl.ds(start, BLK), :], self.dst, self.sem).start()
+                def _(x=x, start=start, chunk=chunk):
+                    ref_i, pair = sources[x]
+                    if pair < 0:
+                        src = kv_pieces[ref_i].at[pl.ds(start, BLK), :]
+                    else:
+                        src = kv_pieces[ref_i].at[chunk, pair]
+                    pltpu.make_async_copy(src, self.dst, self.sem).start()
 
         def wait(self):
             pltpu.make_async_copy(kv_pieces[0].at[pl.ds(0, BLK), :], self.dst, self.sem).wait()
@@ -160,15 +168,15 @@
 def shards(queries, key_cache, value_cache, block_list, block_count, *, n_pb, n_ka):
     kv_local = jnp.concatenate([key_cache, value_cache], axis=1)
     n_half = kv_local.shape[0] // BLK
-    kv_pieces = []
-    shard = None
-    for h in range(n_half):
-        part = kv_local[h * BLK:(h + 1) * BLK]
-        if shard is not None:
-            part, shard = lax.optimization_barrier((part, shard))
-            kv_pieces += pieces_axis(shard, "ka", n_ka)
-        shard = gather_axis(part, "pb", n_pb)
-    kv_pieces += pieces_axis(shard, "ka", n_ka)
+    assert n_half == 2 and n_ka == 4
+    part0, part1 = kv_local[:BLK], kv_local[BLK:]
+    shard = gather_axis(part0, "pb", n_pb)
+    across = lax.ppermute(part1, "ka", [(i, i ^ 2) for i in range(n_ka)])
+    pair, shard = lax.optimization_barrier((jnp.stack([part1, across]), shard))
+    kv_pieces = pieces_axis(shard, "ka", n_ka)
+    both = gather_axis(pair, "pb", n_pb).reshape(n_pb, 2, BLK, part1.shape[1])
+    kv_pieces += [both, lax.ppermute(both, "ka", [(i, i ^ 1) for i in range(n_ka)])]
+    sources = [(x, -1) for x in range(n_ka)] + [(4, 0), (5, 0), (4, 1), (5, 1)]
 
     p = lax.axis_index("pb")
     k = lax.axis_index("ka")
@@ -178,7 +186,7 @@
     qb0 = jnp.stack([(p * n_ka + k) * n_local, k]).astype(jnp.int32)
 
     kernel = functools.partial(
-        attend_kernel, n_local=n_local, n_pieces=len(kv_pieces), n_ka=n_ka, group=16, scale=math.log2(math.e) / math.sqrt(HD)
+        attend_kernel, n_local=n_local, sources=tuple(sources), n_refs=len(kv_pieces), n_ka=n_ka, group=16, scale=math.log2(math.e) / math.sqrt(HD)
     )
     return pl.pallas_call(
         kernel,

time: 73 us -> 66.5 us (0.911)
  waiting for transfers between devices: 45.8 us -> 39 us
    ppermute x6 -> x3, waiting for transfers between devices: 15.6 us -> 3.7 us  [pieces_axis(): lax.ppermute(idx_pieces[x], axis, [(i, i ^ b) for i in range(n)])]
    ppermute x0 -> x2, waiting for transfers between devices: none -> 2.75 us  [the longest x1 2.75 us: shards(): across = lax.ppermute(part1, 'ka', [(i, i ^ 2) for i in range(n_ka)])]
    ppermute x6, waiting for transfers between devices: 30.2 us -> 32.5 us  [gather_axis(): other = lax.ppermute(held, axis, [(i, i ^ b) for i in range(n)])]
    ppermute x6 -> x3, starting transfers between devices: 3.62 us -> 2.02 us  [pieces_axis(): lax.ppermute(idx_pieces[x], axis, [(i, i ^ b) for i in range(n)])]
    ppermute x0 -> x2, starting transfers between devices: none -> 1.59 us  [the longest x1 1.52 us: shards(): across = lax.ppermute(part1, 'ka', [(i, i ^ 2) for i in range(n_ka)])]
  transfers between devices with their start and end apart: 12 -> 11, of which waited for: 9 -> 10; matrix products, arithmetic and copies ran while one was open for 0% -> 1% of each run, Pallas kernels for 0% -> 0%
where the time goes in v18:
time: 66.5 us; the launch traced here: 66 us
  waiting for transfers between devices  39 us (59%)
  Pallas kernels  17.8 us (27%)
  starting transfers between devices  7.34 us (11%)
  local copies, waits for them, and re-layouts  1.06 us (2%)
    ppermute x6, waiting for transfers between devices, gather_axis(): other = lax.ppermute(held, axis, [(i, i ^ b) for i in range(n)])  32.5 us
    pallas_call x1, Pallas kernels, shards(): pl.pallas_call(kernel, out_shape=jax.ShapeDtypeStruct((rows_mine, queries...  17.8 us
    ppermute x6, starting transfers between devices, gather_axis(): other = lax.ppermute(held, axis, [(i, i ^ b) for i in range(n)])  3.73 us
    ppermute x3, waiting for transfers between devices, pieces_axis(): lax.ppermute(idx_pieces[x], axis, [(i, i ^ b) for i in range(n)])  3.7 us
    ppermute x1, waiting for transfers between devices, shards(): across = lax.ppermute(part1, 'ka', [(i, i ^ 2) for i in range(n_ka)])  2.75 us
    ppermute x3, starting transfers between devices, pieces_axis(): lax.ppermute(idx_pieces[x], axis, [(i, i ^ b) for i in range(n)])  2.02 us
    ppermute x1, starting transfers between devices, shards(): across = lax.ppermute(part1, 'ka', [(i, i ^ 2) for i in range(n_ka)])  1.52 us
  transfers between devices with their start and end apart: 11, of which 10 were waited for; matrix products, arithmetic and copies ran while one was open for 1% of the time, Pallas kernels for 0%

profile of v18, /device:TPU:24, one launch (start us, length us, event | category | flops | bytes accessed | tf_op | source)
XLA Modules:
  0.0 66.0 jit_solution(18423871557227335076)
XLA Ops:
  0.0 0.0 copy-start.3
  0.0 0.9 %constant_dynamic-update-slice_fusion.1 = bf16[256,256]{1,0:T(8,128)(2,1)S(1)} fusion(bf16[256,128]{1,0:T(8,128)(2,1)} %param.6), kind=kLoop, calls=%fused_computation.14 | loop fusion | bytes 131072
  0.9 0.0 copy-done.3
  1.0 0.4 collective-permute-start.1
  1.4 5.7 %collective-permute-done.1 = bf16[1,1,1,128,256]{4,3,0,2,1:T(8,128)(2,1)S(1)} collective-permute-done((bf16[1,1,1,128,256]{4,3,0,2,1:T(8,128)(2,1)S(1)}, bf16[1,1,1,128,256]{4,3,0,2,1:T(8,128)(2,1)S(1)}, u32[]{:S(2)}, u32[]{:S(2)}) %collective-permute-start.1) | collective-permute-done | bytes 65568 | tf_op jit(solution)/shard_map/ppermute | solution.py:24
  7.1 0.1 collective-permute-start.2
  7.2 5.0 %collective-permute-done.2 = bf16[2,1,1,128,256]{4,3,0,2,1:T(8,128)(2,1)S(1)} collective-permute-done((bf16[2,1,1,128,256]{4,3,0,2,1:T(8,128)(2,1)S(1)}, bf16[2,1,1,128,256]{4,3,0,2,1:T(8,128)(2,1)S(1)}, u32[]{:S(2)}, u32[]{:S(2)}) %collective-permute-start.2) | collective-permute-done | bytes 131104 | tf_op jit(solution)/shard_map/ppermute | solution.py:24
  12.2 1.6 %collective-permute-start.3 = (bf16[2,2,1,128,256]{4,3,0,2,1:T(8,128)(2,1)S(1)}, bf16[2,2,1,128,256]{4,3,0,2,1:T(8,128)(2,1)S(1)}, u32[]{:S(2)}, u32[]{:S(2)}) collective-permute-start(bf16[2,2,1,128,256]{4,3,0,2,1:T(8,128)(2,1)S(1)} %maximum_select_fusion.3), channel_id=1, source_target_pairs={{0,4},{4,0},{8,12},{12,8},{16,20},{20,16},{24,28},{28,24},{1,5},{5... | collective-permute-start | bytes 786440 | tf_op jit(solution)/shard_map/ppermute | solution.py:24
  13.8 1.5 %collective-permute-start = (bf16[128,256]{1,0:T(8,128)(2,1)S(1)}, bf16[128,256]{1,0:T(8,128)(2,1)S(1)}, u32[]{:S(2)}, u32[]{:S(2)}) collective-permute-start(bf16[128,256]{1,0:T(8,128)(2,1)S(1)} %get-tuple-element.12), channel_id=1, source_target_pairs={{0,2},{1,3},{2,0},{3,1},{4,6},{5,7},{6,4},{7,5},{8,10},{9,11},{10,... | collective-permute-start | bytes 196616 | tf_op jit(solution)/shard_map/ppermute | solution.py:174
  15.3 2.7 %collective-permute-done = bf16[128,256]{1,0:T(8,128)(2,1)S(1)} collective-permute-done((bf16[128,256]{1,0:T(8,128)(2,1)S(1)}, bf16[128,256]{1,0:T(8,128)(2,1)S(1)}, u32[]{:S(2)}, u32[]{:S(2)}) %collective-permute-start) | collective-permute-done | bytes 65568 | tf_op jit(solution)/shard_map/ppermute | solution.py:174
  18.1 1.3 %collective-permute-done.3 = bf16[2,2,1,128,256]{4,3,0,2,1:T(8,128)(2,1)S(1)} collective-permute-done((bf16[2,2,1,128,256]{4,3,0,2,1:T(8,128)(2,1)S(1)}, bf16[2,2,1,128,256]{4,3,0,2,1:T(8,128)(2,1)S(1)}, u32[]{:S(2)}, u32[]{:S(2)}) %collective-permute-start.3) | collective-permute-done | bytes 262176 | tf_op jit(solution)/shard_map/ppermute | solution.py:24
  19.4 0.1 collective-permute-start.7
  19.5 7.3 %collective-permute-done.7 = bf16[1,1,1,2,128,256]{5,4,3,0,2,1:T(8,128)(2,1)S(1)} collective-permute-done((bf16[1,1,1,2,128,256]{5,4,3,0,2,1:T(8,128)(2,1)S(1)}, bf16[1,1,1,2,128,256]{5,4,3,0,2,1:T(8,128)(2,1)S(1)}, u32[]{:S(2)}, u32[]{:S(2)}) %collective-permute-start.7) | collective-permute-done | bytes 131104 | tf_op jit(solution)/shard_map/ppermute | solution.py:24
  26.9 0.1 collective-permute-start.8
  27.0 6.3 %collective-permute-done.8 = bf16[2,1,1,2,128,256]{5,4,3,0,2,1:T(8,128)(2,1)S(1)} collective-permute-done((bf16[2,1,1,2,128,256]{5,4,3,0,2,1:T(8,128)(2,1)S(1)}, bf16[2,1,1,2,128,256]{5,4,3,0,2,1:T(8,128)(2,1)S(1)}, u32[]{:S(2)}, u32[]{:S(2)}) %collective-permute-start.8) | collective-permute-done | bytes 262176 | tf_op jit(solution)/shard_map/ppermute | solution.py:24
  33.3 0.1 maximum_select_fusion.2
  33.4 1.6 %collective-permute-start.9 = (bf16[2,2,1,2,128,256]{5,4,3,0,2,1:T(8,128)(2,1)S(1)}, bf16[2,2,1,2,128,256]{5,4,3,0,2,1:T(8,128)(2,1)S(1)}, u32[]{:S(2)}, u32[]{:S(2)}) collective-permute-start(bf16[2,2,1,2,128,256]{5,4,3,0,2,1:T(8,128)(2,1)S(1)} %maximum_select_fusion.2), channel_id=1, source_target_pairs={{0,4},{4,0},{8,12},{12,8},{16,20},{20,16},{24,28},{28,24},{1,5},{5... | collective-permute-start | bytes 1572872 | tf_op jit(solution)/shard_map/ppermute | solution.py:24
  34.9 1.5 %collective-permute-start.5 = (bf16[1024,256]{1,0:T(8,128)(2,1)S(1)}, bf16[1024,256]{1,0:T(8,128)(2,1)S(1)}, u32[]{:S(2)}, u32[]{:S(2)}) collective-permute-start(bf16[1024,256]{1,0:T(8,128)(2,1)S(1)} %bitcast.21), channel_id=1, source_target_pairs={{0,2},{1,3},{2,0},{3,1},{4,6},{5,7},{6,4},{7,5},{8,10},{9,11},{10,... | collective-permute-start | bytes 1572872 | tf_op jit(solution)/shard_map/ppermute | solution.py:39
  36.4 6.9 %collective-permute-done.9 = bf16[2,2,1,2,128,256]{5,4,3,0,2,1:T(8,128)(2,1)S(1)} collective-permute-done((bf16[2,2,1,2,128,256]{5,4,3,0,2,1:T(8,128)(2,1)S(1)}, bf16[2,2,1,2,128,256]{5,4,3,0,2,1:T(8,128)(2,1)S(1)}, u32[]{:S(2)}, u32[]{:S(2)}) %collective-permute-start.9) | collective-permute-done | bytes 524320 | tf_op jit(solution)/shard_map/ppermute | solution.py:24
  43.4 0.1 maximum_select_fusion
  43.5 0.0 copy-start
  43.5 0.1 copy.7
  43.6 0.1 collective-permute-start.10
  43.7 0.5 collective-permute-start.4
  44.2 0.4 collective-permute-done.5.rest_2_
  44.6 0.0 collective-permute-start.6
  44.6 0.0 copy-start.1
  44.6 0.0 copy-start.2
  44.6 0.1 pad_add_fusion.qb_ref
  44.7 2.6 %collective-permute-done.4.rest_1_ = bf16[1024,256]{1,0:T(8,128)(2,1)} collective-permute-done((bf16[1024,256]{1,0:T(8,128)(2,1)S(1)}, bf16[1024,256]{1,0:T(8,128)(2,1)}, u32[]{:S(2)}, u32[]{:S(2)}) %collective-permute-start.4) | collective-permute-done | bytes 524320 | tf_op jit(solution)/shard_map/ppermute | solution.py:39
  47.2 0.7 %collective-permute-done.6.rest_3_ = bf16[1024,256]{1,0:T(8,128)(2,1)} collective-permute-done((bf16[1024,256]{1,0:T(8,128)(2,1)S(1)}, bf16[1024,256]{1,0:T(8,128)(2,1)}, u32[]{:S(2)}, u32[]{:S(2)}) %collective-permute-start.6) | collective-permute-done | bytes 524320 | tf_op jit(solution)/shard_map/ppermute | solution.py:39
  48.0 0.0 collective-permute-done.10.rest_5_
  48.0 0.0 copy-done
  48.0 0.0 copy-done.1
  48.0 0.0 copy-done.2
  48.0 17.8 %shard_map.55 = bf16[256,512]{1,0:T(8,128)(2,1)} custom-call(s32[8,32]{1,0:T(8,128)S(1)} %copy-done.1, s32[8]{0:T(128)S(1)} %copy-done.2, s32[2]{0:T(128)S(1)} %pad_add_fusion.qb_ref, bf16[1024,512]{1,0:T(8,128)(2,1)S(1)} %copy-done, bf16[1024,256]{1,0:T(8,128)(2,1)S(1)} %bitcast.23, bf16[1024,256]{1,0:T(8,128)(2,1)} %collective-permute-done.4.rest_1_, ...), custom_call_target="tpu_custom_call" | custom-call | tf_op jit(solution)/shard_map/pallas_call | solution.py:191
  (10 shorter events, 0.2 us)
Async XLA Ops:
  0.0 0.9 %copy-start.3 = (bf16[256,128]{1,0:T(8,128)(2,1)S(1)}, bf16[256,128]{1,0:T(8,128)(2,1)}, u32[]{:S(2)}) copy-start(bf16[256,128]{1,0:T(8,128)(2,1)} %param.7) | copy-start | bytes 196612
  1.0 6.1 %collective-permute-start.1 = (bf16[1,1,1,128,256]{4,3,0,2,1:T(8,128)(2,1)S(1)}, bf16[1,1,1,128,256]{4,3,0,2,1:T(8,128)(2,1)S(1)}, u32[]{:S(2)}, u32[]{:S(2)}) collective-permute-start(bf16[1,1,1,128,256]{4,3,0,2,1:T(8,128)(2,1)S(1)} %get-tuple-element.9), channel_id=1, source_target_pairs={{0,16},{4,20},{8,24},{12,28},{16,0},{20,4},{24,8},{28,12},{1,17},{... | collective-permute-start | bytes 196616 | tf_op jit(solution)/shard_map/ppermute | solution.py:24
  7.1 5.1 %collective-permute-start.2 = (bf16[2,1,1,128,256]{4,3,0,2,1:T(8,128)(2,1)S(1)}, bf16[2,1,1,128,256]{4,3,0,2,1:T(8,128)(2,1)S(1)}, u32[]{:S(2)}, u32[]{:S(2)}) collective-permute-start(bf16[2,1,1,128,256]{4,3,0,2,1:T(8,128)(2,1)S(1)} %maximum_select_fusion.6), channel_id=1, source_target_pairs={{0,8},{4,12},{8,0},{12,4},{16,24},{20,28},{24,16},{28,20},{1,9},{5... | collective-permute-start | bytes 393224 | tf_op jit(solution)/shard_map/ppermute | solution.py:24
  12.2 7.1 %collective-permute-start.3 = (bf16[2,2,1,128,256]{4,3,0,2,1:T(8,128)(2,1)S(1)}, bf16[2,2,1,128,256]{4,3,0,2,1:T(8,128)(2,1)S(1)}, u32[]{:S(2)}, u32[]{:S(2)}) collective-permute-start(bf16[2,2,1,128,256]{4,3,0,2,1:T(8,128)(2,1)S(1)} %maximum_select_fusion.3), channel_id=1, source_target_pairs={{0,4},{4,0},{8,12},{12,8},{16,20},{20,16},{24,28},{28,24},{1,5},{5... | collective-permute-start | bytes 786440 | tf_op jit(solution)/shard_map/ppermute | solution.py:24
  13.8 4.3 %collective-permute-start = (bf16[128,256]{1,0:T(8,128)(2,1)S(1)}, bf16[128,256]{1,0:T(8,128)(2,1)S(1)}, u32[]{:S(2)}, u32[]{:S(2)}) collective-permute-start(bf16[128,256]{1,0:T(8,128)(2,1)S(1)} %get-tuple-element.12), channel_id=1, source_target_pairs={{0,2},{1,3},{2,0},{3,1},{4,6},{5,7},{6,4},{7,5},{8,10},{9,11},{10,... | collective-permute-start | bytes 196616 | tf_op jit(solution)/shard_map/ppermute | solution.py:174
  19.4 7.4 %collective-permute-start.7 = (bf16[1,1,1,2,128,256]{5,4,3,0,2,1:T(8,128)(2,1)S(1)}, bf16[1,1,1,2,128,256]{5,4,3,0,2,1:T(8,128)(2,1)S(1)}, u32[]{:S(2)}, u32[]{:S(2)}) collective-permute-start(bf16[1,1,1,2,128,256]{5,4,3,0,2,1:T(8,128)(2,1)S(1)} %bitcast.24), channel_id=1, source_target_pairs={{0,16},{4,20},{8,24},{12,28},{16,0},{20,4},{24,8},{28,12},{1,17},{... | collective-permute-start | bytes 393224 | tf_op jit(solution)/shard_map/ppermute | solution.py:24
  26.9 6.4 %collective-permute-start.8 = (bf16[2,1,1,2,128,256]{5,4,3,0,2,1:T(8,128)(2,1)S(1)}, bf16[2,1,1,2,128,256]{5,4,3,0,2,1:T(8,128)(2,1)S(1)}, u32[]{:S(2)}, u32[]{:S(2)}) collective-permute-start(bf16[2,1,1,2,128,256]{5,4,3,0,2,1:T(8,128)(2,1)S(1)} %maximum_select_fusion.4), channel_id=1, source_target_pairs={{0,8},{4,12},{8,0},{12,4},{16,24},{20,28},{24,16},{28,20},{1,9},{5... | collective-permute-start | bytes 786440 | tf_op jit(solution)/shard_map/ppermute | solution.py:24
  33.4 10.0 %collective-permute-start.9 = (bf16[2,2,1,2,128,256]{5,4,3,0,2,1:T(8,128)(2,1)S(1)}, bf16[2,2,1,2,128,256]{5,4,3,0,2,1:T(8,128)(2,1)S(1)}, u32[]{:S(2)}, u32[]{:S(2)}) collective-permute-start(bf16[2,2,1,2,128,256]{5,4,3,0,2,1:T(8,128)(2,1)S(1)} %maximum_select_fusion.2), channel_id=1, source_target_pairs={{0,4},{4,0},{8,12},{12,8},{16,20},{20,16},{24,28},{28,24},{1,5},{5... | collective-permute-start | bytes 1572872 | tf_op jit(solution)/shard_map/ppermute | solution.py:24
  34.9 9.7 %collective-permute-start.5 = (bf16[1024,256]{1,0:T(8,128)(2,1)S(1)}, bf16[1024,256]{1,0:T(8,128)(2,1)S(1)}, u32[]{:S(2)}, u32[]{:S(2)}) collective-permute-start(bf16[1024,256]{1,0:T(8,128)(2,1)S(1)} %bitcast.21), channel_id=1, source_target_pairs={{0,2},{1,3},{2,0},{3,1},{4,6},{5,7},{6,4},{7,5},{8,10},{9,11},{10,... | collective-permute-start | bytes 1572872 | tf_op jit(solution)/shard_map/ppermute | solution.py:39
  43.5 4.5 %copy-start = (bf16[1024,512]{1,0:T(8,128)(2,1)S(1)}, bf16[1024,512]{1,0:T(8,128)(2,1)}, u32[]{:S(2)}) copy-start(bf16[1024,512]{1,0:T(8,128)(2,1)} %q_ref.1) | copy-start | bytes 3145732
  43.6 4.4 %collective-permute-start.10 = (bf16[8,2,128,256]{3,2,1,0:T(8,128)(2,1)S(1)}, bf16[8,2,128,256]{3,2,1,0:T(8,128)(2,1)}, u32[]{:S(2)}, u32[]{:S(2)}) collective-permute-start(bf16[8,2,128,256]{3,2,1,0:T(8,128)(2,1)S(1)} %bitcast.19), channel_id=1, source_target_pairs={{0,1},{1,0},{2,3},{3,2},{4,5},{5,4},{6,7},{7,6},{8,9},{9,8},{10,11... | collective-permute-start | bytes 3145736 | tf_op jit(solution)/shard_map/ppermute | solution.py:178
  43.7 3.5 %collective-permute-start.4 = (bf16[1024,256]{1,0:T(8,128)(2,1)S(1)}, bf16[1024,256]{1,0:T(8,128)(2,1)}, u32[]{:S(2)}, u32[]{:S(2)}) collective-permute-start(bf16[1024,256]{1,0:T(8,128)(2,1)S(1)} %bitcast.22), channel_id=1, source_target_pairs={{0,1},{1,0},{2,3},{3,2},{4,5},{5,4},{6,7},{7,6},{8,9},{9,8},{10,11... | collective-permute-start | bytes 1572872 | tf_op jit(solution)/shard_map/ppermute | solution.py:39
  44.6 3.4 %collective-permute-start.6 = (bf16[1024,256]{1,0:T(8,128)(2,1)S(1)}, bf16[1024,256]{1,0:T(8,128)(2,1)}, u32[]{:S(2)}, u32[]{:S(2)}) collective-permute-start(bf16[1024,256]{1,0:T(8,128)(2,1)S(1)} %collective-permute-done.5.rest_2_), channel_id=1, source_target_pairs={{0,1},{1,0},{2,3},{3,2},{4,5},{5,4},{6,7},{7,6},{8,9},{9,8},{10,11... | collective-permute-start | bytes 1572872 | tf_op jit(solution)/shard_map/ppermute | solution.py:39
  44.6 3.4 %copy-start.1 = (s32[8,32]{1,0:T(8,128)S(1)}, s32[8,32]{1,0:T(8,128)}, u32[]{:S(2)}) copy-start(s32[8,32]{1,0:T(8,128)} %bl_ref.1) | copy-start | bytes 3076
  44.6 3.4 %copy-start.2 = (s32[8]{0:T(128)S(1)}, s32[8]{0:T(128)}, u32[]{:S(2)}) copy-start(s32[8]{0:T(128)} %cnt_ref.1) | copy-start | bytes 100

commit v19 on v16

--- a/solution.py
+++ b/solution.py
@@ -158,12 +158,12 @@
 
 
 def shards(queries, key_cache, value_cache, block_list, block_count, *, n_pb, n_ka):
-    kv_local = jnp.concatenate([key_cache, value_cache], axis=1)
-    n_half = kv_local.shape[0] // BLK
+    n_half = key_cache.shape[0] // BLK
+    width2 = key_cache.shape[1] + value_cache.shape[1]
     kv_pieces = []
     shard = None
     for h in range(n_half):
-        part = kv_local[h * BLK:(h + 1) * BLK]
+        part = jnp.concatenate([key_cache[h * BLK:(h + 1) * BLK], value_cache[h * BLK:(h + 1) * BLK]], axis=1)
         if h % 2 == 0:
             shard = gather_axis(part, "pb", n_pb)
             continue
@@ -206,8 +206,8 @@
             out_specs=pl.BlockSpec((rows_mine, queries.shape[1]), lambda i, *_: (0, 0)),
             scratch_shapes=[
                 pltpu.SMEM((n_local, listed), jnp.int32),
-                pltpu.VMEM((n_local, listed, BLK, kv_local.shape[1] + HD), jnp.bfloat16),
-                pltpu.VMEM((n_local, BLK, kv_local.shape[1]), jnp.bfloat16),
+                pltpu.VMEM((n_local, listed, BLK, width2 + HD), jnp.bfloat16),
+                pltpu.VMEM((n_local, BLK, width2), jnp.bfloat16),
                 pltpu.SemaphoreType.DMA((n_local, listed)),
                 pltpu.SemaphoreType.DMA((n_local,)),
             ],

time: 64.9 us -> 64.8 us (level)
    unnamed x9 -> x6, local copies, waits for them, and re-layouts: 0.9 us -> 0.01 us
    slice x0 -> x1, local copies, waits for them, and re-layouts: none -> 0.82 us  [shards(): key_cache[h * BLK:(h + 1) * BLK]]
where the time goes in v19:
time: 64.8 us; the launch traced here: 64.3 us
  waiting for transfers between devices  37.3 us (58%)
  Pallas kernels  17.8 us (27%)
  starting transfers between devices  7.47 us (12%)
  local copies, waits for them, and re-layouts  0.95 us (1%)
    ppermute x6, waiting for transfers between devices, gather_axis(): other = lax.ppermute(held, axis, [(i, i ^ b) for i in range(n)])  29.7 us
    pallas_call x1, Pallas kernels, shards(): pl.pallas_call(kernel, out_shape=jax.ShapeDtypeStruct((rows_mine, queries...  17.8 us
    ppermute x6, starting transfers between devices, gather_axis(): other = lax.ppermute(held, axis, [(i, i ^ b) for i in range(n)])  3.73 us
    ppermute x1, waiting for transfers between devices, shards(): across = lax.ppermute(part, 'ka', [(i, i ^ b) for i in range(n_ka)])  2.75 us
    ppermute x3, waiting for transfers between devices, pieces_axis(): lax.ppermute(idx_pieces[x], axis, [(i, i ^ b) for i in range(n)])  2.7 us
    ppermute x2, waiting for transfers between devices, shards(): lax.ppermute(held[x], 'ka', [(i, i ^ step) for i in range(n_ka)])  2.19 us
    ppermute x3, starting transfers between devices, pieces_axis(): lax.ppermute(idx_pieces[x], axis, [(i, i ^ b) for i in range(n)])  1.59 us
    ppermute x1, starting transfers between devices, shards(): across = lax.ppermute(part, 'ka', [(i, i ^ b) for i in range(n_ka)])  1.58 us
  transfers between devices with their start and end apart: 12, of which 10 were waited for; matrix products, arithmetic and copies ran while one was open for 1% of the time, Pallas kernels for 0%

profile of v19, /device:TPU:24, one launch (start us, length us, event | category | flops | bytes accessed | tf_op | source)
XLA Modules:
  0.0 64.3 jit_solution(16829044721015135938)
XLA Ops:
  0.0 0.8 %fusion.6 = (bf16[128,128]{1,0:T(8,128)(2,1)S(1)}, bf16[128,128]{1,0:T(8,128)(2,1)S(1)}, bf16[128,128]{1,0:T(8,128)(2,1)S(1)}, bf16[128,128]{1,0:T(8,128)(2,1)S(1)}) fusion(bf16[256,128]{1,0:T(8,128)(2,1)} %param.6, bf16[256,128]{1,0:T(8,128)(2,1)} %param.7), kind=kLoop, calls=%fused_computation.18 | loop fusion | bytes 262144 | tf_op jit(solution)/shard_map/slice | solution.py:166
  0.8 0.4 collective-permute-start.1
  1.2 5.7 %collective-permute-done.1 = bf16[1,1,1,128,256]{4,3,0,2,1:T(8,128)(2,1)S(1)} collective-permute-done((bf16[1,1,1,128,256]{4,3,0,2,1:T(8,128)(2,1)S(1)}, bf16[1,1,1,128,256]{4,3,0,2,1:T(8,128)(2,1)S(1)}, u32[]{:S(2)}, u32[]{:S(2)}) %collective-permute-start.1) | collective-permute-done | bytes 65568 | tf_op jit(solution)/shard_map/ppermute | solution.py:24
  6.9 0.1 collective-permute-start.2
  7.1 5.0 %collective-permute-done.2 = bf16[2,1,1,128,256]{4,3,0,2,1:T(8,128)(2,1)S(1)} collective-permute-done((bf16[2,1,1,128,256]{4,3,0,2,1:T(8,128)(2,1)S(1)}, bf16[2,1,1,128,256]{4,3,0,2,1:T(8,128)(2,1)S(1)}, u32[]{:S(2)}, u32[]{:S(2)}) %collective-permute-start.2) | collective-permute-done | bytes 131104 | tf_op jit(solution)/shard_map/ppermute | solution.py:24
  12.1 1.6 %collective-permute-start.3 = (bf16[2,2,1,128,256]{4,3,0,2,1:T(8,128)(2,1)S(1)}, bf16[2,2,1,128,256]{4,3,0,2,1:T(8,128)(2,1)S(1)}, u32[]{:S(2)}, u32[]{:S(2)}) collective-permute-start(bf16[2,2,1,128,256]{4,3,0,2,1:T(8,128)(2,1)S(1)} %maximum_select_fusion.3), channel_id=1, source_target_pairs={{0,4},{4,0},{8,12},{12,8},{16,20},{20,16},{24,28},{28,24},{1,5},{5... | collective-permute-start | bytes 786440 | tf_op jit(solution)/shard_map/ppermute | solution.py:24
  13.7 1.6 %collective-permute-start = (bf16[128,256]{1,0:T(8,128)(2,1)S(1)}, bf16[128,256]{1,0:T(8,128)(2,1)S(1)}, u32[]{:S(2)}, u32[]{:S(2)}) collective-permute-start(bf16[128,256]{1,0:T(8,128)(2,1)S(1)} %get-tuple-element.18), channel_id=1, source_target_pairs={{0,2},{1,3},{2,0},{3,1},{4,6},{5,7},{6,4},{7,5},{8,10},{9,11},{10,... | collective-permute-start | bytes 196616 | tf_op jit(solution)/shard_map/ppermute | solution.py:171
  15.3 2.7 %collective-permute-done = bf16[128,256]{1,0:T(8,128)(2,1)S(1)} collective-permute-done((bf16[128,256]{1,0:T(8,128)(2,1)S(1)}, bf16[128,256]{1,0:T(8,128)(2,1)S(1)}, u32[]{:S(2)}, u32[]{:S(2)}) %collective-permute-start) | collective-permute-done | bytes 65568 | tf_op jit(solution)/shard_map/ppermute | solution.py:171
  18.0 1.2 %collective-permute-done.3 = bf16[2,2,1,128,256]{4,3,0,2,1:T(8,128)(2,1)S(1)} collective-permute-done((bf16[2,2,1,128,256]{4,3,0,2,1:T(8,128)(2,1)S(1)}, bf16[2,2,1,128,256]{4,3,0,2,1:T(8,128)(2,1)S(1)}, u32[]{:S(2)}, u32[]{:S(2)}) %collective-permute-start.3) | collective-permute-done | bytes 262176 | tf_op jit(solution)/shard_map/ppermute | solution.py:24
  19.3 0.1 collective-permute-start.7
  19.4 7.3 %collective-permute-done.7 = bf16[1,1,1,2,128,256]{5,4,3,2,1,0:T(8,128)(2,1)S(1)} collective-permute-done((bf16[1,1,1,2,128,256]{5,4,3,2,1,0:T(8,128)(2,1)S(1)}, bf16[1,1,1,2,128,256]{5,4,3,2,1,0:T(8,128)(2,1)S(1)}, u32[]{:S(2)}, u32[]{:S(2)}) %collective-permute-start.7) | collective-permute-done | bytes 131104 | tf_op jit(solution)/shard_map/ppermute | solution.py:24
  26.7 0.1 collective-permute-start.8
  26.8 1.6 %collective-permute-start.5 = (bf16[1024,256]{1,0:T(8,128)(2,1)S(1)}, bf16[1024,256]{1,0:T(8,128)(2,1)S(1)}, u32[]{:S(2)}, u32[]{:S(2)}) collective-permute-start(bf16[1024,256]{1,0:T(8,128)(2,1)S(1)} %bitcast.21), channel_id=1, source_target_pairs={{0,2},{1,3},{2,0},{3,1},{4,6},{5,7},{6,4},{7,5},{8,10},{9,11},{10,... | collective-permute-start | bytes 1572872 | tf_op jit(solution)/shard_map/ppermute | solution.py:39
  28.4 4.7 %collective-permute-done.8 = bf16[2,1,1,2,128,256]{5,4,3,2,1,0:T(8,128)(2,1)S(1)} collective-permute-done((bf16[2,1,1,2,128,256]{5,4,3,2,1,0:T(8,128)(2,1)S(1)}, bf16[2,1,1,2,128,256]{5,4,3,2,1,0:T(8,128)(2,1)S(1)}, u32[]{:S(2)}, u32[]{:S(2)}) %collective-permute-start.8) | collective-permute-done | bytes 262176 | tf_op jit(solution)/shard_map/ppermute | solution.py:24
  33.2 1.6 %collective-permute-start.9 = (bf16[2,2,1,2,128,256]{5,4,3,2,1,0:T(8,128)(2,1)S(1)}, bf16[2,2,1,2,128,256]{5,4,3,2,1,0:T(8,128)(2,1)S(1)}, u32[]{:S(2)}, u32[]{:S(2)}) collective-permute-start(bf16[2,2,1,2,128,256]{5,4,3,2,1,0:T(8,128)(2,1)S(1)} %maximum_select_fusion.2), channel_id=1, source_target_pairs={{0,4},{4,0},{8,12},{12,8},{16,20},{20,16},{24,28},{28,24},{1,5},{5... | collective-permute-start | bytes 1572872 | tf_op jit(solution)/shard_map/ppermute | solution.py:24
  34.8 0.0 collective-permute-start.4
  34.8 2.7 %collective-permute-done.5.rest_2_ = bf16[1024,256]{1,0:T(8,128)(2,1)S(1)} collective-permute-done((bf16[1024,256]{1,0:T(8,128)(2,1)S(1)}, bf16[1024,256]{1,0:T(8,128)(2,1)S(1)}, u32[]{:S(2)}, u32[]{:S(2)}) %collective-permute-start.5) | collective-permute-done | bytes 524320 | tf_op jit(solution)/shard_map/ppermute | solution.py:39
  37.5 0.0 collective-permute-start.6
  37.5 5.7 %collective-permute-done.9 = bf16[2,2,1,2,128,256]{5,4,3,2,1,0:T(8,128)(2,1)S(1)} collective-permute-done((bf16[2,2,1,2,128,256]{5,4,3,2,1,0:T(8,128)(2,1)S(1)}, bf16[2,2,1,2,128,256]{5,4,3,2,1,0:T(8,128)(2,1)S(1)}, u32[]{:S(2)}, u32[]{:S(2)}) %collective-permute-start.9) | collective-permute-done | bytes 524320 | tf_op jit(solution)/shard_map/ppermute | solution.py:24
  43.2 0.1 maximum_select_fusion
  43.3 0.0 copy-start
  43.4 0.1 fusion.5
  43.4 0.1 collective-permute-start.10
  43.5 0.5 collective-permute-start.11
  44.0 0.0 copy-start.1
  44.0 0.0 copy-start.2
  44.0 0.1 pad_add_fusion.qb_ref
  44.1 0.0 collective-permute-done.4.rest_1_
  44.1 0.0 collective-permute-done.6.rest_3_
  44.1 1.4 %collective-permute-done.10.rest_5_ = bf16[1024,256]{1,0:T(8,128)(2,1)} collective-permute-done((bf16[1024,256]{1,0:T(8,128)(2,1)S(1)}, bf16[1024,256]{1,0:T(8,128)(2,1)}, u32[]{:S(2)}, u32[]{:S(2)}) %collective-permute-start.10) | collective-permute-done | bytes 524320 | tf_op jit(solution)/shard_map/ppermute | solution.py:180
  45.6 0.7 %collective-permute-done.11.rest_7_ = bf16[1024,256]{1,0:T(8,128)(2,1)} collective-permute-done((bf16[1024,256]{1,0:T(8,128)(2,1)S(1)}, bf16[1024,256]{1,0:T(8,128)(2,1)}, u32[]{:S(2)}, u32[]{:S(2)}) %collective-permute-start.11) | collective-permute-done | bytes 524320 | tf_op jit(solution)/shard_map/ppermute | solution.py:180
  46.3 0.0 copy-done
  46.3 0.0 copy-done.1
  46.3 0.0 copy-done.2
  46.3 17.8 %shard_map.55 = bf16[256,512]{1,0:T(8,128)(2,1)} custom-call(s32[8,32]{1,0:T(8,128)S(1)} %copy-done.1, s32[8]{0:T(128)S(1)} %copy-done.2, s32[2]{0:T(128)S(1)} %pad_add_fusion.qb_ref, bf16[1024,512]{1,0:T(8,128)(2,1)S(1)} %copy-done, bf16[1024,256]{1,0:T(8,128)(2,1)S(1)} %bitcast.23, bf16[1024,256]{1,0:T(8,128)(2,1)} %collective-permute-done.4.rest_1_, ...), custom_call_target="tpu_custom_call" | custom-call | tf_op jit(solution)/shard_map/pallas_call | solution.py:196
  (11 shorter events, 0.3 us)
Async XLA Ops:
  0.8 6.1 %collective-permute-start.1 = (bf16[1,1,1,128,256]{4,3,0,2,1:T(8,128)(2,1)S(1)}, bf16[1,1,1,128,256]{4,3,0,2,1:T(8,128)(2,1)S(1)}, u32[]{:S(2)}, u32[]{:S(2)}) collective-permute-start(bf16[1,1,1,128,256]{4,3,0,2,1:T(8,128)(2,1)S(1)} %get-tuple-element.11), channel_id=1, source_target_pairs={{0,16},{4,20},{8,24},{12,28},{16,0},{20,4},{24,8},{28,12},{1,17},{... | collective-permute-start | bytes 196616 | tf_op jit(solution)/shard_map/ppermute | solution.py:24
  6.9 5.1 %collective-permute-start.2 = (bf16[2,1,1,128,256]{4,3,0,2,1:T(8,128)(2,1)S(1)}, bf16[2,1,1,128,256]{4,3,0,2,1:T(8,128)(2,1)S(1)}, u32[]{:S(2)}, u32[]{:S(2)}) collective-permute-start(bf16[2,1,1,128,256]{4,3,0,2,1:T(8,128)(2,1)S(1)} %maximum_select_fusion.6), channel_id=1, source_target_pairs={{0,8},{4,12},{8,0},{12,4},{16,24},{20,28},{24,16},{28,20},{1,9},{5... | collective-permute-start | bytes 393224 | tf_op jit(solution)/shard_map/ppermute | solution.py:24
  12.1 7.1 %collective-permute-start.3 = (bf16[2,2,1,128,256]{4,3,0,2,1:T(8,128)(2,1)S(1)}, bf16[2,2,1,128,256]{4,3,0,2,1:T(8,128)(2,1)S(1)}, u32[]{:S(2)}, u32[]{:S(2)}) collective-permute-start(bf16[2,2,1,128,256]{4,3,0,2,1:T(8,128)(2,1)S(1)} %maximum_select_fusion.3), channel_id=1, source_target_pairs={{0,4},{4,0},{8,12},{12,8},{16,20},{20,16},{24,28},{28,24},{1,5},{5... | collective-permute-start | bytes 786440 | tf_op jit(solution)/shard_map/ppermute | solution.py:24
  13.7 4.3 %collective-permute-start = (bf16[128,256]{1,0:T(8,128)(2,1)S(1)}, bf16[128,256]{1,0:T(8,128)(2,1)S(1)}, u32[]{:S(2)}, u32[]{:S(2)}) collective-permute-start(bf16[128,256]{1,0:T(8,128)(2,1)S(1)} %get-tuple-element.18), channel_id=1, source_target_pairs={{0,2},{1,3},{2,0},{3,1},{4,6},{5,7},{6,4},{7,5},{8,10},{9,11},{10,... | collective-permute-start | bytes 196616 | tf_op jit(solution)/shard_map/ppermute | solution.py:171
  19.3 7.4 %collective-permute-start.7 = (bf16[1,1,1,2,128,256]{5,4,3,2,1,0:T(8,128)(2,1)S(1)}, bf16[1,1,1,2,128,256]{5,4,3,2,1,0:T(8,128)(2,1)S(1)}, u32[]{:S(2)}, u32[]{:S(2)}) collective-permute-start(bf16[1,1,1,2,128,256]{5,4,3,2,1,0:T(8,128)(2,1)S(1)} %bitcast.29), channel_id=1, source_target_pairs={{0,16},{4,20},{8,24},{12,28},{16,0},{20,4},{24,8},{28,12},{1,17},{... | collective-permute-start | bytes 393224 | tf_op jit(solution)/shard_map/ppermute | solution.py:24
  26.7 6.4 %collective-permute-start.8 = (bf16[2,1,1,2,128,256]{5,4,3,2,1,0:T(8,128)(2,1)S(1)}, bf16[2,1,1,2,128,256]{5,4,3,2,1,0:T(8,128)(2,1)S(1)}, u32[]{:S(2)}, u32[]{:S(2)}) collective-permute-start(bf16[2,1,1,2,128,256]{5,4,3,2,1,0:T(8,128)(2,1)S(1)} %maximum_select_fusion.4), channel_id=1, source_target_pairs={{0,8},{4,12},{8,0},{12,4},{16,24},{20,28},{24,16},{28,20},{1,9},{5... | collective-permute-start | bytes 786440 | tf_op jit(solution)/shard_map/ppermute | solution.py:24
  26.8 10.7 %collective-permute-start.5 = (bf16[1024,256]{1,0:T(8,128)(2,1)S(1)}, bf16[1024,256]{1,0:T(8,128)(2,1)S(1)}, u32[]{:S(2)}, u32[]{:S(2)}) collective-permute-start(bf16[1024,256]{1,0:T(8,128)(2,1)S(1)} %bitcast.21), channel_id=1, source_target_pairs={{0,2},{1,3},{2,0},{3,1},{4,6},{5,7},{6,4},{7,5},{8,10},{9,11},{10,... | collective-permute-start | bytes 1572872 | tf_op jit(solution)/shard_map/ppermute | solution.py:39
  33.2 10.0 %collective-permute-start.9 = (bf16[2,2,1,2,128,256]{5,4,3,2,1,0:T(8,128)(2,1)S(1)}, bf16[2,2,1,2,128,256]{5,4,3,2,1,0:T(8,128)(2,1)S(1)}, u32[]{:S(2)}, u32[]{:S(2)}) collective-permute-start(bf16[2,2,1,2,128,256]{5,4,3,2,1,0:T(8,128)(2,1)S(1)} %maximum_select_fusion.2), channel_id=1, source_target_pairs={{0,4},{4,0},{8,12},{12,8},{16,20},{20,16},{24,28},{28,24},{1,5},{5... | collective-permute-start | bytes 1572872 | tf_op jit(solution)/shard_map/ppermute | solution.py:24
  34.8 9.3 %collective-permute-start.4 = (bf16[1024,256]{1,0:T(8,128)(2,1)S(1)}, bf16[1024,256]{1,0:T(8,128)(2,1)}, u32[]{:S(2)}, u32[]{:S(2)}) collective-permute-start(bf16[1024,256]{1,0:T(8,128)(2,1)S(1)} %bitcast.22), channel_id=1, source_target_pairs={{0,1},{1,0},{2,3},{3,2},{4,5},{5,4},{6,7},{7,6},{8,9},{9,8},{10,11... | collective-permute-start | bytes 1572872 | tf_op jit(solution)/shard_map/ppermute | solution.py:39
  37.5 6.6 %collective-permute-start.6 = (bf16[1024,256]{1,0:T(8,128)(2,1)S(1)}, bf16[1024,256]{1,0:T(8,128)(2,1)}, u32[]{:S(2)}, u32[]{:S(2)}) collective-permute-start(bf16[1024,256]{1,0:T(8,128)(2,1)S(1)} %collective-permute-done.5.rest_2_), channel_id=1, source_target_pairs={{0,1},{1,0},{2,3},{3,2},{4,5},{5,4},{6,7},{7,6},{8,9},{9,8},{10,11... | collective-permute-start | bytes 1572872 | tf_op jit(solution)/shard_map/ppermute | solution.py:39
  43.3 3.0 %copy-start = (bf16[1024,512]{1,0:T(8,128)(2,1)S(1)}, bf16[1024,512]{1,0:T(8,128)(2,1)}, u32[]{:S(2)}) copy-start(bf16[1024,512]{1,0:T(8,128)(2,1)} %q_ref.1) | copy-start | bytes 3145732
  43.4 2.1 %collective-permute-start.10 = (bf16[1024,256]{1,0:T(8,128)(2,1)S(1)}, bf16[1024,256]{1,0:T(8,128)(2,1)}, u32[]{:S(2)}, u32[]{:S(2)}) collective-permute-start(bf16[1024,256]{1,0:T(8,128)(2,1)S(1)} %bitcast.26), channel_id=1, source_target_pairs={{0,1},{1,0},{2,3},{3,2},{4,5},{5,4},{6,7},{7,6},{8,9},{9,8},{10,11... | collective-permute-start | bytes 1572872 | tf_op jit(solution)/shard_map/ppermute | solution.py:180
  43.5 2.8 %collective-permute-start.11 = (bf16[1024,256]{1,0:T(8,128)(2,1)S(1)}, bf16[1024,256]{1,0:T(8,128)(2,1)}, u32[]{:S(2)}, u32[]{:S(2)}) collective-permute-start(bf16[1024,256]{1,0:T(8,128)(2,1)S(1)} %bitcast.24), channel_id=1, source_target_pairs={{0,1},{1,0},{2,3},{3,2},{4,5},{5,4},{6,7},{7,6},{8,9},{9,8},{10,11... | collective-permute-start | bytes 1572872 | tf_op jit(solution)/shard_map/ppermute | solution.py:180
  44.0 2.3 %copy-start.1 = (s32[8,32]{1,0:T(8,128)S(1)}, s32[8,32]{1,0:T(8,128)}, u32[]{:S(2)}) copy-start(s32[8,32]{1,0:T(8,128)} %bl_ref.1) | copy-start | bytes 3076
  44.0 2.3 %copy-start.2 = (s32[8]{0:T(128)S(1)}, s32[8]{0:T(128)}, u32[]{:S(2)}) copy-start(s32[8]{0:T(128)} %cnt_ref.1) | copy-start | bytes 100

commit v20 on v16

--- a/solution.py
+++ b/solution.py
@@ -169,8 +169,10 @@
             continue
         b = n_ka // 2
         across = lax.ppermute(part, "ka", [(i, i ^ b) for i in range(n_ka)])
-        pair, shard = lax.optimization_barrier((jnp.stack([part, across]), shard))
-        kv_pieces += pieces_axis(shard, "ka", n_ka)
+        mate = lax.ppermute(shard, "ka", [(i, i ^ 1) for i in range(n_ka)])
+        pair, shard, mate = lax.optimization_barrier((jnp.stack([part, across]), shard, mate))
+        other = lax.ppermute(shard, "ka", [(i, i ^ b) for i in range(n_ka)])
+        kv_pieces += [shard, mate, other, lax.ppermute(other, "ka", [(i, i ^ 1) for i in range(n_ka)])]
         shard = None
         both = gather_axis(pair, "pb", n_pb).reshape(n_pb, 2, BLK, part.shape[1])
         held = {0: both[:, 0].reshape(-1, part.shape[1]), b: both[:, 1].reshape(-1, part.shape[1])}

time: 64.9 us -> 76 us (1.17)
  waiting for transfers between devices: 37.4 us -> 48.2 us
    ppermute x6, waiting for transfers between devices: 29.8 us -> 38.9 us  [gather_axis(): other = lax.ppermute(held, axis, [(i, i ^ b) for i in range(n)])]
    ppermute x3, waiting for transfers between devices: 2.7 us -> 4.2 us  [the longest x1 4.19 us: shards(): other = lax.ppermute(shard, 'ka', [(i, i ^ b) for i in range(n_ka)])]
  transfers between devices with their start and end apart: 12 -> 12, of which waited for: 10 -> 10; matrix products, arithmetic and copies ran while one was open for 1% -> 0% of each run, Pallas kernels for 0% -> 0%
where the time goes in v20:
time: 76 us; the launch traced here: 75.5 us
  waiting for transfers between devices  48.2 us (63%)
  Pallas kernels  17.9 us (24%)
  starting transfers between devices  7.54 us (10%)
  local copies, waits for them, and re-layouts  1.06 us (1%)
    ppermute x6, waiting for transfers between devices, gather_axis(): other = lax.ppermute(held, axis, [(i, i ^ b) for i in range(n)])  38.9 us
    pallas_call x1, Pallas kernels, shards(): pl.pallas_call(kernel, out_shape=jax.ShapeDtypeStruct((rows_mine, queries...  17.9 us
    ppermute x1, waiting for transfers between devices, shards(): other = lax.ppermute(shard, 'ka', [(i, i ^ b) for i in range(n_ka)])  4.19 us
    ppermute x6, starting transfers between devices, gather_axis(): other = lax.ppermute(held, axis, [(i, i ^ b) for i in range(n)])  3.73 us
    ppermute x1, waiting for transfers between devices, shards(): across = lax.ppermute(part, 'ka', [(i, i ^ b) for i in range(n_ka)])  2.91 us
    ppermute x2, waiting for transfers between devices, shards(): lax.ppermute(held[x], 'ka', [(i, i ^ step) for i in range(n_ka)])  2.2 us
    ppermute x1, starting transfers between devices, shards(): across = lax.ppermute(part, 'ka', [(i, i ^ b) for i in range(n_ka)])  1.58 us
    ppermute x1, starting transfers between devices, shards(): other = lax.ppermute(shard, 'ka', [(i, i ^ b) for i in range(n_ka)])  1.58 us
  transfers between devices with their start and end apart: 12, of which 10 were waited for; matrix products, arithmetic and copies ran while one was open for 0% of the time, Pallas kernels for 0%

profile of v20, /device:TPU:24, one launch (start us, length us, event | category | flops | bytes accessed | tf_op | source)
XLA Modules:
  0.0 75.5 jit_solution(7186193538925386345)
XLA Ops:
  0.0 0.0 copy-start.3
  0.0 0.9 %constant_dynamic-update-slice_fusion.1 = bf16[256,256]{1,0:T(8,128)(2,1)S(1)} fusion(bf16[256,128]{1,0:T(8,128)(2,1)} %param.6), kind=kLoop, calls=%fused_computation.14 | loop fusion | bytes 131072
  0.9 0.0 copy-done.3
  1.0 0.4 collective-permute-start.1
  1.4 5.7 %collective-permute-done.1 = bf16[1,1,1,128,256]{4,3,0,2,1:T(8,128)(2,1)S(1)} collective-permute-done((bf16[1,1,1,128,256]{4,3,0,2,1:T(8,128)(2,1)S(1)}, bf16[1,1,1,128,256]{4,3,0,2,1:T(8,128)(2,1)S(1)}, u32[]{:S(2)}, u32[]{:S(2)}) %collective-permute-start.1) | collective-permute-done | bytes 65568 | tf_op jit(solution)/shard_map/ppermute | solution.py:24
  7.1 0.1 collective-permute-start.2
  7.2 5.0 %collective-permute-done.2 = bf16[2,1,1,128,256]{4,3,0,2,1:T(8,128)(2,1)S(1)} collective-permute-done((bf16[2,1,1,128,256]{4,3,0,2,1:T(8,128)(2,1)S(1)}, bf16[2,1,1,128,256]{4,3,0,2,1:T(8,128)(2,1)S(1)}, u32[]{:S(2)}, u32[]{:S(2)}) %collective-permute-start.2) | collective-permute-done | bytes 131104 | tf_op jit(solution)/shard_map/ppermute | solution.py:24
  12.2 1.6 %collective-permute-start.3 = (bf16[2,2,1,128,256]{4,3,0,2,1:T(8,128)(2,1)S(1)}, bf16[2,2,1,128,256]{4,3,0,2,1:T(8,128)(2,1)S(1)}, u32[]{:S(2)}, u32[]{:S(2)}) collective-permute-start(bf16[2,2,1,128,256]{4,3,0,2,1:T(8,128)(2,1)S(1)} %maximum_select_fusion.3), channel_id=1, source_target_pairs={{0,4},{4,0},{8,12},{12,8},{16,20},{20,16},{24,28},{28,24},{1,5},{5... | collective-permute-start | bytes 786440 | tf_op jit(solution)/shard_map/ppermute | solution.py:24
  13.8 5.5 %collective-permute-done.3 = bf16[2,2,1,128,256]{4,3,0,2,1:T(8,128)(2,1)S(1)} collective-permute-done((bf16[2,2,1,128,256]{4,3,0,2,1:T(8,128)(2,1)S(1)}, bf16[2,2,1,128,256]{4,3,0,2,1:T(8,128)(2,1)S(1)}, u32[]{:S(2)}, u32[]{:S(2)}) %collective-permute-start.3) | collective-permute-done | bytes 262176 | tf_op jit(solution)/shard_map/ppermute | solution.py:24
  19.4 0.1 collective-permute-start.4
  19.5 1.6 %collective-permute-start = (bf16[128,256]{1,0:T(8,128)(2,1)S(1)}, bf16[128,256]{1,0:T(8,128)(2,1)S(1)}, u32[]{:S(2)}, u32[]{:S(2)}) collective-permute-start(bf16[128,256]{1,0:T(8,128)(2,1)S(1)} %get-tuple-element.16), channel_id=1, source_target_pairs={{0,2},{1,3},{2,0},{3,1},{4,6},{5,7},{6,4},{7,5},{8,10},{9,11},{10,... | collective-permute-start | bytes 196616 | tf_op jit(solution)/shard_map/ppermute | solution.py:171
  21.1 2.9 %collective-permute-done = bf16[128,256]{1,0:T(8,128)(2,1)S(1)} collective-permute-done((bf16[128,256]{1,0:T(8,128)(2,1)S(1)}, bf16[128,256]{1,0:T(8,128)(2,1)S(1)}, u32[]{:S(2)}, u32[]{:S(2)}) %collective-permute-start) | collective-permute-done | bytes 65568 | tf_op jit(solution)/shard_map/ppermute | solution.py:171
  24.0 0.0 collective-permute-done.4.rest_1_
  24.0 0.1 collective-permute-start.7
  24.1 8.7 %collective-permute-done.7 = bf16[1,1,1,2,128,256]{5,4,3,2,1,0:T(8,128)(2,1)S(1)} collective-permute-done((bf16[1,1,1,2,128,256]{5,4,3,2,1,0:T(8,128)(2,1)S(1)}, bf16[1,1,1,2,128,256]{5,4,3,2,1,0:T(8,128)(2,1)S(1)}, u32[]{:S(2)}, u32[]{:S(2)}) %collective-permute-start.7) | collective-permute-done | bytes 131104 | tf_op jit(solution)/shard_map/ppermute | solution.py:24
  32.8 0.1 collective-permute-start.8
  32.9 1.6 %collective-permute-start.5 = (bf16[1024,256]{1,0:T(8,128)(2,1)S(1)}, bf16[1024,256]{1,0:T(8,128)(2,1)}, u32[]{:S(2)}, u32[]{:S(2)}) collective-permute-start(bf16[1024,256]{1,0:T(8,128)(2,1)S(1)} %bitcast.22), channel_id=1, source_target_pairs={{0,2},{1,3},{2,0},{3,1},{4,6},{5,7},{6,4},{7,5},{8,10},{9,11},{10,... | collective-permute-start | bytes 1572872 | tf_op jit(solution)/shard_map/ppermute | solution.py:174
  34.5 6.6 %collective-permute-done.8 = bf16[2,1,1,2,128,256]{5,4,3,2,1,0:T(8,128)(2,1)S(1)} collective-permute-done((bf16[2,1,1,2,128,256]{5,4,3,2,1,0:T(8,128)(2,1)S(1)}, bf16[2,1,1,2,128,256]{5,4,3,2,1,0:T(8,128)(2,1)S(1)}, u32[]{:S(2)}, u32[]{:S(2)}) %collective-permute-start.8) | collective-permute-done | bytes 262176 | tf_op jit(solution)/shard_map/ppermute | solution.py:24
  41.2 1.6 %collective-permute-start.9 = (bf16[2,2,1,2,128,256]{5,4,3,2,1,0:T(8,128)(2,1)S(1)}, bf16[2,2,1,2,128,256]{5,4,3,2,1,0:T(8,128)(2,1)S(1)}, u32[]{:S(2)}, u32[]{:S(2)}) collective-permute-start(bf16[2,2,1,2,128,256]{5,4,3,2,1,0:T(8,128)(2,1)S(1)} %maximum_select_fusion.2), channel_id=1, source_target_pairs={{0,4},{4,0},{8,12},{12,8},{16,20},{20,16},{24,28},{28,24},{1,5},{5... | collective-permute-start | bytes 1572872 | tf_op jit(solution)/shard_map/ppermute | solution.py:24
  42.7 4.2 %collective-permute-done.5.rest_2_ = bf16[1024,256]{1,0:T(8,128)(2,1)} collective-permute-done((bf16[1024,256]{1,0:T(8,128)(2,1)S(1)}, bf16[1024,256]{1,0:T(8,128)(2,1)}, u32[]{:S(2)}, u32[]{:S(2)}) %collective-permute-start.5) | collective-permute-done | bytes 524320 | tf_op jit(solution)/shard_map/ppermute | solution.py:174
  46.9 0.0 collective-permute-start.6
  46.9 7.4 %collective-permute-done.9 = bf16[2,2,1,2,128,256]{5,4,3,2,1,0:T(8,128)(2,1)S(1)} collective-permute-done((bf16[2,2,1,2,128,256]{5,4,3,2,1,0:T(8,128)(2,1)S(1)}, bf16[2,2,1,2,128,256]{5,4,3,2,1,0:T(8,128)(2,1)S(1)}, u32[]{:S(2)}, u32[]{:S(2)}) %collective-permute-start.9) | collective-permute-done | bytes 524320 | tf_op jit(solution)/shard_map/ppermute | solution.py:24
  54.3 0.1 maximum_select_fusion
  54.4 0.0 copy-start
  54.4 0.1 fusion.2
  54.5 0.1 collective-permute-start.10
  54.6 0.5 collective-permute-start.11
  55.1 0.0 copy-start.1
  55.1 0.0 copy-start.2
  55.1 0.1 pad_add_fusion.qb_ref
  55.2 0.0 collective-permute-done.6.rest_3_
  55.2 1.4 %collective-permute-done.10.rest_5_ = bf16[1024,256]{1,0:T(8,128)(2,1)} collective-permute-done((bf16[1024,256]{1,0:T(8,128)(2,1)S(1)}, bf16[1024,256]{1,0:T(8,128)(2,1)}, u32[]{:S(2)}, u32[]{:S(2)}) %collective-permute-start.10) | collective-permute-done | bytes 524320 | tf_op jit(solution)/shard_map/ppermute | solution.py:182
  56.6 0.7 collective-permute-done.11.rest_7_
  57.4 0.0 copy-done
  57.4 0.0 copy-done.1
  57.4 0.0 copy-done.2
  57.4 17.9 %shard_map.55 = bf16[256,512]{1,0:T(8,128)(2,1)} custom-call(s32[8,32]{1,0:T(8,128)S(1)} %copy-done.1, s32[8]{0:T(128)S(1)} %copy-done.2, s32[2]{0:T(128)S(1)} %pad_add_fusion.qb_ref, bf16[1024,512]{1,0:T(8,128)(2,1)S(1)} %copy-done, bf16[1024,256]{1,0:T(8,128)(2,1)S(1)} %bitcast.23, bf16[1024,256]{1,0:T(8,128)(2,1)S(1)} %collective-permute-done.4.rest_1_, ...), custom_call_target="tpu_custom_call" | custom-call | tf_op jit(solution)/shard_map/pallas_call | solution.py:198
  (11 shorter events, 0.3 us)
Async XLA Ops:
  0.0 0.9 %copy-start.3 = (bf16[256,128]{1,0:T(8,128)(2,1)S(1)}, bf16[256,128]{1,0:T(8,128)(2,1)}, u32[]{:S(2)}) copy-start(bf16[256,128]{1,0:T(8,128)(2,1)} %param.7) | copy-start | bytes 196612
  1.0 6.1 %collective-permute-start.1 = (bf16[1,1,1,128,256]{4,3,0,2,1:T(8,128)(2,1)S(1)}, bf16[1,1,1,128,256]{4,3,0,2,1:T(8,128)(2,1)S(1)}, u32[]{:S(2)}, u32[]{:S(2)}) collective-permute-start(bf16[1,1,1,128,256]{4,3,0,2,1:T(8,128)(2,1)S(1)} %get-tuple-element.13), channel_id=1, source_target_pairs={{0,16},{4,20},{8,24},{12,28},{16,0},{20,4},{24,8},{28,12},{1,17},{... | collective-permute-start | bytes 196616 | tf_op jit(solution)/shard_map/ppermute | solution.py:24
  7.1 5.1 %collective-permute-start.2 = (bf16[2,1,1,128,256]{4,3,0,2,1:T(8,128)(2,1)S(1)}, bf16[2,1,1,128,256]{4,3,0,2,1:T(8,128)(2,1)S(1)}, u32[]{:S(2)}, u32[]{:S(2)}) collective-permute-start(bf16[2,1,1,128,256]{4,3,0,2,1:T(8,128)(2,1)S(1)} %maximum_select_fusion.6), channel_id=1, source_target_pairs={{0,8},{4,12},{8,0},{12,4},{16,24},{20,28},{24,16},{28,20},{1,9},{5... | collective-permute-start | bytes 393224 | tf_op jit(solution)/shard_map/ppermute | solution.py:24
  12.2 7.1 %collective-permute-start.3 = (bf16[2,2,1,128,256]{4,3,0,2,1:T(8,128)(2,1)S(1)}, bf16[2,2,1,128,256]{4,3,0,2,1:T(8,128)(2,1)S(1)}, u32[]{:S(2)}, u32[]{:S(2)}) collective-permute-start(bf16[2,2,1,128,256]{4,3,0,2,1:T(8,128)(2,1)S(1)} %maximum_select_fusion.3), channel_id=1, source_target_pairs={{0,4},{4,0},{8,12},{12,8},{16,20},{20,16},{24,28},{28,24},{1,5},{5... | collective-permute-start | bytes 786440 | tf_op jit(solution)/shard_map/ppermute | solution.py:24
  19.4 4.6 %collective-permute-start.4 = (bf16[1024,256]{1,0:T(8,128)(2,1)S(1)}, bf16[1024,256]{1,0:T(8,128)(2,1)S(1)}, u32[]{:S(2)}, u32[]{:S(2)}) collective-permute-start(bf16[1024,256]{1,0:T(8,128)(2,1)S(1)} %bitcast.21), channel_id=1, source_target_pairs={{0,1},{1,0},{2,3},{3,2},{4,5},{5,4},{6,7},{7,6},{8,9},{9,8},{10,11... | collective-permute-start | bytes 1572872 | tf_op jit(solution)/shard_map/ppermute | solution.py:172
  19.5 4.5 %collective-permute-start = (bf16[128,256]{1,0:T(8,128)(2,1)S(1)}, bf16[128,256]{1,0:T(8,128)(2,1)S(1)}, u32[]{:S(2)}, u32[]{:S(2)}) collective-permute-start(bf16[128,256]{1,0:T(8,128)(2,1)S(1)} %get-tuple-element.16), channel_id=1, source_target_pairs={{0,2},{1,3},{2,0},{3,1},{4,6},{5,7},{6,4},{7,5},{8,10},{9,11},{10,... | collective-permute-start | bytes 196616 | tf_op jit(solution)/shard_map/ppermute | solution.py:171
  24.0 8.7 %collective-permute-start.7 = (bf16[1,1,1,2,128,256]{5,4,3,2,1,0:T(8,128)(2,1)S(1)}, bf16[1,1,1,2,128,256]{5,4,3,2,1,0:T(8,128)(2,1)S(1)}, u32[]{:S(2)}, u32[]{:S(2)}) collective-permute-start(bf16[1,1,1,2,128,256]{5,4,3,2,1,0:T(8,128)(2,1)S(1)} %bitcast.29), channel_id=1, source_target_pairs={{0,16},{4,20},{8,24},{12,28},{16,0},{20,4},{24,8},{28,12},{1,17},{... | collective-permute-start | bytes 393224 | tf_op jit(solution)/shard_map/ppermute | solution.py:24
  32.8 8.3 %collective-permute-start.8 = (bf16[2,1,1,2,128,256]{5,4,3,2,1,0:T(8,128)(2,1)S(1)}, bf16[2,1,1,2,128,256]{5,4,3,2,1,0:T(8,128)(2,1)S(1)}, u32[]{:S(2)}, u32[]{:S(2)}) collective-permute-start(bf16[2,1,1,2,128,256]{5,4,3,2,1,0:T(8,128)(2,1)S(1)} %maximum_select_fusion.4), channel_id=1, source_target_pairs={{0,8},{4,12},{8,0},{12,4},{16,24},{20,28},{24,16},{28,20},{1,9},{5... | collective-permute-start | bytes 786440 | tf_op jit(solution)/shard_map/ppermute | solution.py:24
  32.9 14.0 %collective-permute-start.5 = (bf16[1024,256]{1,0:T(8,128)(2,1)S(1)}, bf16[1024,256]{1,0:T(8,128)(2,1)}, u32[]{:S(2)}, u32[]{:S(2)}) collective-permute-start(bf16[1024,256]{1,0:T(8,128)(2,1)S(1)} %bitcast.22), channel_id=1, source_target_pairs={{0,2},{1,3},{2,0},{3,1},{4,6},{5,7},{6,4},{7,5},{8,10},{9,11},{10,... | collective-permute-start | bytes 1572872 | tf_op jit(solution)/shard_map/ppermute | solution.py:174
  41.2 13.2 %collective-permute-start.9 = (bf16[2,2,1,2,128,256]{5,4,3,2,1,0:T(8,128)(2,1)S(1)}, bf16[2,2,1,2,128,256]{5,4,3,2,1,0:T(8,128)(2,1)S(1)}, u32[]{:S(2)}, u32[]{:S(2)}) collective-permute-start(bf16[2,2,1,2,128,256]{5,4,3,2,1,0:T(8,128)(2,1)S(1)} %maximum_select_fusion.2), channel_id=1, source_target_pairs={{0,4},{4,0},{8,12},{12,8},{16,20},{20,16},{24,28},{28,24},{1,5},{5... | collective-permute-start | bytes 1572872 | tf_op jit(solution)/shard_map/ppermute | solution.py:24
  46.9 8.3 %collective-permute-start.6 = (bf16[1024,256]{1,0:T(8,128)(2,1)}, bf16[1024,256]{1,0:T(8,128)(2,1)}, u32[]{:S(2)}, u32[]{:S(2)}) collective-permute-start(bf16[1024,256]{1,0:T(8,128)(2,1)} %collective-permute-done.5.rest_2_), channel_id=1, source_target_pairs={{0,1},{1,0},{2,3},{3,2},{4,5},{5,4},{6,7},{7,6},{8,9},{9,8},{10,11... | collective-permute-start | bytes 1572872 | tf_op jit(solution)/shard_map/ppermute | solution.py:175
  54.4 3.0 %copy-start = (bf16[1024,512]{1,0:T(8,128)(2,1)S(1)}, bf16[1024,512]{1,0:T(8,128)(2,1)}, u32[]{:S(2)}) copy-start(bf16[1024,512]{1,0:T(8,128)(2,1)} %q_ref.1) | copy-start | bytes 3145732
  54.5 2.1 %collective-permute-start.10 = (bf16[1024,256]{1,0:T(8,128)(2,1)S(1)}, bf16[1024,256]{1,0:T(8,128)(2,1)}, u32[]{:S(2)}, u32[]{:S(2)}) collective-permute-start(bf16[1024,256]{1,0:T(8,128)(2,1)S(1)} %bitcast.26), channel_id=1, source_target_pairs={{0,1},{1,0},{2,3},{3,2},{4,5},{5,4},{6,7},{7,6},{8,9},{9,8},{10,11... | collective-permute-start | bytes 1572872 | tf_op jit(solution)/shard_map/ppermute | solution.py:182
  54.6 2.8 %collective-permute-start.11 = (bf16[1024,256]{1,0:T(8,128)(2,1)S(1)}, bf16[1024,256]{1,0:T(8,128)(2,1)}, u32[]{:S(2)}, u32[]{:S(2)}) collective-permute-start(bf16[1024,256]{1,0:T(8,128)(2,1)S(1)} %bitcast.24), channel_id=1, source_target_pairs={{0,1},{1,0},{2,3},{3,2},{4,5},{5,4},{6,7},{7,6},{8,9},{9,8},{10,11... | collective-permute-start | bytes 1572872 | tf_op jit(solution)/shard_map/ppermute | solution.py:182
  55.1 2.3 %copy-start.1 = (s32[8,32]{1,0:T(8,128)S(1)}, s32[8,32]{1,0:T(8,128)}, u32[]{:S(2)}) copy-start(s32[8,32]{1,0:T(8,128)} %bl_ref.1) | copy-start | bytes 3076
  55.1 2.3 %copy-start.2 = (s32[8]{0:T(128)S(1)}, s32[8]{0:T(128)}, u32[]{:S(2)}) copy-start(s32[8]{0:T(128)} %cnt_ref.1) | copy-start | bytes 100
